TPU v7x, 32 devices: a whole 2x2x4 slice. The times are simulated.
32 devices in a mesh: clip: 2 (over x), gx: 8 (over z, y), gy: 2 (over core).
Axes of the slice: x: 2, y: 2, z: 4, core: 2. Of those that a mesh axis runs over, the one named last changes fastest.
Arguments:
- e_field: float32 [3, 128, 128, 128], P(None, ('clip', 'gx'), 'gy'), parts along dimension 1, may hold values from -6 to 6
- h_field: float32 [3, 128, 128, 128], P(None, ('clip', 'gx'), 'gy'), parts along dimension 1, may hold values from -6 to 6
- material: int32 [128, 128, 128], P(('clip', 'gx'), 'gy'), parts along dimension 0, may hold values from 0 to 5
- eps_table: float32 [6], replicated, may hold values from 0.8 to 1.2
- sigma_table: float32 [6], replicated, may hold values from 0 to 2
- angle_orders: int32 [64, 2], replicated, may hold values from -8 to 8
Outputs:
- e_out: float32 [3, 128, 128, 128], P(None, ('clip', 'gx'), 'gy'), parts along dimension 1
- h_out: float32 [3, 128, 128, 128], P(None, ('clip', 'gx'), 'gy'), parts along dimension 1
- far_field: float32 [128, 4], P(('clip', 'gx')), parts along dimension 0
There are 2 independent parts, one for each index of `clip`. A program takes and returns all parts, laid end to end along the dimension named above; an argument that names none is the same for every part. Nothing has to cross between parts.
All inputs are finite; a program needn't handle non-finite values.
Results may differ from a plain program's by a relative error of at most 0.00021.
Values sent between devices are 32-bit elements; how exact they have to be, the bound alone decides.
No kernel may reach another device: no remote copies, remote signals or barrier semaphores. Data moves between devices by JAX's collectives and lax.ppermute only.
A program may use at most 64 MiB of HBM per device.

v0:
```python
import math

import jax
import jax.numpy as jnp
from jax import lax
from jax.sharding import PartitionSpec as P

ITERS = 4


TIME_STEP = 0.5
PHASE_STEP = 0.9


def shifted(value, axis, steps):
    count = lax.axis_size(axis)
    pairs = [(source, (source + steps) % count) for source in range(count)]
    return lax.ppermute(value, axis, pairs)


def forward_z(field):
    upper = jnp.concatenate([field[..., 1:], jnp.zeros_like(field[..., :1])], axis=-1)
    return upper - field


def backward_z(field):
    lower = jnp.concatenate([jnp.zeros_like(field[..., :1]), field[..., :-1]], axis=-1)
    return field - lower


def coefficients(material, eps_table, sigma_table):
    count = eps_table.shape[0]
    labels = jnp.arange(count, dtype=jnp.int32).reshape(count, 1, 1, 1)
    onehot = (material[None] == labels).astype(jnp.float32)
    permit = jnp.sum(onehot * eps_table.reshape(count, 1, 1, 1), axis=0)
    conduct = jnp.sum(onehot * sigma_table.reshape(count, 1, 1, 1), axis=0)
    loss = conduct * TIME_STEP / (2.0 * permit)
    keep = (1.0 - loss) / (1.0 + loss)
    drive = TIME_STEP / (permit * (1.0 + loss))
    return (keep, drive)


def split_step(elec, magn, keep, drive):
    ahead_x = shifted(elec[1:3, 0:1], "gx", -1)
    ahead_y = shifted(jnp.stack([elec[0, :, 0:1], elec[2, :, 0:1]]), "gy", -1)
    ext_x = jnp.concatenate([elec[1:3], ahead_x], axis=1)
    diff_x = ext_x[:, 1:] - ext_x[:, :-1]
    ext_y = jnp.concatenate([jnp.stack([elec[0], elec[2]]), ahead_y], axis=2)
    diff_y = ext_y[:, :, 1:] - ext_y[:, :, :-1]
    magn_x = magn[0] - TIME_STEP * (diff_y[1] - forward_z(elec[1]))
    magn_y = magn[1] - TIME_STEP * (forward_z(elec[0]) - diff_x[1])
    magn_z = magn[2] - TIME_STEP * (diff_x[0] - diff_y[0])
    magn = jnp.stack([magn_x, magn_y, magn_z])
    behind_x = shifted(magn[1:3, -1:], "gx", 1)
    behind_y = shifted(jnp.stack([magn[0, :, -1:], magn[2, :, -1:]]), "gy", 1)
    back_x = jnp.concatenate([behind_x, magn[1:3]], axis=1)
    bdiff_x = back_x[:, 1:] - back_x[:, :-1]
    back_y = jnp.concatenate([behind_y, jnp.stack([magn[0], magn[2]])], axis=2)
    bdiff_y = back_y[:, :, 1:] - back_y[:, :, :-1]
    elec_x = keep * elec[0] + drive * (bdiff_y[1] - backward_z(magn[1]))
    elec_y = keep * elec[1] + drive * (backward_z(magn[0]) - bdiff_x[1])
    elec_z = keep * elec[2] + drive * (bdiff_x[0] - bdiff_y[0])
    return (jnp.stack([elec_x, elec_y, elec_z]), magn)


def local(e_field, h_field, material, eps_table, sigma_table, angle_orders):
    keep, drive = coefficients(material, eps_table, sigma_table)
    cells_x = e_field.shape[1]
    cells_y = e_field.shape[2]
    depth = e_field.shape[3]
    elec = e_field
    magn = h_field
    mon_real = jnp.zeros((2, cells_x, cells_y), jnp.float32)
    mon_imag = jnp.zeros((2, cells_x, cells_y), jnp.float32)
    for number in range(ITERS):
        elec, magn = split_step(elec, magn, keep, drive)
        plane = elec[0:2, :, :, depth - 3]
        mon_real = mon_real + math.cos(PHASE_STEP * (number + 1)) * plane
        mon_imag = mon_imag - math.sin(PHASE_STEP * (number + 1)) * plane
    size_x = lax.axis_size("gx")
    size_y = lax.axis_size("gy")
    total_x = cells_x * size_x
    total_y = cells_y * size_y
    pos_x = lax.axis_index("gx") * cells_x + jnp.arange(cells_x, dtype=jnp.int32)
    pos_y = lax.axis_index("gy") * cells_y + jnp.arange(cells_y, dtype=jnp.int32)
    flat_real = mon_real.reshape(2, cells_x * cells_y).T
    flat_imag = mon_imag.reshape(2, cells_x * cells_y).T
    high = lax.Precision.HIGHEST
    angle_count = angle_orders.shape[0]
    owned = angle_count // size_x
    scale = 1.0 / math.sqrt(total_x * total_y)
    order_x = angle_orders[:, 0]
    order_y = angle_orders[:, 1]
    phase_int = (
        order_x[:, None, None] * pos_x[None, :, None] * total_y
        + order_y[:, None, None] * pos_y[None, None, :] * total_x
    ) % (total_x * total_y)
    theta = phase_int.astype(jnp.float32) * (2.0 * math.pi / (total_x * total_y))
    cosine = jnp.cos(theta).reshape(owned * lax.axis_size("gx"), cells_x * cells_y)
    sine = jnp.sin(theta).reshape(owned * lax.axis_size("gx"), cells_x * cells_y)
    real_part = jnp.dot(
        cosine, flat_real, precision=high, preferred_element_type=jnp.float32
    ) + jnp.dot(sine, flat_imag, precision=high, preferred_element_type=jnp.float32)
    imag_part = jnp.dot(
        cosine, flat_imag, precision=high, preferred_element_type=jnp.float32
    ) - jnp.dot(sine, flat_real, precision=high, preferred_element_type=jnp.float32)
    rows_sum = lax.psum_scatter(
        jnp.stack([real_part[:, 0], imag_part[:, 0], real_part[:, 1], imag_part[:, 1]], axis=1),
        "gx",
        scatter_dimension=0,
        tiled=True,
    )
    far_field = lax.psum(rows_sum, "gy") * scale
    return (elec, magn, far_field)


def solution(mesh):
    return jax.shard_map(
        local,
        mesh=mesh,
        in_specs=(
            P(None, ("clip", "gx"), "gy", None),
            P(None, ("clip", "gx"), "gy", None),
            P(("clip", "gx"), "gy", None),
            P(),
            P(),
            P(),
        ),
        out_specs=(
            P(None, ("clip", "gx"), "gy", None),
            P(None, ("clip", "gx"), "gy", None),
            P(("clip", "gx"), None),
        ),
        check_vma=False,
    )
```

profile of v0, /device:TPU:0, one launch (start us, length us, event | category | flops | bytes accessed | tf_op | source)
XLA Modules:
  0.0 148.8 jit_solution(9321898635787207260)
XLA Ops:
  0.6 0.9 fusion.125
  2.0 0.8 slice.357
  3.0 5.6 %collective-permute-start.1 = (f32[2,1,64,128]{2,1,3,0:T(1,128)S(1)}, f32[2,1,64,128]{2,1,3,0:T(1,128)S(1)}, u32[]{:S(2)}, u32[]{:S(2)}) collective-permute-start(f32[2,1,64,128]{2,1,3,0:T(1,128)S(1)} %copy.141), channel_id=1, source_target_pairs={{0,14},{2,0},{4,2},{6,4},{8,6},{10,8},{12,10},{14,12},{1,15},{3,1}... | collective-permute-start | bytes 196616 | tf_op jit(solution)/shard_map/ppermute | solution.py:18
  8.6 1.2 fusion.124
  9.8 1.0 copy.179
  11.4 1.3 copy.180
  13.7 1.0 copy.174
  15.0 0.9 slice.453
  17.7 0.9 copy-done.48
  18.9 2.0 %fusion.16 = f32[2,8,64,128]{2,1,3,0:T(8,128)S(1)} fusion(f32[2,8,64,128]{2,1,3,0:T(8,128)} %copy.180, f32[2,1,64,128]{2,1,3,0:T(1,128)S(1)} %collective-permute-done.1), kind=kLoop, calls=%fused_computation.82 | loop fusion | flops 262144 | bytes 1114112 | tf_op jit(solution)/shard_map/sub | solution.py:47
  21.1 1.0 slice.457
  23.0 1.2 copy.143
  25.1 1.0 copy.129
  26.9 0.9 slice.461
  27.8 1.3 copy.144
  29.1 2.4 %collective-permute-done.3 = f32[2,1,64,128]{2,1,3,0:T(1,128)S(1)} collective-permute-done((f32[2,1,64,128]{2,1,3,0:T(1,128)}, f32[2,1,64,128]{2,1,3,0:T(1,128)S(1)}, u32[]{:S(2)}, u32[]{:S(2)}) %collective-permute-start.3) | collective-permute-done | bytes 65568 | tf_op jit(solution)/shard_map/ppermute | solution.py:18
  31.5 1.7 %fusion.15 = (f32[2,8,64,128]{2,1,3,0:T(8,128)S(1)}, f32[2,8,64,128]{2,1,3,0:T(8,128)S(1)}) fusion(f32[1,8,64,128]{2,1,3,0:T(8,128)S(1)} %fusion.80, f32[1,8,64,128]{2,1,3,0:T(8,128)S(1)} %bitcast.241, f32[2,1,64,128]{2,1,3,0:T(1,128)S(1)} %collective-permute-done.3, f32[1,8,64,128]{2,1,3,0:T(8,128)S(1)} %bitcast.239, f32[2,8,1,128]{2,1,3,0:T(8,128)} %copy.144), kind=kLoop, calls=%fused_computation.52 | loop fusion | flops 1048576 | bytes 1908736 | tf_op jit(solution)/shard_map/sub | solution.py:57
  33.3 1.3 fusion.72
  35.2 1.6 %fusion.67 = (f32[8,64,128]{1,0,2:T(8,128)S(1)}, f32[8,64,128]{1,0,2:T(8,128)S(1)}, f32[8,64,128]{1,0,2:T(8,128)S(1)}) fusion(f32[2,8,64,128]{2,1,3,0:T(8,128)S(1)} %get-tuple-element.51, f32[8,64,128]{1,0,2:T(8,128)S(1)} %fusion.83, f32[8,64,127]{1,0,2:T(8,128)S(1)} %copy-done.59, f32[1,8,64,128]{2,1,3,0:T(8,128)S(1)} %copy-done.45, ...), kind=kLoop, calls=%fused_computation.153 | loop fusion | flops 851968 | bytes 2357248 | tf_op jit(solution)/shard_map/add | solution.py:61
  36.9 2.3 %collective-permute-start.5 = (f32[2,1,64,128]{2,1,3,0:T(1,128)S(1)}, f32[2,1,64,128]{2,1,3,0:T(1,128)S(1)}, u32[]{:S(2)}, u32[]{:S(2)}) collective-permute-start(f32[2,1,64,128]{2,1,3,0:T(1,128)S(1)} %fusion.94), channel_id=1, source_target_pairs={{0,14},{2,0},{4,2},{6,4},{8,6},{10,8},{12,10},{14,12},{1,15},{3,1}... | collective-permute-start | bytes 196616 | tf_op jit(solution)/shard_map/ppermute | solution.py:18
  39.4 1.5 %fusion.78 = f32[8,64,128]{1,0,2:T(8,128)S(1)} fusion(f32[8,64,128]{1,0,2:T(8,128)S(1)} %get-tuple-element.21, f32[2,8,64,128]{2,1,3,0:T(8,128)} %copy-done.50, f32[8,64,128]{1,0,2:T(8,128)S(1)} %fusion.75, f32[8,64,127]{1,0,2:T(8,128)} %slice.461, f32[8,64,128]{1,0,2:T(8,128)S(1)} %get-tuple-element.20, f32[1,8,64,128]{2,1,3,0:T(8,128)} %copy-done.37), kind=kLoop, calls=%fused_computation.168 | loop fusion | flops 327680 | bytes 1832960 | tf_op jit(solution)/shard_map/add | solution.py:60
  42.4 1.3 copy.149
  43.7 2.0 %fusion.13 = (f32[2,8,64,128]{2,1,3,0:T(8,128)S(1)}, f32[2,8,64,128]{2,1,3,0:T(8,128)S(1)}) fusion(f32[1,8,64,128]{2,1,3,0:T(8,128)S(1)} %copy-done.35, f32[1,8,64,128]{2,1,3,0:T(8,128)S(1)} %bitcast.225, f32[2,1,64,128]{2,1,3,0:T(1,128)S(1)} %collective-permute-done.5, f32[1,8,64,128]{2,1,3,0:T(8,128)S(1)} %bitcast.228, f32[2,8,1,128]{2,1,3,0:T(8,128)} %copy.149), kind=kLoop, calls=%fused_computation.50 | loop fusion | flops 1048576 | bytes 1908736 | tf_op jit(solution)/shard_map/sub | solution.py:47
  49.8 1.3 copy.152
  51.2 3.9 %collective-permute-done.7 = f32[2,1,64,128]{2,1,3,0:T(1,128)S(1)} collective-permute-done((f32[2,1,64,128]{2,1,3,0:T(1,128)S(1)}, f32[2,1,64,128]{2,1,3,0:T(1,128)S(1)}, u32[]{:S(2)}, u32[]{:S(2)}) %collective-permute-start.7) | collective-permute-done | bytes 65568 | tf_op jit(solution)/shard_map/ppermute | solution.py:18
  55.1 1.7 %fusion.11 = (f32[2,8,64,128]{2,1,3,0:T(8,128)S(1)}, f32[2,8,64,128]{2,1,3,0:T(8,128)S(1)}) fusion(f32[1,8,64,128]{2,1,3,0:T(8,128)S(1)} %copy-done.28, f32[1,8,64,128]{2,1,3,0:T(8,128)S(1)} %bitcast.235, f32[2,1,64,128]{2,1,3,0:T(1,128)S(1)} %collective-permute-done.7, f32[1,8,64,128]{2,1,3,0:T(8,128)S(1)} %bitcast.237, f32[2,8,1,128]{2,1,3,0:T(8,128)} %copy.152), kind=kLoop, calls=%fused_computation.48 | loop fusion | flops 1048576 | bytes 1908736 | tf_op jit(solution)/shard_map/sub | solution.py:57
  57.1 0.8 copy-done.14
  59.3 1.0 collective-permute-start.9
  60.3 1.2 copy.154
  61.9 0.8 slice.499
  63.6 1.3 copy.155
  64.9 2.0 %fusion.9 = (f32[2,8,64,128]{2,1,3,0:T(8,128)S(1)}, f32[2,8,64,128]{2,1,3,0:T(8,128)S(1)}) fusion(f32[1,8,64,128]{2,1,3,0:T(8,128)S(1)} %copy-done.31, f32[1,8,64,128]{2,1,3,0:T(8,128)S(1)} %bitcast.213, f32[2,1,64,128]{2,1,3,0:T(1,128)S(1)} %collective-permute-done.9, f32[1,8,64,128]{2,1,3,0:T(8,128)S(1)} %bitcast.216, f32[2,8,1,128]{2,1,3,0:T(8,128)} %copy.155), kind=kLoop, calls=%fused_computation.46 | loop fusion | flops 1048576 | bytes 1908736 | tf_op jit(solution)/shard_map/sub | solution.py:47
  67.0 0.9 copy-done.64
  68.1 1.0 slice.497
  69.3 1.3 collective-permute-start.11
  70.8 1.4 copy.157
  72.2 1.0 slice.496
  73.2 1.2 copy.156
  74.7 0.9 slice.509
  76.4 1.3 copy.158
  77.9 2.3 %fusion.7 = (f32[2,8,64,128]{2,1,3,0:T(8,128)S(1)}, f32[2,8,64,128]{2,1,3,0:T(8,128)S(1)}) fusion(f32[1,8,64,128]{2,1,3,0:T(8,128)} %copy-done.25, f32[1,8,64,128]{2,1,3,0:T(8,128)S(1)} %bitcast.231, f32[2,1,64,128]{2,1,3,0:T(1,128)S(1)} %collective-permute-done.11, f32[1,8,64,128]{2,1,3,0:T(8,128)S(1)} %bitcast.233, f32[2,8,1,128]{2,1,3,0:T(8,128)} %copy.158), kind=kLoop, calls=%fused_computation.44 | loop fusion | flops 1048576 | bytes 1908736 | tf_op jit(solution)/shard_map/sub | solution.py:57
  80.5 0.8 copy-done.1
  83.0 3.4 %collective-permute-start.13 = (f32[2,1,64,128]{2,1,3,0:T(1,128)S(1)}, f32[2,1,64,128]{2,1,3,0:T(1,128)S(1)}, u32[]{:S(2)}, u32[]{:S(2)}) collective-permute-start(f32[2,1,64,128]{2,1,3,0:T(1,128)S(1)} %fusion.90), channel_id=1, source_target_pairs={{0,14},{2,0},{4,2},{6,4},{8,6},{10,8},{12,10},{14,12},{1,15},{3,1}... | collective-permute-start | bytes 196616 | tf_op jit(solution)/shard_map/ppermute | solution.py:18
  86.4 1.2 copy.160
  90.9 1.3 copy.161
  92.3 2.5 %fusion.5 = (f32[2,8,64,128]{2,1,3,0:T(8,128)S(1)}, f32[2,8,64,128]{2,1,3,0:T(8,128)S(1)}) fusion(f32[1,8,64,128]{2,1,3,0:T(8,128)} %copy-done.21, f32[1,8,64,128]{2,1,3,0:T(8,128)S(1)} %bitcast.219, f32[2,1,64,128]{2,1,3,0:T(1,128)S(1)} %collective-permute-done.13, f32[1,8,64,128]{2,1,3,0:T(8,128)S(1)} %bitcast.222, f32[2,8,1,128]{2,1,3,0:T(8,128)} %copy.161), kind=kLoop, calls=%fused_computation.42 | loop fusion | flops 1048576 | bytes 1908736 | tf_op jit(solution)/shard_map/sub | solution.py:47
  94.8 0.9 copy-done.2
  96.1 1.0 slice.517
  97.7 0.9 fusion.38
  98.6 1.2 copy.163
  99.9 2.1 %slice.516 = f32[1,8,1,128]{2,1,3,0:T(8,128)} slice(f32[1,8,64,128]{2,1,3,0:T(8,128)} %bitcast.245), slice={[0:1], [0:8], [63:64], [0:128]} | slice | bytes 8192 | tf_op jit(solution)/shard_map/slice | solution.py:55
  101.9 1.2 copy.162
  103.7 2.6 %pad_maximum_fusion.1 = f32[3,8,64,128]{2,1,3,0:T(8,128)} fusion(f32[1,8,64,128]{2,1,3,0:T(8,128)} %copy-done.33, f32[1,8,64,128]{2,1,3,0:T(8,128)} %bitcast.243, f32[1,8,64,128]{2,1,3,0:T(8,128)} %bitcast.246), kind=kLoop, calls=%fused_computation.1 | loop fusion | flops 393216 | bytes 1572864 | tf_op jit(solution)/shard_map/stack | solution.py:53
  108.0 2.7 %copy.170 = f32[3,8,64,128]{3,2,1,0:T(8,128)} copy(f32[3,8,64,128]{2,1,3,0:T(8,128)} %pad_maximum_fusion.1) | data formatting | bytes 1572864
  110.8 1.3 copy.164
  112.1 3.0 %fusion.3 = (f32[2,8,64,128]{2,1,3,0:T(8,128)S(1)}, f32[2,8,64,128]{2,1,3,0:T(8,128)S(1)}) fusion(f32[1,8,64,128]{2,1,3,0:T(8,128)} %copy-done.33, f32[1,8,64,128]{2,1,3,0:T(8,128)} %bitcast.244, f32[2,1,64,128]{2,1,3,0:T(1,128)S(1)} %collective-permute-done.15, f32[1,8,64,128]{2,1,3,0:T(8,128)} %bitcast.247, f32[2,8,1,128]{2,1,3,0:T(8,128)} %copy.164), kind=kLoop, calls=%fused_computation.40 | loop fusion | flops 1048576 | bytes 1908736 | tf_op jit(solution)/shard_map/sub | solution.py:57
  115.3 0.8 copy-done.10
  117.4 1.4 copy.169
  118.8 1.3 convolution_bitcast_fusion.3
  120.2 1.3 convolution_bitcast_fusion.1
  121.5 1.4 fusion.1
  122.8 1.4 fusion
  124.3 21.4 %all-reduce.16 = f32[64,4]{0,1:T(4,128)S(1)} all-reduce(f32[64,4]{0,1:T(4,128)S(1)} %pad_maximum_fusion.59), channel_id=2, replica_groups=mesh['clip'=2,'gx'=8,'gy'=2] {'gx'}, use_global_device_ids=true, to_apply=%region_2.3.clone | all-reduce | flops 256 | bytes 2048
  145.8 2.4 %psum.7 = f32[8,4]{0,1:T(4,128)S(1)} all-reduce(f32[8,4]{0,1:T(4,128)S(1)} %constant_dynamic-slice_fusion), channel_id=1, replica_groups=mesh['clip'=2,'gx'=8,'gy'=2] {'gy'}, use_global_device_ids=true, to_apply=%region_3.4 | all-reduce | flops 32 | bytes 256 | tf_op jit(solution)/shard_map/psum | solution.py:113
  (244 shorter events, 28.2 us)
Async XLA Ops:
  0.6 9.1 %copy-start.67 = (f32[3,8,64,128]{3,2,1,0:T(8,128)S(1)}, f32[3,8,64,128]{3,2,1,0:T(8,128)}, u32[]{:S(2)}) copy-start(f32[3,8,64,128]{3,2,1,0:T(8,128)} %param.7) | copy-start | bytes 2359300
  1.5 14.4 %collective-permute-start = (f32[2,8,1,128]{3,1,2,0:T(8,128)S(1)}, f32[2,8,1,128]{3,1,2,0:T(8,128)S(1)}, u32[]{:S(2)}, u32[]{:S(2)}) collective-permute-start(f32[2,8,1,128]{3,1,2,0:T(8,128)S(1)} %pad_maximum_fusion.51), channel_id=1, source_target_pairs={{0,1},{1,0},{2,3},{3,2},{4,5},{5,4},{6,7},{7,6},{8,9},{9,8},{10,11... | collective-permute-start | bytes 24584 | tf_op jit(solution)/shard_map/ppermute | solution.py:18
  3.0 16.0 %collective-permute-start.1 = (f32[2,1,64,128]{2,1,3,0:T(1,128)S(1)}, f32[2,1,64,128]{2,1,3,0:T(1,128)S(1)}, u32[]{:S(2)}, u32[]{:S(2)}) collective-permute-start(f32[2,1,64,128]{2,1,3,0:T(1,128)S(1)} %copy.141), channel_id=1, source_target_pairs={{0,14},{2,0},{4,2},{6,4},{8,6},{10,8},{12,10},{14,12},{1,15},{3,1}... | collective-permute-start | bytes 196616 | tf_op jit(solution)/shard_map/ppermute | solution.py:18
  9.8 1.5 %slice-start = ((f32[3,8,64,128]{3,2,1,0:T(8,128)}), f32[2,8,64,128]{3,2,1,0:T(8,128)S(1)}, s32[]{:S(2)}) async-start(f32[3,8,64,128]{3,2,1,0:T(8,128)} %param.6), calls=%async_computation | async-start | bytes 1048576 | tf_op jit(solution)/shard_map/slice | solution.py:46
  11.3 10.7 %copy-start.37 = (f32[1,8,64,128]{2,1,3,0:T(8,128)}, f32[1,8,64,128]{2,1,3,0:T(8,128)S(1)}, u32[]{:S(2)}) copy-start(f32[1,8,64,128]{2,1,3,0:T(8,128)S(1)} %copy.173) | copy-start | bytes 786436
  15.0 2.0 %copy-start.44 = (f32[1,8,64,128]{2,1,3,0:T(8,128)}, f32[1,8,64,128]{2,1,3,0:T(8,128)S(1)}, u32[]{:S(2)}) copy-start(f32[1,8,64,128]{2,1,3,0:T(8,128)S(1)} %copy.178) | copy-start | bytes 786436
  18.7 2.2 %copy-start.52 = (f32[1,8,64,128]{2,1,3,0:T(8,128)S(1)}, f32[1,8,64,128]{2,1,3,0:T(8,128)}, u32[]{:S(2)}) copy-start(f32[1,8,64,128]{2,1,3,0:T(8,128)} %copy.179) | copy-start | bytes 786436
  18.9 2.0 %copy-start.49 = (f32[2,8,64,128]{2,1,3,0:T(8,128)S(1)}, f32[2,8,64,128]{2,1,3,0:T(8,128)}, u32[]{:S(2)}) copy-start(f32[2,8,64,128]{2,1,3,0:T(8,128)} %copy-done.48) | copy-start | bytes 1572868
  21.1 10.5 %copy-start.23 = (f32[1,8,64,128]{2,1,3,0:T(8,128)}, f32[1,8,64,128]{2,1,3,0:T(8,128)S(1)}, u32[]{:S(2)}) copy-start(f32[1,8,64,128]{2,1,3,0:T(8,128)S(1)} %fusion.80) | copy-start | bytes 786436
  22.1 2.4 %copy-start.68 = (s32[8,64,128]{2,1,0:T(8,128)S(1)}, s32[8,64,128]{2,1,0:T(8,128)}, u32[]{:S(2)}) copy-start(s32[8,64,128]{2,1,0:T(8,128)} %param.8) | copy-start | bytes 786436
  22.2 2.3 %copy-start.70 = (f32[6]{0:T(128)S(1)}, f32[6]{0:T(128)}, u32[]{:S(2)}) copy-start(f32[6]{0:T(128)} %param.10) | copy-start | bytes 76
  22.2 2.3 %copy-start.71 = (f32[6]{0:T(128)S(1)}, f32[6]{0:T(128)}, u32[]{:S(2)}) copy-start(f32[6]{0:T(128)} %param.9) | copy-start | bytes 76
  23.0 8.5 %collective-permute-start.3 = (f32[2,1,64,128]{2,1,3,0:T(1,128)}, f32[2,1,64,128]{2,1,3,0:T(1,128)S(1)}, u32[]{:S(2)}, u32[]{:S(2)}) collective-permute-start(f32[2,1,64,128]{2,1,3,0:T(1,128)} %fusion.95), channel_id=1, source_target_pairs={{0,2},{2,4},{4,6},{6,8},{8,10},{10,12},{12,14},{14,0},{1,3},{3,5},... | collective-permute-start | bytes 196616 | tf_op jit(solution)/shard_map/ppermute | solution.py:18
  24.2 3.5 %collective-permute-start.2 = (f32[2,8,1,128]{3,1,2,0:T(8,128)S(1)}, f32[2,8,1,128]{3,1,2,0:T(8,128)S(1)}, u32[]{:S(2)}, u32[]{:S(2)}) collective-permute-start(f32[2,8,1,128]{3,1,2,0:T(8,128)S(1)} %pad_maximum_fusion.52), channel_id=1, source_target_pairs={{0,1},{1,0},{2,3},{3,2},{4,5},{5,4},{6,7},{7,6},{8,9},{9,8},{10,11... | collective-permute-start | bytes 24584 | tf_op jit(solution)/shard_map/ppermute | solution.py:18
  25.0 8.2 %copy-start.46 = (f32[8,64,128]{1,0,2:T(8,128)}, f32[8,64,128]{1,0,2:T(8,128)S(1)}, u32[]{:S(2)}) copy-start(f32[8,64,128]{1,0,2:T(8,128)S(1)} %copy.130) | copy-start | bytes 786436
  29.1 4.2 %copy-start.47 = (f32[8,64,128]{1,0,2:T(8,128)S(1)}, f32[8,64,128]{1,0,2:T(8,128)}, u32[]{:S(2)}) copy-start(f32[8,64,128]{1,0,2:T(8,128)} %copy.129) | copy-start | bytes 786436
  33.3 1.9 %copy-start.59 = (f32[8,64,127]{1,0,2:T(8,128)S(1)}, f32[8,64,127]{1,0,2:T(8,128)}, u32[]{:S(2)}) copy-start(f32[8,64,127]{1,0,2:T(8,128)} %slice.469) | copy-start | bytes 780292
  35.2 4.0 %copy-start.34 = (f32[1,8,64,128]{2,1,3,0:T(8,128)}, f32[1,8,64,128]{2,1,3,0:T(8,128)S(1)}, u32[]{:S(2)}) copy-start(f32[1,8,64,128]{2,1,3,0:T(8,128)S(1)} %get-tuple-element.22) | copy-start | bytes 786436
  36.8 4.1 %copy-start.13 = (f32[8,64,128]{1,0,2:T(8,128)}, f32[8,64,128]{1,0,2:T(8,128)S(1)}, u32[]{:S(2)}) copy-start(f32[8,64,128]{1,0,2:T(8,128)S(1)} %get-tuple-element.20) | copy-start | bytes 786436
  36.8 4.1 %copy-start.17 = (f32[8,64,128]{1,0,2:T(8,128)}, f32[8,64,128]{1,0,2:T(8,128)S(1)}, u32[]{:S(2)}) copy-start(f32[8,64,128]{1,0,2:T(8,128)S(1)} %get-tuple-element.21) | copy-start | bytes 786436
  36.9 6.8 %collective-permute-start.5 = (f32[2,1,64,128]{2,1,3,0:T(1,128)S(1)}, f32[2,1,64,128]{2,1,3,0:T(1,128)S(1)}, u32[]{:S(2)}, u32[]{:S(2)}) collective-permute-start(f32[2,1,64,128]{2,1,3,0:T(1,128)S(1)} %fusion.94), channel_id=1, source_target_pairs={{0,14},{2,0},{4,2},{6,4},{8,6},{10,8},{12,10},{14,12},{1,15},{3,1}... | collective-permute-start | bytes 196616 | tf_op jit(solution)/shard_map/ppermute | solution.py:18
  39.4 2.0 %copy-start.69 = (s32[64,2]{0,1:T(2,128)S(1)}, s32[64,2]{0,1:T(2,128)}, u32[]{:S(2)}) copy-start(s32[64,2]{0,1:T(2,128)} %param.11) | copy-start | bytes 1540
  41.1 1.2 collective-permute-start.4
  41.4 2.3 %copy-start.35 = (f32[1,8,64,128]{2,1,3,0:T(8,128)S(1)}, f32[1,8,64,128]{2,1,3,0:T(8,128)}, u32[]{:S(2)}) copy-start(f32[1,8,64,128]{2,1,3,0:T(8,128)} %copy-done.34) | copy-start | bytes 786436
  43.7 2.0 %copy-start.24 = (f32[1,8,64,128]{2,1,3,0:T(8,128)S(1)}, f32[1,8,64,128]{2,1,3,0:T(8,128)}, u32[]{:S(2)}) copy-start(f32[1,8,64,128]{2,1,3,0:T(8,128)} %copy-done.23) | copy-start | bytes 786436
  46.7 8.4 %collective-permute-start.7 = (f32[2,1,64,128]{2,1,3,0:T(1,128)S(1)}, f32[2,1,64,128]{2,1,3,0:T(1,128)S(1)}, u32[]{:S(2)}, u32[]{:S(2)}) collective-permute-start(f32[2,1,64,128]{2,1,3,0:T(1,128)S(1)} %fusion.93), channel_id=1, source_target_pairs={{0,2},{2,4},{4,6},{6,8},{8,10},{10,12},{12,14},{14,0},{1,3},{3,5},... | collective-permute-start | bytes 196616 | tf_op jit(solution)/shard_map/ppermute | solution.py:18
  47.2 9.9 %copy-start.6 = (f32[8,64,128]{1,0,2:T(8,128)}, f32[8,64,128]{1,0,2:T(8,128)S(1)}, u32[]{:S(2)}) copy-start(f32[8,64,128]{1,0,2:T(8,128)S(1)} %fusion.70) | copy-start | bytes 786436
  47.8 7.3 %copy-start.28 = (f32[1,8,64,128]{2,1,3,0:T(8,128)S(1)}, f32[1,8,64,128]{2,1,3,0:T(8,128)}, u32[]{:S(2)}) copy-start(f32[1,8,64,128]{2,1,3,0:T(8,128)} %copy-done.27) | copy-start | bytes 786436
  47.8 2.0 %collective-permute-start.6 = (f32[2,8,1,128]{3,1,2,0:T(8,128)S(1)}, f32[2,8,1,128]{3,1,2,0:T(8,128)S(1)}, u32[]{:S(2)}, u32[]{:S(2)}) collective-permute-start(f32[2,8,1,128]{3,1,2,0:T(8,128)S(1)} %pad_maximum_fusion.54), channel_id=1, source_target_pairs={{0,1},{1,0},{2,3},{3,2},{4,5},{5,4},{6,7},{7,6},{8,9},{9,8},{10,11... | collective-permute-start | bytes 24584 | tf_op jit(solution)/shard_map/ppermute | solution.py:18
  51.2 5.7 %copy-start.36 = (f32[1,8,64,128]{2,1,3,0:T(8,128)S(1)}, f32[1,8,64,128]{2,1,3,0:T(8,128)}, u32[]{:S(2)}) copy-start(f32[1,8,64,128]{2,1,3,0:T(8,128)} %copy-done.34) | copy-start | bytes 786436
  51.2 5.7 %copy-start.38 = (f32[1,8,64,128]{2,1,3,0:T(8,128)S(1)}, f32[1,8,64,128]{2,1,3,0:T(8,128)}, u32[]{:S(2)}) copy-start(f32[1,8,64,128]{2,1,3,0:T(8,128)} %get-tuple-element.23) | copy-start | bytes 786436
  51.2 5.7 %copy-start.41 = (f32[1,8,64,128]{2,1,3,0:T(8,128)S(1)}, f32[1,8,64,128]{2,1,3,0:T(8,128)}, u32[]{:S(2)}) copy-start(f32[1,8,64,128]{2,1,3,0:T(8,128)} %get-tuple-element.24) | copy-start | bytes 786436
  56.9 1.5 %copy-start.61 = (f32[8,64,127]{1,0,2:T(8,128)S(1)}, f32[8,64,127]{1,0,2:T(8,128)}, u32[]{:S(2)}) copy-start(f32[8,64,127]{1,0,2:T(8,128)} %slice.481) | copy-start | bytes 780292
  59.3 5.6 %collective-permute-start.9 = (f32[2,1,64,128]{2,1,3,0:T(1,128)S(1)}, f32[2,1,64,128]{2,1,3,0:T(1,128)S(1)}, u32[]{:S(2)}, u32[]{:S(2)}) collective-permute-start(f32[2,1,64,128]{2,1,3,0:T(1,128)S(1)} %fusion.92), channel_id=1, source_target_pairs={{0,14},{2,0},{4,2},{6,4},{8,6},{10,8},{12,10},{14,12},{1,15},{3,1}... | collective-permute-start | bytes 196616 | tf_op jit(solution)/shard_map/ppermute | solution.py:18
  61.8 1.8 %collective-permute-start.8 = (f32[2,8,1,128]{3,1,2,0:T(8,128)S(1)}, f32[2,8,1,128]{3,1,2,0:T(8,128)S(1)}, u32[]{:S(2)}, u32[]{:S(2)}) collective-permute-start(f32[2,8,1,128]{3,1,2,0:T(8,128)S(1)} %pad_maximum_fusion.55), channel_id=1, source_target_pairs={{0,1},{1,0},{2,3},{3,2},{4,5},{5,4},{6,7},{7,6},{8,9},{9,8},{10,11... | collective-permute-start | bytes 24584 | tf_op jit(solution)/shard_map/ppermute | solution.py:18
  61.9 3.0 %copy-start.31 = (f32[1,8,64,128]{2,1,3,0:T(8,128)S(1)}, f32[1,8,64,128]{2,1,3,0:T(8,128)}, u32[]{:S(2)}) copy-start(f32[1,8,64,128]{2,1,3,0:T(8,128)} %copy-done.30) | copy-start | bytes 786436
  64.9 2.0 %copy-start.29 = (f32[1,8,64,128]{2,1,3,0:T(8,128)S(1)}, f32[1,8,64,128]{2,1,3,0:T(8,128)}, u32[]{:S(2)}) copy-start(f32[1,8,64,128]{2,1,3,0:T(8,128)} %copy-done.27) | copy-start | bytes 786436
  68.1 9.8 %copy-start = (f32[8,64,128]{1,0,2:T(8,128)}, f32[8,64,128]{1,0,2:T(8,128)S(1)}, u32[]{:S(2)}) copy-start(f32[8,64,128]{1,0,2:T(8,128)S(1)} %fusion.43) | copy-start | bytes 786436
  68.1 2.5 %copy-start.7 = (f32[8,64,128]{1,0,2:T(8,128)S(1)}, f32[8,64,128]{1,0,2:T(8,128)}, u32[]{:S(2)}) copy-start(f32[8,64,128]{1,0,2:T(8,128)} %copy-done.6) | copy-start | bytes 786436
  68.1 2.5 %copy-start.57 = (f32[8,64,127]{1,0,2:T(8,128)S(1)}, f32[8,64,127]{1,0,2:T(8,128)}, u32[]{:S(2)}) copy-start(f32[8,64,127]{1,0,2:T(8,128)} %slice.491) | copy-start | bytes 780292
  69.3 8.6 %collective-permute-start.11 = (f32[2,1,64,128]{2,1,3,0:T(1,128)S(1)}, f32[2,1,64,128]{2,1,3,0:T(1,128)S(1)}, u32[]{:S(2)}, u32[]{:S(2)}) collective-permute-start(f32[2,1,64,128]{2,1,3,0:T(1,128)S(1)} %fusion.91), channel_id=1, source_target_pairs={{0,2},{2,4},{4,6},{6,8},{8,10},{10,12},{12,14},{14,0},{1,3},{3,5},... | collective-permute-start | bytes 196616 | tf_op jit(solution)/shard_map/ppermute | solution.py:18
  70.8 7.2 %copy-start.3 = (f32[8,64,128]{1,0,2:T(8,128)}, f32[8,64,128]{1,0,2:T(8,128)S(1)}, u32[]{:S(2)}) copy-start(f32[8,64,128]{1,0,2:T(8,128)S(1)} %fusion.54) | copy-start | bytes 786436
  74.4 2.0 %collective-permute-start.10 = (f32[2,8,1,128]{3,1,2,0:T(8,128)S(1)}, f32[2,8,1,128]{3,1,2,0:T(8,128)S(1)}, u32[]{:S(2)}, u32[]{:S(2)}) collective-permute-start(f32[2,8,1,128]{3,1,2,0:T(8,128)S(1)} %pad_maximum_fusion.56), channel_id=1, source_target_pairs={{0,1},{1,0},{2,3},{3,2},{4,5},{5,4},{6,7},{7,6},{8,9},{9,8},{10,11... | collective-permute-start | bytes 24584 | tf_op jit(solution)/shard_map/ppermute | solution.py:18
  77.7 2.5 %copy-start.32 = (f32[1,8,64,128]{2,1,3,0:T(8,128)S(1)}, f32[1,8,64,128]{2,1,3,0:T(8,128)}, u32[]{:S(2)}) copy-start(f32[1,8,64,128]{2,1,3,0:T(8,128)} %copy-done.30) | copy-start | bytes 786436
  77.7 2.5 %copy-start.39 = (f32[1,8,64,128]{2,1,3,0:T(8,128)S(1)}, f32[1,8,64,128]{2,1,3,0:T(8,128)}, u32[]{:S(2)}) copy-start(f32[1,8,64,128]{2,1,3,0:T(8,128)} %get-tuple-element.23) | copy-start | bytes 786436
  77.7 2.5 %copy-start.42 = (f32[1,8,64,128]{2,1,3,0:T(8,128)S(1)}, f32[1,8,64,128]{2,1,3,0:T(8,128)}, u32[]{:S(2)}) copy-start(f32[1,8,64,128]{2,1,3,0:T(8,128)} %get-tuple-element.24) | copy-start | bytes 786436
  80.3 1.5 %copy-start.19 = (f32[8,64,128]{1,0,2:T(8,128)S(1)}, f32[8,64,128]{1,0,2:T(8,128)}, u32[]{:S(2)}) copy-start(f32[8,64,128]{1,0,2:T(8,128)} %copy-done.17) | copy-start | bytes 786436
  80.3 1.6 %copy-start.62 = (f32[8,64,127]{1,0,2:T(8,128)S(1)}, f32[8,64,127]{1,0,2:T(8,128)}, u32[]{:S(2)}) copy-start(f32[8,64,127]{1,0,2:T(8,128)} %slice.509) | copy-start | bytes 780292
  80.3 1.8 %copy-start.63 = (f32[8,64,127]{1,0,2:T(8,128)S(1)}, f32[8,64,127]{1,0,2:T(8,128)}, u32[]{:S(2)}) copy-start(f32[8,64,127]{1,0,2:T(8,128)} %slice.501) | copy-start | bytes 780292
  82.4 5.6 %copy-start.72 = (u32[32]{0:T(128)S(1)}, u32[32]{0:T(128)}, u32[]{:S(2)}) copy-start(u32[32]{0:T(128)} %constant.99) | copy-start | bytes 388
  83.0 9.2 %collective-permute-start.13 = (f32[2,1,64,128]{2,1,3,0:T(1,128)S(1)}, f32[2,1,64,128]{2,1,3,0:T(1,128)S(1)}, u32[]{:S(2)}, u32[]{:S(2)}) collective-permute-start(f32[2,1,64,128]{2,1,3,0:T(1,128)S(1)} %fusion.90), channel_id=1, source_target_pairs={{0,14},{2,0},{4,2},{6,4},{8,6},{10,8},{12,10},{14,12},{1,15},{3,1}... | collective-permute-start | bytes 196616 | tf_op jit(solution)/shard_map/ppermute | solution.py:18
  87.9 3.0 %collective-permute-start.12 = (f32[2,8,1,128]{3,1,2,0:T(8,128)S(1)}, f32[2,8,1,128]{3,1,2,0:T(8,128)S(1)}, u32[]{:S(2)}, u32[]{:S(2)}) collective-permute-start(f32[2,8,1,128]{3,1,2,0:T(8,128)S(1)} %pad_maximum_fusion.57), channel_id=1, source_target_pairs={{0,1},{1,0},{2,3},{3,2},{4,5},{5,4},{6,7},{7,6},{8,9},{9,8},{10,11... | collective-permute-start | bytes 24584 | tf_op jit(solution)/shard_map/ppermute | solution.py:18
  92.3 2.5 %copy-start.26 = (f32[1,8,64,128]{2,1,3,0:T(8,128)S(1)}, f32[1,8,64,128]{2,1,3,0:T(8,128)}, u32[]{:S(2)}) copy-start(f32[1,8,64,128]{2,1,3,0:T(8,128)} %copy-done.25) | copy-start | bytes 786436
  96.1 1.6 %copy-start.58 = (f32[8,64,127]{1,0,2:T(8,128)S(1)}, f32[8,64,127]{1,0,2:T(8,128)}, u32[]{:S(2)}) copy-start(f32[8,64,127]{1,0,2:T(8,128)} %slice.511) | copy-start | bytes 780292
  97.2 14.9 %collective-permute-start.15 = (f32[2,1,64,128]{2,1,3,0:T(1,128)S(1)}, f32[2,1,64,128]{2,1,3,0:T(1,128)S(1)}, u32[]{:S(2)}, u32[]{:S(2)}) collective-permute-start(f32[2,1,64,128]{2,1,3,0:T(1,128)S(1)} %fusion.89), channel_id=1, source_target_pairs={{0,2},{2,4},{4,6},{6,8},{8,10},{10,12},{12,14},{14,0},{1,3},{3,5},... | collective-permute-start | bytes 196616 | tf_op jit(solution)/shard_map/ppermute | solution.py:18
  103.1 3.2 %copy-start.9 = (f32[8,64,128]{1,0,2:T(8,128)S(1)}, f32[8,64,128]{1,0,2:T(8,128)}, u32[]{:S(2)}) copy-start(f32[8,64,128]{1,0,2:T(8,128)} %copy-done.8) | copy-start | bytes 786436
  103.1 4.0 %copy-start.11 = (f32[8,64,128]{1,0,2:T(8,128)S(1)}, f32[8,64,128]{1,0,2:T(8,128)}, u32[]{:S(2)}) copy-start(f32[8,64,128]{1,0,2:T(8,128)} %fusion.38) | copy-start | bytes 786436
  103.2 7.6 %collective-permute-start.14 = (f32[2,8,1,128]{3,1,2,0:T(8,128)S(1)}, f32[2,8,1,128]{3,1,2,0:T(8,128)S(1)}, u32[]{:S(2)}, u32[]{:S(2)}) collective-permute-start(f32[2,8,1,128]{3,1,2,0:T(8,128)S(1)} %pad_maximum_fusion.58), channel_id=1, source_target_pairs={{0,1},{1,0},{2,3},{3,2},{4,5},{5,4},{6,7},{7,6},{8,9},{9,8},{10,11... | collective-permute-start | bytes 24584 | tf_op jit(solution)/shard_map/ppermute | solution.py:18
  112.1 3.0 %copy-start.22 = (f32[1,8,64,128]{2,1,3,0:T(8,128)S(1)}, f32[1,8,64,128]{2,1,3,0:T(8,128)}, u32[]{:S(2)}) copy-start(f32[1,8,64,128]{2,1,3,0:T(8,128)} %copy-done.21) | copy-start | bytes 786436
  112.1 3.0 %copy-start.40 = (f32[1,8,64,128]{2,1,3,0:T(8,128)S(1)}, f32[1,8,64,128]{2,1,3,0:T(8,128)}, u32[]{:S(2)}) copy-start(f32[1,8,64,128]{2,1,3,0:T(8,128)} %get-tuple-element.23) | copy-start | bytes 786436
  112.1 3.0 %copy-start.43 = (f32[1,8,64,128]{2,1,3,0:T(8,128)S(1)}, f32[1,8,64,128]{2,1,3,0:T(8,128)}, u32[]{:S(2)}) copy-start(f32[1,8,64,128]{2,1,3,0:T(8,128)} %get-tuple-element.24) | copy-start | bytes 786436
  115.1 1.5 %copy-start.20 = (f32[8,64,128]{1,0,2:T(8,128)S(1)}, f32[8,64,128]{1,0,2:T(8,128)}, u32[]{:S(2)}) copy-start(f32[8,64,128]{1,0,2:T(8,128)} %copy-done.17) | copy-start | bytes 786436
  115.2 1.6 %copy-start.54 = (f32[8,64,127]{1,0,2:T(8,128)S(1)}, f32[8,64,127]{1,0,2:T(8,128)}, u32[]{:S(2)}) copy-start(f32[8,64,127]{1,0,2:T(8,128)} %slice.521) | copy-start | bytes 780292
  115.2 1.8 %copy-start.55 = (f32[8,64,127]{1,0,2:T(8,128)S(1)}, f32[8,64,127]{1,0,2:T(8,128)}, u32[]{:S(2)}) copy-start(f32[8,64,127]{1,0,2:T(8,128)} %slice.522) | copy-start | bytes 780292
  (26 other events, 29.5 us)
where the time goes:
time: 150 us; the launch traced here: 149 us
  local copies, waits for them, and re-layouts  63.3 us (42%)
  other arithmetic  31.2 us (21%)
  blocking collectives  23.9 us (16%)
  starting transfers between devices  16.2 us (11%)
  waiting for transfers between devices  6.64 us (4%)
  matrix products  5.32 us (4%)
  between operations  2.26 us (2%)
    unnamed x1, blocking collectives  21.4 us
    unnamed x157, local copies, waits for them, and re-layouts  19.7 us
    ppermute x16, starting transfers between devices, shifted(): return lax.ppermute(value, axis, pairs)  16.2 us
    slice x16, local copies, waits for them, and re-layouts, split_step(): behind_y = shifted(jnp.stack([magn[0, :, -1:], magn[2, :, -1:]]), 'gy', 1)  13.6 us
    ppermute x8, local copies, waits for them, and re-layouts, shifted(): return lax.ppermute(value, axis, pairs)  9.8 us
    sub x4, other arithmetic, split_step(): bdiff_x = back_x[:, 1:] - back_x[:, :-1]  8.72 us
    sub x4, other arithmetic, split_step(): diff_x = ext_x[:, 1:] - ext_x[:, :-1]  8.38 us
    slice x8, local copies, waits for them, and re-layouts, backward_z(): field[..., :-1]  6.71 us
  transfers between devices with their start and end apart: 16, of which 4 were waited for; matrix products, arithmetic and copies ran while one was open for 36% of the time, Pallas kernels for 0%

commit v1 on v0

--- a/solution.py
+++ b/solution.py
@@ -3,6 +3,8 @@
 import jax
 import jax.numpy as jnp
 from jax import lax
+from jax.experimental import pallas as pl
+from jax.experimental.pallas import tpu as pltpu
 from jax.sharding import PartitionSpec as P
 
 ITERS = 4
@@ -18,62 +20,122 @@
     return lax.ppermute(value, axis, pairs)
 
 
-def forward_z(field):
-    upper = jnp.concatenate([field[..., 1:], jnp.zeros_like(field[..., :1])], axis=-1)
-    return upper - field
-
-
-def backward_z(field):
-    lower = jnp.concatenate([jnp.zeros_like(field[..., :1]), field[..., :-1]], axis=-1)
-    return field - lower
-
-
 def coefficients(material, eps_table, sigma_table):
-    count = eps_table.shape[0]
-    labels = jnp.arange(count, dtype=jnp.int32).reshape(count, 1, 1, 1)
-    onehot = (material[None] == labels).astype(jnp.float32)
-    permit = jnp.sum(onehot * eps_table.reshape(count, 1, 1, 1), axis=0)
-    conduct = jnp.sum(onehot * sigma_table.reshape(count, 1, 1, 1), axis=0)
+    permit = jnp.zeros(material.shape, jnp.float32)
+    conduct = jnp.zeros(material.shape, jnp.float32)
+    for label in range(eps_table.shape[0]):
+        hit = material == label
+        permit = jnp.where(hit, eps_table[label], permit)
+        conduct = jnp.where(hit, sigma_table[label], conduct)
     loss = conduct * TIME_STEP / (2.0 * permit)
     keep = (1.0 - loss) / (1.0 + loss)
     drive = TIME_STEP / (permit * (1.0 + loss))
     return (keep, drive)
 
 
-def split_step(elec, magn, keep, drive):
-    ahead_x = shifted(elec[1:3, 0:1], "gx", -1)
-    ahead_y = shifted(jnp.stack([elec[0, :, 0:1], elec[2, :, 0:1]]), "gy", -1)
-    ext_x = jnp.concatenate([elec[1:3], ahead_x], axis=1)
-    diff_x = ext_x[:, 1:] - ext_x[:, :-1]
-    ext_y = jnp.concatenate([jnp.stack([elec[0], elec[2]]), ahead_y], axis=2)
-    diff_y = ext_y[:, :, 1:] - ext_y[:, :, :-1]
-    magn_x = magn[0] - TIME_STEP * (diff_y[1] - forward_z(elec[1]))
-    magn_y = magn[1] - TIME_STEP * (forward_z(elec[0]) - diff_x[1])
-    magn_z = magn[2] - TIME_STEP * (diff_x[0] - diff_y[0])
-    magn = jnp.stack([magn_x, magn_y, magn_z])
-    behind_x = shifted(magn[1:3, -1:], "gx", 1)
-    behind_y = shifted(jnp.stack([magn[0, :, -1:], magn[2, :, -1:]]), "gy", 1)
-    back_x = jnp.concatenate([behind_x, magn[1:3]], axis=1)
-    bdiff_x = back_x[:, 1:] - back_x[:, :-1]
-    back_y = jnp.concatenate([behind_y, jnp.stack([magn[0], magn[2]])], axis=2)
-    bdiff_y = back_y[:, :, 1:] - back_y[:, :, :-1]
-    elec_x = keep * elec[0] + drive * (bdiff_y[1] - backward_z(magn[1]))
-    elec_y = keep * elec[1] + drive * (backward_z(magn[0]) - bdiff_x[1])
-    elec_z = keep * elec[2] + drive * (bdiff_x[0] - bdiff_y[0])
-    return (jnp.stack([elec_x, elec_y, elec_z]), magn)
+def _z_up(f):
+    depth = f.shape[-1]
+    lane = lax.broadcasted_iota(jnp.int32, f.shape, 1)
+    up = pltpu.roll(f, depth - 1, 1)
+    return jnp.where(lane == depth - 1, 0.0, up) - f
+
+
+def _z_down(f):
+    lane = lax.broadcasted_iota(jnp.int32, f.shape, 1)
+    down = pltpu.roll(f, 1, 1)
+    return f - jnp.where(lane == 0, 0.0, down)
+
+
+def _y_up(f, row):
+    cells = f.shape[0]
+    index = lax.broadcasted_iota(jnp.int32, f.shape, 0)
+    up = pltpu.roll(f, cells - 1, 0)
+    return jnp.where(index == cells - 1, row, up) - f
+
+
+def _y_down(f, row):
+    index = lax.broadcasted_iota(jnp.int32, f.shape, 0)
+    down = pltpu.roll(f, 1, 0)
+    return f - jnp.where(index == 0, row, down)
+
+
+def _magn_kernel(e_ref, h_ref, ax_ref, ay_ref, h_out, bx_out, by_out):
+    planes = e_ref.shape[1]
+    for x in range(planes):
+        ex = e_ref[0, x]
+        ey = e_ref[1, x]
+        ez = e_ref[2, x]
+        if x + 1 < planes:
+            ey_next = e_ref[1, x + 1]
+            ez_next = e_ref[2, x + 1]
+        else:
+            ey_next = ax_ref[0]
+            ez_next = ax_ref[1]
+        hx = h_ref[0, x] - TIME_STEP * (_y_up(ez, ay_ref[1, x]) - _z_up(ey))
+        hy = h_ref[1, x] - TIME_STEP * (_z_up(ex) - (ez_next - ez))
+        hz = h_ref[2, x] - TIME_STEP * ((ey_next - ey) - _y_up(ex, ay_ref[0, x]))
+        h_out[0, x] = hx
+        h_out[1, x] = hy
+        h_out[2, x] = hz
+        cells = hx.shape[0]
+        by_out[0, x] = hx[cells - 1:cells]
+        by_out[1, x] = hz[cells - 1:cells]
+        if x == planes - 1:
+            bx_out[0] = hy
+            bx_out[1] = hz
+
+
+def _elec_kernel(e_ref, h_ref, keep_ref, drive_ref, bx_ref, by_ref, e_out, ax_out, ay_out):
+    planes = e_ref.shape[1]
+    for x in range(planes):
+        hx = h_ref[0, x]
+        hy = h_ref[1, x]
+        hz = h_ref[2, x]
+        if x > 0:
+            hy_prev = h_ref[1, x - 1]
+            hz_prev = h_ref[2, x - 1]
+        else:
+            hy_prev = bx_ref[0]
+            hz_prev = bx_ref[1]
+        keep = keep_ref[x]
+        drive = drive_ref[x]
+        ex = keep * e_ref[0, x] + drive * (_y_down(hz, by_ref[1, x]) - _z_down(hy))
+        ey = keep * e_ref[1, x] + drive * (_z_down(hx) - (hz - hz_prev))
+        ez = keep * e_ref[2, x] + drive * ((hy - hy_prev) - _y_down(hx, by_ref[0, x]))
+        e_out[0, x] = ex
+        e_out[1, x] = ey
+        e_out[2, x] = ez
+        ay_out[0, x] = ex[0:1]
+        ay_out[1, x] = ez[0:1]
+        if x == 0:
+            ax_out[0] = ey
+            ax_out[1] = ez
+
+
+def _edges_of_elec(elec):
+    return (elec[1:3, 0], jnp.stack([elec[0, :, 0:1], elec[2, :, 0:1]]))
 
 
 def local(e_field, h_field, material, eps_table, sigma_table, angle_orders):
     keep, drive = coefficients(material, eps_table, sigma_table)
-    cells_x = e_field.shape[1]
-    cells_y = e_field.shape[2]
-    depth = e_field.shape[3]
+    comps, cells_x, cells_y, depth = e_field.shape
     elec = e_field
     magn = h_field
+    plane_shape = jax.ShapeDtypeStruct((2, cells_y, depth), jnp.float32)
+    row_shape = jax.ShapeDtypeStruct((2, cells_x, 1, depth), jnp.float32)
+    field_shape = jax.ShapeDtypeStruct(e_field.shape, jnp.float32)
+    magn_call = pl.pallas_call(_magn_kernel, out_shape=(field_shape, plane_shape, row_shape))
+    elec_call = pl.pallas_call(_elec_kernel, out_shape=(field_shape, plane_shape, row_shape))
+    edge_x, edge_y = _edges_of_elec(elec)
     mon_real = jnp.zeros((2, cells_x, cells_y), jnp.float32)
     mon_imag = jnp.zeros((2, cells_x, cells_y), jnp.float32)
     for number in range(ITERS):
-        elec, magn = split_step(elec, magn, keep, drive)
+        ahead_x = shifted(edge_x, "gx", -1)
+        ahead_y = shifted(edge_y, "gy", -1)
+        magn, back_x, back_y = magn_call(elec, magn, ahead_x, ahead_y)
+        behind_x = shifted(back_x, "gx", 1)
+        behind_y = shifted(back_y, "gy", 1)
+        elec, edge_x, edge_y = elec_call(elec, magn, keep, drive, behind_x, behind_y)
         plane = elec[0:2, :, :, depth - 3]
         mon_real = mon_real + math.cos(PHASE_STEP * (number + 1)) * plane
         mon_imag = mon_imag - math.sin(PHASE_STEP * (number + 1)) * plane

time: 150 us -> 123 us (0.82)
  local copies, waits for them, and re-layouts: 63.3 us -> 11 us
  Pallas kernels: 0 us -> 20.7 us
  waiting for transfers between devices: 6.64 us -> 26.1 us
  other arithmetic: 31.2 us -> 20.6 us
  blocking collectives: 23.9 us -> 21.6 us
    slice x45 -> x3, local copies, waits for them, and re-layouts: 32.6 us -> 2.12 us  [the longest x1 0.78 us: _edges_of_elec(): return (elec[1:3, 0], jnp.stack([elec[0, :, 0:1], elec[2, :, 0:1]]))]
    pallas_call x0 -> x8, Pallas kernels: none -> 20.7 us  [the longest x4 10.7 us: local(): elec_call(elec, magn, keep, drive, behind_x, behind_y)]
    sub x22 -> x0, other arithmetic: 20 us -> none  [the longest x4 8.72 us: split_step(): bdiff_x = back_x[:, 1:] - back_x[:, :-1]]
    ppermute x16, waiting for transfers between devices: 6.64 us -> 26.1 us  [shifted(): return lax.ppermute(value, axis, pairs)]
    div x0 -> x2, other arithmetic: none -> 18.2 us  [the longest x1 9.61 us: coefficients(): drive = TIME_STEP / (permit * (1.0 + loss))]
    unnamed x157 -> x48, local copies, waits for them, and re-layouts: 19.7 us -> 7.53 us
    ppermute x8 -> x0, local copies, waits for them, and re-layouts: 9.8 us -> none  [shifted(): return lax.ppermute(value, axis, pairs)]
    add x8 -> x0, other arithmetic: 5.45 us -> none  [the longest x3 2.27 us: split_step(): elec_y = keep * elec[1] + drive * (backward_z(magn[0]) - bdiff_x[1])]
  transfers between devices with their start and end apart: 16 -> 16, of which waited for: 4 -> 11; matrix products, arithmetic and copies ran while one was open for 36% -> 17% of each run, Pallas kernels for 0% -> 0%
where the time goes in v1:
time: 123 us; the launch traced here: 122 us
  waiting for transfers between devices  26.1 us (21%)
  blocking collectives  21.6 us (18%)
  Pallas kernels  20.7 us (17%)
  other arithmetic  20.6 us (17%)
  starting transfers between devices  15.2 us (12%)
  local copies, waits for them, and re-layouts  11 us (9%)
  matrix products  5.39 us (4%)
  between operations  1.43 us (1%)
    ppermute x16, waiting for transfers between devices, shifted(): return lax.ppermute(value, axis, pairs)  26.1 us
    unnamed x1, blocking collectives  19.1 us
    ppermute x16, starting transfers between devices, shifted(): return lax.ppermute(value, axis, pairs)  15.2 us
    pallas_call x4, Pallas kernels, local(): elec_call(elec, magn, keep, drive, behind_x, behind_y)  10.7 us
    pallas_call x4, Pallas kernels, local(): magn, back_x, back_y = magn_call(elec, magn, ahead_x, ahead_y)  9.96 us
    div x1, other arithmetic, coefficients(): drive = TIME_STEP / (permit * (1.0 + loss))  9.61 us
    div x1, other arithmetic, coefficients(): keep = (1.0 - loss) / (1.0 + loss)  8.55 us
    unnamed x48, local copies, waits for them, and re-layouts  7.53 us
  transfers between devices with their start and end apart: 16, of which 11 were waited for; matrix products, arithmetic and copies ran while one was open for 17% of the time, Pallas kernels for 0%

profile of v1, /device:TPU:0, one launch (start us, length us, event | category | flops | bytes accessed | tf_op | source)
XLA Modules:
  0.0 121.9 jit_solution(7619445437326335038)
XLA Ops:
  0.6 0.8 fusion.31
  1.4 0.5 collective-permute-start.1
  1.9 0.9 slice_bitcast_fusion
  2.8 5.6 %collective-permute-start = (f32[2,64,128]{2,1,0:T(8,128)S(1)}, f32[2,64,128]{2,1,0:T(8,128)S(1)}, u32[]{:S(2)}, u32[]{:S(2)}) collective-permute-start(f32[2,64,128]{2,1,0:T(8,128)S(1)} %slice_bitcast_fusion), channel_id=1, source_target_pairs={{0,14},{2,0},{4,2},{6,4},{8,6},{10,8},{12,10},{14,12},{1,15},{3,1}... | collective-permute-start | bytes 196616 | tf_op jit(solution)/shard_map/ppermute | solution.py:20
  8.4 0.7 fusion.34
  9.1 0.7 fusion.35
  9.7 9.6 %multiply_divide_fusion = (f32[8,64,128]{2,1,0:T(8,128)}, pred[8,64,128]{2,1,0:T(8,128)(4,1)S(1)}, pred[8,64,128]{2,1,0:T(8,128)(4,1)S(1)}, pred[8,64,128]{2,1,0...) fusion(f32[]{:T(128)} %bitcast.12, f32[]{:T(128)} %bitcast.11, ...), kind=kLoop, calls=%fused_computation.16 | loop fusion | flops 1572864 | bytes 917552 | tf_op jit(solution)/shard_map/div | solution.py:32
  19.3 0.0 collective-permute-done.1.ay_ref
  19.3 0.0 collective-permute-done.ax_ref
  19.3 0.6 copy-done.13
  19.9 0.6 copy-done.3
  20.6 2.5 %shard_map.85 = (f32[3,8,64,128]{3,2,1,0:T(8,128)}, f32[2,64,128]{2,1,0:T(8,128)}, f32[2,8,1,128]{3,2,1,0:T(1,128)}) custom-call(f32[3,8,64,128]{3,2,1,0:T(8,128)} %e_ref.3, f32[3,8,64,128]{3,2,1,0:T(8,128)} %h_ref.1, f32[2,64,128]{2,1,0:T(8,128)} %copy-done.3, f32[2,8,1,128]{3,2,1,0:T(1,128)} %copy-done.13), custom_call_target="tpu_custom_call" | custom-call | tf_op jit(solution)/shard_map/pallas_call | solution.py:135
  23.0 0.0 collective-permute-start.2
  23.0 0.2 collective-permute-start.3
  23.3 8.6 %subtract_divide_fusion.keep_ref = f32[8,64,128]{2,1,0:T(8,128)} fusion(pred[8,64,128]{2,1,0:T(8,128)(4,1)S(1)} %get-tuple-element.53, pred[8,64,128]{2,1,0:T(8,128)(4,1)S(1)} %get-tuple-element.52, pred[8,64,128]{2,1,0:T(8,128)(4,1)S(1)} %get-tuple-element.51, pred[8,64,128]{2,1,0:T(8,128)(4,1)S(1)} %get-tuple-element.50, ...), kind=kLoop, calls=%fused_computation.17 | loop fusion | flops 1179648 | bytes 655408 | tf_op jit(solution)/shard_map/div | solution.py:31
  31.8 0.0 copy-start.4
  31.8 0.6 copy-done.14
  32.4 0.0 copy-done.4
  32.4 2.7 %shard_map.86 = (f32[3,8,64,128]{3,2,1,0:T(8,128)}, f32[2,64,128]{2,1,0:T(8,128)}, f32[2,8,1,128]{3,2,1,0:T(1,128)}) custom-call(f32[3,8,64,128]{3,2,1,0:T(8,128)} %e_ref.3, f32[3,8,64,128]{3,2,1,0:T(8,128)} %get-tuple-element.25.h_ref, f32[8,64,128]{2,1,0:T(8,128)} %subtract_divide_fusion.keep_ref, f32[8,64,128]{2,1,0:T(8,128)} %get-tuple-element.47.drive_ref, ...), custom_call_target="tpu_custom_call" | custom-call | tf_op jit(solution)/shard_map/pallas_call | solution.py:138
  35.1 4.5 %collective-permute-start.4 = (f32[2,64,128]{2,1,0:T(8,128)}, f32[2,64,128]{2,1,0:T(8,128)S(1)}, u32[]{:S(2)}, u32[]{:S(2)}) collective-permute-start(f32[2,64,128]{2,1,0:T(8,128)} %get-tuple-element.29), channel_id=1, source_target_pairs={{0,14},{2,0},{4,2},{6,4},{8,6},{10,8},{12,10},{14,12},{1,15},{3,1}... | collective-permute-start | bytes 196616 | tf_op jit(solution)/shard_map/ppermute | solution.py:20
  39.6 0.2 collective-permute-start.5
  39.8 1.2 collective-permute-done.5.ay_ref
  41.0 1.0 collective-permute-done.4.ax_ref
  42.0 0.6 copy-done.10
  42.6 2.5 %shard_map.87 = (f32[3,8,64,128]{3,2,1,0:T(8,128)}, f32[2,64,128]{2,1,0:T(8,128)}, f32[2,8,1,128]{3,2,1,0:T(1,128)}) custom-call(f32[3,8,64,128]{3,2,1,0:T(8,128)} %get-tuple-element.28.e_ref, f32[3,8,64,128]{3,2,1,0:T(8,128)} %get-tuple-element.25.h_ref, f32[2,64,128]{2,1,0:T(8,128)} %copy-done.10, f32[2,8,1,128]{3,2,1,0:T(1,128)} %copy-done.20), custom_call_target="tpu_custom_call" | custom-call | tf_op jit(solution)/shard_map/pallas_call | solution.py:135
  45.0 0.1 collective-permute-start.7
  45.1 0.6 copy-done.21
  45.7 0.8 collective-permute-done.7.by_ref
  46.5 6.1 %collective-permute-done.6.bx_ref = f32[2,64,128]{2,1,0:T(8,128)S(1)} collective-permute-done((f32[2,64,128]{2,1,0:T(8,128)}, f32[2,64,128]{2,1,0:T(8,128)S(1)}, u32[]{:S(2)}, u32[]{:S(2)}) %collective-permute-start.6) | collective-permute-done | bytes 65568 | tf_op jit(solution)/shard_map/ppermute | solution.py:20
  52.6 0.6 copy-done.7
  53.2 2.7 %shard_map.88 = (f32[3,8,64,128]{3,2,1,0:T(8,128)}, f32[2,64,128]{2,1,0:T(8,128)}, f32[2,8,1,128]{3,2,1,0:T(1,128)}) custom-call(f32[3,8,64,128]{3,2,1,0:T(8,128)} %get-tuple-element.28.e_ref, f32[3,8,64,128]{3,2,1,0:T(8,128)} %get-tuple-element.31.h_ref, f32[8,64,128]{2,1,0:T(8,128)} %subtract_divide_fusion.keep_ref, ...), custom_call_target="tpu_custom_call" | custom-call | tf_op jit(solution)/shard_map/pallas_call | solution.py:138
  55.9 2.0 %collective-permute-start.8 = (f32[2,64,128]{2,1,0:T(8,128)}, f32[2,64,128]{2,1,0:T(8,128)S(1)}, u32[]{:S(2)}, u32[]{:S(2)}) collective-permute-start(f32[2,64,128]{2,1,0:T(8,128)} %get-tuple-element.35), channel_id=1, source_target_pairs={{0,14},{2,0},{4,2},{6,4},{8,6},{10,8},{12,10},{14,12},{1,15},{3,1}... | collective-permute-start | bytes 196616 | tf_op jit(solution)/shard_map/ppermute | solution.py:20
  57.9 1.4 %collective-permute-done.9.ay_ref = f32[2,8,1,128]{3,2,1,0:T(1,128)S(1)} collective-permute-done((f32[2,8,1,128]{3,2,1,0:T(1,128)}, f32[2,8,1,128]{3,2,1,0:T(1,128)S(1)}, u32[]{:S(2)}, u32[]{:S(2)}) %collective-permute-start.9) | collective-permute-done | bytes 8224 | tf_op jit(solution)/shard_map/ppermute | solution.py:20
  59.3 1.1 collective-permute-done.8.ax_ref
  60.3 0.6 copy-done.8
  61.0 2.5 %shard_map.89 = (f32[3,8,64,128]{3,2,1,0:T(8,128)}, f32[2,64,128]{2,1,0:T(8,128)}, f32[2,8,1,128]{3,2,1,0:T(1,128)}) custom-call(f32[3,8,64,128]{3,2,1,0:T(8,128)} %get-tuple-element.34.e_ref, f32[3,8,64,128]{3,2,1,0:T(8,128)} %get-tuple-element.31.h_ref, f32[2,64,128]{2,1,0:T(8,128)} %copy-done.8, f32[2,8,1,128]{3,2,1,0:T(1,128)} %copy-done.18), custom_call_target="tpu_custom_call" | custom-call | tf_op jit(solution)/shard_map/pallas_call | solution.py:135
  63.5 0.1 multiply_multiply_fusion
  63.5 1.3 %collective-permute-done.11.by_ref = f32[2,8,1,128]{3,2,1,0:T(1,128)S(1)} collective-permute-done((f32[2,8,1,128]{3,2,1,0:T(1,128)}, f32[2,8,1,128]{3,2,1,0:T(1,128)S(1)}, u32[]{:S(2)}, u32[]{:S(2)}) %collective-permute-start.11) | collective-permute-done | bytes 8224 | tf_op jit(solution)/shard_map/ppermute | solution.py:20
  64.8 5.8 %collective-permute-done.10.bx_ref = f32[2,64,128]{2,1,0:T(8,128)S(1)} collective-permute-done((f32[2,64,128]{2,1,0:T(8,128)}, f32[2,64,128]{2,1,0:T(8,128)S(1)}, u32[]{:S(2)}, u32[]{:S(2)}) %collective-permute-start.10) | collective-permute-done | bytes 65568 | tf_op jit(solution)/shard_map/ppermute | solution.py:20
  70.6 0.6 copy-done.6
  71.2 2.6 %shard_map.90 = (f32[3,8,64,128]{3,2,1,0:T(8,128)}, f32[2,64,128]{2,1,0:T(8,128)}, f32[2,8,1,128]{3,2,1,0:T(1,128)}) custom-call(f32[3,8,64,128]{3,2,1,0:T(8,128)} %get-tuple-element.34.e_ref, f32[3,8,64,128]{3,2,1,0:T(8,128)} %get-tuple-element.37.h_ref, f32[8,64,128]{2,1,0:T(8,128)} %subtract_divide_fusion.keep_ref, ...), custom_call_target="tpu_custom_call" | custom-call | tf_op jit(solution)/shard_map/pallas_call | solution.py:138
  73.9 2.0 %collective-permute-start.12 = (f32[2,64,128]{2,1,0:T(8,128)}, f32[2,64,128]{2,1,0:T(8,128)S(1)}, u32[]{:S(2)}, u32[]{:S(2)}) collective-permute-start(f32[2,64,128]{2,1,0:T(8,128)} %get-tuple-element.41), channel_id=1, source_target_pairs={{0,14},{2,0},{4,2},{6,4},{8,6},{10,8},{12,10},{14,12},{1,15},{3,1}... | collective-permute-start | bytes 196616 | tf_op jit(solution)/shard_map/ppermute | solution.py:20
  75.9 1.4 %collective-permute-done.13.ay_ref = f32[2,8,1,128]{3,2,1,0:T(1,128)S(1)} collective-permute-done((f32[2,8,1,128]{3,2,1,0:T(1,128)}, f32[2,8,1,128]{3,2,1,0:T(1,128)S(1)}, u32[]{:S(2)}, u32[]{:S(2)}) %collective-permute-start.13) | collective-permute-done | bytes 8224 | tf_op jit(solution)/shard_map/ppermute | solution.py:20
  77.3 1.1 collective-permute-done.12.ax_ref
  78.4 0.6 copy-done.9
  79.0 2.5 %shard_map.91 = (f32[3,8,64,128]{3,2,1,0:T(8,128)}, f32[2,64,128]{2,1,0:T(8,128)}, f32[2,8,1,128]{3,2,1,0:T(1,128)}) custom-call(f32[3,8,64,128]{3,2,1,0:T(8,128)} %get-tuple-element.40.e_ref, f32[3,8,64,128]{3,2,1,0:T(8,128)} %get-tuple-element.37.h_ref, f32[2,64,128]{2,1,0:T(8,128)} %copy-done.9, f32[2,8,1,128]{3,2,1,0:T(1,128)} %copy-done.19), custom_call_target="tpu_custom_call" | custom-call | tf_op jit(solution)/shard_map/pallas_call | solution.py:135
  81.6 0.1 multiply_multiply_fusion.1
  81.6 0.7 copy-done.22
  82.3 0.6 dynamic-slice
  83.5 5.2 %collective-permute-done.14.bx_ref = f32[2,64,128]{2,1,0:T(8,128)S(1)} collective-permute-done((f32[2,64,128]{2,1,0:T(8,128)}, f32[2,64,128]{2,1,0:T(8,128)S(1)}, u32[]{:S(2)}, u32[]{:S(2)}) %collective-permute-start.14) | collective-permute-done | bytes 65568 | tf_op jit(solution)/shard_map/ppermute | solution.py:20
  88.7 0.6 copy-done.5
  89.3 2.8 %shard_map.92 = (f32[3,8,64,128]{3,2,1,0:T(8,128)}, f32[2,64,128]{2,1,0:T(8,128)}, f32[2,8,1,128]{3,2,1,0:T(1,128)}) custom-call(f32[3,8,64,128]{3,2,1,0:T(8,128)} %get-tuple-element.40.e_ref, f32[3,8,64,128]{3,2,1,0:T(8,128)} %get-tuple-element.23.h_ref, f32[8,64,128]{2,1,0:T(8,128)} %subtract_divide_fusion.keep_ref, ...), custom_call_target="tpu_custom_call" | custom-call | tf_op jit(solution)/shard_map/pallas_call | solution.py:138
  92.1 1.7 %multiply_add_fusion = (f32[2,8,64,1]{3,2,1,0:T(8,128)S(1)}, f32[2,8,64,1]{3,2,1,0:T(8,128)S(1)}) fusion(f32[3,8,64,128]{3,2,1,0:T(8,128)} %get-tuple-element.22, f32[3,8,64,128]{3,2,1,0:T(8,128)S(1)} %copy-done.2, f32[3,8,64,128]{3,2,1,0:T(8,128)S(1)} %copy-done.1, f32[3,8,64,128]{3,2,1,0:T(8,128)S(1)} %copy-done), kind=kLoop, calls=%fused_computation.7 | loop fusion | flops 15360 | bytes 24576 | tf_op jit(solution)/shard_map/add | solution.py:140
  93.8 0.2 copy.34
  94.0 0.2 copy.33
  94.2 1.3 %convolution_bitcast_fusion.1 = f32[64,2]{0,1:T(2,128)S(1)} fusion(s32[64,64]{1,0:T(8,128)S(1)} %multiply_multiply_fusion, s32[64,8]{0,1:T(8,128)S(1)} %multiply_multiply_fusion.1, f32[2,8,64,1]{2,0,1,3:T(2,128)S(1)} %copy.34), kind=kOutput, calls=%fused_computation.2 | convolution fusion | flops 1245184 | bytes 23040 | tf_op jit(solution)/shard_map/dot_general | solution.py:166
  95.5 1.4 %convolution_bitcast_fusion.3 = f32[64,2]{0,1:T(2,128)S(1)} fusion(s32[64,64]{1,0:T(8,128)S(1)} %multiply_multiply_fusion, s32[64,8]{0,1:T(8,128)S(1)} %multiply_multiply_fusion.1, f32[2,8,64,1]{2,0,1,3:T(2,128)S(1)} %copy.33), kind=kOutput, calls=%fused_computation.5 | convolution fusion | flops 1245184 | bytes 23040 | tf_op jit(solution)/shard_map/dot_general | solution.py:163
  96.9 1.4 %fusion = f32[64,2]{0,1:T(2,128)S(1)} fusion(f32[64,2]{0,1:T(2,128)S(1)} %convolution_bitcast_fusion.1, s32[64,64]{1,0:T(8,128)S(1)} %multiply_multiply_fusion, s32[64,8]{0,1:T(8,128)S(1)} %multiply_multiply_fusion.1, f32[2,8,64,1]{2,0,1,3:T(2,128)S(1)} %copy.33), kind=kOutput, calls=%fused_computation.1 | convolution fusion | flops 1245312 | bytes 23552 | tf_op jit(solution)/shard_map/dot_general | solution.py:168
  98.2 1.4 %fusion.1 = f32[64,2]{0,1:T(2,128)S(1)} fusion(f32[64,2]{0,1:T(2,128)S(1)} %convolution_bitcast_fusion.3, s32[64,64]{1,0:T(8,128)S(1)} %multiply_multiply_fusion, s32[64,8]{0,1:T(8,128)S(1)} %multiply_multiply_fusion.1, f32[2,8,64,1]{2,0,1,3:T(2,128)S(1)} %copy.34), kind=kOutput, calls=%fused_computation.4 | convolution fusion | flops 1245312 | bytes 23552 | tf_op jit(solution)/shard_map/dot_general | solution.py:165
  99.6 0.1 fusion.32
  99.7 19.1 %all-reduce = f32[64,4]{0,1:T(4,128)S(1)} all-reduce(f32[64,4]{0,1:T(4,128)S(1)} %pad_maximum_fusion.1), channel_id=2, replica_groups=mesh['clip'=2,'gx'=8,'gy'=2] {'gx'}, use_global_device_ids=true, to_apply=%region_0.1.clone | all-reduce | flops 256 | bytes 2048
  118.8 0.1 constant_dynamic-slice_fusion
  118.9 2.4 %psum.7 = f32[8,4]{0,1:T(4,128)S(1)} all-reduce(f32[8,4]{0,1:T(4,128)S(1)} %constant_dynamic-slice_fusion), channel_id=1, replica_groups=mesh['clip'=2,'gx'=8,'gy'=2] {'gy'}, use_global_device_ids=true, to_apply=%region_1.2 | all-reduce | flops 32 | bytes 256 | tf_op jit(solution)/shard_map/psum | solution.py:175
  121.4 0.6 broadcast_multiply_fusion
  (48 shorter events, 0.1 us)
Async XLA Ops:
  1.4 17.9 %collective-permute-start.1 = (f32[2,8,1,128]{3,2,1,0:T(1,128)S(1)}, f32[2,8,1,128]{3,2,1,0:T(1,128)S(1)}, u32[]{:S(2)}, u32[]{:S(2)}) collective-permute-start(f32[2,8,1,128]{3,2,1,0:T(1,128)S(1)} %pad_maximum_fusion), channel_id=1, source_target_pairs={{0,1},{1,0},{2,3},{3,2},{4,5},{5,4},{6,7},{7,6},{8,9},{9,8},{10,11... | collective-permute-start | bytes 24584 | tf_op jit(solution)/shard_map/ppermute | solution.py:20
  1.9 6.4 %copy-start.11 = (f32[6]{0:T(128)S(1)}, f32[6]{0:T(128)}, u32[]{:S(2)}) copy-start(f32[6]{0:T(128)} %param.10) | copy-start | bytes 76
  2.8 16.5 %collective-permute-start = (f32[2,64,128]{2,1,0:T(8,128)S(1)}, f32[2,64,128]{2,1,0:T(8,128)S(1)}, u32[]{:S(2)}, u32[]{:S(2)}) collective-permute-start(f32[2,64,128]{2,1,0:T(8,128)S(1)} %slice_bitcast_fusion), channel_id=1, source_target_pairs={{0,14},{2,0},{4,2},{6,4},{8,6},{10,8},{12,10},{14,12},{1,15},{3,1}... | collective-permute-start | bytes 196616 | tf_op jit(solution)/shard_map/ppermute | solution.py:20
  8.4 0.7 copy-start.12
  19.3 0.6 copy-start.13
  19.9 0.6 copy-start.3
  23.0 8.8 %collective-permute-start.2 = (f32[2,64,128]{2,1,0:T(8,128)}, f32[2,64,128]{2,1,0:T(8,128)S(1)}, u32[]{:S(2)}, u32[]{:S(2)}) collective-permute-start(f32[2,64,128]{2,1,0:T(8,128)} %get-tuple-element.26), channel_id=1, source_target_pairs={{0,2},{2,4},{4,6},{6,8},{8,10},{10,12},{12,14},{14,0},{1,3},{3,5},... | collective-permute-start | bytes 196616 | tf_op jit(solution)/shard_map/ppermute | solution.py:20
  23.0 8.8 %collective-permute-start.3 = (f32[2,8,1,128]{3,2,1,0:T(1,128)}, f32[2,8,1,128]{3,2,1,0:T(1,128)S(1)}, u32[]{:S(2)}, u32[]{:S(2)}) collective-permute-start(f32[2,8,1,128]{3,2,1,0:T(1,128)} %get-tuple-element.27), channel_id=1, source_target_pairs={{0,1},{1,0},{2,3},{3,2},{4,5},{5,4},{6,7},{7,6},{8,9},{9,8},{10,11... | collective-permute-start | bytes 24584 | tf_op jit(solution)/shard_map/ppermute | solution.py:20
  31.8 0.6 copy-start.14
  31.8 0.6 copy-start.4
  35.1 6.8 %collective-permute-start.4 = (f32[2,64,128]{2,1,0:T(8,128)}, f32[2,64,128]{2,1,0:T(8,128)S(1)}, u32[]{:S(2)}, u32[]{:S(2)}) collective-permute-start(f32[2,64,128]{2,1,0:T(8,128)} %get-tuple-element.29), channel_id=1, source_target_pairs={{0,14},{2,0},{4,2},{6,4},{8,6},{10,8},{12,10},{14,12},{1,15},{3,1}... | collective-permute-start | bytes 196616 | tf_op jit(solution)/shard_map/ppermute | solution.py:20
  39.6 1.4 %collective-permute-start.5 = (f32[2,8,1,128]{3,2,1,0:T(1,128)}, f32[2,8,1,128]{3,2,1,0:T(1,128)S(1)}, u32[]{:S(2)}, u32[]{:S(2)}) collective-permute-start(f32[2,8,1,128]{3,2,1,0:T(1,128)} %get-tuple-element.30), channel_id=1, source_target_pairs={{0,1},{1,0},{2,3},{3,2},{4,5},{5,4},{6,7},{7,6},{8,9},{9,8},{10,11... | collective-permute-start | bytes 24584 | tf_op jit(solution)/shard_map/ppermute | solution.py:20
  41.0 1.0 copy-start.20
  42.0 0.6 copy-start.10
  45.0 0.7 copy-start.21
  45.0 7.5 %collective-permute-start.6 = (f32[2,64,128]{2,1,0:T(8,128)}, f32[2,64,128]{2,1,0:T(8,128)S(1)}, u32[]{:S(2)}, u32[]{:S(2)}) collective-permute-start(f32[2,64,128]{2,1,0:T(8,128)} %get-tuple-element.32), channel_id=1, source_target_pairs={{0,2},{2,4},{4,6},{6,8},{8,10},{10,12},{12,14},{14,0},{1,3},{3,5},... | collective-permute-start | bytes 196616 | tf_op jit(solution)/shard_map/ppermute | solution.py:20
  45.0 1.4 %collective-permute-start.7 = (f32[2,8,1,128]{3,2,1,0:T(1,128)}, f32[2,8,1,128]{3,2,1,0:T(1,128)S(1)}, u32[]{:S(2)}, u32[]{:S(2)}) collective-permute-start(f32[2,8,1,128]{3,2,1,0:T(1,128)} %get-tuple-element.33), channel_id=1, source_target_pairs={{0,1},{1,0},{2,3},{3,2},{4,5},{5,4},{6,7},{7,6},{8,9},{9,8},{10,11... | collective-permute-start | bytes 24584 | tf_op jit(solution)/shard_map/ppermute | solution.py:20
  46.5 6.1 %copy-start.17 = (f32[2,8,1,128]{3,2,1,0:T(1,128)}, f32[2,8,1,128]{3,2,1,0:T(1,128)S(1)}, u32[]{:S(2)}) copy-start(f32[2,8,1,128]{3,2,1,0:T(1,128)S(1)} %collective-permute-done.7.by_ref) | copy-start | bytes 24580
  52.6 0.6 copy-start.7
  55.9 4.5 %collective-permute-start.8 = (f32[2,64,128]{2,1,0:T(8,128)}, f32[2,64,128]{2,1,0:T(8,128)S(1)}, u32[]{:S(2)}, u32[]{:S(2)}) collective-permute-start(f32[2,64,128]{2,1,0:T(8,128)} %get-tuple-element.35), channel_id=1, source_target_pairs={{0,14},{2,0},{4,2},{6,4},{8,6},{10,8},{12,10},{14,12},{1,15},{3,1}... | collective-permute-start | bytes 196616 | tf_op jit(solution)/shard_map/ppermute | solution.py:20
  57.9 1.4 %collective-permute-start.9 = (f32[2,8,1,128]{3,2,1,0:T(1,128)}, f32[2,8,1,128]{3,2,1,0:T(1,128)S(1)}, u32[]{:S(2)}, u32[]{:S(2)}) collective-permute-start(f32[2,8,1,128]{3,2,1,0:T(1,128)} %get-tuple-element.36), channel_id=1, source_target_pairs={{0,1},{1,0},{2,3},{3,2},{4,5},{5,4},{6,7},{7,6},{8,9},{9,8},{10,11... | collective-permute-start | bytes 24584 | tf_op jit(solution)/shard_map/ppermute | solution.py:20
  59.3 1.1 copy-start.18
  60.3 0.6 copy-start.8
  63.4 7.2 %collective-permute-start.10 = (f32[2,64,128]{2,1,0:T(8,128)}, f32[2,64,128]{2,1,0:T(8,128)S(1)}, u32[]{:S(2)}, u32[]{:S(2)}) collective-permute-start(f32[2,64,128]{2,1,0:T(8,128)} %get-tuple-element.38), channel_id=1, source_target_pairs={{0,2},{2,4},{4,6},{6,8},{8,10},{10,12},{12,14},{14,0},{1,3},{3,5},... | collective-permute-start | bytes 196616 | tf_op jit(solution)/shard_map/ppermute | solution.py:20
  63.4 1.4 %collective-permute-start.11 = (f32[2,8,1,128]{3,2,1,0:T(1,128)}, f32[2,8,1,128]{3,2,1,0:T(1,128)S(1)}, u32[]{:S(2)}, u32[]{:S(2)}) collective-permute-start(f32[2,8,1,128]{3,2,1,0:T(1,128)} %get-tuple-element.39), channel_id=1, source_target_pairs={{0,1},{1,0},{2,3},{3,2},{4,5},{5,4},{6,7},{7,6},{8,9},{9,8},{10,11... | collective-permute-start | bytes 24584 | tf_op jit(solution)/shard_map/ppermute | solution.py:20
  64.8 5.8 %copy-start.16 = (f32[2,8,1,128]{3,2,1,0:T(1,128)}, f32[2,8,1,128]{3,2,1,0:T(1,128)S(1)}, u32[]{:S(2)}) copy-start(f32[2,8,1,128]{3,2,1,0:T(1,128)S(1)} %collective-permute-done.11.by_ref) | copy-start | bytes 24580
  70.6 0.6 copy-start.6
  73.9 4.5 %collective-permute-start.12 = (f32[2,64,128]{2,1,0:T(8,128)}, f32[2,64,128]{2,1,0:T(8,128)S(1)}, u32[]{:S(2)}, u32[]{:S(2)}) collective-permute-start(f32[2,64,128]{2,1,0:T(8,128)} %get-tuple-element.41), channel_id=1, source_target_pairs={{0,14},{2,0},{4,2},{6,4},{8,6},{10,8},{12,10},{14,12},{1,15},{3,1}... | collective-permute-start | bytes 196616 | tf_op jit(solution)/shard_map/ppermute | solution.py:20
  75.9 1.4 %collective-permute-start.13 = (f32[2,8,1,128]{3,2,1,0:T(1,128)}, f32[2,8,1,128]{3,2,1,0:T(1,128)S(1)}, u32[]{:S(2)}, u32[]{:S(2)}) collective-permute-start(f32[2,8,1,128]{3,2,1,0:T(1,128)} %get-tuple-element.42), channel_id=1, source_target_pairs={{0,1},{1,0},{2,3},{3,2},{4,5},{5,4},{6,7},{7,6},{8,9},{9,8},{10,11... | collective-permute-start | bytes 24584 | tf_op jit(solution)/shard_map/ppermute | solution.py:20
  77.3 1.1 copy-start.19
  78.4 0.6 copy-start.9
  79.0 13.1 %copy-start.2 = (f32[3,8,64,128]{3,2,1,0:T(8,128)S(1)}, f32[3,8,64,128]{3,2,1,0:T(8,128)}, u32[]{:S(2)}) copy-start(f32[3,8,64,128]{3,2,1,0:T(8,128)} %get-tuple-element.40.e_ref) | copy-start | bytes 2359300
  81.5 7.2 %collective-permute-start.14 = (f32[2,64,128]{2,1,0:T(8,128)}, f32[2,64,128]{2,1,0:T(8,128)S(1)}, u32[]{:S(2)}, u32[]{:S(2)}) collective-permute-start(f32[2,64,128]{2,1,0:T(8,128)} %get-tuple-element.44), channel_id=1, source_target_pairs={{0,2},{2,4},{4,6},{6,8},{8,10},{10,12},{12,14},{14,0},{1,3},{3,5},... | collective-permute-start | bytes 196616 | tf_op jit(solution)/shard_map/ppermute | solution.py:20
  81.5 2.0 %collective-permute-start.15 = (f32[2,8,1,128]{3,2,1,0:T(1,128)}, f32[2,8,1,128]{3,2,1,0:T(1,128)S(1)}, u32[]{:S(2)}, u32[]{:S(2)}) collective-permute-start(f32[2,8,1,128]{3,2,1,0:T(1,128)} %get-tuple-element.45), channel_id=1, source_target_pairs={{0,1},{1,0},{2,3},{3,2},{4,5},{5,4},{6,7},{7,6},{8,9},{9,8},{10,11... | collective-permute-start | bytes 24584 | tf_op jit(solution)/shard_map/ppermute | solution.py:20
  81.6 0.7 copy-start.22
  83.5 5.2 %copy-start.15 = (f32[2,8,1,128]{3,2,1,0:T(1,128)}, f32[2,8,1,128]{3,2,1,0:T(1,128)S(1)}, u32[]{:S(2)}) copy-start(f32[2,8,1,128]{3,2,1,0:T(1,128)S(1)} %collective-permute-done.15.by_ref) | copy-start | bytes 24580
  88.7 0.6 copy-start.5
  89.3 2.8 %copy-start = (f32[3,8,64,128]{3,2,1,0:T(8,128)S(1)}, f32[3,8,64,128]{3,2,1,0:T(8,128)}, u32[]{:S(2)}) copy-start(f32[3,8,64,128]{3,2,1,0:T(8,128)} %get-tuple-element.28.e_ref) | copy-start | bytes 2359300
  89.3 2.8 %copy-start.1 = (f32[3,8,64,128]{3,2,1,0:T(8,128)S(1)}, f32[3,8,64,128]{3,2,1,0:T(8,128)}, u32[]{:S(2)}) copy-start(f32[3,8,64,128]{3,2,1,0:T(8,128)} %get-tuple-element.34.e_ref) | copy-start | bytes 2359300

commit v2 on v1

--- a/solution.py
+++ b/solution.py
@@ -20,17 +20,31 @@
     return lax.ppermute(value, axis, pairs)
 
 
+def _coef_kernel(eps_ref, sigma_ref, mat_ref, keep_out, drive_out):
+    planes = mat_ref.shape[0]
+    for x in range(planes):
+        material = mat_ref[x]
+        permit = jnp.zeros(material.shape, jnp.float32)
+        conduct = jnp.zeros(material.shape, jnp.float32)
+        for label in range(eps_ref.shape[0]):
+            hit = material == label
+            permit = jnp.where(hit, eps_ref[label], permit)
+            conduct = jnp.where(hit, sigma_ref[label], conduct)
+        loss = conduct * TIME_STEP / (2.0 * permit)
+        keep_out[x] = (1.0 - loss) / (1.0 + loss)
+        drive_out[x] = TIME_STEP / (permit * (1.0 + loss))
+
+
 def coefficients(material, eps_table, sigma_table):
-    permit = jnp.zeros(material.shape, jnp.float32)
-    conduct = jnp.zeros(material.shape, jnp.float32)
-    for label in range(eps_table.shape[0]):
-        hit = material == label
-        permit = jnp.where(hit, eps_table[label], permit)
-        conduct = jnp.where(hit, sigma_table[label], conduct)
-    loss = conduct * TIME_STEP / (2.0 * permit)
-    keep = (1.0 - loss) / (1.0 + loss)
-    drive = TIME_STEP / (permit * (1.0 + loss))
-    return (keep, drive)
+    scalar = pl.BlockSpec(memory_space=pltpu.SMEM)
+    whole = pl.BlockSpec(memory_space=pltpu.VMEM)
+    out = jax.ShapeDtypeStruct(material.shape, jnp.float32)
+    return pl.pallas_call(
+        _coef_kernel,
+        out_shape=(out, out),
+        in_specs=[scalar, scalar, whole],
+        out_specs=(whole, whole),
+    )(eps_table, sigma_table, material)
 
 
 def _z_up(f):
@@ -166,13 +180,9 @@
     imag_part = jnp.dot(
         cosine, flat_imag, precision=high, preferred_element_type=jnp.float32
     ) - jnp.dot(sine, flat_real, precision=high, preferred_element_type=jnp.float32)
-    rows_sum = lax.psum_scatter(
-        jnp.stack([real_part[:, 0], imag_part[:, 0], real_part[:, 1], imag_part[:, 1]], axis=1),
-        "gx",
-        scatter_dimension=0,
-        tiled=True,
-    )
-    far_field = lax.psum(rows_sum, "gy") * scale
+    terms = jnp.stack([real_part[:, 0], imag_part[:, 0], real_part[:, 1], imag_part[:, 1]], axis=1)
+    total = lax.psum(terms, ("gx", "gy"))
+    far_field = lax.dynamic_slice_in_dim(total, lax.axis_index("gx") * owned, owned, 0) * scale
     return (elec, magn, far_field)
 
 

time: 123 us -> 116 us (0.943)
  other arithmetic: 20.6 us -> 2.48 us
  waiting for transfers between devices: 26.1 us -> 35.3 us
  blocking collectives: 21.6 us -> 29.5 us
  starting transfers between devices: 15.2 us -> 11.3 us
  local copies, waits for them, and re-layouts: 11 us -> 8.34 us
  Pallas kernels: 20.7 us -> 22.7 us
    psum x1, blocking collectives: 2.44 us -> 29.5 us  [local(): total = lax.psum(terms, ('gx', 'gy'))]
    unnamed x1 -> x0, blocking collectives: 19.1 us -> none
    div x2 -> x0, other arithmetic: 18.2 us -> none  [the longest x1 9.61 us: coefficients(): drive = TIME_STEP / (permit * (1.0 + loss))]
    ppermute x16, waiting for transfers between devices: 26.1 us -> 35.3 us  [shifted(): return lax.ppermute(value, axis, pairs)]
    ppermute x16, starting transfers between devices: 15.2 us -> 11.3 us  [shifted(): return lax.ppermute(value, axis, pairs)]
    pallas_call x0 -> x1, Pallas kernels: none -> 2.01 us  [coefficients(): pl.pallas_call(_coef_kernel, out_shape=(out, out), in_specs=[scalar, scal...]
    slice x2 -> x0, local copies, waits for them, and re-layouts: 1.34 us -> none  [the longest x1 0.68 us: coefficients(): conduct = jnp.where(hit, sigma_table[label], conduct)]
    unnamed x48 -> x40, local copies, waits for them, and re-layouts: 7.53 us -> 6.21 us
  transfers between devices with their start and end apart: 16 -> 16, of which waited for: 11 -> 14; matrix products, arithmetic and copies ran while one was open for 17% -> 1% of each run, Pallas kernels for 0% -> 2%
where the time goes in v2:
time: 116 us
  waiting for transfers between devices  35.3 us (30%)
  blocking collectives  29.5 us (25%)
  Pallas kernels  22.7 us (20%)
  starting transfers between devices  11.3 us (10%)
  local copies, waits for them, and re-layouts  8.34 us (7%)
  matrix products  5.39 us (5%)
  other arithmetic  2.48 us (2%)
    ppermute x16, waiting for transfers between devices, shifted(): return lax.ppermute(value, axis, pairs)  35.3 us
    psum x1, blocking collectives, local(): total = lax.psum(terms, ('gx', 'gy'))  29.5 us
    ppermute x16, starting transfers between devices, shifted(): return lax.ppermute(value, axis, pairs)  11.3 us
    pallas_call x4, Pallas kernels, local(): elec_call(elec, magn, keep, drive, behind_x, behind_y)  10.7 us
    pallas_call x4, Pallas kernels, local(): magn, back_x, back_y = magn_call(elec, magn, ahead_x, ahead_y)  9.96 us
    unnamed x40, local copies, waits for them, and re-layouts  6.21 us
  transfers between devices with their start and end apart: 16, of which 14 were waited for; matrix products, arithmetic and copies ran while one was open for 1% of the time, Pallas kernels for 2%

profile of v2, /device:TPU:0, one launch (start us, length us, event | category | flops | bytes accessed | tf_op | source)
XLA Modules:
  0.0 115.7 jit_solution(17001047329830987920)
XLA Ops:
  0.6 0.9 slice_bitcast_fusion
  1.5 6.0 %collective-permute-start = (f32[2,64,128]{2,1,0:T(8,128)S(1)}, f32[2,64,128]{2,1,0:T(8,128)S(1)}, u32[]{:S(2)}, u32[]{:S(2)}) collective-permute-start(f32[2,64,128]{2,1,0:T(8,128)S(1)} %slice_bitcast_fusion), channel_id=1, source_target_pairs={{0,14},{2,0},{4,2},{6,4},{8,6},{10,8},{12,10},{14,12},{1,15},{3,1}... | collective-permute-start | bytes 196616 | tf_op jit(solution)/shard_map/ppermute | solution.py:20
  7.5 0.8 fusion.31
  8.3 0.1 collective-permute-start.1
  8.4 1.2 %collective-permute-done.1.ay_ref = f32[2,8,1,128]{3,2,1,0:T(1,128)S(1)} collective-permute-done((f32[2,8,1,128]{3,2,1,0:T(1,128)S(1)}, f32[2,8,1,128]{3,2,1,0:T(1,128)S(1)}, u32[]{:S(2)}, u32[]{:S(2)}) %collective-permute-start.1) | collective-permute-done | bytes 8224 | tf_op jit(solution)/shard_map/ppermute | solution.py:20
  9.5 0.0 collective-permute-done.ax_ref
  9.5 0.6 copy-done.18
  10.1 0.6 copy-done.6
  10.7 2.5 %shard_map.85 = (f32[3,8,64,128]{3,2,1,0:T(8,128)}, f32[2,64,128]{2,1,0:T(8,128)}, f32[2,8,1,128]{3,2,1,0:T(1,128)}) custom-call(f32[3,8,64,128]{3,2,1,0:T(8,128)} %e_ref.3, f32[3,8,64,128]{3,2,1,0:T(8,128)} %h_ref.1, f32[2,64,128]{2,1,0:T(8,128)} %copy-done.6, f32[2,8,1,128]{3,2,1,0:T(1,128)} %copy-done.18), custom_call_target="tpu_custom_call" | custom-call | tf_op jit(solution)/shard_map/pallas_call | solution.py:149
  13.2 0.0 collective-permute-start.2
  13.2 0.2 collective-permute-start.3
  13.4 2.0 %shard_map.86 = (f32[8,64,128]{2,1,0:T(8,128)}, f32[8,64,128]{2,1,0:T(8,128)}) custom-call(f32[6]{0:T(128)} %eps_ref.1, f32[6]{0:T(128)} %sigma_ref.1, s32[8,64,128]{2,1,0:T(8,128)} %mat_ref.1), custom_call_target="tpu_custom_call" | custom-call | tf_op jit(solution)/shard_map/pallas_call | solution.py:42
  15.4 0.0 collective-permute-done.3.by_ref
  15.4 5.0 %collective-permute-done.2.bx_ref = f32[2,64,128]{2,1,0:T(8,128)S(1)} collective-permute-done((f32[2,64,128]{2,1,0:T(8,128)}, f32[2,64,128]{2,1,0:T(8,128)S(1)}, u32[]{:S(2)}, u32[]{:S(2)}) %collective-permute-start.2) | collective-permute-done | bytes 65568 | tf_op jit(solution)/shard_map/ppermute | solution.py:20
  20.4 0.6 copy-done.7
  21.0 2.6 %shard_map.87 = (f32[3,8,64,128]{3,2,1,0:T(8,128)}, f32[2,64,128]{2,1,0:T(8,128)}, f32[2,8,1,128]{3,2,1,0:T(1,128)}) custom-call(f32[3,8,64,128]{3,2,1,0:T(8,128)} %e_ref.3, f32[3,8,64,128]{3,2,1,0:T(8,128)} %get-tuple-element.27.h_ref, f32[8,64,128]{2,1,0:T(8,128)} %get-tuple-element.28.keep_ref, f32[8,64,128]{2,1,0:T(8,128)} %get-tuple-element.29.drive_ref, ...), custom_call_target="tpu_custom_call" | custom-call | tf_op jit(solution)/shard_map/pallas_call | solution.py:152
  23.7 1.6 %collective-permute-start.4 = (f32[2,64,128]{2,1,0:T(8,128)}, f32[2,64,128]{2,1,0:T(8,128)S(1)}, u32[]{:S(2)}, u32[]{:S(2)}) collective-permute-start(f32[2,64,128]{2,1,0:T(8,128)} %get-tuple-element.33), channel_id=1, source_target_pairs={{0,14},{2,0},{4,2},{6,4},{8,6},{10,8},{12,10},{14,12},{1,15},{3,1}... | collective-permute-start | bytes 196616 | tf_op jit(solution)/shard_map/ppermute | solution.py:20
  25.3 0.0 collective-permute-start.5
  25.3 1.4 %collective-permute-done.5.ay_ref = f32[2,8,1,128]{3,2,1,0:T(1,128)S(1)} collective-permute-done((f32[2,8,1,128]{3,2,1,0:T(1,128)}, f32[2,8,1,128]{3,2,1,0:T(1,128)S(1)}, u32[]{:S(2)}, u32[]{:S(2)}) %collective-permute-start.5) | collective-permute-done | bytes 8224 | tf_op jit(solution)/shard_map/ppermute | solution.py:20
  26.7 1.4 %collective-permute-done.4.ax_ref = f32[2,64,128]{2,1,0:T(8,128)S(1)} collective-permute-done((f32[2,64,128]{2,1,0:T(8,128)}, f32[2,64,128]{2,1,0:T(8,128)S(1)}, u32[]{:S(2)}, u32[]{:S(2)}) %collective-permute-start.4) | collective-permute-done | bytes 65568 | tf_op jit(solution)/shard_map/ppermute | solution.py:20
  28.1 0.6 copy-done.10
  28.8 2.5 %shard_map.88 = (f32[3,8,64,128]{3,2,1,0:T(8,128)}, f32[2,64,128]{2,1,0:T(8,128)}, f32[2,8,1,128]{3,2,1,0:T(1,128)}) custom-call(f32[3,8,64,128]{3,2,1,0:T(8,128)} %get-tuple-element.32.e_ref, f32[3,8,64,128]{3,2,1,0:T(8,128)} %get-tuple-element.27.h_ref, f32[2,64,128]{2,1,0:T(8,128)} %copy-done.10, f32[2,8,1,128]{3,2,1,0:T(1,128)} %copy-done.17), custom_call_target="tpu_custom_call" | custom-call | tf_op jit(solution)/shard_map/pallas_call | solution.py:149
  31.2 0.0 collective-permute-start.6
  31.2 0.1 collective-permute-start.7
  31.3 0.6 copy-done.19
  31.9 0.8 collective-permute-done.7.by_ref
  32.7 5.7 %collective-permute-done.6.bx_ref = f32[2,64,128]{2,1,0:T(8,128)S(1)} collective-permute-done((f32[2,64,128]{2,1,0:T(8,128)}, f32[2,64,128]{2,1,0:T(8,128)S(1)}, u32[]{:S(2)}, u32[]{:S(2)}) %collective-permute-start.6) | collective-permute-done | bytes 65568 | tf_op jit(solution)/shard_map/ppermute | solution.py:20
  38.4 0.6 copy-done.5
  39.0 2.6 %shard_map.89 = (f32[3,8,64,128]{3,2,1,0:T(8,128)}, f32[2,64,128]{2,1,0:T(8,128)}, f32[2,8,1,128]{3,2,1,0:T(1,128)}) custom-call(f32[3,8,64,128]{3,2,1,0:T(8,128)} %get-tuple-element.32.e_ref, f32[3,8,64,128]{3,2,1,0:T(8,128)} %get-tuple-element.35.h_ref, f32[8,64,128]{2,1,0:T(8,128)} %get-tuple-element.28.keep_ref, ...), custom_call_target="tpu_custom_call" | custom-call | tf_op jit(solution)/shard_map/pallas_call | solution.py:152
  41.7 1.6 %collective-permute-start.8 = (f32[2,64,128]{2,1,0:T(8,128)}, f32[2,64,128]{2,1,0:T(8,128)S(1)}, u32[]{:S(2)}, u32[]{:S(2)}) collective-permute-start(f32[2,64,128]{2,1,0:T(8,128)} %get-tuple-element.39), channel_id=1, source_target_pairs={{0,14},{2,0},{4,2},{6,4},{8,6},{10,8},{12,10},{14,12},{1,15},{3,1}... | collective-permute-start | bytes 196616 | tf_op jit(solution)/shard_map/ppermute | solution.py:20
  43.3 1.4 %collective-permute-done.9.ay_ref = f32[2,8,1,128]{3,2,1,0:T(1,128)S(1)} collective-permute-done((f32[2,8,1,128]{3,2,1,0:T(1,128)}, f32[2,8,1,128]{3,2,1,0:T(1,128)S(1)}, u32[]{:S(2)}, u32[]{:S(2)}) %collective-permute-start.9) | collective-permute-done | bytes 8224 | tf_op jit(solution)/shard_map/ppermute | solution.py:20
  44.7 1.4 %collective-permute-done.8.ax_ref = f32[2,64,128]{2,1,0:T(8,128)S(1)} collective-permute-done((f32[2,64,128]{2,1,0:T(8,128)}, f32[2,64,128]{2,1,0:T(8,128)S(1)}, u32[]{:S(2)}, u32[]{:S(2)}) %collective-permute-start.8) | collective-permute-done | bytes 65568 | tf_op jit(solution)/shard_map/ppermute | solution.py:20
  46.2 0.6 copy-done.8
  46.8 2.5 %shard_map.90 = (f32[3,8,64,128]{3,2,1,0:T(8,128)}, f32[2,64,128]{2,1,0:T(8,128)}, f32[2,8,1,128]{3,2,1,0:T(1,128)}) custom-call(f32[3,8,64,128]{3,2,1,0:T(8,128)} %get-tuple-element.38.e_ref, f32[3,8,64,128]{3,2,1,0:T(8,128)} %get-tuple-element.35.h_ref, f32[2,64,128]{2,1,0:T(8,128)} %copy-done.8, f32[2,8,1,128]{3,2,1,0:T(1,128)} %copy-done.15), custom_call_target="tpu_custom_call" | custom-call | tf_op jit(solution)/shard_map/pallas_call | solution.py:149
  49.3 0.0 collective-permute-start.10
  49.3 0.0 collective-permute-start.11
  49.3 0.1 multiply_multiply_fusion
  49.3 1.3 %collective-permute-done.11.by_ref = f32[2,8,1,128]{3,2,1,0:T(1,128)S(1)} collective-permute-done((f32[2,8,1,128]{3,2,1,0:T(1,128)}, f32[2,8,1,128]{3,2,1,0:T(1,128)S(1)}, u32[]{:S(2)}, u32[]{:S(2)}) %collective-permute-start.11) | collective-permute-done | bytes 8224 | tf_op jit(solution)/shard_map/ppermute | solution.py:20
  50.6 5.8 %collective-permute-done.10.bx_ref = f32[2,64,128]{2,1,0:T(8,128)S(1)} collective-permute-done((f32[2,64,128]{2,1,0:T(8,128)}, f32[2,64,128]{2,1,0:T(8,128)S(1)}, u32[]{:S(2)}, u32[]{:S(2)}) %collective-permute-start.10) | collective-permute-done | bytes 65568 | tf_op jit(solution)/shard_map/ppermute | solution.py:20
  56.4 0.6 copy-done.3
  57.1 2.7 %shard_map.91 = (f32[3,8,64,128]{3,2,1,0:T(8,128)}, f32[2,64,128]{2,1,0:T(8,128)}, f32[2,8,1,128]{3,2,1,0:T(1,128)}) custom-call(f32[3,8,64,128]{3,2,1,0:T(8,128)} %get-tuple-element.38.e_ref, f32[3,8,64,128]{3,2,1,0:T(8,128)} %get-tuple-element.41.h_ref, f32[8,64,128]{2,1,0:T(8,128)} %get-tuple-element.28.keep_ref, ...), custom_call_target="tpu_custom_call" | custom-call | tf_op jit(solution)/shard_map/pallas_call | solution.py:152
  59.7 1.6 %collective-permute-start.12 = (f32[2,64,128]{2,1,0:T(8,128)}, f32[2,64,128]{2,1,0:T(8,128)S(1)}, u32[]{:S(2)}, u32[]{:S(2)}) collective-permute-start(f32[2,64,128]{2,1,0:T(8,128)} %get-tuple-element.45), channel_id=1, source_target_pairs={{0,14},{2,0},{4,2},{6,4},{8,6},{10,8},{12,10},{14,12},{1,15},{3,1}... | collective-permute-start | bytes 196616 | tf_op jit(solution)/shard_map/ppermute | solution.py:20
  61.4 0.0 collective-permute-start.13
  61.4 1.4 %collective-permute-done.13.ay_ref = f32[2,8,1,128]{3,2,1,0:T(1,128)S(1)} collective-permute-done((f32[2,8,1,128]{3,2,1,0:T(1,128)}, f32[2,8,1,128]{3,2,1,0:T(1,128)S(1)}, u32[]{:S(2)}, u32[]{:S(2)}) %collective-permute-start.13) | collective-permute-done | bytes 8224 | tf_op jit(solution)/shard_map/ppermute | solution.py:20
  62.7 1.4 %collective-permute-done.12.ax_ref = f32[2,64,128]{2,1,0:T(8,128)S(1)} collective-permute-done((f32[2,64,128]{2,1,0:T(8,128)}, f32[2,64,128]{2,1,0:T(8,128)S(1)}, u32[]{:S(2)}, u32[]{:S(2)}) %collective-permute-start.12) | collective-permute-done | bytes 65568 | tf_op jit(solution)/shard_map/ppermute | solution.py:20
  64.2 0.6 copy-done.9
  64.8 2.5 %shard_map.92 = (f32[3,8,64,128]{3,2,1,0:T(8,128)}, f32[2,64,128]{2,1,0:T(8,128)}, f32[2,8,1,128]{3,2,1,0:T(1,128)}) custom-call(f32[3,8,64,128]{3,2,1,0:T(8,128)} %get-tuple-element.44.e_ref, f32[3,8,64,128]{3,2,1,0:T(8,128)} %get-tuple-element.41.h_ref, f32[2,64,128]{2,1,0:T(8,128)} %copy-done.9, f32[2,8,1,128]{3,2,1,0:T(1,128)} %copy-done.16), custom_call_target="tpu_custom_call" | custom-call | tf_op jit(solution)/shard_map/pallas_call | solution.py:149
  67.4 0.0 collective-permute-start.14
  67.4 0.0 collective-permute-start.15
  67.4 0.1 multiply_multiply_fusion.1
  67.4 1.3 %collective-permute-done.15.by_ref = f32[2,8,1,128]{3,2,1,0:T(1,128)S(1)} collective-permute-done((f32[2,8,1,128]{3,2,1,0:T(1,128)}, f32[2,8,1,128]{3,2,1,0:T(1,128)S(1)}, u32[]{:S(2)}, u32[]{:S(2)}) %collective-permute-start.15) | collective-permute-done | bytes 8224 | tf_op jit(solution)/shard_map/ppermute | solution.py:20
  68.7 5.8 %collective-permute-done.14.bx_ref = f32[2,64,128]{2,1,0:T(8,128)S(1)} collective-permute-done((f32[2,64,128]{2,1,0:T(8,128)}, f32[2,64,128]{2,1,0:T(8,128)S(1)}, u32[]{:S(2)}, u32[]{:S(2)}) %collective-permute-start.14) | collective-permute-done | bytes 65568 | tf_op jit(solution)/shard_map/ppermute | solution.py:20
  74.5 0.6 copy-done.4
  75.2 2.8 %shard_map.93 = (f32[3,8,64,128]{3,2,1,0:T(8,128)}, f32[2,64,128]{2,1,0:T(8,128)}, f32[2,8,1,128]{3,2,1,0:T(1,128)}) custom-call(f32[3,8,64,128]{3,2,1,0:T(8,128)} %get-tuple-element.44.e_ref, f32[3,8,64,128]{3,2,1,0:T(8,128)} %get-tuple-element.25.h_ref, f32[8,64,128]{2,1,0:T(8,128)} %get-tuple-element.28.keep_ref, ...), custom_call_target="tpu_custom_call" | custom-call | tf_op jit(solution)/shard_map/pallas_call | solution.py:152
  77.9 1.7 %multiply_add_fusion = (f32[2,8,64,1]{3,2,1,0:T(8,128)S(1)}, f32[2,8,64,1]{3,2,1,0:T(8,128)S(1)}) fusion(f32[3,8,64,128]{3,2,1,0:T(8,128)} %get-tuple-element.24, f32[3,8,64,128]{3,2,1,0:T(8,128)S(1)} %copy-done.2, f32[3,8,64,128]{3,2,1,0:T(8,128)S(1)} %copy-done.1, f32[3,8,64,128]{3,2,1,0:T(8,128)S(1)} %copy-done), kind=kLoop, calls=%fused_computation.7 | loop fusion | flops 15360 | bytes 24576 | tf_op jit(solution)/shard_map/add | solution.py:154
  79.6 0.2 copy.27
  79.8 0.2 copy.26
  80.0 1.3 %convolution_bitcast_fusion.1 = f32[64,2]{0,1:T(2,128)S(1)} fusion(s32[64,64]{1,0:T(8,128)S(1)} %multiply_multiply_fusion, s32[64,8]{0,1:T(8,128)S(1)} %multiply_multiply_fusion.1, f32[2,8,64,1]{2,0,1,3:T(2,128)S(1)} %copy.27), kind=kOutput, calls=%fused_computation.2 | convolution fusion | flops 1245184 | bytes 23040 | tf_op jit(solution)/shard_map/dot_general | solution.py:180
  81.3 1.4 %convolution_bitcast_fusion.3 = f32[64,2]{0,1:T(2,128)S(1)} fusion(s32[64,64]{1,0:T(8,128)S(1)} %multiply_multiply_fusion, s32[64,8]{0,1:T(8,128)S(1)} %multiply_multiply_fusion.1, f32[2,8,64,1]{2,0,1,3:T(2,128)S(1)} %copy.26), kind=kOutput, calls=%fused_computation.5 | convolution fusion | flops 1245184 | bytes 23040 | tf_op jit(solution)/shard_map/dot_general | solution.py:177
  82.7 1.4 %fusion = f32[64,2]{0,1:T(2,128)S(1)} fusion(f32[64,2]{0,1:T(2,128)S(1)} %convolution_bitcast_fusion.1, s32[64,64]{1,0:T(8,128)S(1)} %multiply_multiply_fusion, s32[64,8]{0,1:T(8,128)S(1)} %multiply_multiply_fusion.1, f32[2,8,64,1]{2,0,1,3:T(2,128)S(1)} %copy.26), kind=kOutput, calls=%fused_computation.1 | convolution fusion | flops 1245312 | bytes 23552 | tf_op jit(solution)/shard_map/dot_general | solution.py:182
  84.1 1.4 %fusion.1 = f32[64,2]{0,1:T(2,128)S(1)} fusion(f32[64,2]{0,1:T(2,128)S(1)} %convolution_bitcast_fusion.3, s32[64,64]{1,0:T(8,128)S(1)} %multiply_multiply_fusion, s32[64,8]{0,1:T(8,128)S(1)} %multiply_multiply_fusion.1, f32[2,8,64,1]{2,0,1,3:T(2,128)S(1)} %copy.27), kind=kOutput, calls=%fused_computation.4 | convolution fusion | flops 1245312 | bytes 23552 | tf_op jit(solution)/shard_map/dot_general | solution.py:179
  85.4 0.1 fusion.32
  85.5 29.5 %psum.7 = f32[64,4]{0,1:T(4,128)S(1)} all-reduce(f32[64,4]{0,1:T(4,128)S(1)} %pad_maximum_fusion.1), channel_id=1, replica_groups=mesh['clip'=2,'gx'=8,'gy'=2] {'gx','gy'}, use_global_device_ids=true, to_apply=%region_0.1 | all-reduce | flops 256 | bytes 2048 | tf_op jit(solution)/shard_map/psum | solution.py:184
  115.0 0.7 dynamic-slice_multiply_fusion
  (36 shorter events, 0.1 us)
Async XLA Ops:
  1.5 8.0 %collective-permute-start = (f32[2,64,128]{2,1,0:T(8,128)S(1)}, f32[2,64,128]{2,1,0:T(8,128)S(1)}, u32[]{:S(2)}, u32[]{:S(2)}) collective-permute-start(f32[2,64,128]{2,1,0:T(8,128)S(1)} %slice_bitcast_fusion), channel_id=1, source_target_pairs={{0,14},{2,0},{4,2},{6,4},{8,6},{10,8},{12,10},{14,12},{1,15},{3,1}... | collective-permute-start | bytes 196616 | tf_op jit(solution)/shard_map/ppermute | solution.py:20
  8.3 1.2 %collective-permute-start.1 = (f32[2,8,1,128]{3,2,1,0:T(1,128)S(1)}, f32[2,8,1,128]{3,2,1,0:T(1,128)S(1)}, u32[]{:S(2)}, u32[]{:S(2)}) collective-permute-start(f32[2,8,1,128]{3,2,1,0:T(1,128)S(1)} %pad_maximum_fusion), channel_id=1, source_target_pairs={{0,1},{1,0},{2,3},{3,2},{4,5},{5,4},{6,7},{7,6},{8,9},{9,8},{10,11... | collective-permute-start | bytes 24584 | tf_op jit(solution)/shard_map/ppermute | solution.py:20
  9.5 0.6 copy-start.18
  10.1 0.6 copy-start.6
  13.2 7.2 %collective-permute-start.2 = (f32[2,64,128]{2,1,0:T(8,128)}, f32[2,64,128]{2,1,0:T(8,128)S(1)}, u32[]{:S(2)}, u32[]{:S(2)}) collective-permute-start(f32[2,64,128]{2,1,0:T(8,128)} %get-tuple-element.30), channel_id=1, source_target_pairs={{0,2},{2,4},{4,6},{6,8},{8,10},{10,12},{12,14},{14,0},{1,3},{3,5},... | collective-permute-start | bytes 196616 | tf_op jit(solution)/shard_map/ppermute | solution.py:20
  13.2 2.2 %collective-permute-start.3 = (f32[2,8,1,128]{3,2,1,0:T(1,128)}, f32[2,8,1,128]{3,2,1,0:T(1,128)S(1)}, u32[]{:S(2)}, u32[]{:S(2)}) collective-permute-start(f32[2,8,1,128]{3,2,1,0:T(1,128)} %get-tuple-element.31), channel_id=1, source_target_pairs={{0,1},{1,0},{2,3},{3,2},{4,5},{5,4},{6,7},{7,6},{8,9},{9,8},{10,11... | collective-permute-start | bytes 24584 | tf_op jit(solution)/shard_map/ppermute | solution.py:20
  15.4 5.0 %copy-start.14 = (f32[2,8,1,128]{3,2,1,0:T(1,128)}, f32[2,8,1,128]{3,2,1,0:T(1,128)S(1)}, u32[]{:S(2)}) copy-start(f32[2,8,1,128]{3,2,1,0:T(1,128)S(1)} %collective-permute-done.3.by_ref) | copy-start | bytes 24580
  20.4 0.6 copy-start.7
  23.7 4.5 %collective-permute-start.4 = (f32[2,64,128]{2,1,0:T(8,128)}, f32[2,64,128]{2,1,0:T(8,128)S(1)}, u32[]{:S(2)}, u32[]{:S(2)}) collective-permute-start(f32[2,64,128]{2,1,0:T(8,128)} %get-tuple-element.33), channel_id=1, source_target_pairs={{0,14},{2,0},{4,2},{6,4},{8,6},{10,8},{12,10},{14,12},{1,15},{3,1}... | collective-permute-start | bytes 196616 | tf_op jit(solution)/shard_map/ppermute | solution.py:20
  25.3 1.4 %collective-permute-start.5 = (f32[2,8,1,128]{3,2,1,0:T(1,128)}, f32[2,8,1,128]{3,2,1,0:T(1,128)S(1)}, u32[]{:S(2)}, u32[]{:S(2)}) collective-permute-start(f32[2,8,1,128]{3,2,1,0:T(1,128)} %get-tuple-element.34), channel_id=1, source_target_pairs={{0,1},{1,0},{2,3},{3,2},{4,5},{5,4},{6,7},{7,6},{8,9},{9,8},{10,11... | collective-permute-start | bytes 24584 | tf_op jit(solution)/shard_map/ppermute | solution.py:20
  26.7 1.5 %copy-start.17 = (f32[2,8,1,128]{3,2,1,0:T(1,128)}, f32[2,8,1,128]{3,2,1,0:T(1,128)S(1)}, u32[]{:S(2)}) copy-start(f32[2,8,1,128]{3,2,1,0:T(1,128)S(1)} %collective-permute-done.5.ay_ref) | copy-start | bytes 24580
  28.1 0.6 copy-start.10
  31.2 0.7 copy-start.19
  31.2 7.2 %collective-permute-start.6 = (f32[2,64,128]{2,1,0:T(8,128)}, f32[2,64,128]{2,1,0:T(8,128)S(1)}, u32[]{:S(2)}, u32[]{:S(2)}) collective-permute-start(f32[2,64,128]{2,1,0:T(8,128)} %get-tuple-element.36), channel_id=1, source_target_pairs={{0,2},{2,4},{4,6},{6,8},{8,10},{10,12},{12,14},{14,0},{1,3},{3,5},... | collective-permute-start | bytes 196616 | tf_op jit(solution)/shard_map/ppermute | solution.py:20
  31.2 1.4 %collective-permute-start.7 = (f32[2,8,1,128]{3,2,1,0:T(1,128)}, f32[2,8,1,128]{3,2,1,0:T(1,128)S(1)}, u32[]{:S(2)}, u32[]{:S(2)}) collective-permute-start(f32[2,8,1,128]{3,2,1,0:T(1,128)} %get-tuple-element.37), channel_id=1, source_target_pairs={{0,1},{1,0},{2,3},{3,2},{4,5},{5,4},{6,7},{7,6},{8,9},{9,8},{10,11... | collective-permute-start | bytes 24584 | tf_op jit(solution)/shard_map/ppermute | solution.py:20
  32.7 5.7 %copy-start.13 = (f32[2,8,1,128]{3,2,1,0:T(1,128)}, f32[2,8,1,128]{3,2,1,0:T(1,128)S(1)}, u32[]{:S(2)}) copy-start(f32[2,8,1,128]{3,2,1,0:T(1,128)S(1)} %collective-permute-done.7.by_ref) | copy-start | bytes 24580
  38.4 0.6 copy-start.5
  41.7 4.5 %collective-permute-start.8 = (f32[2,64,128]{2,1,0:T(8,128)}, f32[2,64,128]{2,1,0:T(8,128)S(1)}, u32[]{:S(2)}, u32[]{:S(2)}) collective-permute-start(f32[2,64,128]{2,1,0:T(8,128)} %get-tuple-element.39), channel_id=1, source_target_pairs={{0,14},{2,0},{4,2},{6,4},{8,6},{10,8},{12,10},{14,12},{1,15},{3,1}... | collective-permute-start | bytes 196616 | tf_op jit(solution)/shard_map/ppermute | solution.py:20
  43.3 1.4 %collective-permute-start.9 = (f32[2,8,1,128]{3,2,1,0:T(1,128)}, f32[2,8,1,128]{3,2,1,0:T(1,128)S(1)}, u32[]{:S(2)}, u32[]{:S(2)}) collective-permute-start(f32[2,8,1,128]{3,2,1,0:T(1,128)} %get-tuple-element.40), channel_id=1, source_target_pairs={{0,1},{1,0},{2,3},{3,2},{4,5},{5,4},{6,7},{7,6},{8,9},{9,8},{10,11... | collective-permute-start | bytes 24584 | tf_op jit(solution)/shard_map/ppermute | solution.py:20
  44.7 1.5 %copy-start.15 = (f32[2,8,1,128]{3,2,1,0:T(1,128)}, f32[2,8,1,128]{3,2,1,0:T(1,128)S(1)}, u32[]{:S(2)}) copy-start(f32[2,8,1,128]{3,2,1,0:T(1,128)S(1)} %collective-permute-done.9.ay_ref) | copy-start | bytes 24580
  46.2 0.6 copy-start.8
  49.3 7.2 %collective-permute-start.10 = (f32[2,64,128]{2,1,0:T(8,128)}, f32[2,64,128]{2,1,0:T(8,128)S(1)}, u32[]{:S(2)}, u32[]{:S(2)}) collective-permute-start(f32[2,64,128]{2,1,0:T(8,128)} %get-tuple-element.42), channel_id=1, source_target_pairs={{0,2},{2,4},{4,6},{6,8},{8,10},{10,12},{12,14},{14,0},{1,3},{3,5},... | collective-permute-start | bytes 196616 | tf_op jit(solution)/shard_map/ppermute | solution.py:20
  49.3 1.4 %collective-permute-start.11 = (f32[2,8,1,128]{3,2,1,0:T(1,128)}, f32[2,8,1,128]{3,2,1,0:T(1,128)S(1)}, u32[]{:S(2)}, u32[]{:S(2)}) collective-permute-start(f32[2,8,1,128]{3,2,1,0:T(1,128)} %get-tuple-element.43), channel_id=1, source_target_pairs={{0,1},{1,0},{2,3},{3,2},{4,5},{5,4},{6,7},{7,6},{8,9},{9,8},{10,11... | collective-permute-start | bytes 24584 | tf_op jit(solution)/shard_map/ppermute | solution.py:20
  50.6 5.8 %copy-start.11 = (f32[2,8,1,128]{3,2,1,0:T(1,128)}, f32[2,8,1,128]{3,2,1,0:T(1,128)S(1)}, u32[]{:S(2)}) copy-start(f32[2,8,1,128]{3,2,1,0:T(1,128)S(1)} %collective-permute-done.11.by_ref) | copy-start | bytes 24580
  56.4 0.6 copy-start.3
  59.7 4.5 %collective-permute-start.12 = (f32[2,64,128]{2,1,0:T(8,128)}, f32[2,64,128]{2,1,0:T(8,128)S(1)}, u32[]{:S(2)}, u32[]{:S(2)}) collective-permute-start(f32[2,64,128]{2,1,0:T(8,128)} %get-tuple-element.45), channel_id=1, source_target_pairs={{0,14},{2,0},{4,2},{6,4},{8,6},{10,8},{12,10},{14,12},{1,15},{3,1}... | collective-permute-start | bytes 196616 | tf_op jit(solution)/shard_map/ppermute | solution.py:20
  61.4 1.4 %collective-permute-start.13 = (f32[2,8,1,128]{3,2,1,0:T(1,128)}, f32[2,8,1,128]{3,2,1,0:T(1,128)S(1)}, u32[]{:S(2)}, u32[]{:S(2)}) collective-permute-start(f32[2,8,1,128]{3,2,1,0:T(1,128)} %get-tuple-element.46), channel_id=1, source_target_pairs={{0,1},{1,0},{2,3},{3,2},{4,5},{5,4},{6,7},{7,6},{8,9},{9,8},{10,11... | collective-permute-start | bytes 24584 | tf_op jit(solution)/shard_map/ppermute | solution.py:20
  62.7 1.5 %copy-start.16 = (f32[2,8,1,128]{3,2,1,0:T(1,128)}, f32[2,8,1,128]{3,2,1,0:T(1,128)S(1)}, u32[]{:S(2)}) copy-start(f32[2,8,1,128]{3,2,1,0:T(1,128)S(1)} %collective-permute-done.13.ay_ref) | copy-start | bytes 24580
  64.2 0.6 copy-start.9
  64.8 13.1 %copy-start.2 = (f32[3,8,64,128]{3,2,1,0:T(8,128)S(1)}, f32[3,8,64,128]{3,2,1,0:T(8,128)}, u32[]{:S(2)}) copy-start(f32[3,8,64,128]{3,2,1,0:T(8,128)} %get-tuple-element.44.e_ref) | copy-start | bytes 2359300
  67.4 7.2 %collective-permute-start.14 = (f32[2,64,128]{2,1,0:T(8,128)}, f32[2,64,128]{2,1,0:T(8,128)S(1)}, u32[]{:S(2)}, u32[]{:S(2)}) collective-permute-start(f32[2,64,128]{2,1,0:T(8,128)} %get-tuple-element.48), channel_id=1, source_target_pairs={{0,2},{2,4},{4,6},{6,8},{8,10},{10,12},{12,14},{14,0},{1,3},{3,5},... | collective-permute-start | bytes 196616 | tf_op jit(solution)/shard_map/ppermute | solution.py:20
  67.4 1.4 %collective-permute-start.15 = (f32[2,8,1,128]{3,2,1,0:T(1,128)}, f32[2,8,1,128]{3,2,1,0:T(1,128)S(1)}, u32[]{:S(2)}, u32[]{:S(2)}) collective-permute-start(f32[2,8,1,128]{3,2,1,0:T(1,128)} %get-tuple-element.49), channel_id=1, source_target_pairs={{0,1},{1,0},{2,3},{3,2},{4,5},{5,4},{6,7},{7,6},{8,9},{9,8},{10,11... | collective-permute-start | bytes 24584 | tf_op jit(solution)/shard_map/ppermute | solution.py:20
  68.7 5.8 %copy-start.12 = (f32[2,8,1,128]{3,2,1,0:T(1,128)}, f32[2,8,1,128]{3,2,1,0:T(1,128)S(1)}, u32[]{:S(2)}) copy-start(f32[2,8,1,128]{3,2,1,0:T(1,128)S(1)} %collective-permute-done.15.by_ref) | copy-start | bytes 24580
  74.5 0.6 copy-start.4
  75.2 2.8 %copy-start = (f32[3,8,64,128]{3,2,1,0:T(8,128)S(1)}, f32[3,8,64,128]{3,2,1,0:T(8,128)}, u32[]{:S(2)}) copy-start(f32[3,8,64,128]{3,2,1,0:T(8,128)} %get-tuple-element.32.e_ref) | copy-start | bytes 2359300
  75.2 2.8 %copy-start.1 = (f32[3,8,64,128]{3,2,1,0:T(8,128)S(1)}, f32[3,8,64,128]{3,2,1,0:T(8,128)}, u32[]{:S(2)}) copy-start(f32[3,8,64,128]{3,2,1,0:T(8,128)} %get-tuple-element.38.e_ref) | copy-start | bytes 2359300

commit v3 on v2

--- a/solution.py
+++ b/solution.py
@@ -128,6 +128,34 @@
 
 def _edges_of_elec(elec):
     return (elec[1:3, 0], jnp.stack([elec[0, :, 0:1], elec[2, :, 0:1]]))
+
+
+def scatter_sum(rows, axis, owned):
+    count = lax.axis_size(axis)
+    index = lax.axis_index(axis)
+    if count & (count - 1):
+        return lax.psum_scatter(rows, axis, scatter_dimension=0, tiled=True)
+    stride = count // 2
+    while stride >= 1:
+        half = rows.shape[0] // 2
+        lower = rows[:half]
+        upper = rows[half:]
+        high = (index & stride) != 0
+        keep = jnp.where(high, upper, lower)
+        send = jnp.where(high, lower, upper)
+        pairs = [(source, source ^ stride) for source in range(count)]
+        rows = keep + lax.ppermute(send, axis, pairs)
+        stride //= 2
+    return rows
+
+
+def pair_sum(value, axis):
+    count = lax.axis_size(axis)
+    if count == 1:
+        return value
+    if count == 2:
+        return value + lax.ppermute(value, axis, [(0, 1), (1, 0)])
+    return lax.psum(value, axis)
 
 
 def local(e_field, h_field, material, eps_table, sigma_table, angle_orders):
@@ -181,8 +209,8 @@
         cosine, flat_imag, precision=high, preferred_element_type=jnp.float32
     ) - jnp.dot(sine, flat_real, precision=high, preferred_element_type=jnp.float32)
     terms = jnp.stack([real_part[:, 0], imag_part[:, 0], real_part[:, 1], imag_part[:, 1]], axis=1)
-    total = lax.psum(terms, ("gx", "gy"))
-    far_field = lax.dynamic_slice_in_dim(total, lax.axis_index("gx") * owned, owned, 0) * scale
+    far_field = scatter_sum(terms, "gx", owned)
+    far_field = pair_sum(far_field, "gy") * scale
     return (elec, magn, far_field)
 
 

time: 116 us -> 99.9 us (0.86)
  blocking collectives: 29.5 us -> 0 us
  waiting for transfers between devices: 35.3 us -> 48.1 us
    psum x1 -> x0, blocking collectives: 29.5 us -> none  [local(): total = lax.psum(terms, ('gx', 'gy'))]
    ppermute x0 -> x4, waiting for transfers between devices: none -> 12.8 us  [the longest x3 11.6 us: scatter_sum(): rows = keep + lax.ppermute(send, axis, pairs)]
  transfers between devices with their start and end apart: 16 -> 20, of which waited for: 14 -> 18; matrix products, arithmetic and copies ran while one was open for 1% -> 1% of each run, Pallas kernels for 2% -> 2%
where the time goes in v3:
time: 99.9 us; the launch traced here: 99.4 us
  waiting for transfers between devices  48.1 us (48%)
  Pallas kernels  22.7 us (23%)
  starting transfers between devices  11.3 us (11%)
  local copies, waits for them, and re-layouts  8.34 us (8%)
  matrix products  5.39 us (5%)
  other arithmetic  2.85 us (3%)
    ppermute x16, waiting for transfers between devices, shifted(): return lax.ppermute(value, axis, pairs)  35.3 us
    ppermute x3, waiting for transfers between devices, scatter_sum(): rows = keep + lax.ppermute(send, axis, pairs)  11.6 us
    ppermute x16, starting transfers between devices, shifted(): return lax.ppermute(value, axis, pairs)  11.3 us
    pallas_call x4, Pallas kernels, local(): elec_call(elec, magn, keep, drive, behind_x, behind_y)  10.7 us
    pallas_call x4, Pallas kernels, local(): magn, back_x, back_y = magn_call(elec, magn, ahead_x, ahead_y)  9.96 us
    unnamed x40, local copies, waits for them, and re-layouts  6.21 us
    pallas_call x1, Pallas kernels, coefficients(): pl.pallas_call(_coef_kernel, out_shape=(out, out), in_specs=[scalar, scal...  2.01 us
  transfers between devices with their start and end apart: 20, of which 18 were waited for; matrix products, arithmetic and copies ran while one was open for 1% of the time, Pallas kernels for 2%

profile of v3, /device:TPU:0, one launch (start us, length us, event | category | flops | bytes accessed | tf_op | source)
XLA Modules:
  0.0 99.4 jit_solution(6662677343351676874)
XLA Ops:
  0.6 0.9 slice_bitcast_fusion
  1.5 6.0 %collective-permute-start = (f32[2,64,128]{2,1,0:T(8,128)S(1)}, f32[2,64,128]{2,1,0:T(8,128)S(1)}, u32[]{:S(2)}, u32[]{:S(2)}) collective-permute-start(f32[2,64,128]{2,1,0:T(8,128)S(1)} %slice_bitcast_fusion), channel_id=1, source_target_pairs={{0,14},{2,0},{4,2},{6,4},{8,6},{10,8},{12,10},{14,12},{1,15},{3,1}... | collective-permute-start | bytes 196616 | tf_op jit(solution)/shard_map/ppermute | solution.py:20
  7.5 0.8 fusion.31
  8.3 0.1 collective-permute-start.1
  8.4 1.2 %collective-permute-done.1.ay_ref = f32[2,8,1,128]{3,2,1,0:T(1,128)S(1)} collective-permute-done((f32[2,8,1,128]{3,2,1,0:T(1,128)S(1)}, f32[2,8,1,128]{3,2,1,0:T(1,128)S(1)}, u32[]{:S(2)}, u32[]{:S(2)}) %collective-permute-start.1) | collective-permute-done | bytes 8224 | tf_op jit(solution)/shard_map/ppermute | solution.py:20
  9.5 0.6 copy-done.18
  10.1 0.6 copy-done.6
  10.7 2.5 %shard_map.85 = (f32[3,8,64,128]{3,2,1,0:T(8,128)}, f32[2,64,128]{2,1,0:T(8,128)}, f32[2,8,1,128]{3,2,1,0:T(1,128)}) custom-call(f32[3,8,64,128]{3,2,1,0:T(8,128)} %e_ref.3, f32[3,8,64,128]{3,2,1,0:T(8,128)} %h_ref.1, f32[2,64,128]{2,1,0:T(8,128)} %copy-done.6, f32[2,8,1,128]{3,2,1,0:T(1,128)} %copy-done.18), custom_call_target="tpu_custom_call" | custom-call | tf_op jit(solution)/shard_map/pallas_call | solution.py:177
  13.2 0.2 collective-permute-start.3
  13.4 2.0 %shard_map.86 = (f32[8,64,128]{2,1,0:T(8,128)}, f32[8,64,128]{2,1,0:T(8,128)}) custom-call(f32[6]{0:T(128)} %eps_ref.1, f32[6]{0:T(128)} %sigma_ref.1, s32[8,64,128]{2,1,0:T(8,128)} %mat_ref.1), custom_call_target="tpu_custom_call" | custom-call | tf_op jit(solution)/shard_map/pallas_call | solution.py:42
  15.4 5.0 %collective-permute-done.2.bx_ref = f32[2,64,128]{2,1,0:T(8,128)S(1)} collective-permute-done((f32[2,64,128]{2,1,0:T(8,128)}, f32[2,64,128]{2,1,0:T(8,128)S(1)}, u32[]{:S(2)}, u32[]{:S(2)}) %collective-permute-start.2) | collective-permute-done | bytes 65568 | tf_op jit(solution)/shard_map/ppermute | solution.py:20
  20.4 0.6 copy-done.7
  21.0 2.7 %shard_map.87 = (f32[3,8,64,128]{3,2,1,0:T(8,128)}, f32[2,64,128]{2,1,0:T(8,128)}, f32[2,8,1,128]{3,2,1,0:T(1,128)}) custom-call(f32[3,8,64,128]{3,2,1,0:T(8,128)} %e_ref.3, f32[3,8,64,128]{3,2,1,0:T(8,128)} %get-tuple-element.27.h_ref, f32[8,64,128]{2,1,0:T(8,128)} %get-tuple-element.28.keep_ref, f32[8,64,128]{2,1,0:T(8,128)} %get-tuple-element.29.drive_ref, ...), custom_call_target="tpu_custom_call" | custom-call | tf_op jit(solution)/shard_map/pallas_call | solution.py:180
  23.7 1.6 %collective-permute-start.4 = (f32[2,64,128]{2,1,0:T(8,128)}, f32[2,64,128]{2,1,0:T(8,128)S(1)}, u32[]{:S(2)}, u32[]{:S(2)}) collective-permute-start(f32[2,64,128]{2,1,0:T(8,128)} %get-tuple-element.33), channel_id=1, source_target_pairs={{0,14},{2,0},{4,2},{6,4},{8,6},{10,8},{12,10},{14,12},{1,15},{3,1}... | collective-permute-start | bytes 196616 | tf_op jit(solution)/shard_map/ppermute | solution.py:20
  25.3 1.4 %collective-permute-done.5.ay_ref = f32[2,8,1,128]{3,2,1,0:T(1,128)S(1)} collective-permute-done((f32[2,8,1,128]{3,2,1,0:T(1,128)}, f32[2,8,1,128]{3,2,1,0:T(1,128)S(1)}, u32[]{:S(2)}, u32[]{:S(2)}) %collective-permute-start.5) | collective-permute-done | bytes 8224 | tf_op jit(solution)/shard_map/ppermute | solution.py:20
  26.7 1.4 %collective-permute-done.4.ax_ref = f32[2,64,128]{2,1,0:T(8,128)S(1)} collective-permute-done((f32[2,64,128]{2,1,0:T(8,128)}, f32[2,64,128]{2,1,0:T(8,128)S(1)}, u32[]{:S(2)}, u32[]{:S(2)}) %collective-permute-start.4) | collective-permute-done | bytes 65568 | tf_op jit(solution)/shard_map/ppermute | solution.py:20
  28.2 0.6 copy-done.10
  28.8 2.5 %shard_map.88 = (f32[3,8,64,128]{3,2,1,0:T(8,128)}, f32[2,64,128]{2,1,0:T(8,128)}, f32[2,8,1,128]{3,2,1,0:T(1,128)}) custom-call(f32[3,8,64,128]{3,2,1,0:T(8,128)} %get-tuple-element.32.e_ref, f32[3,8,64,128]{3,2,1,0:T(8,128)} %get-tuple-element.27.h_ref, f32[2,64,128]{2,1,0:T(8,128)} %copy-done.10, f32[2,8,1,128]{3,2,1,0:T(1,128)} %copy-done.17), custom_call_target="tpu_custom_call" | custom-call | tf_op jit(solution)/shard_map/pallas_call | solution.py:177
  31.3 0.1 collective-permute-start.7
  31.3 0.6 copy-done.19
  31.9 0.8 collective-permute-done.7.by_ref
  32.7 5.7 %collective-permute-done.6.bx_ref = f32[2,64,128]{2,1,0:T(8,128)S(1)} collective-permute-done((f32[2,64,128]{2,1,0:T(8,128)}, f32[2,64,128]{2,1,0:T(8,128)S(1)}, u32[]{:S(2)}, u32[]{:S(2)}) %collective-permute-start.6) | collective-permute-done | bytes 65568 | tf_op jit(solution)/shard_map/ppermute | solution.py:20
  38.4 0.6 copy-done.4
  39.1 2.7 %shard_map.89 = (f32[3,8,64,128]{3,2,1,0:T(8,128)}, f32[2,64,128]{2,1,0:T(8,128)}, f32[2,8,1,128]{3,2,1,0:T(1,128)}) custom-call(f32[3,8,64,128]{3,2,1,0:T(8,128)} %get-tuple-element.32.e_ref, f32[3,8,64,128]{3,2,1,0:T(8,128)} %get-tuple-element.35.h_ref, f32[8,64,128]{2,1,0:T(8,128)} %get-tuple-element.28.keep_ref, ...), custom_call_target="tpu_custom_call" | custom-call | tf_op jit(solution)/shard_map/pallas_call | solution.py:180
  41.7 1.6 %collective-permute-start.8 = (f32[2,64,128]{2,1,0:T(8,128)}, f32[2,64,128]{2,1,0:T(8,128)S(1)}, u32[]{:S(2)}, u32[]{:S(2)}) collective-permute-start(f32[2,64,128]{2,1,0:T(8,128)} %get-tuple-element.39), channel_id=1, source_target_pairs={{0,14},{2,0},{4,2},{6,4},{8,6},{10,8},{12,10},{14,12},{1,15},{3,1}... | collective-permute-start | bytes 196616 | tf_op jit(solution)/shard_map/ppermute | solution.py:20
  43.4 1.4 %collective-permute-done.9.ay_ref = f32[2,8,1,128]{3,2,1,0:T(1,128)S(1)} collective-permute-done((f32[2,8,1,128]{3,2,1,0:T(1,128)}, f32[2,8,1,128]{3,2,1,0:T(1,128)S(1)}, u32[]{:S(2)}, u32[]{:S(2)}) %collective-permute-start.9) | collective-permute-done | bytes 8224 | tf_op jit(solution)/shard_map/ppermute | solution.py:20
  44.7 1.4 %collective-permute-done.8.ax_ref = f32[2,64,128]{2,1,0:T(8,128)S(1)} collective-permute-done((f32[2,64,128]{2,1,0:T(8,128)}, f32[2,64,128]{2,1,0:T(8,128)S(1)}, u32[]{:S(2)}, u32[]{:S(2)}) %collective-permute-start.8) | collective-permute-done | bytes 65568 | tf_op jit(solution)/shard_map/ppermute | solution.py:20
  46.2 0.6 copy-done.8
  46.8 2.5 %shard_map.90 = (f32[3,8,64,128]{3,2,1,0:T(8,128)}, f32[2,64,128]{2,1,0:T(8,128)}, f32[2,8,1,128]{3,2,1,0:T(1,128)}) custom-call(f32[3,8,64,128]{3,2,1,0:T(8,128)} %get-tuple-element.38.e_ref, f32[3,8,64,128]{3,2,1,0:T(8,128)} %get-tuple-element.35.h_ref, f32[2,64,128]{2,1,0:T(8,128)} %copy-done.8, f32[2,8,1,128]{3,2,1,0:T(1,128)} %copy-done.15), custom_call_target="tpu_custom_call" | custom-call | tf_op jit(solution)/shard_map/pallas_call | solution.py:177
  49.3 0.1 multiply_multiply_fusion
  49.4 1.3 %collective-permute-done.11.by_ref = f32[2,8,1,128]{3,2,1,0:T(1,128)S(1)} collective-permute-done((f32[2,8,1,128]{3,2,1,0:T(1,128)}, f32[2,8,1,128]{3,2,1,0:T(1,128)S(1)}, u32[]{:S(2)}, u32[]{:S(2)}) %collective-permute-start.11) | collective-permute-done | bytes 8224 | tf_op jit(solution)/shard_map/ppermute | solution.py:20
  50.7 5.8 %collective-permute-done.10.bx_ref = f32[2,64,128]{2,1,0:T(8,128)S(1)} collective-permute-done((f32[2,64,128]{2,1,0:T(8,128)}, f32[2,64,128]{2,1,0:T(8,128)S(1)}, u32[]{:S(2)}, u32[]{:S(2)}) %collective-permute-start.10) | collective-permute-done | bytes 65568 | tf_op jit(solution)/shard_map/ppermute | solution.py:20
  56.5 0.6 copy-done.3
  57.1 2.6 %shard_map.91 = (f32[3,8,64,128]{3,2,1,0:T(8,128)}, f32[2,64,128]{2,1,0:T(8,128)}, f32[2,8,1,128]{3,2,1,0:T(1,128)}) custom-call(f32[3,8,64,128]{3,2,1,0:T(8,128)} %get-tuple-element.38.e_ref, f32[3,8,64,128]{3,2,1,0:T(8,128)} %get-tuple-element.41.h_ref, f32[8,64,128]{2,1,0:T(8,128)} %get-tuple-element.28.keep_ref, ...), custom_call_target="tpu_custom_call" | custom-call | tf_op jit(solution)/shard_map/pallas_call | solution.py:180
  59.7 1.6 %collective-permute-start.12 = (f32[2,64,128]{2,1,0:T(8,128)}, f32[2,64,128]{2,1,0:T(8,128)S(1)}, u32[]{:S(2)}, u32[]{:S(2)}) collective-permute-start(f32[2,64,128]{2,1,0:T(8,128)} %get-tuple-element.45), channel_id=1, source_target_pairs={{0,14},{2,0},{4,2},{6,4},{8,6},{10,8},{12,10},{14,12},{1,15},{3,1}... | collective-permute-start | bytes 196616 | tf_op jit(solution)/shard_map/ppermute | solution.py:20
  61.4 1.4 %collective-permute-done.13.ay_ref = f32[2,8,1,128]{3,2,1,0:T(1,128)S(1)} collective-permute-done((f32[2,8,1,128]{3,2,1,0:T(1,128)}, f32[2,8,1,128]{3,2,1,0:T(1,128)S(1)}, u32[]{:S(2)}, u32[]{:S(2)}) %collective-permute-start.13) | collective-permute-done | bytes 8224 | tf_op jit(solution)/shard_map/ppermute | solution.py:20
  62.8 1.4 %collective-permute-done.12.ax_ref = f32[2,64,128]{2,1,0:T(8,128)S(1)} collective-permute-done((f32[2,64,128]{2,1,0:T(8,128)}, f32[2,64,128]{2,1,0:T(8,128)S(1)}, u32[]{:S(2)}, u32[]{:S(2)}) %collective-permute-start.12) | collective-permute-done | bytes 65568 | tf_op jit(solution)/shard_map/ppermute | solution.py:20
  64.2 0.6 copy-done.9
  64.8 2.5 %shard_map.92 = (f32[3,8,64,128]{3,2,1,0:T(8,128)}, f32[2,64,128]{2,1,0:T(8,128)}, f32[2,8,1,128]{3,2,1,0:T(1,128)}) custom-call(f32[3,8,64,128]{3,2,1,0:T(8,128)} %get-tuple-element.44.e_ref, f32[3,8,64,128]{3,2,1,0:T(8,128)} %get-tuple-element.41.h_ref, f32[2,64,128]{2,1,0:T(8,128)} %copy-done.9, f32[2,8,1,128]{3,2,1,0:T(1,128)} %copy-done.16), custom_call_target="tpu_custom_call" | custom-call | tf_op jit(solution)/shard_map/pallas_call | solution.py:177
  67.4 0.1 multiply_multiply_fusion.1
  67.5 1.3 %collective-permute-done.15.by_ref = f32[2,8,1,128]{3,2,1,0:T(1,128)S(1)} collective-permute-done((f32[2,8,1,128]{3,2,1,0:T(1,128)}, f32[2,8,1,128]{3,2,1,0:T(1,128)S(1)}, u32[]{:S(2)}, u32[]{:S(2)}) %collective-permute-start.15) | collective-permute-done | bytes 8224 | tf_op jit(solution)/shard_map/ppermute | solution.py:20
  68.8 5.8 %collective-permute-done.14.bx_ref = f32[2,64,128]{2,1,0:T(8,128)S(1)} collective-permute-done((f32[2,64,128]{2,1,0:T(8,128)}, f32[2,64,128]{2,1,0:T(8,128)S(1)}, u32[]{:S(2)}, u32[]{:S(2)}) %collective-permute-start.14) | collective-permute-done | bytes 65568 | tf_op jit(solution)/shard_map/ppermute | solution.py:20
  74.6 0.6 copy-done.5
  75.2 2.8 %shard_map.93 = (f32[3,8,64,128]{3,2,1,0:T(8,128)}, f32[2,64,128]{2,1,0:T(8,128)}, f32[2,8,1,128]{3,2,1,0:T(1,128)}) custom-call(f32[3,8,64,128]{3,2,1,0:T(8,128)} %get-tuple-element.44.e_ref, f32[3,8,64,128]{3,2,1,0:T(8,128)} %get-tuple-element.25.h_ref, f32[8,64,128]{2,1,0:T(8,128)} %get-tuple-element.28.keep_ref, ...), custom_call_target="tpu_custom_call" | custom-call | tf_op jit(solution)/shard_map/pallas_call | solution.py:180
  77.9 1.7 %multiply_add_fusion = (f32[2,8,64,1]{3,2,1,0:T(8,128)S(1)}, f32[2,8,64,1]{3,2,1,0:T(8,128)S(1)}) fusion(f32[3,8,64,128]{3,2,1,0:T(8,128)} %get-tuple-element.24, f32[3,8,64,128]{3,2,1,0:T(8,128)S(1)} %copy-done.2, f32[3,8,64,128]{3,2,1,0:T(8,128)S(1)} %copy-done.1, f32[3,8,64,128]{3,2,1,0:T(8,128)S(1)} %copy-done), kind=kLoop, calls=%fused_computation.7 | loop fusion | flops 15360 | bytes 24576 | tf_op jit(solution)/shard_map/add | solution.py:182
  79.6 0.2 copy.27
  79.8 0.2 copy.26
  80.0 1.3 %convolution_bitcast_fusion.1 = f32[64,2]{0,1:T(2,128)S(1)} fusion(s32[64,64]{1,0:T(8,128)S(1)} %multiply_multiply_fusion, s32[64,8]{0,1:T(8,128)S(1)} %multiply_multiply_fusion.1, f32[2,8,64,1]{2,0,1,3:T(2,128)S(1)} %copy.27), kind=kOutput, calls=%fused_computation.2 | convolution fusion | flops 1245184 | bytes 23040 | tf_op jit(solution)/shard_map/dot_general | solution.py:208
  81.4 1.4 %convolution_bitcast_fusion.3 = f32[64,2]{0,1:T(2,128)S(1)} fusion(s32[64,64]{1,0:T(8,128)S(1)} %multiply_multiply_fusion, s32[64,8]{0,1:T(8,128)S(1)} %multiply_multiply_fusion.1, f32[2,8,64,1]{2,0,1,3:T(2,128)S(1)} %copy.26), kind=kOutput, calls=%fused_computation.5 | convolution fusion | flops 1245184 | bytes 23040 | tf_op jit(solution)/shard_map/dot_general | solution.py:205
  82.7 1.4 %fusion = f32[64,2]{0,1:T(2,128)S(1)} fusion(f32[64,2]{0,1:T(2,128)S(1)} %convolution_bitcast_fusion.1, s32[64,64]{1,0:T(8,128)S(1)} %multiply_multiply_fusion, s32[64,8]{0,1:T(8,128)S(1)} %multiply_multiply_fusion.1, f32[2,8,64,1]{2,0,1,3:T(2,128)S(1)} %copy.26), kind=kOutput, calls=%fused_computation.1 | convolution fusion | flops 1245312 | bytes 23552 | tf_op jit(solution)/shard_map/dot_general | solution.py:210
  84.1 1.4 %fusion.1 = f32[64,2]{0,1:T(2,128)S(1)} fusion(f32[64,2]{0,1:T(2,128)S(1)} %convolution_bitcast_fusion.3, s32[64,64]{1,0:T(8,128)S(1)} %multiply_multiply_fusion, s32[64,8]{0,1:T(8,128)S(1)} %multiply_multiply_fusion.1, f32[2,8,64,1]{2,0,1,3:T(2,128)S(1)} %copy.27), kind=kOutput, calls=%fused_computation.4 | convolution fusion | flops 1245312 | bytes 23552 | tf_op jit(solution)/shard_map/dot_general | solution.py:207
  85.4 0.1 fusion.32
  85.5 0.1 slice_select_fusion.2
  85.6 0.0 collective-permute-start.16
  85.6 4.5 %collective-permute-done.16 = f32[32,4]{0,1:T(4,128)S(1)} collective-permute-done((f32[32,4]{0,1:T(4,128)S(1)}, f32[32,4]{0,1:T(4,128)S(1)}, u32[]{:S(2)}, u32[]{:S(2)}) %collective-permute-start.16) | collective-permute-done | bytes 544 | tf_op jit(solution)/shard_map/ppermute | solution.py:147
  90.1 0.1 select_add_fusion.2
  90.2 0.1 slice_select_fusion.1
  90.2 3.6 %collective-permute-done.17 = f32[16,4]{0,1:T(4,128)S(1)} collective-permute-done((f32[16,4]{0,1:T(4,128)S(1)}, f32[16,4]{0,1:T(4,128)S(1)}, u32[]{:S(2)}, u32[]{:S(2)}) %collective-permute-start.17) | collective-permute-done | bytes 288 | tf_op jit(solution)/shard_map/ppermute | solution.py:147
  93.8 0.1 select_add_fusion.1
  93.9 0.1 slice_select_fusion
  94.0 3.6 %collective-permute-done.18 = f32[8,4]{0,1:T(4,128)S(1)} collective-permute-done((f32[8,4]{0,1:T(4,128)S(1)}, f32[8,4]{0,1:T(4,128)S(1)}, u32[]{:S(2)}, u32[]{:S(2)}) %collective-permute-start.18) | collective-permute-done | bytes 160 | tf_op jit(solution)/shard_map/ppermute | solution.py:147
  97.6 0.1 select_add_fusion
  97.6 1.2 %collective-permute-done.19 = f32[8,4]{0,1:T(4,128)S(1)} collective-permute-done((f32[8,4]{0,1:T(4,128)S(1)}, f32[8,4]{0,1:T(4,128)S(1)}, u32[]{:S(2)}, u32[]{:S(2)}) %collective-permute-start.19) | collective-permute-done | bytes 160 | tf_op jit(solution)/shard_map/ppermute | solution.py:157
  98.8 0.6 add_multiply_fusion
  (49 shorter events, 0.1 us)
Async XLA Ops:
  1.5 8.0 %collective-permute-start = (f32[2,64,128]{2,1,0:T(8,128)S(1)}, f32[2,64,128]{2,1,0:T(8,128)S(1)}, u32[]{:S(2)}, u32[]{:S(2)}) collective-permute-start(f32[2,64,128]{2,1,0:T(8,128)S(1)} %slice_bitcast_fusion), channel_id=1, source_target_pairs={{0,14},{2,0},{4,2},{6,4},{8,6},{10,8},{12,10},{14,12},{1,15},{3,1}... | collective-permute-start | bytes 196616 | tf_op jit(solution)/shard_map/ppermute | solution.py:20
  8.3 1.2 %collective-permute-start.1 = (f32[2,8,1,128]{3,2,1,0:T(1,128)S(1)}, f32[2,8,1,128]{3,2,1,0:T(1,128)S(1)}, u32[]{:S(2)}, u32[]{:S(2)}) collective-permute-start(f32[2,8,1,128]{3,2,1,0:T(1,128)S(1)} %pad_maximum_fusion), channel_id=1, source_target_pairs={{0,1},{1,0},{2,3},{3,2},{4,5},{5,4},{6,7},{7,6},{8,9},{9,8},{10,11... | collective-permute-start | bytes 24584 | tf_op jit(solution)/shard_map/ppermute | solution.py:20
  9.5 0.6 copy-start.18
  10.1 0.6 copy-start.6
  13.2 7.2 %collective-permute-start.2 = (f32[2,64,128]{2,1,0:T(8,128)}, f32[2,64,128]{2,1,0:T(8,128)S(1)}, u32[]{:S(2)}, u32[]{:S(2)}) collective-permute-start(f32[2,64,128]{2,1,0:T(8,128)} %get-tuple-element.30), channel_id=1, source_target_pairs={{0,2},{2,4},{4,6},{6,8},{8,10},{10,12},{12,14},{14,0},{1,3},{3,5},... | collective-permute-start | bytes 196616 | tf_op jit(solution)/shard_map/ppermute | solution.py:20
  13.2 2.2 %collective-permute-start.3 = (f32[2,8,1,128]{3,2,1,0:T(1,128)}, f32[2,8,1,128]{3,2,1,0:T(1,128)S(1)}, u32[]{:S(2)}, u32[]{:S(2)}) collective-permute-start(f32[2,8,1,128]{3,2,1,0:T(1,128)} %get-tuple-element.31), channel_id=1, source_target_pairs={{0,1},{1,0},{2,3},{3,2},{4,5},{5,4},{6,7},{7,6},{8,9},{9,8},{10,11... | collective-permute-start | bytes 24584 | tf_op jit(solution)/shard_map/ppermute | solution.py:20
  15.4 5.0 %copy-start.14 = (f32[2,8,1,128]{3,2,1,0:T(1,128)}, f32[2,8,1,128]{3,2,1,0:T(1,128)S(1)}, u32[]{:S(2)}) copy-start(f32[2,8,1,128]{3,2,1,0:T(1,128)S(1)} %collective-permute-done.3.by_ref) | copy-start | bytes 24580
  20.4 0.6 copy-start.7
  23.7 4.5 %collective-permute-start.4 = (f32[2,64,128]{2,1,0:T(8,128)}, f32[2,64,128]{2,1,0:T(8,128)S(1)}, u32[]{:S(2)}, u32[]{:S(2)}) collective-permute-start(f32[2,64,128]{2,1,0:T(8,128)} %get-tuple-element.33), channel_id=1, source_target_pairs={{0,14},{2,0},{4,2},{6,4},{8,6},{10,8},{12,10},{14,12},{1,15},{3,1}... | collective-permute-start | bytes 196616 | tf_op jit(solution)/shard_map/ppermute | solution.py:20
  25.3 1.4 %collective-permute-start.5 = (f32[2,8,1,128]{3,2,1,0:T(1,128)}, f32[2,8,1,128]{3,2,1,0:T(1,128)S(1)}, u32[]{:S(2)}, u32[]{:S(2)}) collective-permute-start(f32[2,8,1,128]{3,2,1,0:T(1,128)} %get-tuple-element.34), channel_id=1, source_target_pairs={{0,1},{1,0},{2,3},{3,2},{4,5},{5,4},{6,7},{7,6},{8,9},{9,8},{10,11... | collective-permute-start | bytes 24584 | tf_op jit(solution)/shard_map/ppermute | solution.py:20
  26.7 1.5 %copy-start.17 = (f32[2,8,1,128]{3,2,1,0:T(1,128)}, f32[2,8,1,128]{3,2,1,0:T(1,128)S(1)}, u32[]{:S(2)}) copy-start(f32[2,8,1,128]{3,2,1,0:T(1,128)S(1)} %collective-permute-done.5.ay_ref) | copy-start | bytes 24580
  28.2 0.6 copy-start.10
  31.2 0.7 copy-start.19
  31.2 7.2 %collective-permute-start.6 = (f32[2,64,128]{2,1,0:T(8,128)}, f32[2,64,128]{2,1,0:T(8,128)S(1)}, u32[]{:S(2)}, u32[]{:S(2)}) collective-permute-start(f32[2,64,128]{2,1,0:T(8,128)} %get-tuple-element.36), channel_id=1, source_target_pairs={{0,2},{2,4},{4,6},{6,8},{8,10},{10,12},{12,14},{14,0},{1,3},{3,5},... | collective-permute-start | bytes 196616 | tf_op jit(solution)/shard_map/ppermute | solution.py:20
  31.3 1.4 %collective-permute-start.7 = (f32[2,8,1,128]{3,2,1,0:T(1,128)}, f32[2,8,1,128]{3,2,1,0:T(1,128)S(1)}, u32[]{:S(2)}, u32[]{:S(2)}) collective-permute-start(f32[2,8,1,128]{3,2,1,0:T(1,128)} %get-tuple-element.37), channel_id=1, source_target_pairs={{0,1},{1,0},{2,3},{3,2},{4,5},{5,4},{6,7},{7,6},{8,9},{9,8},{10,11... | collective-permute-start | bytes 24584 | tf_op jit(solution)/shard_map/ppermute | solution.py:20
  32.7 5.7 %copy-start.12 = (f32[2,8,1,128]{3,2,1,0:T(1,128)}, f32[2,8,1,128]{3,2,1,0:T(1,128)S(1)}, u32[]{:S(2)}) copy-start(f32[2,8,1,128]{3,2,1,0:T(1,128)S(1)} %collective-permute-done.7.by_ref) | copy-start | bytes 24580
  38.4 0.6 copy-start.4
  41.7 4.5 %collective-permute-start.8 = (f32[2,64,128]{2,1,0:T(8,128)}, f32[2,64,128]{2,1,0:T(8,128)S(1)}, u32[]{:S(2)}, u32[]{:S(2)}) collective-permute-start(f32[2,64,128]{2,1,0:T(8,128)} %get-tuple-element.39), channel_id=1, source_target_pairs={{0,14},{2,0},{4,2},{6,4},{8,6},{10,8},{12,10},{14,12},{1,15},{3,1}... | collective-permute-start | bytes 196616 | tf_op jit(solution)/shard_map/ppermute | solution.py:20
  43.4 1.4 %collective-permute-start.9 = (f32[2,8,1,128]{3,2,1,0:T(1,128)}, f32[2,8,1,128]{3,2,1,0:T(1,128)S(1)}, u32[]{:S(2)}, u32[]{:S(2)}) collective-permute-start(f32[2,8,1,128]{3,2,1,0:T(1,128)} %get-tuple-element.40), channel_id=1, source_target_pairs={{0,1},{1,0},{2,3},{3,2},{4,5},{5,4},{6,7},{7,6},{8,9},{9,8},{10,11... | collective-permute-start | bytes 24584 | tf_op jit(solution)/shard_map/ppermute | solution.py:20
  44.7 1.5 %copy-start.15 = (f32[2,8,1,128]{3,2,1,0:T(1,128)}, f32[2,8,1,128]{3,2,1,0:T(1,128)S(1)}, u32[]{:S(2)}) copy-start(f32[2,8,1,128]{3,2,1,0:T(1,128)S(1)} %collective-permute-done.9.ay_ref) | copy-start | bytes 24580
  46.2 0.6 copy-start.8
  49.3 7.2 %collective-permute-start.10 = (f32[2,64,128]{2,1,0:T(8,128)}, f32[2,64,128]{2,1,0:T(8,128)S(1)}, u32[]{:S(2)}, u32[]{:S(2)}) collective-permute-start(f32[2,64,128]{2,1,0:T(8,128)} %get-tuple-element.42), channel_id=1, source_target_pairs={{0,2},{2,4},{4,6},{6,8},{8,10},{10,12},{12,14},{14,0},{1,3},{3,5},... | collective-permute-start | bytes 196616 | tf_op jit(solution)/shard_map/ppermute | solution.py:20
  49.3 1.4 %collective-permute-start.11 = (f32[2,8,1,128]{3,2,1,0:T(1,128)}, f32[2,8,1,128]{3,2,1,0:T(1,128)S(1)}, u32[]{:S(2)}, u32[]{:S(2)}) collective-permute-start(f32[2,8,1,128]{3,2,1,0:T(1,128)} %get-tuple-element.43), channel_id=1, source_target_pairs={{0,1},{1,0},{2,3},{3,2},{4,5},{5,4},{6,7},{7,6},{8,9},{9,8},{10,11... | collective-permute-start | bytes 24584 | tf_op jit(solution)/shard_map/ppermute | solution.py:20
  50.7 5.8 %copy-start.11 = (f32[2,8,1,128]{3,2,1,0:T(1,128)}, f32[2,8,1,128]{3,2,1,0:T(1,128)S(1)}, u32[]{:S(2)}) copy-start(f32[2,8,1,128]{3,2,1,0:T(1,128)S(1)} %collective-permute-done.11.by_ref) | copy-start | bytes 24580
  56.5 0.6 copy-start.3
  59.7 4.5 %collective-permute-start.12 = (f32[2,64,128]{2,1,0:T(8,128)}, f32[2,64,128]{2,1,0:T(8,128)S(1)}, u32[]{:S(2)}, u32[]{:S(2)}) collective-permute-start(f32[2,64,128]{2,1,0:T(8,128)} %get-tuple-element.45), channel_id=1, source_target_pairs={{0,14},{2,0},{4,2},{6,4},{8,6},{10,8},{12,10},{14,12},{1,15},{3,1}... | collective-permute-start | bytes 196616 | tf_op jit(solution)/shard_map/ppermute | solution.py:20
  61.4 1.4 %collective-permute-start.13 = (f32[2,8,1,128]{3,2,1,0:T(1,128)}, f32[2,8,1,128]{3,2,1,0:T(1,128)S(1)}, u32[]{:S(2)}, u32[]{:S(2)}) collective-permute-start(f32[2,8,1,128]{3,2,1,0:T(1,128)} %get-tuple-element.46), channel_id=1, source_target_pairs={{0,1},{1,0},{2,3},{3,2},{4,5},{5,4},{6,7},{7,6},{8,9},{9,8},{10,11... | collective-permute-start | bytes 24584 | tf_op jit(solution)/shard_map/ppermute | solution.py:20
  62.8 1.5 %copy-start.16 = (f32[2,8,1,128]{3,2,1,0:T(1,128)}, f32[2,8,1,128]{3,2,1,0:T(1,128)S(1)}, u32[]{:S(2)}) copy-start(f32[2,8,1,128]{3,2,1,0:T(1,128)S(1)} %collective-permute-done.13.ay_ref) | copy-start | bytes 24580
  64.2 0.6 copy-start.9
  64.8 13.1 %copy-start.2 = (f32[3,8,64,128]{3,2,1,0:T(8,128)S(1)}, f32[3,8,64,128]{3,2,1,0:T(8,128)}, u32[]{:S(2)}) copy-start(f32[3,8,64,128]{3,2,1,0:T(8,128)} %get-tuple-element.44.e_ref) | copy-start | bytes 2359300
  67.4 7.2 %collective-permute-start.14 = (f32[2,64,128]{2,1,0:T(8,128)}, f32[2,64,128]{2,1,0:T(8,128)S(1)}, u32[]{:S(2)}, u32[]{:S(2)}) collective-permute-start(f32[2,64,128]{2,1,0:T(8,128)} %get-tuple-element.48), channel_id=1, source_target_pairs={{0,2},{2,4},{4,6},{6,8},{8,10},{10,12},{12,14},{14,0},{1,3},{3,5},... | collective-permute-start | bytes 196616 | tf_op jit(solution)/shard_map/ppermute | solution.py:20
  67.4 1.4 %collective-permute-start.15 = (f32[2,8,1,128]{3,2,1,0:T(1,128)}, f32[2,8,1,128]{3,2,1,0:T(1,128)S(1)}, u32[]{:S(2)}, u32[]{:S(2)}) collective-permute-start(f32[2,8,1,128]{3,2,1,0:T(1,128)} %get-tuple-element.49), channel_id=1, source_target_pairs={{0,1},{1,0},{2,3},{3,2},{4,5},{5,4},{6,7},{7,6},{8,9},{9,8},{10,11... | collective-permute-start | bytes 24584 | tf_op jit(solution)/shard_map/ppermute | solution.py:20
  68.8 5.8 %copy-start.13 = (f32[2,8,1,128]{3,2,1,0:T(1,128)}, f32[2,8,1,128]{3,2,1,0:T(1,128)S(1)}, u32[]{:S(2)}) copy-start(f32[2,8,1,128]{3,2,1,0:T(1,128)S(1)} %collective-permute-done.15.by_ref) | copy-start | bytes 24580
  74.5 0.6 copy-start.5
  75.2 2.8 %copy-start = (f32[3,8,64,128]{3,2,1,0:T(8,128)S(1)}, f32[3,8,64,128]{3,2,1,0:T(8,128)}, u32[]{:S(2)}) copy-start(f32[3,8,64,128]{3,2,1,0:T(8,128)} %get-tuple-element.32.e_ref) | copy-start | bytes 2359300
  75.2 2.8 %copy-start.1 = (f32[3,8,64,128]{3,2,1,0:T(8,128)S(1)}, f32[3,8,64,128]{3,2,1,0:T(8,128)}, u32[]{:S(2)}) copy-start(f32[3,8,64,128]{3,2,1,0:T(8,128)} %get-tuple-element.38.e_ref) | copy-start | bytes 2359300
  85.6 4.5 %collective-permute-start.16 = (f32[32,4]{0,1:T(4,128)S(1)}, f32[32,4]{0,1:T(4,128)S(1)}, u32[]{:S(2)}, u32[]{:S(2)}) collective-permute-start(f32[32,4]{0,1:T(4,128)S(1)} %slice_select_fusion.2), channel_id=1, source_target_pairs={{0,8},{2,10},{4,12},{6,14},{8,0},{10,2},{12,4},{14,6},{1,9},{3,11}... | collective-permute-start | bytes 1544 | tf_op jit(solution)/shard_map/ppermute | solution.py:147
  90.2 3.6 %collective-permute-start.17 = (f32[16,4]{0,1:T(4,128)S(1)}, f32[16,4]{0,1:T(4,128)S(1)}, u32[]{:S(2)}, u32[]{:S(2)}) collective-permute-start(f32[16,4]{0,1:T(4,128)S(1)} %slice_select_fusion.1), channel_id=1, source_target_pairs={{0,4},{2,6},{4,0},{6,2},{8,12},{10,14},{12,8},{14,10},{1,5},{3,7},... | collective-permute-start | bytes 776 | tf_op jit(solution)/shard_map/ppermute | solution.py:147
  94.0 3.6 %collective-permute-start.18 = (f32[8,4]{0,1:T(4,128)S(1)}, f32[8,4]{0,1:T(4,128)S(1)}, u32[]{:S(2)}, u32[]{:S(2)}) collective-permute-start(f32[8,4]{0,1:T(4,128)S(1)} %slice_select_fusion), channel_id=1, source_target_pairs={{0,2},{2,0},{4,6},{6,4},{8,10},{10,8},{12,14},{14,12},{1,3},{3,1},... | collective-permute-start | bytes 392 | tf_op jit(solution)/shard_map/ppermute | solution.py:147
  97.6 1.2 %collective-permute-start.19 = (f32[8,4]{0,1:T(4,128)S(1)}, f32[8,4]{0,1:T(4,128)S(1)}, u32[]{:S(2)}, u32[]{:S(2)}) collective-permute-start(f32[8,4]{0,1:T(4,128)S(1)} %select_add_fusion), channel_id=1, source_target_pairs={{0,1},{1,0},{2,3},{3,2},{4,5},{5,4},{6,7},{7,6},{8,9},{9,8},{10,11... | collective-permute-start | bytes 392 | tf_op jit(solution)/shard_map/ppermute | solution.py:157

commit v4 on v3

--- a/solution.py
+++ b/solution.py
@@ -73,8 +73,15 @@
     return f - jnp.where(index == 0, row, down)
 
 
-def _magn_kernel(e_ref, h_ref, ax_ref, ay_ref, h_out, bx_out, by_out):
+def _step_kernel(e_ref, h_ref, keep_ref, drive_ref, xlo_ref, xhi_ref, ylo_ref, yhi_ref,
+                 c1_ref, c2_ref, e_out, h_out, xlo_out, xhi_out, ylo_out, yhi_out, c1_out, c2_out):
     planes = e_ref.shape[1]
+    cells = e_ref.shape[2]
+    ex_p = xlo_ref[0]
+    ey_p = xlo_ref[1]
+    ez_p = xlo_ref[2]
+    hy_prev = xlo_ref[3] - TIME_STEP * (_z_up(ex_p) - (e_ref[2, 0] - ez_p))
+    hz_prev = xlo_ref[4] - TIME_STEP * ((e_ref[1, 0] - ey_p) - _y_up(ex_p, c1_ref[...]))
     for x in range(planes):
         ex = e_ref[0, x]
         ey = e_ref[1, x]
@@ -82,52 +89,84 @@
         if x + 1 < planes:
             ey_next = e_ref[1, x + 1]
             ez_next = e_ref[2, x + 1]
+            ey_m_next = ylo_ref[1, x + 1]
         else:
-            ey_next = ax_ref[0]
-            ez_next = ax_ref[1]
-        hx = h_ref[0, x] - TIME_STEP * (_y_up(ez, ay_ref[1, x]) - _z_up(ey))
+            ey_next = xhi_ref[0]
+            ez_next = xhi_ref[1]
+            ey_m_next = c2_ref[...]
+        hx = h_ref[0, x] - TIME_STEP * (_y_up(ez, yhi_ref[1, x]) - _z_up(ey))
         hy = h_ref[1, x] - TIME_STEP * (_z_up(ex) - (ez_next - ez))
-        hz = h_ref[2, x] - TIME_STEP * ((ey_next - ey) - _y_up(ex, ay_ref[0, x]))
+        hz = h_ref[2, x] - TIME_STEP * ((ey_next - ey) - _y_up(ex, yhi_ref[0, x]))
+        ex_m = ylo_ref[0, x]
+        ey_m = ylo_ref[1, x]
+        ez_m = ylo_ref[2, x]
+        hx_r = ylo_ref[3, x] - TIME_STEP * ((ez[0:1] - ez_m) - _z_up(ey_m))
+        hz_r = ylo_ref[4, x] - TIME_STEP * ((ey_m_next - ey_m) - (ex[0:1] - ex_m))
+        keep = keep_ref[x]
+        drive = drive_ref[x]
+        ex_new = keep * ex + drive * (_y_down(hz, hz_r) - _z_down(hy))
+        ey_new = keep * ey + drive * (_z_down(hx) - (hz - hz_prev))
+        ez_new = keep * ez + drive * ((hy - hy_prev) - _y_down(hx, hx_r))
+        e_out[0, x] = ex_new
+        e_out[1, x] = ey_new
+        e_out[2, x] = ez_new
         h_out[0, x] = hx
         h_out[1, x] = hy
         h_out[2, x] = hz
-        cells = hx.shape[0]
-        by_out[0, x] = hx[cells - 1:cells]
-        by_out[1, x] = hz[cells - 1:cells]
+        last = slice(cells - 1, cells)
+        ylo_out[0, x] = ex_new[last]
+        ylo_out[1, x] = ey_new[last]
+        ylo_out[2, x] = ez_new[last]
+        ylo_out[3, x] = hx[last]
+        ylo_out[4, x] = hz[last]
+        yhi_out[0, x] = ex_new[0:1]
+        yhi_out[1, x] = ez_new[0:1]
+        if x == 0:
+            xhi_out[0] = ey_new
+            xhi_out[1] = ez_new
+            c2_out[...] = ey_new[last]
         if x == planes - 1:
-            bx_out[0] = hy
-            bx_out[1] = hz
-
-
-def _elec_kernel(e_ref, h_ref, keep_ref, drive_ref, bx_ref, by_ref, e_out, ax_out, ay_out):
-    planes = e_ref.shape[1]
-    for x in range(planes):
-        hx = h_ref[0, x]
-        hy = h_ref[1, x]
-        hz = h_ref[2, x]
-        if x > 0:
-            hy_prev = h_ref[1, x - 1]
-            hz_prev = h_ref[2, x - 1]
-        else:
-            hy_prev = bx_ref[0]
-            hz_prev = bx_ref[1]
-        keep = keep_ref[x]
-        drive = drive_ref[x]
-        ex = keep * e_ref[0, x] + drive * (_y_down(hz, by_ref[1, x]) - _z_down(hy))
-        ey = keep * e_ref[1, x] + drive * (_z_down(hx) - (hz - hz_prev))
-        ez = keep * e_ref[2, x] + drive * ((hy - hy_prev) - _y_down(hx, by_ref[0, x]))
-        e_out[0, x] = ex
-        e_out[1, x] = ey
-        e_out[2, x] = ez
-        ay_out[0, x] = ex[0:1]
-        ay_out[1, x] = ez[0:1]
-        if x == 0:
-            ax_out[0] = ey
-            ax_out[1] = ez
-
-
-def _edges_of_elec(elec):
-    return (elec[1:3, 0], jnp.stack([elec[0, :, 0:1], elec[2, :, 0:1]]))
+            xlo_out[0] = ex_new
+            xlo_out[1] = ey_new
+            xlo_out[2] = ez_new
+            xlo_out[3] = hy
+            xlo_out[4] = hz
+            c1_out[...] = ex_new[0:1]
+        hy_prev = hy
+        hz_prev = hz
+
+
+def _halo_of(elec, magn):
+    cells = elec.shape[2]
+    last = slice(cells - 1, cells)
+    xlo = jnp.stack([elec[0, -1], elec[1, -1], elec[2, -1], magn[1, -1], magn[2, -1]])
+    xhi = elec[1:3, 0]
+    ylo = jnp.stack([elec[0, :, last], elec[1, :, last], elec[2, :, last], magn[0, :, last], magn[2, :, last]])
+    yhi = jnp.stack([elec[0, :, 0:1], elec[2, :, 0:1]])
+    return (xlo, xhi, ylo, yhi, elec[0, -1, 0:1], elec[1, 0, last])
+
+
+def diagonal(value, step_x, step_y):
+    count_x = lax.axis_size("gx")
+    count_y = lax.axis_size("gy")
+    pairs = []
+    for a in range(count_x):
+        for b in range(count_y):
+            target = ((a + step_x) % count_x) * count_y + (b + step_y) % count_y
+            pairs.append((a * count_y + b, target))
+    return lax.ppermute(value, ("gx", "gy"), pairs)
+
+
+def exchange(halo):
+    xlo, xhi, ylo, yhi, c1, c2 = halo
+    return (
+        shifted(xlo, "gx", 1),
+        shifted(xhi, "gx", -1),
+        shifted(ylo, "gy", 1),
+        shifted(yhi, "gy", -1),
+        diagonal(c1, 1, -1),
+        diagonal(c2, -1, 1),
+    )
 
 
 def scatter_sum(rows, axis, owned):
@@ -163,21 +202,23 @@
     comps, cells_x, cells_y, depth = e_field.shape
     elec = e_field
     magn = h_field
-    plane_shape = jax.ShapeDtypeStruct((2, cells_y, depth), jnp.float32)
-    row_shape = jax.ShapeDtypeStruct((2, cells_x, 1, depth), jnp.float32)
-    field_shape = jax.ShapeDtypeStruct(e_field.shape, jnp.float32)
-    magn_call = pl.pallas_call(_magn_kernel, out_shape=(field_shape, plane_shape, row_shape))
-    elec_call = pl.pallas_call(_elec_kernel, out_shape=(field_shape, plane_shape, row_shape))
-    edge_x, edge_y = _edges_of_elec(elec)
-    mon_real = jnp.zeros((2, cells_x, cells_y), jnp.float32)
-    mon_imag = jnp.zeros((2, cells_x, cells_y), jnp.float32)
+    f32 = jnp.float32
+    field_shape = jax.ShapeDtypeStruct(e_field.shape, f32)
+    halo_shapes = (
+        jax.ShapeDtypeStruct((5, cells_y, depth), f32),
+        jax.ShapeDtypeStruct((2, cells_y, depth), f32),
+        jax.ShapeDtypeStruct((5, cells_x, 1, depth), f32),
+        jax.ShapeDtypeStruct((2, cells_x, 1, depth), f32),
+        jax.ShapeDtypeStruct((1, depth), f32),
+        jax.ShapeDtypeStruct((1, depth), f32),
+    )
+    step_call = pl.pallas_call(_step_kernel, out_shape=(field_shape, field_shape) + halo_shapes)
+    halo = _halo_of(elec, magn)
+    mon_real = jnp.zeros((2, cells_x, cells_y), f32)
+    mon_imag = jnp.zeros((2, cells_x, cells_y), f32)
     for number in range(ITERS):
-        ahead_x = shifted(edge_x, "gx", -1)
-        ahead_y = shifted(edge_y, "gy", -1)
-        magn, back_x, back_y = magn_call(elec, magn, ahead_x, ahead_y)
-        behind_x = shifted(back_x, "gx", 1)
-        behind_y = shifted(back_y, "gy", 1)
-        elec, edge_x, edge_y = elec_call(elec, magn, keep, drive, behind_x, behind_y)
+        received = exchange(halo)
+        elec, magn, *halo = step_call(elec, magn, keep, drive, *received)
         plane = elec[0:2, :, :, depth - 3]
         mon_real = mon_real + math.cos(PHASE_STEP * (number + 1)) * plane
         mon_imag = mon_imag - math.sin(PHASE_STEP * (number + 1)) * plane

time: 99.9 us -> 92 us (0.921)
  waiting for transfers between devices: 48.1 us -> 23.9 us
  starting transfers between devices: 11.3 us -> 29 us
  Pallas kernels: 22.7 us -> 16 us
  local copies, waits for them, and re-layouts: 8.34 us -> 13.1 us
    ppermute x16, waiting for transfers between devices: 35.3 us -> 0.04 us  [shifted(): return lax.ppermute(value, axis, pairs)]
    ppermute x0 -> x8, waiting for transfers between devices: none -> 14.5 us  [diagonal(): return lax.ppermute(value, ('gx', 'gy'), pairs)]
    ppermute x16, starting transfers between devices: 11.3 us -> 22.4 us  [shifted(): return lax.ppermute(value, axis, pairs)]
    pallas_call x8 -> x4, Pallas kernels: 20.7 us -> 13.9 us  [local(): elec, magn, *halo = step_call(elec, magn, keep, drive, *received)]
    ppermute x3, starting transfers between devices: 0.02 us -> 3.51 us  [scatter_sum(): rows = keep + lax.ppermute(send, axis, pairs)]
    ppermute x3, waiting for transfers between devices: 11.6 us -> 8.15 us  [scatter_sum(): rows = keep + lax.ppermute(send, axis, pairs)]
    ppermute x0 -> x8, starting transfers between devices: none -> 3 us  [diagonal(): return lax.ppermute(value, ('gx', 'gy'), pairs)]
    slice x1 -> x3, local copies, waits for them, and re-layouts: 0.78 us -> 2.47 us  [the longest x1 0.9 us: _halo_of(): elec[0, :, last]]
  transfers between devices with their start and end apart: 20 -> 28, of which waited for: 18 -> 11; matrix products, arithmetic and copies ran while one was open for 1% -> 7% of each run, Pallas kernels for 2% -> 2%
where the time goes in v4:
time: 92 us; the launch traced here: 91.2 us
  starting transfers between devices  29 us (32%)
  waiting for transfers between devices  23.9 us (26%)
  Pallas kernels  16 us (17%)
  local copies, waits for them, and re-layouts  13.1 us (14%)
  matrix products  5.39 us (6%)
  other arithmetic  2.87 us (3%)
  between operations  1.03 us (1%)
    ppermute x16, starting transfers between devices, shifted(): return lax.ppermute(value, axis, pairs)  22.4 us
    ppermute x8, waiting for transfers between devices, diagonal(): return lax.ppermute(value, ('gx', 'gy'), pairs)  14.5 us
    pallas_call x4, Pallas kernels, local(): elec, magn, *halo = step_call(elec, magn, keep, drive, *received)  13.9 us
    ppermute x3, waiting for transfers between devices, scatter_sum(): rows = keep + lax.ppermute(send, axis, pairs)  8.15 us
    unnamed x72, local copies, waits for them, and re-layouts  7.8 us
    ppermute x3, starting transfers between devices, scatter_sum(): rows = keep + lax.ppermute(send, axis, pairs)  3.51 us
    ppermute x8, starting transfers between devices, diagonal(): return lax.ppermute(value, ('gx', 'gy'), pairs)  3 us
    pallas_call x1, Pallas kernels, coefficients(): pl.pallas_call(_coef_kernel, out_shape=(out, out), in_specs=[scalar, scal...  2.04 us
  transfers between devices with their start and end apart: 28, of which 11 were waited for; matrix products, arithmetic and copies ran while one was open for 7% of the time, Pallas kernels for 2%

profile of v4, /device:TPU:0, one launch (start us, length us, event | category | flops | bytes accessed | tf_op | source)
XLA Modules:
  0.0 91.2 jit_solution(16473035541522768361)
XLA Ops:
  0.6 0.8 fusion.32
  1.4 0.9 slice.98
  2.4 0.5 collective-permute-start.2
  2.9 0.8 fusion.31
  3.7 0.1 collective-permute-start.3
  3.8 0.8 bitcast_dynamic-update-slice_fusion.4
  4.5 0.8 bitcast_dynamic-update-slice_fusion.3
  5.3 0.8 bitcast_dynamic-update-slice_fusion.2
  6.1 0.8 bitcast_dynamic-update-slice_fusion.1
  6.8 0.8 bitcast_dynamic-update-slice_fusion
  7.6 3.0 %collective-permute-start = (f32[5,64,128]{2,1,0:T(8,128)S(1)}, f32[5,64,128]{2,1,0:T(8,128)S(1)}, u32[]{:S(2)}, u32[]{:S(2)}) collective-permute-start(f32[5,64,128]{2,1,0:T(8,128)S(1)} %bitcast_dynamic-update-slice_fusion), channel_id=1, source_target_pairs={{0,2},{2,4},{4,6},{6,8},{8,10},{10,12},{12,14},{14,0},{1,3},{3,5},... | collective-permute-start | bytes 491528 | tf_op jit(solution)/shard_map/ppermute | solution.py:20
  10.6 0.8 slice_bitcast_fusion
  11.4 3.0 %collective-permute-start.1 = (f32[2,64,128]{2,1,0:T(8,128)S(1)}, f32[2,64,128]{2,1,0:T(8,128)S(1)}, u32[]{:S(2)}, u32[]{:S(2)}) collective-permute-start(f32[2,64,128]{2,1,0:T(8,128)S(1)} %slice_bitcast_fusion), channel_id=1, source_target_pairs={{0,14},{2,0},{4,2},{6,4},{8,6},{10,8},{12,10},{14,12},{1,15},{3,1}... | collective-permute-start | bytes 196616 | tf_op jit(solution)/shard_map/ppermute | solution.py:20
  14.4 0.7 slice_bitcast_fusion.3
  15.2 5.7 %collective-permute-done.4.c1_ref = f32[1,128]{1,0:T(1,128)S(1)} collective-permute-done((f32[1,128]{1,0:T(1,128)S(1)}, f32[1,128]{1,0:T(1,128)S(1)}, u32[]{:S(2)}, u32[]{:S(2)}) %collective-permute-start.4) | collective-permute-done | bytes 544 | tf_op jit(solution)/shard_map/ppermute | solution.py:157
  20.8 0.5 copy-done.24
  21.3 2.0 %shard_map.85 = (f32[8,64,128]{2,1,0:T(8,128)}, f32[8,64,128]{2,1,0:T(8,128)}) custom-call(f32[6]{0:T(128)} %eps_ref.1, f32[6]{0:T(128)} %sigma_ref.1, s32[8,64,128]{2,1,0:T(8,128)} %mat_ref.1), custom_call_target="tpu_custom_call" | custom-call | tf_op jit(solution)/shard_map/pallas_call | solution.py:42
  23.4 0.9 %collective-permute-done.5.c2_ref = f32[1,128]{1,0:T(1,128)S(1)} collective-permute-done((f32[1,128]{1,0:T(1,128)S(1)}, f32[1,128]{1,0:T(1,128)S(1)}, u32[]{:S(2)}, u32[]{:S(2)}) %collective-permute-start.5) | collective-permute-done | bytes 544 | tf_op jit(solution)/shard_map/ppermute | solution.py:157
  24.4 0.5 copy-done.27
  24.8 0.1 copy-done.15
  25.0 3.4 %shard_map.86 = (f32[3,8,64,128]{3,2,1,0:T(8,128)}, f32[3,8,64,128]{3,2,1,0:T(8,128)}, f32[5,64,128]{2,1,0:T(8,128)}, f32[2,64,128]{2,1,0:T(8,128)}, f32[5,8,1,1...) custom-call(f32[3,8,64,128]{3,2,1,0:T(8,128)} %e_ref.1, ...), custom_call_target="tpu_custom_call" | custom-call | tf_op jit(solution)/shard_map/pallas_call | solution.py:221
  28.5 0.9 collective-permute-start.10
  29.4 4.7 %collective-permute-start.7 = (f32[2,64,128]{2,1,0:T(8,128)}, f32[2,64,128]{2,1,0:T(8,128)S(1)}, u32[]{:S(2)}, u32[]{:S(2)}) collective-permute-start(f32[2,64,128]{2,1,0:T(8,128)} %get-tuple-element.36), channel_id=1, source_target_pairs={{0,14},{2,0},{4,2},{6,4},{8,6},{10,8},{12,10},{14,12},{1,15},{3,1}... | collective-permute-start | bytes 196616 | tf_op jit(solution)/shard_map/ppermute | solution.py:20
  34.1 0.5 collective-permute-start.9
  34.6 0.5 copy-done.22
  35.1 0.4 collective-permute-start.11
  35.5 2.6 %collective-permute-done.11.c2_ref = f32[1,128]{1,0:T(1,128)S(1)} collective-permute-done((f32[1,128]{1,0:T(1,128)S(1)}, f32[1,128]{1,0:T(1,128)S(1)}, u32[]{:S(2)}, u32[]{:S(2)}) %collective-permute-start.11) | collective-permute-done | bytes 544 | tf_op jit(solution)/shard_map/ppermute | solution.py:157
  38.2 0.4 copy-done.25
  38.6 0.1 copy-done.17
  38.8 3.4 %shard_map.87 = (f32[3,8,64,128]{3,2,1,0:T(8,128)}, f32[3,8,64,128]{3,2,1,0:T(8,128)}, f32[5,64,128]{2,1,0:T(8,128)}, f32[2,64,128]{2,1,0:T(8,128)}, f32[5,8,1,1...) custom-call(f32[3,8,64,128]{3,2,1,0:T(8,128)} %get-tuple-element.33.e_ref, ...), custom_call_target="tpu_custom_call" | custom-call | tf_op jit(solution)/shard_map/pallas_call | solution.py:221
  42.4 0.3 collective-permute-start.12
  42.7 4.4 %collective-permute-start.13 = (f32[2,64,128]{2,1,0:T(8,128)}, f32[2,64,128]{2,1,0:T(8,128)S(1)}, u32[]{:S(2)}, u32[]{:S(2)}) collective-permute-start(f32[2,64,128]{2,1,0:T(8,128)} %get-tuple-element.44), channel_id=1, source_target_pairs={{0,14},{2,0},{4,2},{6,4},{8,6},{10,8},{12,10},{14,12},{1,15},{3,1}... | collective-permute-start | bytes 196616 | tf_op jit(solution)/shard_map/ppermute | solution.py:20
  47.1 0.5 collective-permute-start.15
  47.7 0.6 collective-permute-done.16.c1_ref
  48.2 0.5 copy-done.20
  48.7 0.9 collective-permute-start.17
  49.7 2.1 %collective-permute-done.17.c2_ref = f32[1,128]{1,0:T(1,128)S(1)} collective-permute-done((f32[1,128]{1,0:T(1,128)S(1)}, f32[1,128]{1,0:T(1,128)S(1)}, u32[]{:S(2)}, u32[]{:S(2)}) %collective-permute-start.17) | collective-permute-done | bytes 544 | tf_op jit(solution)/shard_map/ppermute | solution.py:157
  51.8 0.5 copy-done.23
  52.5 3.5 %shard_map.88 = (f32[3,8,64,128]{3,2,1,0:T(8,128)}, f32[3,8,64,128]{3,2,1,0:T(8,128)}, f32[5,64,128]{2,1,0:T(8,128)}, f32[2,64,128]{2,1,0:T(8,128)}, f32[5,8,1,1...) custom-call(f32[3,8,64,128]{3,2,1,0:T(8,128)} %get-tuple-element.41.e_ref, ...), custom_call_target="tpu_custom_call" | custom-call | tf_op jit(solution)/shard_map/pallas_call | solution.py:221
  56.1 4.7 %collective-permute-start.19 = (f32[2,64,128]{2,1,0:T(8,128)}, f32[2,64,128]{2,1,0:T(8,128)S(1)}, u32[]{:S(2)}, u32[]{:S(2)}) collective-permute-start(f32[2,64,128]{2,1,0:T(8,128)} %get-tuple-element.52), channel_id=1, source_target_pairs={{0,14},{2,0},{4,2},{6,4},{8,6},{10,8},{12,10},{14,12},{1,15},{3,1}... | collective-permute-start | bytes 196616 | tf_op jit(solution)/shard_map/ppermute | solution.py:20
  60.8 0.5 collective-permute-start.21
  61.3 0.5 collective-permute-done.22.c1_ref
  61.9 0.5 copy-done.21
  62.4 0.8 collective-permute-start.23
  63.2 2.2 %collective-permute-done.23.c2_ref = f32[1,128]{1,0:T(1,128)S(1)} collective-permute-done((f32[1,128]{1,0:T(1,128)S(1)}, f32[1,128]{1,0:T(1,128)S(1)}, u32[]{:S(2)}, u32[]{:S(2)}) %collective-permute-start.23) | collective-permute-done | bytes 544 | tf_op jit(solution)/shard_map/ppermute | solution.py:157
  65.5 0.5 copy-done.26
  66.1 3.6 %shard_map.89 = (f32[3,8,64,128]{3,2,1,0:T(8,128)}, f32[3,8,64,128]{3,2,1,0:T(8,128)}, f32[5,64,128]{2,1,0:T(8,128)}, f32[2,64,128]{2,1,0:T(8,128)}, f32[5,8,1,1...) custom-call(f32[3,8,64,128]{3,2,1,0:T(8,128)} %get-tuple-element.49.e_ref, ...), custom_call_target="tpu_custom_call" | custom-call | tf_op jit(solution)/shard_map/pallas_call | solution.py:221
  69.7 1.7 %multiply_add_fusion = (f32[2,8,64,1]{3,2,1,0:T(8,128)S(1)}, f32[2,8,64,1]{3,2,1,0:T(8,128)S(1)}) fusion(f32[3,8,64,128]{3,2,1,0:T(8,128)} %get-tuple-element.28, f32[3,8,64,128]{3,2,1,0:T(8,128)S(1)} %copy-done.2, f32[3,8,64,128]{3,2,1,0:T(8,128)S(1)} %copy-done.1, f32[3,8,64,128]{3,2,1,0:T(8,128)S(1)} %copy-done), kind=kLoop, calls=%fused_computation.7 | loop fusion | flops 15360 | bytes 24576 | tf_op jit(solution)/shard_map/add | solution.py:223
  71.4 0.2 copy.27
  71.6 0.2 copy.26
  71.8 1.3 %convolution_bitcast_fusion.1 = f32[64,2]{0,1:T(2,128)S(1)} fusion(s32[64,64]{1,0:T(8,128)S(1)} %multiply_multiply_fusion, s32[64,8]{0,1:T(8,128)S(1)} %multiply_multiply_fusion.1, f32[2,8,64,1]{2,0,1,3:T(2,128)S(1)} %copy.27), kind=kOutput, calls=%fused_computation.2 | convolution fusion | flops 1245184 | bytes 23040 | tf_op jit(solution)/shard_map/dot_general | solution.py:249
  73.1 1.4 %convolution_bitcast_fusion.3 = f32[64,2]{0,1:T(2,128)S(1)} fusion(s32[64,64]{1,0:T(8,128)S(1)} %multiply_multiply_fusion, s32[64,8]{0,1:T(8,128)S(1)} %multiply_multiply_fusion.1, f32[2,8,64,1]{2,0,1,3:T(2,128)S(1)} %copy.26), kind=kOutput, calls=%fused_computation.5 | convolution fusion | flops 1245184 | bytes 23040 | tf_op jit(solution)/shard_map/dot_general | solution.py:246
  74.5 1.4 %fusion = f32[64,2]{0,1:T(2,128)S(1)} fusion(f32[64,2]{0,1:T(2,128)S(1)} %convolution_bitcast_fusion.1, s32[64,64]{1,0:T(8,128)S(1)} %multiply_multiply_fusion, s32[64,8]{0,1:T(8,128)S(1)} %multiply_multiply_fusion.1, f32[2,8,64,1]{2,0,1,3:T(2,128)S(1)} %copy.26), kind=kOutput, calls=%fused_computation.1 | convolution fusion | flops 1245312 | bytes 23552 | tf_op jit(solution)/shard_map/dot_general | solution.py:251
  75.9 1.4 %fusion.1 = f32[64,2]{0,1:T(2,128)S(1)} fusion(f32[64,2]{0,1:T(2,128)S(1)} %convolution_bitcast_fusion.3, s32[64,64]{1,0:T(8,128)S(1)} %multiply_multiply_fusion, s32[64,8]{0,1:T(8,128)S(1)} %multiply_multiply_fusion.1, f32[2,8,64,1]{2,0,1,3:T(2,128)S(1)} %copy.27), kind=kOutput, calls=%fused_computation.4 | convolution fusion | flops 1245312 | bytes 23552 | tf_op jit(solution)/shard_map/dot_general | solution.py:248
  77.4 1.8 %collective-permute-start.24 = (f32[32,4]{0,1:T(4,128)S(1)}, f32[32,4]{0,1:T(4,128)S(1)}, u32[]{:S(2)}, u32[]{:S(2)}) collective-permute-start(f32[32,4]{0,1:T(4,128)S(1)} %slice_select_fusion.2), channel_id=1, source_target_pairs={{0,8},{2,10},{4,12},{6,14},{8,0},{10,2},{12,4},{14,6},{1,9},{3,11}... | collective-permute-start | bytes 1544 | tf_op jit(solution)/shard_map/ppermute | solution.py:186
  79.2 2.6 %collective-permute-done.24 = f32[32,4]{0,1:T(4,128)S(1)} collective-permute-done((f32[32,4]{0,1:T(4,128)S(1)}, f32[32,4]{0,1:T(4,128)S(1)}, u32[]{:S(2)}, u32[]{:S(2)}) %collective-permute-start.24) | collective-permute-done | bytes 544 | tf_op jit(solution)/shard_map/ppermute | solution.py:186
  82.0 0.1 slice_select_fusion.1
  82.0 1.1 %collective-permute-start.25 = (f32[16,4]{0,1:T(4,128)S(1)}, f32[16,4]{0,1:T(4,128)S(1)}, u32[]{:S(2)}, u32[]{:S(2)}) collective-permute-start(f32[16,4]{0,1:T(4,128)S(1)} %slice_select_fusion.1), channel_id=1, source_target_pairs={{0,4},{2,6},{4,0},{6,2},{8,12},{10,14},{12,8},{14,10},{1,5},{3,7},... | collective-permute-start | bytes 776 | tf_op jit(solution)/shard_map/ppermute | solution.py:186
  83.1 2.5 %collective-permute-done.25 = f32[16,4]{0,1:T(4,128)S(1)} collective-permute-done((f32[16,4]{0,1:T(4,128)S(1)}, f32[16,4]{0,1:T(4,128)S(1)}, u32[]{:S(2)}, u32[]{:S(2)}) %collective-permute-start.25) | collective-permute-done | bytes 288 | tf_op jit(solution)/shard_map/ppermute | solution.py:186
  85.7 0.1 slice_select_fusion
  85.8 0.6 collective-permute-start.26
  86.4 3.0 %collective-permute-done.26 = f32[8,4]{0,1:T(4,128)S(1)} collective-permute-done((f32[8,4]{0,1:T(4,128)S(1)}, f32[8,4]{0,1:T(4,128)S(1)}, u32[]{:S(2)}, u32[]{:S(2)}) %collective-permute-start.26) | collective-permute-done | bytes 160 | tf_op jit(solution)/shard_map/ppermute | solution.py:186
  89.4 1.2 %collective-permute-done.27 = f32[8,4]{0,1:T(4,128)S(1)} collective-permute-done((f32[8,4]{0,1:T(4,128)S(1)}, f32[8,4]{0,1:T(4,128)S(1)}, u32[]{:S(2)}, u32[]{:S(2)}) %collective-permute-start.27) | collective-permute-done | bytes 160 | tf_op jit(solution)/shard_map/ppermute | solution.py:196
  90.6 0.6 add_multiply_fusion
  (98 shorter events, 1.4 us)
Async XLA Ops:
  2.4 21.9 %collective-permute-start.2 = (f32[5,8,1,128]{3,2,1,0:T(1,128)S(1)}, f32[5,8,1,128]{3,2,1,0:T(1,128)S(1)}, u32[]{:S(2)}, u32[]{:S(2)}) collective-permute-start(f32[5,8,1,128]{3,2,1,0:T(1,128)S(1)} %pad_maximum_fusion), channel_id=1, source_target_pairs={{0,1},{1,0},{2,3},{3,2},{4,5},{5,4},{6,7},{7,6},{8,9},{9,8},{10,11... | collective-permute-start | bytes 61448 | tf_op jit(solution)/shard_map/ppermute | solution.py:20
  3.7 20.6 %collective-permute-start.3 = (f32[2,8,1,128]{3,2,1,0:T(1,128)S(1)}, f32[2,8,1,128]{3,2,1,0:T(1,128)S(1)}, u32[]{:S(2)}, u32[]{:S(2)}) collective-permute-start(f32[2,8,1,128]{3,2,1,0:T(1,128)S(1)} %pad_maximum_fusion.1), channel_id=1, source_target_pairs={{0,1},{1,0},{2,3},{3,2},{4,5},{5,4},{6,7},{7,6},{8,9},{9,8},{10,11... | collective-permute-start | bytes 24584 | tf_op jit(solution)/shard_map/ppermute | solution.py:20
  7.6 16.7 %collective-permute-start = (f32[5,64,128]{2,1,0:T(8,128)S(1)}, f32[5,64,128]{2,1,0:T(8,128)S(1)}, u32[]{:S(2)}, u32[]{:S(2)}) collective-permute-start(f32[5,64,128]{2,1,0:T(8,128)S(1)} %bitcast_dynamic-update-slice_fusion), channel_id=1, source_target_pairs={{0,2},{2,4},{4,6},{6,8},{8,10},{10,12},{12,14},{14,0},{1,3},{3,5},... | collective-permute-start | bytes 491528 | tf_op jit(solution)/shard_map/ppermute | solution.py:20
  11.4 12.9 %collective-permute-start.1 = (f32[2,64,128]{2,1,0:T(8,128)S(1)}, f32[2,64,128]{2,1,0:T(8,128)S(1)}, u32[]{:S(2)}, u32[]{:S(2)}) collective-permute-start(f32[2,64,128]{2,1,0:T(8,128)S(1)} %slice_bitcast_fusion), channel_id=1, source_target_pairs={{0,14},{2,0},{4,2},{6,4},{8,6},{10,8},{12,10},{14,12},{1,15},{3,1}... | collective-permute-start | bytes 196616 | tf_op jit(solution)/shard_map/ppermute | solution.py:20
  15.2 5.7 %collective-permute-start.4 = (f32[1,128]{1,0:T(1,128)S(1)}, f32[1,128]{1,0:T(1,128)S(1)}, u32[]{:S(2)}, u32[]{:S(2)}) collective-permute-start(f32[1,128]{1,0:T(1,128)S(1)} %get-tuple-element.62), channel_id=1, source_target_pairs={{0,3},{1,2},{2,5},{3,4},{4,7},{5,6},{6,9},{7,8},{8,11},{9,10},{10,... | collective-permute-start | bytes 1544 | tf_op jit(solution)/shard_map/ppermute | solution.py:157
  20.8 0.5 copy-start.24
  21.3 3.0 %collective-permute-start.5 = (f32[1,128]{1,0:T(1,128)S(1)}, f32[1,128]{1,0:T(1,128)S(1)}, u32[]{:S(2)}, u32[]{:S(2)}) collective-permute-start(f32[1,128]{1,0:T(1,128)S(1)} %get-tuple-element.61), channel_id=1, source_target_pairs={{0,15},{1,14},{2,1},{3,0},{4,3},{5,2},{6,5},{7,4},{8,7},{9,6},{10,... | collective-permute-start | bytes 1544 | tf_op jit(solution)/shard_map/ppermute | solution.py:157
  24.3 0.5 copy-start.27
  24.3 0.6 copy-start.15
  24.3 0.6 copy-start.11
  24.3 0.6 copy-start.10
  24.3 0.7 copy-start.6
  28.5 5.6 %copy-start.30 = (f32[2,8,1,128]{3,2,1,0:T(1,128)S(1)}, f32[2,8,1,128]{3,2,1,0:T(1,128)}, u32[]{:S(2)}) copy-start(f32[2,8,1,128]{3,2,1,0:T(1,128)} %get-tuple-element.38) | copy-start | bytes 24580
  28.5 6.1 %collective-permute-start.10 = (f32[1,128]{1,0:T(1,128)}, f32[1,128]{1,0:T(1,128)S(1)}, u32[]{:S(2)}, u32[]{:S(2)}) collective-permute-start(f32[1,128]{1,0:T(1,128)} %get-tuple-element.39), channel_id=1, source_target_pairs={{0,3},{1,2},{2,5},{3,4},{4,7},{5,6},{6,9},{7,8},{8,11},{9,10},{10,... | collective-permute-start | bytes 1544 | tf_op jit(solution)/shard_map/ppermute | solution.py:157
  29.4 8.8 %collective-permute-start.6 = (f32[5,64,128]{2,1,0:T(8,128)}, f32[5,64,128]{2,1,0:T(8,128)S(1)}, u32[]{:S(2)}, u32[]{:S(2)}) collective-permute-start(f32[5,64,128]{2,1,0:T(8,128)} %get-tuple-element.35), channel_id=1, source_target_pairs={{0,2},{2,4},{4,6},{6,8},{8,10},{10,12},{12,14},{14,0},{1,3},{3,5},... | collective-permute-start | bytes 491528 | tf_op jit(solution)/shard_map/ppermute | solution.py:20
  29.4 8.8 %collective-permute-start.7 = (f32[2,64,128]{2,1,0:T(8,128)}, f32[2,64,128]{2,1,0:T(8,128)S(1)}, u32[]{:S(2)}, u32[]{:S(2)}) collective-permute-start(f32[2,64,128]{2,1,0:T(8,128)} %get-tuple-element.36), channel_id=1, source_target_pairs={{0,14},{2,0},{4,2},{6,4},{8,6},{10,8},{12,10},{14,12},{1,15},{3,1}... | collective-permute-start | bytes 196616 | tf_op jit(solution)/shard_map/ppermute | solution.py:20
  34.1 4.0 %collective-permute-start.8 = (f32[5,8,1,128]{3,2,1,0:T(1,128)}, f32[5,8,1,128]{3,2,1,0:T(1,128)S(1)}, u32[]{:S(2)}, u32[]{:S(2)}) collective-permute-start(f32[5,8,1,128]{3,2,1,0:T(1,128)} %get-tuple-element.37), channel_id=1, source_target_pairs={{0,1},{1,0},{2,3},{3,2},{4,5},{5,4},{6,7},{7,6},{8,9},{9,8},{10,11... | collective-permute-start | bytes 61448 | tf_op jit(solution)/shard_map/ppermute | solution.py:20
  34.1 1.0 %copy-start.33 = (f32[1,128]{1,0:T(1,128)S(1)}, f32[1,128]{1,0:T(1,128)}, u32[]{:S(2)}) copy-start(f32[1,128]{1,0:T(1,128)} %get-tuple-element.40) | copy-start | bytes 1540
  34.1 1.4 %copy-start.19 = (s32[64,2]{0,1:T(2,128)S(1)}, s32[64,2]{0,1:T(2,128)}, u32[]{:S(2)}) copy-start(s32[64,2]{0,1:T(2,128)} %param.11) | copy-start | bytes 1540
  34.1 4.0 %collective-permute-start.9 = (f32[2,8,1,128]{3,2,1,0:T(1,128)S(1)}, f32[2,8,1,128]{3,2,1,0:T(1,128)S(1)}, u32[]{:S(2)}, u32[]{:S(2)}) collective-permute-start(f32[2,8,1,128]{3,2,1,0:T(1,128)S(1)} %copy-done.30), channel_id=1, source_target_pairs={{0,1},{1,0},{2,3},{3,2},{4,5},{5,4},{6,7},{7,6},{8,9},{9,8},{10,11... | collective-permute-start | bytes 24584 | tf_op jit(solution)/shard_map/ppermute | solution.py:20
  34.6 0.5 copy-start.22
  35.1 3.0 %collective-permute-start.11 = (f32[1,128]{1,0:T(1,128)S(1)}, f32[1,128]{1,0:T(1,128)S(1)}, u32[]{:S(2)}, u32[]{:S(2)}) collective-permute-start(f32[1,128]{1,0:T(1,128)S(1)} %copy-done.33), channel_id=1, source_target_pairs={{0,15},{1,14},{2,1},{3,0},{4,3},{5,2},{6,5},{7,4},{8,7},{9,6},{10,... | collective-permute-start | bytes 1544 | tf_op jit(solution)/shard_map/ppermute | solution.py:157
  38.1 0.5 copy-start.25
  38.1 0.6 copy-start.17
  38.1 0.6 copy-start.13
  38.1 0.6 copy-start.8
  38.1 0.7 copy-start.4
  42.3 4.9 %copy-start.28 = (f32[2,8,1,128]{3,2,1,0:T(1,128)S(1)}, f32[2,8,1,128]{3,2,1,0:T(1,128)}, u32[]{:S(2)}) copy-start(f32[2,8,1,128]{3,2,1,0:T(1,128)} %get-tuple-element.46) | copy-start | bytes 24580
  42.3 5.9 %collective-permute-start.16 = (f32[1,128]{1,0:T(1,128)}, f32[1,128]{1,0:T(1,128)S(1)}, u32[]{:S(2)}, u32[]{:S(2)}) collective-permute-start(f32[1,128]{1,0:T(1,128)} %get-tuple-element.47), channel_id=1, source_target_pairs={{0,3},{1,2},{2,5},{3,4},{4,7},{5,6},{6,9},{7,8},{8,11},{9,10},{10,... | collective-permute-start | bytes 1544 | tf_op jit(solution)/shard_map/ppermute | solution.py:157
  42.4 9.4 %collective-permute-start.12 = (f32[5,64,128]{2,1,0:T(8,128)}, f32[5,64,128]{2,1,0:T(8,128)S(1)}, u32[]{:S(2)}, u32[]{:S(2)}) collective-permute-start(f32[5,64,128]{2,1,0:T(8,128)} %get-tuple-element.43), channel_id=1, source_target_pairs={{0,2},{2,4},{4,6},{6,8},{8,10},{10,12},{12,14},{14,0},{1,3},{3,5},... | collective-permute-start | bytes 491528 | tf_op jit(solution)/shard_map/ppermute | solution.py:20
  42.7 9.1 %collective-permute-start.13 = (f32[2,64,128]{2,1,0:T(8,128)}, f32[2,64,128]{2,1,0:T(8,128)S(1)}, u32[]{:S(2)}, u32[]{:S(2)}) collective-permute-start(f32[2,64,128]{2,1,0:T(8,128)} %get-tuple-element.44), channel_id=1, source_target_pairs={{0,14},{2,0},{4,2},{6,4},{8,6},{10,8},{12,10},{14,12},{1,15},{3,1}... | collective-permute-start | bytes 196616 | tf_op jit(solution)/shard_map/ppermute | solution.py:20
  47.1 4.6 %collective-permute-start.14 = (f32[5,8,1,128]{3,2,1,0:T(1,128)}, f32[5,8,1,128]{3,2,1,0:T(1,128)S(1)}, u32[]{:S(2)}, u32[]{:S(2)}) collective-permute-start(f32[5,8,1,128]{3,2,1,0:T(1,128)} %get-tuple-element.45), channel_id=1, source_target_pairs={{0,1},{1,0},{2,3},{3,2},{4,5},{5,4},{6,7},{7,6},{8,9},{9,8},{10,11... | collective-permute-start | bytes 61448 | tf_op jit(solution)/shard_map/ppermute | solution.py:20
  47.1 1.6 %copy-start.31 = (f32[1,128]{1,0:T(1,128)S(1)}, f32[1,128]{1,0:T(1,128)}, u32[]{:S(2)}) copy-start(f32[1,128]{1,0:T(1,128)} %get-tuple-element.48) | copy-start | bytes 1540
  47.1 4.6 %collective-permute-start.15 = (f32[2,8,1,128]{3,2,1,0:T(1,128)S(1)}, f32[2,8,1,128]{3,2,1,0:T(1,128)S(1)}, u32[]{:S(2)}, u32[]{:S(2)}) collective-permute-start(f32[2,8,1,128]{3,2,1,0:T(1,128)S(1)} %copy-done.28), channel_id=1, source_target_pairs={{0,1},{1,0},{2,3},{3,2},{4,5},{5,4},{6,7},{7,6},{8,9},{9,8},{10,11... | collective-permute-start | bytes 24584 | tf_op jit(solution)/shard_map/ppermute | solution.py:20
  48.2 0.5 copy-start.20
  48.7 3.0 %collective-permute-start.17 = (f32[1,128]{1,0:T(1,128)S(1)}, f32[1,128]{1,0:T(1,128)S(1)}, u32[]{:S(2)}, u32[]{:S(2)}) collective-permute-start(f32[1,128]{1,0:T(1,128)S(1)} %copy-done.31), channel_id=1, source_target_pairs={{0,15},{1,14},{2,1},{3,0},{4,3},{5,2},{6,5},{7,4},{8,7},{9,6},{10,... | collective-permute-start | bytes 1544 | tf_op jit(solution)/shard_map/ppermute | solution.py:157
  51.7 0.6 copy-start.23
  51.7 0.6 copy-start.16
  51.8 0.6 copy-start.12
  51.8 0.6 copy-start.7
  51.8 0.7 copy-start.3
  55.9 4.9 %copy-start.29 = (f32[2,8,1,128]{3,2,1,0:T(1,128)S(1)}, f32[2,8,1,128]{3,2,1,0:T(1,128)}, u32[]{:S(2)}) copy-start(f32[2,8,1,128]{3,2,1,0:T(1,128)} %get-tuple-element.54) | copy-start | bytes 24580
  55.9 5.9 %collective-permute-start.22 = (f32[1,128]{1,0:T(1,128)}, f32[1,128]{1,0:T(1,128)S(1)}, u32[]{:S(2)}, u32[]{:S(2)}) collective-permute-start(f32[1,128]{1,0:T(1,128)} %get-tuple-element.55), channel_id=1, source_target_pairs={{0,3},{1,2},{2,5},{3,4},{4,7},{5,6},{6,9},{7,8},{8,11},{9,10},{10,... | collective-permute-start | bytes 1544 | tf_op jit(solution)/shard_map/ppermute | solution.py:157
  56.0 6.4 %copy-start.32 = (f32[1,128]{1,0:T(1,128)S(1)}, f32[1,128]{1,0:T(1,128)}, u32[]{:S(2)}) copy-start(f32[1,128]{1,0:T(1,128)} %get-tuple-element.56) | copy-start | bytes 1540
  56.0 13.7 %copy-start.2 = (f32[3,8,64,128]{3,2,1,0:T(8,128)S(1)}, f32[3,8,64,128]{3,2,1,0:T(8,128)}, u32[]{:S(2)}) copy-start(f32[3,8,64,128]{3,2,1,0:T(8,128)} %get-tuple-element.49.e_ref) | copy-start | bytes 2359300
  56.0 9.4 %collective-permute-start.18 = (f32[5,64,128]{2,1,0:T(8,128)}, f32[5,64,128]{2,1,0:T(8,128)S(1)}, u32[]{:S(2)}, u32[]{:S(2)}) collective-permute-start(f32[5,64,128]{2,1,0:T(8,128)} %get-tuple-element.51), channel_id=1, source_target_pairs={{0,2},{2,4},{4,6},{6,8},{8,10},{10,12},{12,14},{14,0},{1,3},{3,5},... | collective-permute-start | bytes 491528 | tf_op jit(solution)/shard_map/ppermute | solution.py:20
  56.1 9.3 %collective-permute-start.19 = (f32[2,64,128]{2,1,0:T(8,128)}, f32[2,64,128]{2,1,0:T(8,128)S(1)}, u32[]{:S(2)}, u32[]{:S(2)}) collective-permute-start(f32[2,64,128]{2,1,0:T(8,128)} %get-tuple-element.52), channel_id=1, source_target_pairs={{0,14},{2,0},{4,2},{6,4},{8,6},{10,8},{12,10},{14,12},{1,15},{3,1}... | collective-permute-start | bytes 196616 | tf_op jit(solution)/shard_map/ppermute | solution.py:20
  60.8 4.6 %collective-permute-start.20 = (f32[5,8,1,128]{3,2,1,0:T(1,128)}, f32[5,8,1,128]{3,2,1,0:T(1,128)S(1)}, u32[]{:S(2)}, u32[]{:S(2)}) collective-permute-start(f32[5,8,1,128]{3,2,1,0:T(1,128)} %get-tuple-element.53), channel_id=1, source_target_pairs={{0,1},{1,0},{2,3},{3,2},{4,5},{5,4},{6,7},{7,6},{8,9},{9,8},{10,11... | collective-permute-start | bytes 61448 | tf_op jit(solution)/shard_map/ppermute | solution.py:20
  60.8 4.6 %collective-permute-start.21 = (f32[2,8,1,128]{3,2,1,0:T(1,128)S(1)}, f32[2,8,1,128]{3,2,1,0:T(1,128)S(1)}, u32[]{:S(2)}, u32[]{:S(2)}) collective-permute-start(f32[2,8,1,128]{3,2,1,0:T(1,128)S(1)} %copy-done.29), channel_id=1, source_target_pairs={{0,1},{1,0},{2,3},{3,2},{4,5},{5,4},{6,7},{7,6},{8,9},{9,8},{10,11... | collective-permute-start | bytes 24584 | tf_op jit(solution)/shard_map/ppermute | solution.py:20
  61.9 0.5 copy-start.21
  62.4 3.0 %collective-permute-start.23 = (f32[1,128]{1,0:T(1,128)S(1)}, f32[1,128]{1,0:T(1,128)S(1)}, u32[]{:S(2)}, u32[]{:S(2)}) collective-permute-start(f32[1,128]{1,0:T(1,128)S(1)} %copy-done.32), channel_id=1, source_target_pairs={{0,15},{1,14},{2,1},{3,0},{4,3},{5,2},{6,5},{7,4},{8,7},{9,6},{10,... | collective-permute-start | bytes 1544 | tf_op jit(solution)/shard_map/ppermute | solution.py:157
  65.4 0.6 copy-start.26
  65.4 0.6 copy-start.18
  65.4 0.6 copy-start.14
  65.4 0.6 copy-start.9
  65.5 0.7 copy-start.5
  66.1 3.6 %copy-start = (f32[3,8,64,128]{3,2,1,0:T(8,128)S(1)}, f32[3,8,64,128]{3,2,1,0:T(8,128)}, u32[]{:S(2)}) copy-start(f32[3,8,64,128]{3,2,1,0:T(8,128)} %get-tuple-element.33.e_ref) | copy-start | bytes 2359300
  66.1 3.6 %copy-start.1 = (f32[3,8,64,128]{3,2,1,0:T(8,128)S(1)}, f32[3,8,64,128]{3,2,1,0:T(8,128)}, u32[]{:S(2)}) copy-start(f32[3,8,64,128]{3,2,1,0:T(8,128)} %get-tuple-element.41.e_ref) | copy-start | bytes 2359300
  77.4 4.5 %collective-permute-start.24 = (f32[32,4]{0,1:T(4,128)S(1)}, f32[32,4]{0,1:T(4,128)S(1)}, u32[]{:S(2)}, u32[]{:S(2)}) collective-permute-start(f32[32,4]{0,1:T(4,128)S(1)} %slice_select_fusion.2), channel_id=1, source_target_pairs={{0,8},{2,10},{4,12},{6,14},{8,0},{10,2},{12,4},{14,6},{1,9},{3,11}... | collective-permute-start | bytes 1544 | tf_op jit(solution)/shard_map/ppermute | solution.py:186
  82.0 3.6 %collective-permute-start.25 = (f32[16,4]{0,1:T(4,128)S(1)}, f32[16,4]{0,1:T(4,128)S(1)}, u32[]{:S(2)}, u32[]{:S(2)}) collective-permute-start(f32[16,4]{0,1:T(4,128)S(1)} %slice_select_fusion.1), channel_id=1, source_target_pairs={{0,4},{2,6},{4,0},{6,2},{8,12},{10,14},{12,8},{14,10},{1,5},{3,7},... | collective-permute-start | bytes 776 | tf_op jit(solution)/shard_map/ppermute | solution.py:186
  85.8 3.6 %collective-permute-start.26 = (f32[8,4]{0,1:T(4,128)S(1)}, f32[8,4]{0,1:T(4,128)S(1)}, u32[]{:S(2)}, u32[]{:S(2)}) collective-permute-start(f32[8,4]{0,1:T(4,128)S(1)} %slice_select_fusion), channel_id=1, source_target_pairs={{0,2},{2,0},{4,6},{6,4},{8,10},{10,8},{12,14},{14,12},{1,3},{3,1},... | collective-permute-start | bytes 392 | tf_op jit(solution)/shard_map/ppermute | solution.py:186
  89.4 1.2 %collective-permute-start.27 = (f32[8,4]{0,1:T(4,128)S(1)}, f32[8,4]{0,1:T(4,128)S(1)}, u32[]{:S(2)}, u32[]{:S(2)}) collective-permute-start(f32[8,4]{0,1:T(4,128)S(1)} %select_add_fusion), channel_id=1, source_target_pairs={{0,1},{1,0},{2,3},{3,2},{4,5},{5,4},{6,7},{7,6},{8,9},{9,8},{10,11... | collective-permute-start | bytes 392 | tf_op jit(solution)/shard_map/ppermute | solution.py:196

commit v5 on v4

--- a/solution.py
+++ b/solution.py
@@ -73,8 +73,12 @@
     return f - jnp.where(index == 0, row, down)
 
 
-def _step_kernel(e_ref, h_ref, keep_ref, drive_ref, xlo_ref, xhi_ref, ylo_ref, yhi_ref,
-                 c1_ref, c2_ref, e_out, h_out, xlo_out, xhi_out, ylo_out, yhi_out, c1_out, c2_out):
+def _step_kernel(e_ref, h_ref, keep_ref, drive_ref, xlo_ref, xhi_ref, y_ref, c1_ref, c2_ref,
+                 e_out, h_out, xlo_out, xhi_out, y_out, c1_out, c2_out):
+    ylo_ref = y_ref
+    yhi_ref = y_ref.at[5:7]
+    ylo_out = y_out
+    yhi_out = y_out.at[5:7]
     planes = e_ref.shape[1]
     cells = e_ref.shape[2]
     ex_p = xlo_ref[0]
@@ -136,14 +140,29 @@
         hz_prev = hz
 
 
-def _halo_of(elec, magn):
-    cells = elec.shape[2]
+def _halo_kernel(e_ref, h_ref, xlo_out, xhi_out, y_out, c1_out, c2_out):
+    planes = e_ref.shape[1]
+    cells = e_ref.shape[2]
     last = slice(cells - 1, cells)
-    xlo = jnp.stack([elec[0, -1], elec[1, -1], elec[2, -1], magn[1, -1], magn[2, -1]])
-    xhi = elec[1:3, 0]
-    ylo = jnp.stack([elec[0, :, last], elec[1, :, last], elec[2, :, last], magn[0, :, last], magn[2, :, last]])
-    yhi = jnp.stack([elec[0, :, 0:1], elec[2, :, 0:1]])
-    return (xlo, xhi, ylo, yhi, elec[0, -1, 0:1], elec[1, 0, last])
+    for x in range(planes):
+        ex = e_ref[0, x]
+        ez = e_ref[2, x]
+        y_out[0, x] = ex[last]
+        y_out[1, x] = e_ref[1, x][last]
+        y_out[2, x] = ez[last]
+        y_out[3, x] = h_ref[0, x][last]
+        y_out[4, x] = h_ref[2, x][last]
+        y_out[5, x] = ex[0:1]
+        y_out[6, x] = ez[0:1]
+    xhi_out[0] = e_ref[1, 0]
+    xhi_out[1] = e_ref[2, 0]
+    c2_out[...] = e_ref[1, 0][last]
+    xlo_out[0] = e_ref[0, planes - 1]
+    xlo_out[1] = e_ref[1, planes - 1]
+    xlo_out[2] = e_ref[2, planes - 1]
+    xlo_out[3] = h_ref[1, planes - 1]
+    xlo_out[4] = h_ref[2, planes - 1]
+    c1_out[...] = e_ref[0, planes - 1][0:1]
 
 
 def diagonal(value, step_x, step_y):
@@ -158,15 +177,44 @@
 
 
 def exchange(halo):
-    xlo, xhi, ylo, yhi, c1, c2 = halo
+    xlo, xhi, rows, c1, c2 = halo
+    if lax.axis_size("gy") == 2:
+        rows = shifted(rows, "gy", 1)
+    else:
+        rows = jnp.concatenate([shifted(rows[0:5], "gy", 1), shifted(rows[5:7], "gy", -1)])
     return (
         shifted(xlo, "gx", 1),
         shifted(xhi, "gx", -1),
-        shifted(ylo, "gy", 1),
-        shifted(yhi, "gy", -1),
+        rows,
         diagonal(c1, 1, -1),
         diagonal(c2, -1, 1),
     )
+
+
+def trig_basis(angle_orders, cells_x, cells_y):
+    size_x = lax.axis_size("gx")
+    size_y = lax.axis_size("gy")
+    total_x = cells_x * size_x
+    total_y = cells_y * size_y
+    pos_x = lax.axis_index("gx") * cells_x + jnp.arange(cells_x, dtype=jnp.int32)
+    pos_y = lax.axis_index("gy") * cells_y + jnp.arange(cells_y, dtype=jnp.int32)
+    order_x = angle_orders[:, 0]
+    order_y = angle_orders[:, 1]
+    phase_int = (
+        order_x[:, None, None] * pos_x[None, :, None] * total_y
+        + order_y[:, None, None] * pos_y[None, None, :] * total_x
+    ) % (total_x * total_y)
+    theta = phase_int.astype(jnp.float32) * (2.0 * math.pi / (total_x * total_y))
+    theta = theta.reshape(angle_orders.shape[0], cells_x * cells_y)
+    return jnp.concatenate([jnp.cos(theta), jnp.sin(theta)])
+
+
+def transform(basis, columns):
+    return jnp.dot(basis, columns, precision=lax.Precision.HIGHEST, preferred_element_type=jnp.float32)
+
+
+def flat(plane):
+    return plane.reshape(plane.shape[0], -1).T
 
 
 def scatter_sum(rows, axis, owned):
@@ -198,58 +246,54 @@
 
 
 def local(e_field, h_field, material, eps_table, sigma_table, angle_orders):
-    keep, drive = coefficients(material, eps_table, sigma_table)
     comps, cells_x, cells_y, depth = e_field.shape
-    elec = e_field
-    magn = h_field
     f32 = jnp.float32
     field_shape = jax.ShapeDtypeStruct(e_field.shape, f32)
     halo_shapes = (
         jax.ShapeDtypeStruct((5, cells_y, depth), f32),
         jax.ShapeDtypeStruct((2, cells_y, depth), f32),
-        jax.ShapeDtypeStruct((5, cells_x, 1, depth), f32),
-        jax.ShapeDtypeStruct((2, cells_x, 1, depth), f32),
+        jax.ShapeDtypeStruct((7, cells_x, 1, depth), f32),
         jax.ShapeDtypeStruct((1, depth), f32),
         jax.ShapeDtypeStruct((1, depth), f32),
     )
     step_call = pl.pallas_call(_step_kernel, out_shape=(field_shape, field_shape) + halo_shapes)
-    halo = _halo_of(elec, magn)
+    halo = pl.pallas_call(_halo_kernel, out_shape=halo_shapes)(e_field, h_field)
+    received = exchange(halo)
+    keep, drive = coefficients(material, eps_table, sigma_table)
+    basis = trig_basis(angle_orders, cells_x, cells_y)
+    keep, drive, basis, received = lax.optimization_barrier((keep, drive, basis, received))
+    angle_count = angle_orders.shape[0]
+    elec = e_field
+    magn = h_field
     mon_real = jnp.zeros((2, cells_x, cells_y), f32)
     mon_imag = jnp.zeros((2, cells_x, cells_y), f32)
+    early = jnp.zeros((2 * angle_count, 4), f32)
     for number in range(ITERS):
-        received = exchange(halo)
+        if number > 0:
+            received = exchange(halo)
+        if number == ITERS - 1 and number > 0:
+            early = transform(basis, jnp.concatenate([flat(mon_real), flat(mon_imag)], axis=1))
+            early, received = lax.optimization_barrier((early, received))
         elec, magn, *halo = step_call(elec, magn, keep, drive, *received)
-        plane = elec[0:2, :, :, depth - 3]
-        mon_real = mon_real + math.cos(PHASE_STEP * (number + 1)) * plane
-        mon_imag = mon_imag - math.sin(PHASE_STEP * (number + 1)) * plane
-    size_x = lax.axis_size("gx")
-    size_y = lax.axis_size("gy")
-    total_x = cells_x * size_x
-    total_y = cells_y * size_y
-    pos_x = lax.axis_index("gx") * cells_x + jnp.arange(cells_x, dtype=jnp.int32)
-    pos_y = lax.axis_index("gy") * cells_y + jnp.arange(cells_y, dtype=jnp.int32)
-    flat_real = mon_real.reshape(2, cells_x * cells_y).T
-    flat_imag = mon_imag.reshape(2, cells_x * cells_y).T
-    high = lax.Precision.HIGHEST
-    angle_count = angle_orders.shape[0]
-    owned = angle_count // size_x
-    scale = 1.0 / math.sqrt(total_x * total_y)
-    order_x = angle_orders[:, 0]
-    order_y = angle_orders[:, 1]
-    phase_int = (
-        order_x[:, None, None] * pos_x[None, :, None] * total_y
-        + order_y[:, None, None] * pos_y[None, None, :] * total_x
-    ) % (total_x * total_y)
-    theta = phase_int.astype(jnp.float32) * (2.0 * math.pi / (total_x * total_y))
-    cosine = jnp.cos(theta).reshape(owned * lax.axis_size("gx"), cells_x * cells_y)
-    sine = jnp.sin(theta).reshape(owned * lax.axis_size("gx"), cells_x * cells_y)
-    real_part = jnp.dot(
-        cosine, flat_real, precision=high, preferred_element_type=jnp.float32
-    ) + jnp.dot(sine, flat_imag, precision=high, preferred_element_type=jnp.float32)
-    imag_part = jnp.dot(
-        cosine, flat_imag, precision=high, preferred_element_type=jnp.float32
-    ) - jnp.dot(sine, flat_real, precision=high, preferred_element_type=jnp.float32)
-    terms = jnp.stack([real_part[:, 0], imag_part[:, 0], real_part[:, 1], imag_part[:, 1]], axis=1)
+        if number < ITERS - 1:
+            plane = elec[0:2, :, :, depth - 3]
+            mon_real = mon_real + math.cos(PHASE_STEP * (number + 1)) * plane
+            mon_imag = mon_imag - math.sin(PHASE_STEP * (number + 1)) * plane
+    late = transform(basis, flat(elec[0:2, :, :, depth - 3]))
+    cos_last = math.cos(PHASE_STEP * ITERS)
+    sin_last = math.sin(PHASE_STEP * ITERS)
+    cos_rows = slice(0, angle_count)
+    sin_rows = slice(angle_count, 2 * angle_count)
+    columns = []
+    for comp in range(2):
+        cos_p = late[cos_rows, comp]
+        sin_p = late[sin_rows, comp]
+        real = early[cos_rows, comp] + early[sin_rows, 2 + comp] + (cos_last * cos_p - sin_last * sin_p)
+        imag = early[cos_rows, 2 + comp] - early[sin_rows, comp] - (sin_last * cos_p + cos_last * sin_p)
+        columns += [real, imag]
+    terms = jnp.stack(columns, axis=1)
+    owned = angle_count // lax.axis_size("gx")
+    scale = 1.0 / math.sqrt(cells_x * lax.axis_size("gx") * cells_y * lax.axis_size("gy"))
     far_field = scatter_sum(terms, "gx", owned)
     far_field = pair_sum(far_field, "gy") * scale
     return (elec, magn, far_field)

time: 92 us -> 85.9 us (0.934)
  waiting for transfers between devices: 23.9 us -> 15.5 us
  starting transfers between devices: 29 us -> 36.3 us
  matrix products: 5.39 us -> 0.53 us
  local copies, waits for them, and re-layouts: 13.1 us -> 10.4 us
  Pallas kernels: 16 us -> 18 us
  other arithmetic: 2.87 us -> 3.8 us
    ppermute x8, starting transfers between devices: 3 us -> 15.2 us  [diagonal(): return lax.ppermute(value, ('gx', 'gy'), pairs)]
    ppermute x8, waiting for transfers between devices: 14.5 us -> 3.62 us  [diagonal(): return lax.ppermute(value, ('gx', 'gy'), pairs)]
    dot_general x4 -> x2, matrix products: 5.39 us -> 0.53 us  [transform(): jnp.dot(basis, columns, precision=lax.Precision.HIGHEST, preferred_elemen...]
    ppermute x3, starting transfers between devices: 3.51 us -> 0.96 us  [scatter_sum(): rows = keep + lax.ppermute(send, axis, pairs)]
    ppermute x3, waiting for transfers between devices: 8.15 us -> 10.7 us  [scatter_sum(): rows = keep + lax.ppermute(send, axis, pairs)]
    ppermute x16 -> x12, starting transfers between devices: 22.4 us -> 20.2 us  [shifted(): return lax.ppermute(value, axis, pairs)]
    pallas_call x0 -> x1, Pallas kernels: none -> 2.09 us  [local(): halo = pl.pallas_call(_halo_kernel, out_shape=halo_shapes)(e_field, h_field)]
    squeeze x2 -> x0, local copies, waits for them, and re-layouts: 1.55 us -> none  [the longest x1 0.84 us: _halo_of(): xhi = elec[1:3, 0]]
  transfers between devices with their start and end apart: 28 -> 24, of which waited for: 11 -> 10; matrix products, arithmetic and copies ran while one was open for 7% -> 4% of each run, Pallas kernels for 2% -> 2%
where the time goes in v5:
time: 85.9 us; the launch traced here: 85.4 us
  starting transfers between devices  36.3 us (42%)
  Pallas kernels  18 us (21%)
  waiting for transfers between devices  15.5 us (18%)
  local copies, waits for them, and re-layouts  10.4 us (12%)
  other arithmetic  3.8 us (4%)
  between operations  0.9 us (1%)
    ppermute x12, starting transfers between devices, shifted(): return lax.ppermute(value, axis, pairs)  20.2 us
    ppermute x8, starting transfers between devices, diagonal(): return lax.ppermute(value, ('gx', 'gy'), pairs)  15.2 us
    pallas_call x4, Pallas kernels, local(): elec, magn, *halo = step_call(elec, magn, keep, drive, *received)  13.9 us
    ppermute x3, waiting for transfers between devices, scatter_sum(): rows = keep + lax.ppermute(send, axis, pairs)  10.7 us
    unnamed x62, local copies, waits for them, and re-layouts  8.49 us
    ppermute x8, waiting for transfers between devices, diagonal(): return lax.ppermute(value, ('gx', 'gy'), pairs)  3.62 us
    pallas_call x1, Pallas kernels, local(): halo = pl.pallas_call(_halo_kernel, out_shape=halo_shapes)(e_field, h_field)  2.09 us
    pallas_call x1, Pallas kernels, coefficients(): pl.pallas_call(_coef_kernel, out_shape=(out, out), in_specs=[scalar, scal...  2.01 us
  transfers between devices with their start and end apart: 24, of which 10 were waited for; matrix products, arithmetic and copies ran while one was open for 4% of the time, Pallas kernels for 2%

profile of v5, /device:TPU:0, one launch (start us, length us, event | category | flops | bytes accessed | tf_op | source)
XLA Modules:
  0.0 85.4 jit_solution(16162677581489637360)
XLA Ops:
  0.6 2.1 %shard_map.86 = (f32[5,64,128]{2,1,0:T(8,128)}, f32[2,64,128]{2,1,0:T(8,128)}, f32[7,8,1,128]{3,2,1,0:T(1,128)}, f32[1,128]{1,0:T(1,128)}, f32[1,128]{1,0:T(1,128)}) custom-call(f32[3,8,64,128]{3,2,1,0:T(8,128)} %e_ref.3, f32[3,8,64,128]{3,2,1,0:T(8,128)} %h_ref.3), custom_call_target="tpu_custom_call" | custom-call | tf_op jit(solution)/shard_map/pallas_call | solution.py:260
  2.7 3.0 %collective-permute-start = (f32[5,64,128]{2,1,0:T(8,128)}, f32[5,64,128]{2,1,0:T(8,128)S(1)}, u32[]{:S(2)}, u32[]{:S(2)}) collective-permute-start(f32[5,64,128]{2,1,0:T(8,128)} %get-tuple-element.49), channel_id=1, source_target_pairs={{0,2},{2,4},{4,6},{6,8},{8,10},{10,12},{12,14},{14,0},{1,3},{3,5},... | collective-permute-start | bytes 491528 | tf_op jit(solution)/shard_map/ppermute | solution.py:20
  5.7 3.0 %collective-permute-start.1 = (f32[2,64,128]{2,1,0:T(8,128)}, f32[2,64,128]{2,1,0:T(8,128)S(1)}, u32[]{:S(2)}, u32[]{:S(2)}) collective-permute-start(f32[2,64,128]{2,1,0:T(8,128)} %get-tuple-element.50), channel_id=1, source_target_pairs={{0,14},{2,0},{4,2},{6,4},{8,6},{10,8},{12,10},{14,12},{1,15},{3,1}... | collective-permute-start | bytes 196616 | tf_op jit(solution)/shard_map/ppermute | solution.py:20
  8.7 0.7 copy-done.24
  9.4 0.6 copy-done.23
  10.0 3.8 %collective-permute-start.4 = (f32[1,128]{1,0:T(1,128)S(1)}, f32[1,128]{1,0:T(1,128)S(1)}, u32[]{:S(2)}, u32[]{:S(2)}) collective-permute-start(f32[1,128]{1,0:T(1,128)S(1)} %copy-done.23), channel_id=1, source_target_pairs={{0,15},{1,14},{2,1},{3,0},{4,3},{5,2},{6,5},{7,4},{8,7},{9,6},{10,... | collective-permute-start | bytes 1544 | tf_op jit(solution)/shard_map/ppermute | solution.py:176
  13.8 0.7 copy-done.14
  14.5 0.1 multiply_multiply_fusion.1
  14.6 0.1 copy.9
  14.7 0.1 multiply_multiply_fusion
  14.8 0.1 broadcast_add_fusion
  14.9 0.1 add.99
  15.0 0.5 fusion.4
  15.6 2.0 %shard_map.85 = (f32[8,64,128]{2,1,0:T(8,128)}, f32[8,64,128]{2,1,0:T(8,128)}) custom-call(f32[6]{0:T(128)} %eps_ref.1, f32[6]{0:T(128)} %sigma_ref.1, s32[8,64,128]{2,1,0:T(8,128)} %mat_ref.1), custom_call_target="tpu_custom_call" | custom-call | tf_op jit(solution)/shard_map/pallas_call | solution.py:42
  17.7 0.4 copy-done.15
  18.1 0.1 copy-done.16
  18.3 3.4 %shard_map.87 = (f32[3,8,64,128]{3,2,1,0:T(8,128)}, f32[3,8,64,128]{3,2,1,0:T(8,128)}, f32[5,64,128]{2,1,0:T(8,128)}, f32[2,64,128]{2,1,0:T(8,128)}, f32[7,8,1,1...) custom-call(f32[3,8,64,128]{3,2,1,0:T(8,128)} %e_ref.3, f32[3,8,64,128]{3,2,1,0:T(8,128)} %h_ref.3, ...), custom_call_target="tpu_custom_call" | custom-call | tf_op jit(solution)/shard_map/pallas_call | solution.py:277
  21.8 4.7 %collective-permute-start.6 = (f32[2,64,128]{2,1,0:T(8,128)}, f32[2,64,128]{2,1,0:T(8,128)S(1)}, u32[]{:S(2)}, u32[]{:S(2)}) collective-permute-start(f32[2,64,128]{2,1,0:T(8,128)} %get-tuple-element.64), channel_id=1, source_target_pairs={{0,14},{2,0},{4,2},{6,4},{8,6},{10,8},{12,10},{14,12},{1,15},{3,1}... | collective-permute-start | bytes 196616 | tf_op jit(solution)/shard_map/ppermute | solution.py:20
  26.5 0.6 copy-done.30
  27.1 0.7 copy-done.29
  27.8 3.8 %collective-permute-start.9 = (f32[1,128]{1,0:T(1,128)S(1)}, f32[1,128]{1,0:T(1,128)S(1)}, u32[]{:S(2)}, u32[]{:S(2)}) collective-permute-start(f32[1,128]{1,0:T(1,128)S(1)} %copy-done.29), channel_id=1, source_target_pairs={{0,15},{1,14},{2,1},{3,0},{4,3},{5,2},{6,5},{7,4},{8,7},{9,6},{10,... | collective-permute-start | bytes 1544 | tf_op jit(solution)/shard_map/ppermute | solution.py:176
  31.6 1.2 %collective-permute-done.8.c1_ref = f32[1,128]{1,0:T(1,128)S(1)} collective-permute-done((f32[1,128]{1,0:T(1,128)S(1)}, f32[1,128]{1,0:T(1,128)S(1)}, u32[]{:S(2)}, u32[]{:S(2)}) %collective-permute-start.8) | collective-permute-done | bytes 544 | tf_op jit(solution)/shard_map/ppermute | solution.py:176
  32.8 0.1 collective-permute-done.9.c2_ref
  32.9 0.4 copy-done.21
  33.3 0.1 copy-done.22
  33.6 3.5 %shard_map.88 = (f32[3,8,64,128]{3,2,1,0:T(8,128)}, f32[3,8,64,128]{3,2,1,0:T(8,128)}, f32[5,64,128]{2,1,0:T(8,128)}, f32[2,64,128]{2,1,0:T(8,128)}, f32[7,8,1,1...) custom-call(f32[3,8,64,128]{3,2,1,0:T(8,128)} %get-tuple-element.61.e_ref, ...), custom_call_target="tpu_custom_call" | custom-call | tf_op jit(solution)/shard_map/pallas_call | solution.py:277
  37.0 4.7 %collective-permute-start.11 = (f32[2,64,128]{2,1,0:T(8,128)}, f32[2,64,128]{2,1,0:T(8,128)S(1)}, u32[]{:S(2)}, u32[]{:S(2)}) collective-permute-start(f32[2,64,128]{2,1,0:T(8,128)} %get-tuple-element.71), channel_id=1, source_target_pairs={{0,14},{2,0},{4,2},{6,4},{8,6},{10,8},{12,10},{14,12},{1,15},{3,1}... | collective-permute-start | bytes 196616 | tf_op jit(solution)/shard_map/ppermute | solution.py:20
  41.7 0.7 copy-done.28
  42.4 0.7 copy-done.27
  43.1 3.8 %collective-permute-start.14 = (f32[1,128]{1,0:T(1,128)S(1)}, f32[1,128]{1,0:T(1,128)S(1)}, u32[]{:S(2)}, u32[]{:S(2)}) collective-permute-start(f32[1,128]{1,0:T(1,128)S(1)} %copy-done.27), channel_id=1, source_target_pairs={{0,15},{1,14},{2,1},{3,0},{4,3},{5,2},{6,5},{7,4},{8,7},{9,6},{10,... | collective-permute-start | bytes 1544 | tf_op jit(solution)/shard_map/ppermute | solution.py:176
  46.8 1.2 %collective-permute-done.13.c1_ref = f32[1,128]{1,0:T(1,128)S(1)} collective-permute-done((f32[1,128]{1,0:T(1,128)S(1)}, f32[1,128]{1,0:T(1,128)S(1)}, u32[]{:S(2)}, u32[]{:S(2)}) %collective-permute-start.13) | collective-permute-done | bytes 544 | tf_op jit(solution)/shard_map/ppermute | solution.py:176
  48.1 0.1 collective-permute-done.14.c2_ref
  48.2 0.4 copy-done.18
  48.6 0.1 copy-done.20
  48.9 3.6 %shard_map.89 = (f32[3,8,64,128]{3,2,1,0:T(8,128)}, f32[3,8,64,128]{3,2,1,0:T(8,128)}, f32[5,64,128]{2,1,0:T(8,128)}, f32[2,64,128]{2,1,0:T(8,128)}, f32[7,8,1,1...) custom-call(f32[3,8,64,128]{3,2,1,0:T(8,128)} %get-tuple-element.68.e_ref, ...), custom_call_target="tpu_custom_call" | custom-call | tf_op jit(solution)/shard_map/pallas_call | solution.py:277
  52.4 4.7 %collective-permute-start.16 = (f32[2,64,128]{2,1,0:T(8,128)}, f32[2,64,128]{2,1,0:T(8,128)S(1)}, u32[]{:S(2)}, u32[]{:S(2)}) collective-permute-start(f32[2,64,128]{2,1,0:T(8,128)} %get-tuple-element.79), channel_id=1, source_target_pairs={{0,14},{2,0},{4,2},{6,4},{8,6},{10,8},{12,10},{14,12},{1,15},{3,1}... | collective-permute-start | bytes 196616 | tf_op jit(solution)/shard_map/ppermute | solution.py:20
  57.2 1.8 %add_reduce_fusion = (f32[2,8,64]{2,1,0:T(8,128)S(1)}, f32[2,8,64]{2,1,0:T(8,128)S(1)}) fusion(f32[3,8,64,128]{3,2,1,0:T(8,128)} %get-tuple-element.75.e_ref, f32[3,8,64,128]{3,2,1,0:T(8,128)S(1)} %copy-done.1, f32[3,8,64,128]{3,2,1,0:T(8,128)S(1)} %copy-done), kind=kLoop, calls=%fused_computation.2 | loop fusion | flops 11264 | bytes 20480 | tf_op jit(solution)/shard_map/add | solution.py:280
  59.0 0.1 add.103
  59.1 0.1 sub.44
  59.1 0.6 copy-done.26
  59.7 0.7 copy-done.25
  60.4 3.8 %collective-permute-start.19 = (f32[1,128]{1,0:T(1,128)S(1)}, f32[1,128]{1,0:T(1,128)S(1)}, u32[]{:S(2)}, u32[]{:S(2)}) collective-permute-start(f32[1,128]{1,0:T(1,128)S(1)} %copy-done.25), channel_id=1, source_target_pairs={{0,15},{1,14},{2,1},{3,0},{4,3},{5,2},{6,5},{7,4},{8,7},{9,6},{10,... | collective-permute-start | bytes 1544 | tf_op jit(solution)/shard_map/ppermute | solution.py:176
  64.2 0.3 fusion.5
  64.4 1.0 %collective-permute-done.18.c1_ref = f32[1,128]{1,0:T(1,128)S(1)} collective-permute-done((f32[1,128]{1,0:T(1,128)S(1)}, f32[1,128]{1,0:T(1,128)S(1)}, u32[]{:S(2)}, u32[]{:S(2)}) %collective-permute-start.18) | collective-permute-done | bytes 544 | tf_op jit(solution)/shard_map/ppermute | solution.py:176
  65.4 0.1 collective-permute-done.19.c2_ref
  65.5 0.4 copy-done.17
  65.9 0.1 copy-done.19
  66.2 3.4 %shard_map.90 = (f32[3,8,64,128]{3,2,1,0:T(8,128)}, f32[3,8,64,128]{3,2,1,0:T(8,128)}, f32[5,64,128]{2,1,0:T(8,128)}, f32[2,64,128]{2,1,0:T(8,128)}, f32[7,8,1,1...) custom-call(f32[3,8,64,128]{3,2,1,0:T(8,128)} %get-tuple-element.75.e_ref, ...), custom_call_target="tpu_custom_call" | custom-call | tf_op jit(solution)/shard_map/pallas_call | solution.py:277
  69.6 1.4 %slice_reduce_fusion = f32[2,8,64]{2,1,0:T(8,128)S(1)} fusion(f32[3,8,64,128]{3,2,1,0:T(8,128)} %get-tuple-element.44), kind=kLoop, calls=%fused_computation | loop fusion | bytes 8192 | tf_op jit(solution)/shard_map/slice | solution.py:282
  71.1 0.1 reshape_squeeze.3
  71.1 0.3 fusion.10
  71.4 0.1 subtract_add_fusion.1
  71.6 0.1 slice_select_fusion.2
  71.7 4.5 %collective-permute-done.20 = f32[32,4]{0,1:T(4,128)S(1)} collective-permute-done((f32[32,4]{0,1:T(4,128)S(1)}, f32[32,4]{0,1:T(4,128)S(1)}, u32[]{:S(2)}, u32[]{:S(2)}) %collective-permute-start.20) | collective-permute-done | bytes 544 | tf_op jit(solution)/shard_map/ppermute | solution.py:234
  76.1 0.1 select_add_fusion.2
  76.2 0.1 slice_select_fusion.1
  76.3 3.6 %collective-permute-done.21 = f32[16,4]{0,1:T(4,128)S(1)} collective-permute-done((f32[16,4]{0,1:T(4,128)S(1)}, f32[16,4]{0,1:T(4,128)S(1)}, u32[]{:S(2)}, u32[]{:S(2)}) %collective-permute-start.21) | collective-permute-done | bytes 288 | tf_op jit(solution)/shard_map/ppermute | solution.py:234
  79.9 0.1 select_add_fusion.1
  79.9 0.1 slice_select_fusion
  80.0 0.9 %collective-permute-start.22 = (f32[8,4]{0,1:T(4,128)S(1)}, f32[8,4]{0,1:T(4,128)S(1)}, u32[]{:S(2)}, u32[]{:S(2)}) collective-permute-start(f32[8,4]{0,1:T(4,128)S(1)} %slice_select_fusion), channel_id=1, source_target_pairs={{0,2},{2,0},{4,6},{6,4},{8,10},{10,8},{12,14},{14,12},{1,3},{3,1},... | collective-permute-start | bytes 392 | tf_op jit(solution)/shard_map/ppermute | solution.py:234
  81.0 2.6 %collective-permute-done.22 = f32[8,4]{0,1:T(4,128)S(1)} collective-permute-done((f32[8,4]{0,1:T(4,128)S(1)}, f32[8,4]{0,1:T(4,128)S(1)}, u32[]{:S(2)}, u32[]{:S(2)}) %collective-permute-start.22) | collective-permute-done | bytes 160 | tf_op jit(solution)/shard_map/ppermute | solution.py:234
  83.6 0.1 select_add_fusion
  83.7 1.2 %collective-permute-done.23 = f32[8,4]{0,1:T(4,128)S(1)} collective-permute-done((f32[8,4]{0,1:T(4,128)S(1)}, f32[8,4]{0,1:T(4,128)S(1)}, u32[]{:S(2)}, u32[]{:S(2)}) %collective-permute-start.23) | collective-permute-done | bytes 160 | tf_op jit(solution)/shard_map/ppermute | solution.py:244
  84.8 0.6 add_multiply_fusion
  (78 shorter events, 0.7 us)
Async XLA Ops:
  2.7 14.9 %collective-permute-start = (f32[5,64,128]{2,1,0:T(8,128)}, f32[5,64,128]{2,1,0:T(8,128)S(1)}, u32[]{:S(2)}, u32[]{:S(2)}) collective-permute-start(f32[5,64,128]{2,1,0:T(8,128)} %get-tuple-element.49), channel_id=1, source_target_pairs={{0,2},{2,4},{4,6},{6,8},{8,10},{10,12},{12,14},{14,0},{1,3},{3,5},... | collective-permute-start | bytes 491528 | tf_op jit(solution)/shard_map/ppermute | solution.py:20
  5.7 11.9 %collective-permute-start.1 = (f32[2,64,128]{2,1,0:T(8,128)}, f32[2,64,128]{2,1,0:T(8,128)S(1)}, u32[]{:S(2)}, u32[]{:S(2)}) collective-permute-start(f32[2,64,128]{2,1,0:T(8,128)} %get-tuple-element.50), channel_id=1, source_target_pairs={{0,14},{2,0},{4,2},{6,4},{8,6},{10,8},{12,10},{14,12},{1,15},{3,1}... | collective-permute-start | bytes 196616 | tf_op jit(solution)/shard_map/ppermute | solution.py:20
  8.7 0.7 copy-start.24
  8.7 8.9 %collective-permute-start.2 = (f32[7,8,1,128]{3,2,1,0:T(1,128)}, f32[7,8,1,128]{3,2,1,0:T(1,128)S(1)}, u32[]{:S(2)}, u32[]{:S(2)}) collective-permute-start(f32[7,8,1,128]{3,2,1,0:T(1,128)} %get-tuple-element.51), channel_id=1, source_target_pairs={{0,1},{1,0},{2,3},{3,2},{4,5},{5,4},{6,7},{7,6},{8,9},{9,8},{10,11... | collective-permute-start | bytes 86024 | tf_op jit(solution)/shard_map/ppermute | solution.py:20
  9.4 0.6 copy-start.23
  9.4 8.2 %collective-permute-start.3 = (f32[1,128]{1,0:T(1,128)S(1)}, f32[1,128]{1,0:T(1,128)S(1)}, u32[]{:S(2)}, u32[]{:S(2)}) collective-permute-start(f32[1,128]{1,0:T(1,128)S(1)} %copy-done.24), channel_id=1, source_target_pairs={{0,3},{1,2},{2,5},{3,4},{4,7},{5,6},{6,9},{7,8},{8,11},{9,10},{10,... | collective-permute-start | bytes 1544 | tf_op jit(solution)/shard_map/ppermute | solution.py:176
  10.0 7.6 %collective-permute-start.4 = (f32[1,128]{1,0:T(1,128)S(1)}, f32[1,128]{1,0:T(1,128)S(1)}, u32[]{:S(2)}, u32[]{:S(2)}) collective-permute-start(f32[1,128]{1,0:T(1,128)S(1)} %copy-done.23), channel_id=1, source_target_pairs={{0,15},{1,14},{2,1},{3,0},{4,3},{5,2},{6,5},{7,4},{8,7},{9,6},{10,... | collective-permute-start | bytes 1544 | tf_op jit(solution)/shard_map/ppermute | solution.py:176
  13.8 0.7 copy-start.14
  17.6 0.5 copy-start.15
  17.6 0.6 copy-start.16
  17.6 0.6 copy-start.10
  17.6 0.6 copy-start.6
  17.6 0.7 copy-start.2
  21.8 11.1 %collective-permute-start.5 = (f32[5,64,128]{2,1,0:T(8,128)}, f32[5,64,128]{2,1,0:T(8,128)S(1)}, u32[]{:S(2)}, u32[]{:S(2)}) collective-permute-start(f32[5,64,128]{2,1,0:T(8,128)} %get-tuple-element.63), channel_id=1, source_target_pairs={{0,2},{2,4},{4,6},{6,8},{8,10},{10,12},{12,14},{14,0},{1,3},{3,5},... | collective-permute-start | bytes 491528 | tf_op jit(solution)/shard_map/ppermute | solution.py:20
  21.8 11.1 %collective-permute-start.6 = (f32[2,64,128]{2,1,0:T(8,128)}, f32[2,64,128]{2,1,0:T(8,128)S(1)}, u32[]{:S(2)}, u32[]{:S(2)}) collective-permute-start(f32[2,64,128]{2,1,0:T(8,128)} %get-tuple-element.64), channel_id=1, source_target_pairs={{0,14},{2,0},{4,2},{6,4},{8,6},{10,8},{12,10},{14,12},{1,15},{3,1}... | collective-permute-start | bytes 196616 | tf_op jit(solution)/shard_map/ppermute | solution.py:20
  26.5 0.6 copy-start.30
  26.5 6.4 %collective-permute-start.7 = (f32[7,8,1,128]{3,2,1,0:T(1,128)}, f32[7,8,1,128]{3,2,1,0:T(1,128)S(1)}, u32[]{:S(2)}, u32[]{:S(2)}) collective-permute-start(f32[7,8,1,128]{3,2,1,0:T(1,128)} %get-tuple-element.65), channel_id=1, source_target_pairs={{0,1},{1,0},{2,3},{3,2},{4,5},{5,4},{6,7},{7,6},{8,9},{9,8},{10,11... | collective-permute-start | bytes 86024 | tf_op jit(solution)/shard_map/ppermute | solution.py:20
  27.1 0.7 copy-start.29
  27.1 5.7 %collective-permute-start.8 = (f32[1,128]{1,0:T(1,128)S(1)}, f32[1,128]{1,0:T(1,128)S(1)}, u32[]{:S(2)}, u32[]{:S(2)}) collective-permute-start(f32[1,128]{1,0:T(1,128)S(1)} %copy-done.30), channel_id=1, source_target_pairs={{0,3},{1,2},{2,5},{3,4},{4,7},{5,6},{6,9},{7,8},{8,11},{9,10},{10,... | collective-permute-start | bytes 1544 | tf_op jit(solution)/shard_map/ppermute | solution.py:176
  27.8 5.1 %collective-permute-start.9 = (f32[1,128]{1,0:T(1,128)S(1)}, f32[1,128]{1,0:T(1,128)S(1)}, u32[]{:S(2)}, u32[]{:S(2)}) collective-permute-start(f32[1,128]{1,0:T(1,128)S(1)} %copy-done.29), channel_id=1, source_target_pairs={{0,15},{1,14},{2,1},{3,0},{4,3},{5,2},{6,5},{7,4},{8,7},{9,6},{10,... | collective-permute-start | bytes 1544 | tf_op jit(solution)/shard_map/ppermute | solution.py:176
  32.8 0.5 copy-start.21
  32.8 0.6 copy-start.22
  32.9 0.6 copy-start.13
  32.9 0.6 copy-start.9
  32.9 0.7 copy-start.5
  37.0 11.2 %collective-permute-start.10 = (f32[5,64,128]{2,1,0:T(8,128)}, f32[5,64,128]{2,1,0:T(8,128)S(1)}, u32[]{:S(2)}, u32[]{:S(2)}) collective-permute-start(f32[5,64,128]{2,1,0:T(8,128)} %get-tuple-element.70), channel_id=1, source_target_pairs={{0,2},{2,4},{4,6},{6,8},{8,10},{10,12},{12,14},{14,0},{1,3},{3,5},... | collective-permute-start | bytes 491528 | tf_op jit(solution)/shard_map/ppermute | solution.py:20
  37.0 11.1 %collective-permute-start.11 = (f32[2,64,128]{2,1,0:T(8,128)}, f32[2,64,128]{2,1,0:T(8,128)S(1)}, u32[]{:S(2)}, u32[]{:S(2)}) collective-permute-start(f32[2,64,128]{2,1,0:T(8,128)} %get-tuple-element.71), channel_id=1, source_target_pairs={{0,14},{2,0},{4,2},{6,4},{8,6},{10,8},{12,10},{14,12},{1,15},{3,1}... | collective-permute-start | bytes 196616 | tf_op jit(solution)/shard_map/ppermute | solution.py:20
  41.7 0.7 copy-start.28
  41.7 6.4 %collective-permute-start.12 = (f32[7,8,1,128]{3,2,1,0:T(1,128)}, f32[7,8,1,128]{3,2,1,0:T(1,128)S(1)}, u32[]{:S(2)}, u32[]{:S(2)}) collective-permute-start(f32[7,8,1,128]{3,2,1,0:T(1,128)} %get-tuple-element.72), channel_id=1, source_target_pairs={{0,1},{1,0},{2,3},{3,2},{4,5},{5,4},{6,7},{7,6},{8,9},{9,8},{10,11... | collective-permute-start | bytes 86024 | tf_op jit(solution)/shard_map/ppermute | solution.py:20
  42.4 0.7 copy-start.27
  42.4 5.7 %collective-permute-start.13 = (f32[1,128]{1,0:T(1,128)S(1)}, f32[1,128]{1,0:T(1,128)S(1)}, u32[]{:S(2)}, u32[]{:S(2)}) collective-permute-start(f32[1,128]{1,0:T(1,128)S(1)} %copy-done.28), channel_id=1, source_target_pairs={{0,3},{1,2},{2,5},{3,4},{4,7},{5,6},{6,9},{7,8},{8,11},{9,10},{10,... | collective-permute-start | bytes 1544 | tf_op jit(solution)/shard_map/ppermute | solution.py:176
  43.1 5.1 %collective-permute-start.14 = (f32[1,128]{1,0:T(1,128)S(1)}, f32[1,128]{1,0:T(1,128)S(1)}, u32[]{:S(2)}, u32[]{:S(2)}) collective-permute-start(f32[1,128]{1,0:T(1,128)S(1)} %copy-done.27), channel_id=1, source_target_pairs={{0,15},{1,14},{2,1},{3,0},{4,3},{5,2},{6,5},{7,4},{8,7},{9,6},{10,... | collective-permute-start | bytes 1544 | tf_op jit(solution)/shard_map/ppermute | solution.py:176
  48.1 0.5 copy-start.18
  48.1 0.6 copy-start.20
  48.1 0.6 copy-start.12
  48.2 0.6 copy-start.8
  48.2 0.7 copy-start.4
  48.8 8.3 %copy-start = (f32[3,8,64,128]{3,2,1,0:T(8,128)S(1)}, f32[3,8,64,128]{3,2,1,0:T(8,128)}, u32[]{:S(2)}) copy-start(f32[3,8,64,128]{3,2,1,0:T(8,128)} %get-tuple-element.61.e_ref) | copy-start | bytes 2359300
  48.8 8.3 %copy-start.1 = (f32[3,8,64,128]{3,2,1,0:T(8,128)S(1)}, f32[3,8,64,128]{3,2,1,0:T(8,128)}, u32[]{:S(2)}) copy-start(f32[3,8,64,128]{3,2,1,0:T(8,128)} %get-tuple-element.68.e_ref) | copy-start | bytes 2359300
  52.4 13.1 %collective-permute-start.15 = (f32[5,64,128]{2,1,0:T(8,128)}, f32[5,64,128]{2,1,0:T(8,128)S(1)}, u32[]{:S(2)}, u32[]{:S(2)}) collective-permute-start(f32[5,64,128]{2,1,0:T(8,128)} %get-tuple-element.78), channel_id=1, source_target_pairs={{0,2},{2,4},{4,6},{6,8},{8,10},{10,12},{12,14},{14,0},{1,3},{3,5},... | collective-permute-start | bytes 491528 | tf_op jit(solution)/shard_map/ppermute | solution.py:20
  52.4 13.1 %collective-permute-start.16 = (f32[2,64,128]{2,1,0:T(8,128)}, f32[2,64,128]{2,1,0:T(8,128)S(1)}, u32[]{:S(2)}, u32[]{:S(2)}) collective-permute-start(f32[2,64,128]{2,1,0:T(8,128)} %get-tuple-element.79), channel_id=1, source_target_pairs={{0,14},{2,0},{4,2},{6,4},{8,6},{10,8},{12,10},{14,12},{1,15},{3,1}... | collective-permute-start | bytes 196616 | tf_op jit(solution)/shard_map/ppermute | solution.py:20
  57.2 8.3 %collective-permute-start.17 = (f32[7,8,1,128]{3,2,1,0:T(1,128)}, f32[7,8,1,128]{3,2,1,0:T(1,128)S(1)}, u32[]{:S(2)}, u32[]{:S(2)}) collective-permute-start(f32[7,8,1,128]{3,2,1,0:T(1,128)} %get-tuple-element.80), channel_id=1, source_target_pairs={{0,1},{1,0},{2,3},{3,2},{4,5},{5,4},{6,7},{7,6},{8,9},{9,8},{10,11... | collective-permute-start | bytes 86024 | tf_op jit(solution)/shard_map/ppermute | solution.py:20
  59.1 0.6 copy-start.26
  59.7 0.7 copy-start.25
  59.7 5.7 %collective-permute-start.18 = (f32[1,128]{1,0:T(1,128)S(1)}, f32[1,128]{1,0:T(1,128)S(1)}, u32[]{:S(2)}, u32[]{:S(2)}) collective-permute-start(f32[1,128]{1,0:T(1,128)S(1)} %copy-done.26), channel_id=1, source_target_pairs={{0,3},{1,2},{2,5},{3,4},{4,7},{5,6},{6,9},{7,8},{8,11},{9,10},{10,... | collective-permute-start | bytes 1544 | tf_op jit(solution)/shard_map/ppermute | solution.py:176
  60.4 5.1 %collective-permute-start.19 = (f32[1,128]{1,0:T(1,128)S(1)}, f32[1,128]{1,0:T(1,128)S(1)}, u32[]{:S(2)}, u32[]{:S(2)}) collective-permute-start(f32[1,128]{1,0:T(1,128)S(1)} %copy-done.25), channel_id=1, source_target_pairs={{0,15},{1,14},{2,1},{3,0},{4,3},{5,2},{6,5},{7,4},{8,7},{9,6},{10,... | collective-permute-start | bytes 1544 | tf_op jit(solution)/shard_map/ppermute | solution.py:176
  65.4 0.5 copy-start.17
  65.5 0.6 copy-start.19
  65.5 0.6 copy-start.11
  65.5 0.6 copy-start.7
  65.5 0.7 copy-start.3
  71.6 4.5 %collective-permute-start.20 = (f32[32,4]{0,1:T(4,128)S(1)}, f32[32,4]{0,1:T(4,128)S(1)}, u32[]{:S(2)}, u32[]{:S(2)}) collective-permute-start(f32[32,4]{0,1:T(4,128)S(1)} %slice_select_fusion.2), channel_id=1, source_target_pairs={{0,8},{2,10},{4,12},{6,14},{8,0},{10,2},{12,4},{14,6},{1,9},{3,11}... | collective-permute-start | bytes 1544 | tf_op jit(solution)/shard_map/ppermute | solution.py:234
  76.3 3.6 %collective-permute-start.21 = (f32[16,4]{0,1:T(4,128)S(1)}, f32[16,4]{0,1:T(4,128)S(1)}, u32[]{:S(2)}, u32[]{:S(2)}) collective-permute-start(f32[16,4]{0,1:T(4,128)S(1)} %slice_select_fusion.1), channel_id=1, source_target_pairs={{0,4},{2,6},{4,0},{6,2},{8,12},{10,14},{12,8},{14,10},{1,5},{3,7},... | collective-permute-start | bytes 776 | tf_op jit(solution)/shard_map/ppermute | solution.py:234
  80.0 3.6 %collective-permute-start.22 = (f32[8,4]{0,1:T(4,128)S(1)}, f32[8,4]{0,1:T(4,128)S(1)}, u32[]{:S(2)}, u32[]{:S(2)}) collective-permute-start(f32[8,4]{0,1:T(4,128)S(1)} %slice_select_fusion), channel_id=1, source_target_pairs={{0,2},{2,0},{4,6},{6,4},{8,10},{10,8},{12,14},{14,12},{1,3},{3,1},... | collective-permute-start | bytes 392 | tf_op jit(solution)/shard_map/ppermute | solution.py:234
  83.7 1.2 %collective-permute-start.23 = (f32[8,4]{0,1:T(4,128)S(1)}, f32[8,4]{0,1:T(4,128)S(1)}, u32[]{:S(2)}, u32[]{:S(2)}) collective-permute-start(f32[8,4]{0,1:T(4,128)S(1)} %select_add_fusion), channel_id=1, source_target_pairs={{0,1},{1,0},{2,3},{3,2},{4,5},{5,4},{6,7},{7,6},{8,9},{9,8},{10,11... | collective-permute-start | bytes 392 | tf_op jit(solution)/shard_map/ppermute | solution.py:244

commit v6 on v5

--- a/solution.py
+++ b/solution.py
@@ -73,8 +73,10 @@
     return f - jnp.where(index == 0, row, down)
 
 
-def _step_kernel(e_ref, h_ref, keep_ref, drive_ref, xlo_ref, xhi_ref, y_ref, c1_ref, c2_ref,
-                 e_out, h_out, xlo_out, xhi_out, y_out, c1_out, c2_out):
+def _step_kernel(e_ref, h_ref, keep_ref, drive_ref, xlo_ref, xhi_ref, y_ref,
+                 e_out, h_out, xlo_out, xhi_out, y_out):
+    c1_ref = y_ref.at[7, 0]
+    c2_ref = y_ref.at[8, 0]
     ylo_ref = y_ref
     yhi_ref = y_ref.at[5:7]
     ylo_out = y_out
@@ -128,19 +130,17 @@
         if x == 0:
             xhi_out[0] = ey_new
             xhi_out[1] = ez_new
-            c2_out[...] = ey_new[last]
         if x == planes - 1:
             xlo_out[0] = ex_new
             xlo_out[1] = ey_new
             xlo_out[2] = ez_new
             xlo_out[3] = hy
             xlo_out[4] = hz
-            c1_out[...] = ex_new[0:1]
         hy_prev = hy
         hz_prev = hz
 
 
-def _halo_kernel(e_ref, h_ref, xlo_out, xhi_out, y_out, c1_out, c2_out):
+def _halo_kernel(e_ref, h_ref, xlo_out, xhi_out, y_out):
     planes = e_ref.shape[1]
     cells = e_ref.shape[2]
     last = slice(cells - 1, cells)
@@ -156,39 +156,28 @@
         y_out[6, x] = ez[0:1]
     xhi_out[0] = e_ref[1, 0]
     xhi_out[1] = e_ref[2, 0]
-    c2_out[...] = e_ref[1, 0][last]
     xlo_out[0] = e_ref[0, planes - 1]
     xlo_out[1] = e_ref[1, planes - 1]
     xlo_out[2] = e_ref[2, planes - 1]
     xlo_out[3] = h_ref[1, planes - 1]
     xlo_out[4] = h_ref[2, planes - 1]
-    c1_out[...] = e_ref[0, planes - 1][0:1]
-
-
-def diagonal(value, step_x, step_y):
-    count_x = lax.axis_size("gx")
-    count_y = lax.axis_size("gy")
-    pairs = []
-    for a in range(count_x):
-        for b in range(count_y):
-            target = ((a + step_x) % count_x) * count_y + (b + step_y) % count_y
-            pairs.append((a * count_y + b, target))
-    return lax.ppermute(value, ("gx", "gy"), pairs)
 
 
 def exchange(halo):
-    xlo, xhi, rows, c1, c2 = halo
+    xlo, xhi, rows = halo
+    xlo = shifted(xlo, "gx", 1)
+    xhi = shifted(xhi, "gx", -1)
+    cells = xhi.shape[1]
+    corners = jnp.zeros((2,) + rows.shape[1:], rows.dtype)
+    corners = corners.at[0, 0].set(xlo[0, 0:1]).at[1, 0].set(xhi[0, cells - 1:cells])
+    message = jnp.concatenate([rows, corners])
     if lax.axis_size("gy") == 2:
-        rows = shifted(rows, "gy", 1)
+        rows = shifted(message, "gy", 1)
     else:
-        rows = jnp.concatenate([shifted(rows[0:5], "gy", 1), shifted(rows[5:7], "gy", -1)])
-    return (
-        shifted(xlo, "gx", 1),
-        shifted(xhi, "gx", -1),
-        rows,
-        diagonal(c1, 1, -1),
-        diagonal(c2, -1, 1),
-    )
+        before = shifted(message, "gy", 1)
+        after = shifted(message, "gy", -1)
+        rows = jnp.concatenate([before[0:5], after[5:8], before[8:9]])
+    return (xlo, xhi, rows)
 
 
 def trig_basis(angle_orders, cells_x, cells_y):
@@ -253,8 +242,6 @@
         jax.ShapeDtypeStruct((5, cells_y, depth), f32),
         jax.ShapeDtypeStruct((2, cells_y, depth), f32),
         jax.ShapeDtypeStruct((7, cells_x, 1, depth), f32),
-        jax.ShapeDtypeStruct((1, depth), f32),
-        jax.ShapeDtypeStruct((1, depth), f32),
     )
     step_call = pl.pallas_call(_step_kernel, out_shape=(field_shape, field_shape) + halo_shapes)
     halo = pl.pallas_call(_halo_kernel, out_shape=halo_shapes)(e_field, h_field)

time: 85.9 us -> 82.1 us (0.956)
  starting transfers between devices: 36.3 us -> 20.6 us
  waiting for transfers between devices: 15.5 us -> 30.2 us
  local copies, waits for them, and re-layouts: 10.4 us -> 5.81 us
  other arithmetic: 3.8 us -> 5.52 us
    ppermute x12, waiting for transfers between devices: 0.03 us -> 17.6 us  [shifted(): return lax.ppermute(value, axis, pairs)]
    ppermute x8 -> x0, starting transfers between devices: 15.2 us -> none  [diagonal(): return lax.ppermute(value, ('gx', 'gy'), pairs)]
    unnamed x62 -> x34, local copies, waits for them, and re-layouts: 8.49 us -> 3.86 us
    ppermute x8 -> x0, waiting for transfers between devices: 3.62 us -> none  [diagonal(): return lax.ppermute(value, ('gx', 'gy'), pairs)]
    concatenate x0 -> x4, other arithmetic: none -> 1.72 us  [exchange(): message = jnp.concatenate([rows, corners])]
  transfers between devices with their start and end apart: 24 -> 16, of which waited for: 10 -> 12; matrix products, arithmetic and copies ran while one was open for 4% -> 4% of each run, Pallas kernels for 2% -> 2%
where the time goes in v6:
time: 82.1 us; the launch traced here: 81.5 us
  waiting for transfers between devices  30.2 us (37%)
  starting transfers between devices  20.6 us (25%)
  Pallas kernels  18 us (22%)
  local copies, waits for them, and re-layouts  5.81 us (7%)
  other arithmetic  5.52 us (7%)
  between operations  0.85 us (1%)
    ppermute x12, starting transfers between devices, shifted(): return lax.ppermute(value, axis, pairs)  20.5 us
    ppermute x12, waiting for transfers between devices, shifted(): return lax.ppermute(value, axis, pairs)  17.6 us
    pallas_call x4, Pallas kernels, local(): elec, magn, *halo = step_call(elec, magn, keep, drive, *received)  13.9 us
    ppermute x3, waiting for transfers between devices, scatter_sum(): rows = keep + lax.ppermute(send, axis, pairs)  11.5 us
    unnamed x34, local copies, waits for them, and re-layouts  3.86 us
    pallas_call x1, Pallas kernels, local(): halo = pl.pallas_call(_halo_kernel, out_shape=halo_shapes)(e_field, h_field)  2.08 us
    pallas_call x1, Pallas kernels, coefficients(): pl.pallas_call(_coef_kernel, out_shape=(out, out), in_specs=[scalar, scal...  2.02 us
    add x1, other arithmetic, local(): mon_real = mon_real + math.cos(PHASE_STEP * (number + 1)) * plane  1.81 us
  transfers between devices with their start and end apart: 16, of which 12 were waited for; matrix products, arithmetic and copies ran while one was open for 4% of the time, Pallas kernels for 2%

profile of v6, /device:TPU:0, one launch (start us, length us, event | category | flops | bytes accessed | tf_op | source)
XLA Modules:
  0.0 81.5 jit_solution(15559602523211246165)
XLA Ops:
  0.6 2.1 %shard_map.86 = (f32[5,64,128]{2,1,0:T(8,128)}, f32[2,64,128]{2,1,0:T(8,128)}, f32[7,8,1,128]{3,2,1,0:T(1,128)}) custom-call(f32[3,8,64,128]{3,2,1,0:T(8,128)} %e_ref.3, f32[3,8,64,128]{3,2,1,0:T(8,128)} %h_ref.3), custom_call_target="tpu_custom_call" | custom-call | tf_op jit(solution)/shard_map/pallas_call | solution.py:247
  2.7 3.0 %collective-permute-start = (f32[5,64,128]{2,1,0:T(8,128)}, f32[5,64,128]{2,1,0:T(8,128)S(1)}, u32[]{:S(2)}, u32[]{:S(2)}) collective-permute-start(f32[5,64,128]{2,1,0:T(8,128)} %get-tuple-element.133), channel_id=1, source_target_pairs={{0,2},{2,4},{4,6},{6,8},{8,10},{10,12},{12,14},{14,0},{1,3},{3,5},... | collective-permute-start | bytes 491528 | tf_op jit(solution)/shard_map/ppermute | solution.py:20
  5.7 3.0 %collective-permute-start.1 = (f32[2,64,128]{2,1,0:T(8,128)}, f32[2,64,128]{2,1,0:T(8,128)S(1)}, u32[]{:S(2)}, u32[]{:S(2)}) collective-permute-start(f32[2,64,128]{2,1,0:T(8,128)} %get-tuple-element.134), channel_id=1, source_target_pairs={{0,14},{2,0},{4,2},{6,4},{8,6},{10,8},{12,10},{14,12},{1,15},{3,1}... | collective-permute-start | bytes 196616 | tf_op jit(solution)/shard_map/ppermute | solution.py:20
  8.7 0.7 copy-done.16
  9.4 0.1 multiply_multiply_fusion.1
  9.5 0.1 copy.9
  9.6 0.1 multiply_multiply_fusion
  9.6 0.1 broadcast_add_fusion
  9.8 0.1 add.123
  9.9 0.5 fusion.4
  10.4 2.8 %collective-permute-done.xlo_ref = f32[5,64,128]{2,1,0:T(8,128)S(1)} collective-permute-done((f32[5,64,128]{2,1,0:T(8,128)}, f32[5,64,128]{2,1,0:T(8,128)S(1)}, u32[]{:S(2)}, u32[]{:S(2)}) %collective-permute-start) | collective-permute-done | bytes 163872 | tf_op jit(solution)/shard_map/ppermute | solution.py:20
  13.2 0.4 collective-permute-done.1.xhi_ref
  13.7 0.1 collective-permute-start.2
  13.8 0.1 copy-done.2
  13.9 0.4 copy-done.6
  14.3 2.0 %shard_map.85 = (f32[8,64,128]{2,1,0:T(8,128)}, f32[8,64,128]{2,1,0:T(8,128)}) custom-call(f32[6]{0:T(128)} %eps_ref.1, f32[6]{0:T(128)} %sigma_ref.1, s32[8,64,128]{2,1,0:T(8,128)} %mat_ref.1), custom_call_target="tpu_custom_call" | custom-call | tf_op jit(solution)/shard_map/pallas_call | solution.py:42
  16.3 0.0 collective-permute-done.2.y_ref
  16.3 0.6 copy-done.10
  16.9 3.5 %shard_map.87 = (f32[3,8,64,128]{3,2,1,0:T(8,128)}, f32[3,8,64,128]{3,2,1,0:T(8,128)}, f32[5,64,128]{2,1,0:T(8,128)}, f32[2,64,128]{2,1,0:T(8,128)}, f32[7,8,1,128]{3,2,1,0:T(1,128)}) custom-call(f32[3,8,64,128]{3,2,1,0:T(8,128)} %e_ref.3, f32[3,8,64,128]{3,2,1,0:T(8,128)} %h_ref.3, f32[8,64,128]{2,1,0:T(8,128)} %get-tuple-element.136.keep_ref, ...), custom_call_target="tpu_custom_call" | custom-call | tf_op jit(solution)/shard_map/pallas_call | solution.py:264
  20.4 0.0 collective-permute-start.3
  20.4 4.7 %collective-permute-start.4 = (f32[2,64,128]{2,1,0:T(8,128)}, f32[2,64,128]{2,1,0:T(8,128)S(1)}, u32[]{:S(2)}, u32[]{:S(2)}) collective-permute-start(f32[2,64,128]{2,1,0:T(8,128)} %get-tuple-element.144), channel_id=1, source_target_pairs={{0,14},{2,0},{4,2},{6,4},{8,6},{10,8},{12,10},{14,12},{1,15},{3,1}... | collective-permute-start | bytes 196616 | tf_op jit(solution)/shard_map/ppermute | solution.py:20
  25.1 4.3 %collective-permute-done.3.xlo_ref = f32[5,64,128]{2,1,0:T(8,128)S(1)} collective-permute-done((f32[5,64,128]{2,1,0:T(8,128)}, f32[5,64,128]{2,1,0:T(8,128)S(1)}, u32[]{:S(2)}, u32[]{:S(2)}) %collective-permute-start.3) | collective-permute-done | bytes 163872 | tf_op jit(solution)/shard_map/ppermute | solution.py:20
  29.5 0.8 %pad_maximum_fusion.2 = f32[9,8,1,128]{3,2,1,0:T(1,128)S(1)} fusion(f32[2,8,1,128]{3,2,1,0:T(1,128)S(1)} %constant_dynamic-update-slice_fusion.2, f32[7,8,1,128]{3,2,1,0:T(1,128)} %get-tuple-element.145), kind=kLoop, calls=%fused_computation.12 | loop fusion | flops 9216 | bytes 73728 | tf_op jit(solution)/shard_map/concatenate | solution.py:173
  30.3 0.1 collective-permute-start.5
  30.4 1.2 %collective-permute-done.5.y_ref = f32[9,8,1,128]{3,2,1,0:T(1,128)S(1)} collective-permute-done((f32[9,8,1,128]{3,2,1,0:T(1,128)S(1)}, f32[9,8,1,128]{3,2,1,0:T(1,128)S(1)}, u32[]{:S(2)}, u32[]{:S(2)}) %collective-permute-start.5) | collective-permute-done | bytes 36896 | tf_op jit(solution)/shard_map/ppermute | solution.py:20
  31.6 0.6 copy-done.13
  32.2 3.4 %shard_map.88 = (f32[3,8,64,128]{3,2,1,0:T(8,128)}, f32[3,8,64,128]{3,2,1,0:T(8,128)}, f32[5,64,128]{2,1,0:T(8,128)}, f32[2,64,128]{2,1,0:T(8,128)}, f32[7,8,1,128]{3,2,1,0:T(1,128)}) custom-call(f32[3,8,64,128]{3,2,1,0:T(8,128)} %get-tuple-element.141.e_ref, f32[3,8,64,128]{3,2,1,0:T(8,128)} %get-tuple-element.142.h_ref, ...), custom_call_target="tpu_custom_call" | custom-call | tf_op jit(solution)/shard_map/pallas_call | solution.py:264
  35.7 4.7 %collective-permute-start.7 = (f32[2,64,128]{2,1,0:T(8,128)}, f32[2,64,128]{2,1,0:T(8,128)S(1)}, u32[]{:S(2)}, u32[]{:S(2)}) collective-permute-start(f32[2,64,128]{2,1,0:T(8,128)} %get-tuple-element.149), channel_id=1, source_target_pairs={{0,14},{2,0},{4,2},{6,4},{8,6},{10,8},{12,10},{14,12},{1,15},{3,1}... | collective-permute-start | bytes 196616 | tf_op jit(solution)/shard_map/ppermute | solution.py:20
  40.4 4.5 %collective-permute-done.6.xlo_ref = f32[5,64,128]{2,1,0:T(8,128)S(1)} collective-permute-done((f32[5,64,128]{2,1,0:T(8,128)}, f32[5,64,128]{2,1,0:T(8,128)S(1)}, u32[]{:S(2)}, u32[]{:S(2)}) %collective-permute-start.6) | collective-permute-done | bytes 163872 | tf_op jit(solution)/shard_map/ppermute | solution.py:20
  44.9 0.8 %pad_maximum_fusion.3 = f32[9,8,1,128]{3,2,1,0:T(1,128)S(1)} fusion(f32[2,8,1,128]{3,2,1,0:T(1,128)S(1)} %constant_dynamic-update-slice_fusion.1, f32[7,8,1,128]{3,2,1,0:T(1,128)} %get-tuple-element.150), kind=kLoop, calls=%fused_computation.13 | loop fusion | flops 9216 | bytes 73728 | tf_op jit(solution)/shard_map/concatenate | solution.py:173
  45.7 0.1 collective-permute-start.8
  45.8 1.2 %collective-permute-done.8.y_ref = f32[9,8,1,128]{3,2,1,0:T(1,128)S(1)} collective-permute-done((f32[9,8,1,128]{3,2,1,0:T(1,128)S(1)}, f32[9,8,1,128]{3,2,1,0:T(1,128)S(1)}, u32[]{:S(2)}, u32[]{:S(2)}) %collective-permute-start.8) | collective-permute-done | bytes 36896 | tf_op jit(solution)/shard_map/ppermute | solution.py:20
  47.0 0.6 copy-done.12
  47.6 3.6 %shard_map.89 = (f32[3,8,64,128]{3,2,1,0:T(8,128)}, f32[3,8,64,128]{3,2,1,0:T(8,128)}, f32[5,64,128]{2,1,0:T(8,128)}, f32[2,64,128]{2,1,0:T(8,128)}, f32[7,8,1,128]{3,2,1,0:T(1,128)}) custom-call(f32[3,8,64,128]{3,2,1,0:T(8,128)} %get-tuple-element.146.e_ref, f32[3,8,64,128]{3,2,1,0:T(8,128)} %get-tuple-element.147.h_ref, ...), custom_call_target="tpu_custom_call" | custom-call | tf_op jit(solution)/shard_map/pallas_call | solution.py:264
  51.2 0.0 collective-permute-start.9
  51.2 4.7 %collective-permute-start.10 = (f32[2,64,128]{2,1,0:T(8,128)}, f32[2,64,128]{2,1,0:T(8,128)S(1)}, u32[]{:S(2)}, u32[]{:S(2)}) collective-permute-start(f32[2,64,128]{2,1,0:T(8,128)} %get-tuple-element.155), channel_id=1, source_target_pairs={{0,14},{2,0},{4,2},{6,4},{8,6},{10,8},{12,10},{14,12},{1,15},{3,1}... | collective-permute-start | bytes 196616 | tf_op jit(solution)/shard_map/ppermute | solution.py:20
  55.9 1.8 %add_reduce_fusion = (f32[2,8,64]{2,1,0:T(8,128)S(1)}, f32[2,8,64]{2,1,0:T(8,128)S(1)}) fusion(f32[3,8,64,128]{3,2,1,0:T(8,128)} %get-tuple-element.151.e_ref, f32[3,8,64,128]{3,2,1,0:T(8,128)S(1)} %copy-done.1, f32[3,8,64,128]{3,2,1,0:T(8,128)S(1)} %copy-done), kind=kLoop, calls=%fused_computation.2 | loop fusion | flops 11264 | bytes 20480 | tf_op jit(solution)/shard_map/add | solution.py:267
  57.7 0.1 add.127
  57.8 0.1 sub.44
  57.9 2.5 %collective-permute-done.9.xlo_ref = f32[5,64,128]{2,1,0:T(8,128)S(1)} collective-permute-done((f32[5,64,128]{2,1,0:T(8,128)}, f32[5,64,128]{2,1,0:T(8,128)S(1)}, u32[]{:S(2)}, u32[]{:S(2)}) %collective-permute-start.9) | collective-permute-done | bytes 163872 | tf_op jit(solution)/shard_map/ppermute | solution.py:20
  60.4 0.1 collective-permute-start.11
  60.5 0.3 fusion.5
  60.8 0.2 copy-done.3
  61.0 0.0 copy-done.7
  61.0 0.7 collective-permute-done.11.y_ref
  61.7 0.6 copy-done.11
  62.3 3.4 %shard_map.90 = (f32[3,8,64,128]{3,2,1,0:T(8,128)}, f32[3,8,64,128]{3,2,1,0:T(8,128)}, f32[5,64,128]{2,1,0:T(8,128)}, f32[2,64,128]{2,1,0:T(8,128)}, f32[7,8,1,128]{3,2,1,0:T(1,128)}) custom-call(f32[3,8,64,128]{3,2,1,0:T(8,128)} %get-tuple-element.151.e_ref, f32[3,8,64,128]{3,2,1,0:T(8,128)} %get-tuple-element.152.h_ref, ...), custom_call_target="tpu_custom_call" | custom-call | tf_op jit(solution)/shard_map/pallas_call | solution.py:264
  65.7 1.4 %slice_reduce_fusion = f32[2,8,64]{2,1,0:T(8,128)S(1)} fusion(f32[3,8,64,128]{3,2,1,0:T(8,128)} %get-tuple-element.128), kind=kLoop, calls=%fused_computation | loop fusion | bytes 8192 | tf_op jit(solution)/shard_map/slice | solution.py:269
  67.2 0.1 reshape_squeeze.3
  67.2 0.3 fusion.10
  67.5 0.1 subtract_add_fusion.1
  67.7 0.1 slice_select_fusion.2
  67.7 0.1 collective-permute-start.12
  67.9 4.3 %collective-permute-done.12 = f32[32,4]{0,1:T(4,128)S(1)} collective-permute-done((f32[32,4]{0,1:T(4,128)S(1)}, f32[32,4]{0,1:T(4,128)S(1)}, u32[]{:S(2)}, u32[]{:S(2)}) %collective-permute-start.12) | collective-permute-done | bytes 544 | tf_op jit(solution)/shard_map/ppermute | solution.py:223
  72.2 0.1 select_add_fusion.2
  72.3 0.1 slice_select_fusion.1
  72.4 3.6 %collective-permute-done.13 = f32[16,4]{0,1:T(4,128)S(1)} collective-permute-done((f32[16,4]{0,1:T(4,128)S(1)}, f32[16,4]{0,1:T(4,128)S(1)}, u32[]{:S(2)}, u32[]{:S(2)}) %collective-permute-start.13) | collective-permute-done | bytes 288 | tf_op jit(solution)/shard_map/ppermute | solution.py:223
  76.0 0.1 select_add_fusion.1
  76.0 0.1 slice_select_fusion
  76.1 0.0 collective-permute-start.14
  76.1 3.6 %collective-permute-done.14 = f32[8,4]{0,1:T(4,128)S(1)} collective-permute-done((f32[8,4]{0,1:T(4,128)S(1)}, f32[8,4]{0,1:T(4,128)S(1)}, u32[]{:S(2)}, u32[]{:S(2)}) %collective-permute-start.14) | collective-permute-done | bytes 160 | tf_op jit(solution)/shard_map/ppermute | solution.py:223
  79.7 0.1 select_add_fusion
  79.8 1.2 %collective-permute-done.15 = f32[8,4]{0,1:T(4,128)S(1)} collective-permute-done((f32[8,4]{0,1:T(4,128)S(1)}, f32[8,4]{0,1:T(4,128)S(1)}, u32[]{:S(2)}, u32[]{:S(2)}) %collective-permute-start.15) | collective-permute-done | bytes 160 | tf_op jit(solution)/shard_map/ppermute | solution.py:233
  80.9 0.6 add_multiply_fusion
  (50 shorter events, 0.3 us)
Async XLA Ops:
  2.7 10.5 %collective-permute-start = (f32[5,64,128]{2,1,0:T(8,128)}, f32[5,64,128]{2,1,0:T(8,128)S(1)}, u32[]{:S(2)}, u32[]{:S(2)}) collective-permute-start(f32[5,64,128]{2,1,0:T(8,128)} %get-tuple-element.133), channel_id=1, source_target_pairs={{0,2},{2,4},{4,6},{6,8},{8,10},{10,12},{12,14},{14,0},{1,3},{3,5},... | collective-permute-start | bytes 491528 | tf_op jit(solution)/shard_map/ppermute | solution.py:20
  5.7 8.0 %collective-permute-start.1 = (f32[2,64,128]{2,1,0:T(8,128)}, f32[2,64,128]{2,1,0:T(8,128)S(1)}, u32[]{:S(2)}, u32[]{:S(2)}) collective-permute-start(f32[2,64,128]{2,1,0:T(8,128)} %get-tuple-element.134), channel_id=1, source_target_pairs={{0,14},{2,0},{4,2},{6,4},{8,6},{10,8},{12,10},{14,12},{1,15},{3,1}... | collective-permute-start | bytes 196616 | tf_op jit(solution)/shard_map/ppermute | solution.py:20
  8.7 0.7 copy-start.16
  9.9 3.8 %copy-start.14 = (f32[7,8,1,128]{3,2,1,0:T(1,128)S(1)}, f32[7,8,1,128]{3,2,1,0:T(1,128)}, u32[]{:S(2)}) copy-start(f32[7,8,1,128]{3,2,1,0:T(1,128)} %get-tuple-element.135) | copy-start | bytes 86020
  13.2 0.7 copy-start.2
  13.7 0.6 copy-start.6
  13.7 2.6 %collective-permute-start.2 = (f32[9,8,1,128]{3,2,1,0:T(1,128)S(1)}, f32[9,8,1,128]{3,2,1,0:T(1,128)S(1)}, u32[]{:S(2)}, u32[]{:S(2)}) collective-permute-start(f32[9,8,1,128]{3,2,1,0:T(1,128)S(1)} %pad_maximum_fusion.1), channel_id=1, source_target_pairs={{0,1},{1,0},{2,3},{3,2},{4,5},{5,4},{6,7},{7,6},{8,9},{9,8},{10,11... | collective-permute-start | bytes 110600 | tf_op jit(solution)/shard_map/ppermute | solution.py:20
  16.3 0.6 copy-start.10
  20.4 9.1 %collective-permute-start.3 = (f32[5,64,128]{2,1,0:T(8,128)}, f32[5,64,128]{2,1,0:T(8,128)S(1)}, u32[]{:S(2)}, u32[]{:S(2)}) collective-permute-start(f32[5,64,128]{2,1,0:T(8,128)} %get-tuple-element.143), channel_id=1, source_target_pairs={{0,2},{2,4},{4,6},{6,8},{8,10},{10,12},{12,14},{14,0},{1,3},{3,5},... | collective-permute-start | bytes 491528 | tf_op jit(solution)/shard_map/ppermute | solution.py:20
  20.4 9.1 %collective-permute-start.4 = (f32[2,64,128]{2,1,0:T(8,128)}, f32[2,64,128]{2,1,0:T(8,128)S(1)}, u32[]{:S(2)}, u32[]{:S(2)}) collective-permute-start(f32[2,64,128]{2,1,0:T(8,128)} %get-tuple-element.144), channel_id=1, source_target_pairs={{0,14},{2,0},{4,2},{6,4},{8,6},{10,8},{12,10},{14,12},{1,15},{3,1}... | collective-permute-start | bytes 196616 | tf_op jit(solution)/shard_map/ppermute | solution.py:20
  29.5 2.2 %copy-start.5 = (f32[5,64,128]{2,1,0:T(8,128)}, f32[5,64,128]{2,1,0:T(8,128)S(1)}, u32[]{:S(2)}) copy-start(f32[5,64,128]{2,1,0:T(8,128)S(1)} %collective-permute-done.3.xlo_ref) | copy-start | bytes 491524
  29.5 2.1 %copy-start.9 = (f32[2,64,128]{2,1,0:T(8,128)}, f32[2,64,128]{2,1,0:T(8,128)S(1)}, u32[]{:S(2)}) copy-start(f32[2,64,128]{2,1,0:T(8,128)S(1)} %collective-permute-done.4.xhi_ref) | copy-start | bytes 196612
  30.3 1.3 %collective-permute-start.5 = (f32[9,8,1,128]{3,2,1,0:T(1,128)S(1)}, f32[9,8,1,128]{3,2,1,0:T(1,128)S(1)}, u32[]{:S(2)}, u32[]{:S(2)}) collective-permute-start(f32[9,8,1,128]{3,2,1,0:T(1,128)S(1)} %pad_maximum_fusion.2), channel_id=1, source_target_pairs={{0,1},{1,0},{2,3},{3,2},{4,5},{5,4},{6,7},{7,6},{8,9},{9,8},{10,11... | collective-permute-start | bytes 110600 | tf_op jit(solution)/shard_map/ppermute | solution.py:20
  31.6 0.6 copy-start.13
  35.7 9.2 %collective-permute-start.6 = (f32[5,64,128]{2,1,0:T(8,128)}, f32[5,64,128]{2,1,0:T(8,128)S(1)}, u32[]{:S(2)}, u32[]{:S(2)}) collective-permute-start(f32[5,64,128]{2,1,0:T(8,128)} %get-tuple-element.148), channel_id=1, source_target_pairs={{0,2},{2,4},{4,6},{6,8},{8,10},{10,12},{12,14},{14,0},{1,3},{3,5},... | collective-permute-start | bytes 491528 | tf_op jit(solution)/shard_map/ppermute | solution.py:20
  35.7 9.2 %collective-permute-start.7 = (f32[2,64,128]{2,1,0:T(8,128)}, f32[2,64,128]{2,1,0:T(8,128)S(1)}, u32[]{:S(2)}, u32[]{:S(2)}) collective-permute-start(f32[2,64,128]{2,1,0:T(8,128)} %get-tuple-element.149), channel_id=1, source_target_pairs={{0,14},{2,0},{4,2},{6,4},{8,6},{10,8},{12,10},{14,12},{1,15},{3,1}... | collective-permute-start | bytes 196616 | tf_op jit(solution)/shard_map/ppermute | solution.py:20
  44.8 2.2 %copy-start.4 = (f32[5,64,128]{2,1,0:T(8,128)}, f32[5,64,128]{2,1,0:T(8,128)S(1)}, u32[]{:S(2)}) copy-start(f32[5,64,128]{2,1,0:T(8,128)S(1)} %collective-permute-done.6.xlo_ref) | copy-start | bytes 491524
  44.9 2.1 %copy-start.8 = (f32[2,64,128]{2,1,0:T(8,128)}, f32[2,64,128]{2,1,0:T(8,128)S(1)}, u32[]{:S(2)}) copy-start(f32[2,64,128]{2,1,0:T(8,128)S(1)} %collective-permute-done.7.xhi_ref) | copy-start | bytes 196612
  45.7 1.3 %collective-permute-start.8 = (f32[9,8,1,128]{3,2,1,0:T(1,128)S(1)}, f32[9,8,1,128]{3,2,1,0:T(1,128)S(1)}, u32[]{:S(2)}, u32[]{:S(2)}) collective-permute-start(f32[9,8,1,128]{3,2,1,0:T(1,128)S(1)} %pad_maximum_fusion.3), channel_id=1, source_target_pairs={{0,1},{1,0},{2,3},{3,2},{4,5},{5,4},{6,7},{7,6},{8,9},{9,8},{10,11... | collective-permute-start | bytes 110600 | tf_op jit(solution)/shard_map/ppermute | solution.py:20
  47.0 0.6 copy-start.12
  47.6 8.3 %copy-start = (f32[3,8,64,128]{3,2,1,0:T(8,128)S(1)}, f32[3,8,64,128]{3,2,1,0:T(8,128)}, u32[]{:S(2)}) copy-start(f32[3,8,64,128]{3,2,1,0:T(8,128)} %get-tuple-element.141.e_ref) | copy-start | bytes 2359300
  47.6 8.3 %copy-start.1 = (f32[3,8,64,128]{3,2,1,0:T(8,128)S(1)}, f32[3,8,64,128]{3,2,1,0:T(8,128)}, u32[]{:S(2)}) copy-start(f32[3,8,64,128]{3,2,1,0:T(8,128)} %get-tuple-element.146.e_ref) | copy-start | bytes 2359300
  51.2 9.2 %collective-permute-start.9 = (f32[5,64,128]{2,1,0:T(8,128)}, f32[5,64,128]{2,1,0:T(8,128)S(1)}, u32[]{:S(2)}, u32[]{:S(2)}) collective-permute-start(f32[5,64,128]{2,1,0:T(8,128)} %get-tuple-element.154), channel_id=1, source_target_pairs={{0,2},{2,4},{4,6},{6,8},{8,10},{10,12},{12,14},{14,0},{1,3},{3,5},... | collective-permute-start | bytes 491528 | tf_op jit(solution)/shard_map/ppermute | solution.py:20
  51.2 9.2 %collective-permute-start.10 = (f32[2,64,128]{2,1,0:T(8,128)}, f32[2,64,128]{2,1,0:T(8,128)S(1)}, u32[]{:S(2)}, u32[]{:S(2)}) collective-permute-start(f32[2,64,128]{2,1,0:T(8,128)} %get-tuple-element.155), channel_id=1, source_target_pairs={{0,14},{2,0},{4,2},{6,4},{8,6},{10,8},{12,10},{14,12},{1,15},{3,1}... | collective-permute-start | bytes 196616 | tf_op jit(solution)/shard_map/ppermute | solution.py:20
  57.7 2.7 %copy-start.15 = (f32[7,8,1,128]{3,2,1,0:T(1,128)S(1)}, f32[7,8,1,128]{3,2,1,0:T(1,128)}, u32[]{:S(2)}) copy-start(f32[7,8,1,128]{3,2,1,0:T(1,128)} %get-tuple-element.156) | copy-start | bytes 86020
  60.3 0.7 copy-start.3
  60.4 0.7 copy-start.7
  60.4 1.3 %collective-permute-start.11 = (f32[9,8,1,128]{3,2,1,0:T(1,128)S(1)}, f32[9,8,1,128]{3,2,1,0:T(1,128)S(1)}, u32[]{:S(2)}, u32[]{:S(2)}) collective-permute-start(f32[9,8,1,128]{3,2,1,0:T(1,128)S(1)} %pad_maximum_fusion.4), channel_id=1, source_target_pairs={{0,1},{1,0},{2,3},{3,2},{4,5},{5,4},{6,7},{7,6},{8,9},{9,8},{10,11... | collective-permute-start | bytes 110600 | tf_op jit(solution)/shard_map/ppermute | solution.py:20
  61.7 0.6 copy-start.11
  67.7 4.5 %collective-permute-start.12 = (f32[32,4]{0,1:T(4,128)S(1)}, f32[32,4]{0,1:T(4,128)S(1)}, u32[]{:S(2)}, u32[]{:S(2)}) collective-permute-start(f32[32,4]{0,1:T(4,128)S(1)} %slice_select_fusion.2), channel_id=1, source_target_pairs={{0,8},{2,10},{4,12},{6,14},{8,0},{10,2},{12,4},{14,6},{1,9},{3,11}... | collective-permute-start | bytes 1544 | tf_op jit(solution)/shard_map/ppermute | solution.py:223
  72.4 3.6 %collective-permute-start.13 = (f32[16,4]{0,1:T(4,128)S(1)}, f32[16,4]{0,1:T(4,128)S(1)}, u32[]{:S(2)}, u32[]{:S(2)}) collective-permute-start(f32[16,4]{0,1:T(4,128)S(1)} %slice_select_fusion.1), channel_id=1, source_target_pairs={{0,4},{2,6},{4,0},{6,2},{8,12},{10,14},{12,8},{14,10},{1,5},{3,7},... | collective-permute-start | bytes 776 | tf_op jit(solution)/shard_map/ppermute | solution.py:223
  76.1 3.6 %collective-permute-start.14 = (f32[8,4]{0,1:T(4,128)S(1)}, f32[8,4]{0,1:T(4,128)S(1)}, u32[]{:S(2)}, u32[]{:S(2)}) collective-permute-start(f32[8,4]{0,1:T(4,128)S(1)} %slice_select_fusion), channel_id=1, source_target_pairs={{0,2},{2,0},{4,6},{6,4},{8,10},{10,8},{12,14},{14,12},{1,3},{3,1},... | collective-permute-start | bytes 392 | tf_op jit(solution)/shard_map/ppermute | solution.py:223
  79.8 1.2 %collective-permute-start.15 = (f32[8,4]{0,1:T(4,128)S(1)}, f32[8,4]{0,1:T(4,128)S(1)}, u32[]{:S(2)}, u32[]{:S(2)}) collective-permute-start(f32[8,4]{0,1:T(4,128)S(1)} %select_add_fusion), channel_id=1, source_target_pairs={{0,1},{1,0},{2,3},{3,2},{4,5},{5,4},{6,7},{7,6},{8,9},{9,8},{10,11... | collective-permute-start | bytes 392 | tf_op jit(solution)/shard_map/ppermute | solution.py:233

commit v7 on v6

--- a/solution.py
+++ b/solution.py
@@ -73,8 +73,8 @@
     return f - jnp.where(index == 0, row, down)
 
 
-def _step_kernel(e_ref, h_ref, keep_ref, drive_ref, xlo_ref, xhi_ref, y_ref,
-                 e_out, h_out, xlo_out, xhi_out, y_out):
+def _step_body(e_ref, h_ref, keep_ref, drive_ref, xlo_ref, xhi_ref, y_ref,
+               e_out, h_out, xlo_out, xhi_out, y_out, ready, done):
     c1_ref = y_ref.at[7, 0]
     c2_ref = y_ref.at[8, 0]
     ylo_ref = y_ref
@@ -83,12 +83,15 @@
     yhi_out = y_out.at[5:7]
     planes = e_ref.shape[1]
     cells = e_ref.shape[2]
+    ready(0)
     ex_p = xlo_ref[0]
     ey_p = xlo_ref[1]
     ez_p = xlo_ref[2]
     hy_prev = xlo_ref[3] - TIME_STEP * (_z_up(ex_p) - (e_ref[2, 0] - ez_p))
     hz_prev = xlo_ref[4] - TIME_STEP * ((e_ref[1, 0] - ey_p) - _y_up(ex_p, c1_ref[...]))
     for x in range(planes):
+        if x + 1 < planes:
+            ready(x + 1)
         ex = e_ref[0, x]
         ey = e_ref[1, x]
         ez = e_ref[2, x]
@@ -119,6 +122,7 @@
         h_out[0, x] = hx
         h_out[1, x] = hy
         h_out[2, x] = hz
+        done(x)
         last = slice(cells - 1, cells)
         ylo_out[0, x] = ex_new[last]
         ylo_out[1, x] = ey_new[last]
@@ -138,6 +142,41 @@
             xlo_out[4] = hz
         hy_prev = hy
         hz_prev = hz
+
+
+def _step_kernel(e_hbm, h_hbm, keep_hbm, drive_hbm, xlo_ref, xhi_ref, y_ref,
+                 e_hbm_out, h_hbm_out, xlo_out, xhi_out, y_out,
+                 e_v, h_v, keep_v, drive_v, e_new, h_new, in_sem, out_sem):
+    planes = e_hbm.shape[1]
+
+    def fetch(x):
+        return [
+            pltpu.make_async_copy(e_hbm.at[:, x], e_v.at[:, x], in_sem.at[0, x]),
+            pltpu.make_async_copy(h_hbm.at[:, x], h_v.at[:, x], in_sem.at[1, x]),
+            pltpu.make_async_copy(keep_hbm.at[x], keep_v.at[x], in_sem.at[2, x]),
+            pltpu.make_async_copy(drive_hbm.at[x], drive_v.at[x], in_sem.at[3, x]),
+        ]
+
+    fetches = [fetch(x) for x in range(planes)]
+    for group in fetches:
+        for copy in group:
+            copy.start()
+    stores = []
+
+    def ready(x):
+        for copy in fetches[x]:
+            copy.wait()
+
+    def done(x):
+        for source, target, index in ((e_new, e_hbm_out, 0), (h_new, h_hbm_out, 1)):
+            copy = pltpu.make_async_copy(source.at[:, x], target.at[:, x], out_sem.at[index, x])
+            copy.start()
+            stores.append(copy)
+
+    _step_body(e_v, h_v, keep_v, drive_v, xlo_ref, xhi_ref, y_ref,
+               e_new, h_new, xlo_out, xhi_out, y_out, ready, done)
+    for copy in stores:
+        copy.wait()
 
 
 def _halo_kernel(e_ref, h_ref, xlo_out, xhi_out, y_out):
@@ -243,7 +282,24 @@
         jax.ShapeDtypeStruct((2, cells_y, depth), f32),
         jax.ShapeDtypeStruct((7, cells_x, 1, depth), f32),
     )
-    step_call = pl.pallas_call(_step_kernel, out_shape=(field_shape, field_shape) + halo_shapes)
+    vmem = pl.BlockSpec(memory_space=pltpu.VMEM)
+    anywhere = pl.BlockSpec(memory_space=pl.ANY)
+    step_call = pl.pallas_call(
+        _step_kernel,
+        out_shape=(field_shape, field_shape) + halo_shapes,
+        in_specs=[anywhere] * 4 + [vmem] * 3,
+        out_specs=(anywhere, anywhere) + (vmem,) * 3,
+        scratch_shapes=[
+            pltpu.VMEM(e_field.shape, f32),
+            pltpu.VMEM(e_field.shape, f32),
+            pltpu.VMEM(material.shape, f32),
+            pltpu.VMEM(material.shape, f32),
+            pltpu.VMEM(e_field.shape, f32),
+            pltpu.VMEM(e_field.shape, f32),
+            pltpu.SemaphoreType.DMA((4, cells_x)),
+            pltpu.SemaphoreType.DMA((2, cells_x)),
+        ],
+    )
     halo = pl.pallas_call(_halo_kernel, out_shape=halo_shapes)(e_field, h_field)
     received = exchange(halo)
     keep, drive = coefficients(material, eps_table, sigma_table)

time: 82.1 us -> 89.2 us (1.086)
  Pallas kernels: 18 us -> 24.8 us
    pallas_call x4, Pallas kernels: 13.9 us -> 20.7 us  [local(): elec, magn, *halo = step_call(elec, magn, keep, drive, *received)]
where the time goes in v7:
time: 89.2 us; the launch traced here: 88.5 us
  waiting for transfers between devices  30.2 us (34%)
  Pallas kernels  24.8 us (28%)
  starting transfers between devices  20.7 us (23%)
  local copies, waits for them, and re-layouts  5.81 us (7%)
  other arithmetic  5.52 us (6%)
  between operations  0.9 us (1%)
    pallas_call x4, Pallas kernels, local(): elec, magn, *halo = step_call(elec, magn, keep, drive, *received)  20.7 us
    ppermute x12, starting transfers between devices, shifted(): return lax.ppermute(value, axis, pairs)  20.6 us
    ppermute x12, waiting for transfers between devices, shifted(): return lax.ppermute(value, axis, pairs)  17.6 us
    ppermute x3, waiting for transfers between devices, scatter_sum(): rows = keep + lax.ppermute(send, axis, pairs)  11.5 us
    unnamed x34, local copies, waits for them, and re-layouts  3.86 us
    pallas_call x1, Pallas kernels, local(): halo = pl.pallas_call(_halo_kernel, out_shape=halo_shapes)(e_field, h_field)  2.08 us
    pallas_call x1, Pallas kernels, coefficients(): pl.pallas_call(_coef_kernel, out_shape=(out, out), in_specs=[scalar, scal...  2.02 us
    add x1, other arithmetic, local(): mon_real = mon_real + math.cos(PHASE_STEP * (number + 1)) * plane  1.81 us
  transfers between devices with their start and end apart: 16, of which 12 were waited for; matrix products, arithmetic and copies ran while one was open for 4% of the time, Pallas kernels for 2%

profile of v7, /device:TPU:0, one launch (start us, length us, event | category | flops | bytes accessed | tf_op | source)
XLA Modules:
  0.0 88.5 jit_solution(17151976254438274541)
XLA Ops:
  0.6 2.1 %shard_map.86 = (f32[5,64,128]{2,1,0:T(8,128)}, f32[2,64,128]{2,1,0:T(8,128)}, f32[7,8,1,128]{3,2,1,0:T(1,128)}) custom-call(f32[3,8,64,128]{3,2,1,0:T(8,128)} %e_hbm.1, f32[3,8,64,128]{3,2,1,0:T(8,128)} %h_hbm.1), custom_call_target="tpu_custom_call" | custom-call | tf_op jit(solution)/shard_map/pallas_call | solution.py:303
  2.7 3.0 %collective-permute-start = (f32[5,64,128]{2,1,0:T(8,128)}, f32[5,64,128]{2,1,0:T(8,128)S(1)}, u32[]{:S(2)}, u32[]{:S(2)}) collective-permute-start(f32[5,64,128]{2,1,0:T(8,128)} %get-tuple-element.133), channel_id=1, source_target_pairs={{0,2},{2,4},{4,6},{6,8},{8,10},{10,12},{12,14},{14,0},{1,3},{3,5},... | collective-permute-start | bytes 491528 | tf_op jit(solution)/shard_map/ppermute | solution.py:20
  5.7 3.0 %collective-permute-start.1 = (f32[2,64,128]{2,1,0:T(8,128)}, f32[2,64,128]{2,1,0:T(8,128)S(1)}, u32[]{:S(2)}, u32[]{:S(2)}) collective-permute-start(f32[2,64,128]{2,1,0:T(8,128)} %get-tuple-element.134), channel_id=1, source_target_pairs={{0,14},{2,0},{4,2},{6,4},{8,6},{10,8},{12,10},{14,12},{1,15},{3,1}... | collective-permute-start | bytes 196616 | tf_op jit(solution)/shard_map/ppermute | solution.py:20
  8.7 0.7 copy-done.16
  9.4 0.1 multiply_multiply_fusion.1
  9.5 0.1 copy.9
  9.6 0.1 multiply_multiply_fusion
  9.6 0.1 broadcast_add_fusion
  9.8 0.1 add.123
  9.9 0.5 fusion.4
  10.4 2.8 %collective-permute-done.xlo_ref = f32[5,64,128]{2,1,0:T(8,128)S(1)} collective-permute-done((f32[5,64,128]{2,1,0:T(8,128)}, f32[5,64,128]{2,1,0:T(8,128)S(1)}, u32[]{:S(2)}, u32[]{:S(2)}) %collective-permute-start) | collective-permute-done | bytes 163872 | tf_op jit(solution)/shard_map/ppermute | solution.py:20
  13.2 0.4 collective-permute-done.1.xhi_ref
  13.7 0.1 collective-permute-start.2
  13.8 0.1 copy-done.2
  13.9 0.4 copy-done.6
  14.3 2.0 %shard_map.85 = (f32[8,64,128]{2,1,0:T(8,128)}, f32[8,64,128]{2,1,0:T(8,128)}) custom-call(f32[6]{0:T(128)} %eps_ref.1, f32[6]{0:T(128)} %sigma_ref.1, s32[8,64,128]{2,1,0:T(8,128)} %mat_ref.1), custom_call_target="tpu_custom_call" | custom-call | tf_op jit(solution)/shard_map/pallas_call | solution.py:42
  16.3 0.0 collective-permute-done.2.y_ref
  16.3 0.6 copy-done.10
  16.9 5.1 %shard_map.87 = (f32[3,8,64,128]{3,2,1,0:T(8,128)}, f32[3,8,64,128]{3,2,1,0:T(8,128)}, f32[5,64,128]{2,1,0:T(8,128)}, f32[2,64,128]{2,1,0:T(8,128)}, f32[7,8,1,128]{3,2,1,0:T(1,128)}) custom-call(f32[3,8,64,128]{3,2,1,0:T(8,128)} %e_hbm.1, f32[3,8,64,128]{3,2,1,0:T(8,128)} %h_hbm.1, f32[8,64,128]{2,1,0:T(8,128)} %get-tuple-element.136.keep_hbm, ...), custom_call_target="tpu_custom_call" | custom-call | tf_op jit(solution)/shard_map/pallas_call | solution.py:320
  22.1 0.1 collective-permute-start.3
  22.1 4.7 %collective-permute-start.4 = (f32[2,64,128]{2,1,0:T(8,128)}, f32[2,64,128]{2,1,0:T(8,128)S(1)}, u32[]{:S(2)}, u32[]{:S(2)}) collective-permute-start(f32[2,64,128]{2,1,0:T(8,128)} %get-tuple-element.144), channel_id=1, source_target_pairs={{0,14},{2,0},{4,2},{6,4},{8,6},{10,8},{12,10},{14,12},{1,15},{3,1}... | collective-permute-start | bytes 196616 | tf_op jit(solution)/shard_map/ppermute | solution.py:20
  26.9 4.3 %collective-permute-done.3.xlo_ref = f32[5,64,128]{2,1,0:T(8,128)S(1)} collective-permute-done((f32[5,64,128]{2,1,0:T(8,128)}, f32[5,64,128]{2,1,0:T(8,128)S(1)}, u32[]{:S(2)}, u32[]{:S(2)}) %collective-permute-start.3) | collective-permute-done | bytes 163872 | tf_op jit(solution)/shard_map/ppermute | solution.py:20
  31.2 0.8 pad_maximum_fusion.2
  32.1 0.1 collective-permute-start.5
  32.1 1.2 %collective-permute-done.5.y_ref = f32[9,8,1,128]{3,2,1,0:T(1,128)S(1)} collective-permute-done((f32[9,8,1,128]{3,2,1,0:T(1,128)S(1)}, f32[9,8,1,128]{3,2,1,0:T(1,128)S(1)}, u32[]{:S(2)}, u32[]{:S(2)}) %collective-permute-start.5) | collective-permute-done | bytes 36896 | tf_op jit(solution)/shard_map/ppermute | solution.py:20
  33.3 0.6 copy-done.13
  34.0 5.1 %shard_map.88 = (f32[3,8,64,128]{3,2,1,0:T(8,128)}, f32[3,8,64,128]{3,2,1,0:T(8,128)}, f32[5,64,128]{2,1,0:T(8,128)}, f32[2,64,128]{2,1,0:T(8,128)}, f32[7,8,1,128]{3,2,1,0:T(1,128)}) custom-call(f32[3,8,64,128]{3,2,1,0:T(8,128)} %get-tuple-element.141.e_hbm, f32[3,8,64,128]{3,2,1,0:T(8,128)} %get-tuple-element.142.h_hbm, ...), custom_call_target="tpu_custom_call" | custom-call | tf_op jit(solution)/shard_map/pallas_call | solution.py:320
  39.1 0.1 collective-permute-start.6
  39.2 4.7 %collective-permute-start.7 = (f32[2,64,128]{2,1,0:T(8,128)}, f32[2,64,128]{2,1,0:T(8,128)S(1)}, u32[]{:S(2)}, u32[]{:S(2)}) collective-permute-start(f32[2,64,128]{2,1,0:T(8,128)} %get-tuple-element.149), channel_id=1, source_target_pairs={{0,14},{2,0},{4,2},{6,4},{8,6},{10,8},{12,10},{14,12},{1,15},{3,1}... | collective-permute-start | bytes 196616 | tf_op jit(solution)/shard_map/ppermute | solution.py:20
  43.9 4.5 %collective-permute-done.6.xlo_ref = f32[5,64,128]{2,1,0:T(8,128)S(1)} collective-permute-done((f32[5,64,128]{2,1,0:T(8,128)}, f32[5,64,128]{2,1,0:T(8,128)S(1)}, u32[]{:S(2)}, u32[]{:S(2)}) %collective-permute-start.6) | collective-permute-done | bytes 163872 | tf_op jit(solution)/shard_map/ppermute | solution.py:20
  48.4 0.8 pad_maximum_fusion.3
  49.2 0.1 collective-permute-start.8
  49.3 1.2 %collective-permute-done.8.y_ref = f32[9,8,1,128]{3,2,1,0:T(1,128)S(1)} collective-permute-done((f32[9,8,1,128]{3,2,1,0:T(1,128)S(1)}, f32[9,8,1,128]{3,2,1,0:T(1,128)S(1)}, u32[]{:S(2)}, u32[]{:S(2)}) %collective-permute-start.8) | collective-permute-done | bytes 36896 | tf_op jit(solution)/shard_map/ppermute | solution.py:20
  50.5 0.6 copy-done.12
  51.1 5.3 %shard_map.89 = (f32[3,8,64,128]{3,2,1,0:T(8,128)}, f32[3,8,64,128]{3,2,1,0:T(8,128)}, f32[5,64,128]{2,1,0:T(8,128)}, f32[2,64,128]{2,1,0:T(8,128)}, f32[7,8,1,128]{3,2,1,0:T(1,128)}) custom-call(f32[3,8,64,128]{3,2,1,0:T(8,128)} %get-tuple-element.146.e_hbm, f32[3,8,64,128]{3,2,1,0:T(8,128)} %get-tuple-element.147.h_hbm, ...), custom_call_target="tpu_custom_call" | custom-call | tf_op jit(solution)/shard_map/pallas_call | solution.py:320
  56.4 0.1 collective-permute-start.9
  56.4 4.7 %collective-permute-start.10 = (f32[2,64,128]{2,1,0:T(8,128)}, f32[2,64,128]{2,1,0:T(8,128)S(1)}, u32[]{:S(2)}, u32[]{:S(2)}) collective-permute-start(f32[2,64,128]{2,1,0:T(8,128)} %get-tuple-element.155), channel_id=1, source_target_pairs={{0,14},{2,0},{4,2},{6,4},{8,6},{10,8},{12,10},{14,12},{1,15},{3,1}... | collective-permute-start | bytes 196616 | tf_op jit(solution)/shard_map/ppermute | solution.py:20
  61.2 1.8 %add_reduce_fusion = (f32[2,8,64]{2,1,0:T(8,128)S(1)}, f32[2,8,64]{2,1,0:T(8,128)S(1)}) fusion(f32[3,8,64,128]{3,2,1,0:T(8,128)} %get-tuple-element.151.e_hbm, f32[3,8,64,128]{3,2,1,0:T(8,128)S(1)} %copy-done.1, f32[3,8,64,128]{3,2,1,0:T(8,128)S(1)} %copy-done), kind=kLoop, calls=%fused_computation.2 | loop fusion | flops 11264 | bytes 20480 | tf_op jit(solution)/shard_map/add | solution.py:323
  63.0 0.1 add.127
  63.1 0.1 sub.44
  63.1 2.5 %collective-permute-done.9.xlo_ref = f32[5,64,128]{2,1,0:T(8,128)S(1)} collective-permute-done((f32[5,64,128]{2,1,0:T(8,128)}, f32[5,64,128]{2,1,0:T(8,128)S(1)}, u32[]{:S(2)}, u32[]{:S(2)}) %collective-permute-start.9) | collective-permute-done | bytes 163872 | tf_op jit(solution)/shard_map/ppermute | solution.py:20
  65.7 0.1 collective-permute-start.11
  65.8 0.3 fusion.5
  66.0 0.2 copy-done.3
  66.3 0.0 copy-done.7
  66.3 0.7 collective-permute-done.11.y_ref
  67.0 0.6 copy-done.11
  67.6 5.1 %shard_map.90 = (f32[3,8,64,128]{3,2,1,0:T(8,128)}, f32[3,8,64,128]{3,2,1,0:T(8,128)}, f32[5,64,128]{2,1,0:T(8,128)}, f32[2,64,128]{2,1,0:T(8,128)}, f32[7,8,1,128]{3,2,1,0:T(1,128)}) custom-call(f32[3,8,64,128]{3,2,1,0:T(8,128)} %get-tuple-element.151.e_hbm, f32[3,8,64,128]{3,2,1,0:T(8,128)} %get-tuple-element.152.h_hbm, ...), custom_call_target="tpu_custom_call" | custom-call | tf_op jit(solution)/shard_map/pallas_call | solution.py:320
  72.7 1.4 %slice_reduce_fusion = f32[2,8,64]{2,1,0:T(8,128)S(1)} fusion(f32[3,8,64,128]{3,2,1,0:T(8,128)} %get-tuple-element.128), kind=kLoop, calls=%fused_computation | loop fusion | bytes 8192 | tf_op jit(solution)/shard_map/slice | solution.py:325
  74.2 0.1 reshape_squeeze.3
  74.2 0.3 fusion.10
  74.5 0.1 subtract_add_fusion.1
  74.7 0.1 slice_select_fusion.2
  74.7 0.1 collective-permute-start.12
  74.9 4.3 %collective-permute-done.12 = f32[32,4]{0,1:T(4,128)S(1)} collective-permute-done((f32[32,4]{0,1:T(4,128)S(1)}, f32[32,4]{0,1:T(4,128)S(1)}, u32[]{:S(2)}, u32[]{:S(2)}) %collective-permute-start.12) | collective-permute-done | bytes 544 | tf_op jit(solution)/shard_map/ppermute | solution.py:262
  79.2 0.1 select_add_fusion.2
  79.3 0.1 slice_select_fusion.1
  79.4 3.6 %collective-permute-done.13 = f32[16,4]{0,1:T(4,128)S(1)} collective-permute-done((f32[16,4]{0,1:T(4,128)S(1)}, f32[16,4]{0,1:T(4,128)S(1)}, u32[]{:S(2)}, u32[]{:S(2)}) %collective-permute-start.13) | collective-permute-done | bytes 288 | tf_op jit(solution)/shard_map/ppermute | solution.py:262
  83.0 0.1 select_add_fusion.1
  83.0 0.1 slice_select_fusion
  83.1 3.6 %collective-permute-done.14 = f32[8,4]{0,1:T(4,128)S(1)} collective-permute-done((f32[8,4]{0,1:T(4,128)S(1)}, f32[8,4]{0,1:T(4,128)S(1)}, u32[]{:S(2)}, u32[]{:S(2)}) %collective-permute-start.14) | collective-permute-done | bytes 160 | tf_op jit(solution)/shard_map/ppermute | solution.py:262
  86.7 0.1 select_add_fusion
  86.8 1.2 %collective-permute-done.15 = f32[8,4]{0,1:T(4,128)S(1)} collective-permute-done((f32[8,4]{0,1:T(4,128)S(1)}, f32[8,4]{0,1:T(4,128)S(1)}, u32[]{:S(2)}, u32[]{:S(2)}) %collective-permute-start.15) | collective-permute-done | bytes 160 | tf_op jit(solution)/shard_map/ppermute | solution.py:272
  87.9 0.6 add_multiply_fusion
  (50 shorter events, 0.3 us)
Async XLA Ops:
  2.7 10.5 %collective-permute-start = (f32[5,64,128]{2,1,0:T(8,128)}, f32[5,64,128]{2,1,0:T(8,128)S(1)}, u32[]{:S(2)}, u32[]{:S(2)}) collective-permute-start(f32[5,64,128]{2,1,0:T(8,128)} %get-tuple-element.133), channel_id=1, source_target_pairs={{0,2},{2,4},{4,6},{6,8},{8,10},{10,12},{12,14},{14,0},{1,3},{3,5},... | collective-permute-start | bytes 491528 | tf_op jit(solution)/shard_map/ppermute | solution.py:20
  5.7 8.0 %collective-permute-start.1 = (f32[2,64,128]{2,1,0:T(8,128)}, f32[2,64,128]{2,1,0:T(8,128)S(1)}, u32[]{:S(2)}, u32[]{:S(2)}) collective-permute-start(f32[2,64,128]{2,1,0:T(8,128)} %get-tuple-element.134), channel_id=1, source_target_pairs={{0,14},{2,0},{4,2},{6,4},{8,6},{10,8},{12,10},{14,12},{1,15},{3,1}... | collective-permute-start | bytes 196616 | tf_op jit(solution)/shard_map/ppermute | solution.py:20
  8.7 0.7 copy-start.16
  9.9 3.8 %copy-start.14 = (f32[7,8,1,128]{3,2,1,0:T(1,128)S(1)}, f32[7,8,1,128]{3,2,1,0:T(1,128)}, u32[]{:S(2)}) copy-start(f32[7,8,1,128]{3,2,1,0:T(1,128)} %get-tuple-element.135) | copy-start | bytes 86020
  13.2 0.7 copy-start.2
  13.7 0.6 copy-start.6
  13.7 2.6 %collective-permute-start.2 = (f32[9,8,1,128]{3,2,1,0:T(1,128)S(1)}, f32[9,8,1,128]{3,2,1,0:T(1,128)S(1)}, u32[]{:S(2)}, u32[]{:S(2)}) collective-permute-start(f32[9,8,1,128]{3,2,1,0:T(1,128)S(1)} %pad_maximum_fusion.1), channel_id=1, source_target_pairs={{0,1},{1,0},{2,3},{3,2},{4,5},{5,4},{6,7},{7,6},{8,9},{9,8},{10,11... | collective-permute-start | bytes 110600 | tf_op jit(solution)/shard_map/ppermute | solution.py:20
  16.3 0.6 copy-start.10
  22.1 9.1 %collective-permute-start.3 = (f32[5,64,128]{2,1,0:T(8,128)}, f32[5,64,128]{2,1,0:T(8,128)S(1)}, u32[]{:S(2)}, u32[]{:S(2)}) collective-permute-start(f32[5,64,128]{2,1,0:T(8,128)} %get-tuple-element.143), channel_id=1, source_target_pairs={{0,2},{2,4},{4,6},{6,8},{8,10},{10,12},{12,14},{14,0},{1,3},{3,5},... | collective-permute-start | bytes 491528 | tf_op jit(solution)/shard_map/ppermute | solution.py:20
  22.1 9.1 %collective-permute-start.4 = (f32[2,64,128]{2,1,0:T(8,128)}, f32[2,64,128]{2,1,0:T(8,128)S(1)}, u32[]{:S(2)}, u32[]{:S(2)}) collective-permute-start(f32[2,64,128]{2,1,0:T(8,128)} %get-tuple-element.144), channel_id=1, source_target_pairs={{0,14},{2,0},{4,2},{6,4},{8,6},{10,8},{12,10},{14,12},{1,15},{3,1}... | collective-permute-start | bytes 196616 | tf_op jit(solution)/shard_map/ppermute | solution.py:20
  31.2 2.2 %copy-start.5 = (f32[5,64,128]{2,1,0:T(8,128)}, f32[5,64,128]{2,1,0:T(8,128)S(1)}, u32[]{:S(2)}) copy-start(f32[5,64,128]{2,1,0:T(8,128)S(1)} %collective-permute-done.3.xlo_ref) | copy-start | bytes 491524
  31.2 2.1 %copy-start.9 = (f32[2,64,128]{2,1,0:T(8,128)}, f32[2,64,128]{2,1,0:T(8,128)S(1)}, u32[]{:S(2)}) copy-start(f32[2,64,128]{2,1,0:T(8,128)S(1)} %collective-permute-done.4.xhi_ref) | copy-start | bytes 196612
  32.1 1.3 %collective-permute-start.5 = (f32[9,8,1,128]{3,2,1,0:T(1,128)S(1)}, f32[9,8,1,128]{3,2,1,0:T(1,128)S(1)}, u32[]{:S(2)}, u32[]{:S(2)}) collective-permute-start(f32[9,8,1,128]{3,2,1,0:T(1,128)S(1)} %pad_maximum_fusion.2), channel_id=1, source_target_pairs={{0,1},{1,0},{2,3},{3,2},{4,5},{5,4},{6,7},{7,6},{8,9},{9,8},{10,11... | collective-permute-start | bytes 110600 | tf_op jit(solution)/shard_map/ppermute | solution.py:20
  33.3 0.6 copy-start.13
  39.1 9.2 %collective-permute-start.6 = (f32[5,64,128]{2,1,0:T(8,128)}, f32[5,64,128]{2,1,0:T(8,128)S(1)}, u32[]{:S(2)}, u32[]{:S(2)}) collective-permute-start(f32[5,64,128]{2,1,0:T(8,128)} %get-tuple-element.148), channel_id=1, source_target_pairs={{0,2},{2,4},{4,6},{6,8},{8,10},{10,12},{12,14},{14,0},{1,3},{3,5},... | collective-permute-start | bytes 491528 | tf_op jit(solution)/shard_map/ppermute | solution.py:20
  39.2 9.2 %collective-permute-start.7 = (f32[2,64,128]{2,1,0:T(8,128)}, f32[2,64,128]{2,1,0:T(8,128)S(1)}, u32[]{:S(2)}, u32[]{:S(2)}) collective-permute-start(f32[2,64,128]{2,1,0:T(8,128)} %get-tuple-element.149), channel_id=1, source_target_pairs={{0,14},{2,0},{4,2},{6,4},{8,6},{10,8},{12,10},{14,12},{1,15},{3,1}... | collective-permute-start | bytes 196616 | tf_op jit(solution)/shard_map/ppermute | solution.py:20
  48.3 2.2 %copy-start.4 = (f32[5,64,128]{2,1,0:T(8,128)}, f32[5,64,128]{2,1,0:T(8,128)S(1)}, u32[]{:S(2)}) copy-start(f32[5,64,128]{2,1,0:T(8,128)S(1)} %collective-permute-done.6.xlo_ref) | copy-start | bytes 491524
  48.4 2.1 %copy-start.8 = (f32[2,64,128]{2,1,0:T(8,128)}, f32[2,64,128]{2,1,0:T(8,128)S(1)}, u32[]{:S(2)}) copy-start(f32[2,64,128]{2,1,0:T(8,128)S(1)} %collective-permute-done.7.xhi_ref) | copy-start | bytes 196612
  49.2 1.3 %collective-permute-start.8 = (f32[9,8,1,128]{3,2,1,0:T(1,128)S(1)}, f32[9,8,1,128]{3,2,1,0:T(1,128)S(1)}, u32[]{:S(2)}, u32[]{:S(2)}) collective-permute-start(f32[9,8,1,128]{3,2,1,0:T(1,128)S(1)} %pad_maximum_fusion.3), channel_id=1, source_target_pairs={{0,1},{1,0},{2,3},{3,2},{4,5},{5,4},{6,7},{7,6},{8,9},{9,8},{10,11... | collective-permute-start | bytes 110600 | tf_op jit(solution)/shard_map/ppermute | solution.py:20
  50.5 0.6 copy-start.12
  51.1 10.1 %copy-start = (f32[3,8,64,128]{3,2,1,0:T(8,128)S(1)}, f32[3,8,64,128]{3,2,1,0:T(8,128)}, u32[]{:S(2)}) copy-start(f32[3,8,64,128]{3,2,1,0:T(8,128)} %get-tuple-element.141.e_hbm) | copy-start | bytes 2359300
  51.1 10.1 %copy-start.1 = (f32[3,8,64,128]{3,2,1,0:T(8,128)S(1)}, f32[3,8,64,128]{3,2,1,0:T(8,128)}, u32[]{:S(2)}) copy-start(f32[3,8,64,128]{3,2,1,0:T(8,128)} %get-tuple-element.146.e_hbm) | copy-start | bytes 2359300
  56.4 9.2 %collective-permute-start.9 = (f32[5,64,128]{2,1,0:T(8,128)}, f32[5,64,128]{2,1,0:T(8,128)S(1)}, u32[]{:S(2)}, u32[]{:S(2)}) collective-permute-start(f32[5,64,128]{2,1,0:T(8,128)} %get-tuple-element.154), channel_id=1, source_target_pairs={{0,2},{2,4},{4,6},{6,8},{8,10},{10,12},{12,14},{14,0},{1,3},{3,5},... | collective-permute-start | bytes 491528 | tf_op jit(solution)/shard_map/ppermute | solution.py:20
  56.4 9.2 %collective-permute-start.10 = (f32[2,64,128]{2,1,0:T(8,128)}, f32[2,64,128]{2,1,0:T(8,128)S(1)}, u32[]{:S(2)}, u32[]{:S(2)}) collective-permute-start(f32[2,64,128]{2,1,0:T(8,128)} %get-tuple-element.155), channel_id=1, source_target_pairs={{0,14},{2,0},{4,2},{6,4},{8,6},{10,8},{12,10},{14,12},{1,15},{3,1}... | collective-permute-start | bytes 196616 | tf_op jit(solution)/shard_map/ppermute | solution.py:20
  63.0 2.7 %copy-start.15 = (f32[7,8,1,128]{3,2,1,0:T(1,128)S(1)}, f32[7,8,1,128]{3,2,1,0:T(1,128)}, u32[]{:S(2)}) copy-start(f32[7,8,1,128]{3,2,1,0:T(1,128)} %get-tuple-element.156) | copy-start | bytes 86020
  65.6 0.7 copy-start.3
  65.6 0.7 copy-start.7
  65.7 1.3 %collective-permute-start.11 = (f32[9,8,1,128]{3,2,1,0:T(1,128)S(1)}, f32[9,8,1,128]{3,2,1,0:T(1,128)S(1)}, u32[]{:S(2)}, u32[]{:S(2)}) collective-permute-start(f32[9,8,1,128]{3,2,1,0:T(1,128)S(1)} %pad_maximum_fusion.4), channel_id=1, source_target_pairs={{0,1},{1,0},{2,3},{3,2},{4,5},{5,4},{6,7},{7,6},{8,9},{9,8},{10,11... | collective-permute-start | bytes 110600 | tf_op jit(solution)/shard_map/ppermute | solution.py:20
  67.0 0.6 copy-start.11
  74.7 4.5 %collective-permute-start.12 = (f32[32,4]{0,1:T(4,128)S(1)}, f32[32,4]{0,1:T(4,128)S(1)}, u32[]{:S(2)}, u32[]{:S(2)}) collective-permute-start(f32[32,4]{0,1:T(4,128)S(1)} %slice_select_fusion.2), channel_id=1, source_target_pairs={{0,8},{2,10},{4,12},{6,14},{8,0},{10,2},{12,4},{14,6},{1,9},{3,11}... | collective-permute-start | bytes 1544 | tf_op jit(solution)/shard_map/ppermute | solution.py:262
  79.4 3.6 %collective-permute-start.13 = (f32[16,4]{0,1:T(4,128)S(1)}, f32[16,4]{0,1:T(4,128)S(1)}, u32[]{:S(2)}, u32[]{:S(2)}) collective-permute-start(f32[16,4]{0,1:T(4,128)S(1)} %slice_select_fusion.1), channel_id=1, source_target_pairs={{0,4},{2,6},{4,0},{6,2},{8,12},{10,14},{12,8},{14,10},{1,5},{3,7},... | collective-permute-start | bytes 776 | tf_op jit(solution)/shard_map/ppermute | solution.py:262
  83.1 3.6 %collective-permute-start.14 = (f32[8,4]{0,1:T(4,128)S(1)}, f32[8,4]{0,1:T(4,128)S(1)}, u32[]{:S(2)}, u32[]{:S(2)}) collective-permute-start(f32[8,4]{0,1:T(4,128)S(1)} %slice_select_fusion), channel_id=1, source_target_pairs={{0,2},{2,0},{4,6},{6,4},{8,10},{10,8},{12,14},{14,12},{1,3},{3,1},... | collective-permute-start | bytes 392 | tf_op jit(solution)/shard_map/ppermute | solution.py:262
  86.8 1.2 %collective-permute-start.15 = (f32[8,4]{0,1:T(4,128)S(1)}, f32[8,4]{0,1:T(4,128)S(1)}, u32[]{:S(2)}, u32[]{:S(2)}) collective-permute-start(f32[8,4]{0,1:T(4,128)S(1)} %select_add_fusion), channel_id=1, source_target_pairs={{0,1},{1,0},{2,3},{3,2},{4,5},{5,4},{6,7},{7,6},{8,9},{9,8},{10,11... | collective-permute-start | bytes 392 | tf_op jit(solution)/shard_map/ppermute | solution.py:272

commit v8 on v6

--- a/solution.py
+++ b/solution.py
@@ -1,3 +1,4 @@
+import functools
 import math
 
 import jax
@@ -73,46 +74,63 @@
     return f - jnp.where(index == 0, row, down)
 
 
-def _step_kernel(e_ref, h_ref, keep_ref, drive_ref, xlo_ref, xhi_ref, y_ref,
-                 e_out, h_out, xlo_out, xhi_out, y_out):
-    c1_ref = y_ref.at[7, 0]
-    c2_ref = y_ref.at[8, 0]
-    ylo_ref = y_ref
-    yhi_ref = y_ref.at[5:7]
-    ylo_out = y_out
-    yhi_out = y_out.at[5:7]
-    planes = e_ref.shape[1]
-    cells = e_ref.shape[2]
+def _magn_plane(elec, magn, x, planes, xhi_ref, yhi_ref):
+    ex = elec(0, x)
+    ey = elec(1, x)
+    ez = elec(2, x)
+    if x + 1 < planes:
+        ey_next = elec(1, x + 1)
+        ez_next = elec(2, x + 1)
+    else:
+        ey_next = xhi_ref[0]
+        ez_next = xhi_ref[1]
+    hx = magn(0, x) - TIME_STEP * (_y_up(ez, yhi_ref[1, x]) - _z_up(ey))
+    hy = magn(1, x) - TIME_STEP * (_z_up(ex) - (ez_next - ez))
+    hz = magn(2, x) - TIME_STEP * ((ey_next - ey) - _y_up(ex, yhi_ref[0, x]))
+    return (ex, ey, ez, hx, hy, hz)
+
+
+def _magn_before(elec, xlo_ref, c1_ref):
     ex_p = xlo_ref[0]
     ey_p = xlo_ref[1]
     ez_p = xlo_ref[2]
-    hy_prev = xlo_ref[3] - TIME_STEP * (_z_up(ex_p) - (e_ref[2, 0] - ez_p))
-    hz_prev = xlo_ref[4] - TIME_STEP * ((e_ref[1, 0] - ey_p) - _y_up(ex_p, c1_ref[...]))
+    hy = xlo_ref[3] - TIME_STEP * (_z_up(ex_p) - (elec(2, 0) - ez_p))
+    hz = xlo_ref[4] - TIME_STEP * ((elec(1, 0) - ey_p) - _y_up(ex_p, c1_ref[...]))
+    return (hy, hz)
+
+
+def _elec_plane(x, planes, old, hy_prev, hz_prev, ylo_ref, c2_ref, keep, drive):
+    ex, ey, ez, hx, hy, hz = old
+    if x + 1 < planes:
+        ey_m_next = ylo_ref[1, x + 1]
+    else:
+        ey_m_next = c2_ref[...]
+    ex_m = ylo_ref[0, x]
+    ey_m = ylo_ref[1, x]
+    ez_m = ylo_ref[2, x]
+    hx_r = ylo_ref[3, x] - TIME_STEP * ((ez[0:1] - ez_m) - _z_up(ey_m))
+    hz_r = ylo_ref[4, x] - TIME_STEP * ((ey_m_next - ey_m) - (ex[0:1] - ex_m))
+    ex_new = keep * ex + drive * (_y_down(hz, hz_r) - _z_down(hy))
+    ey_new = keep * ey + drive * (_z_down(hx) - (hz - hz_prev))
+    ez_new = keep * ez + drive * ((hy - hy_prev) - _y_down(hx, hx_r))
+    return (ex_new, ey_new, ez_new)
+
+
+def _step_kernel(e_ref, h_ref, keep_ref, drive_ref, xlo_ref, xhi_ref, y_ref, e_out, h_out, y_out):
+    c1_ref = y_ref.at[7, 0]
+    c2_ref = y_ref.at[8, 0]
+    yhi_ref = y_ref.at[5:7]
+    planes = e_ref.shape[1]
+    cells = e_ref.shape[2]
+    elec = lambda comp, x: e_ref[comp, x]
+    magn = lambda comp, x: h_ref[comp, x]
+    hy_prev, hz_prev = _magn_before(elec, xlo_ref, c1_ref)
     for x in range(planes):
-        ex = e_ref[0, x]
-        ey = e_ref[1, x]
-        ez = e_ref[2, x]
-        if x + 1 < planes:
-            ey_next = e_ref[1, x + 1]
-            ez_next = e_ref[2, x + 1]
-            ey_m_next = ylo_ref[1, x + 1]
-        else:
-            ey_next = xhi_ref[0]
-            ez_next = xhi_ref[1]
-            ey_m_next = c2_ref[...]
-        hx = h_ref[0, x] - TIME_STEP * (_y_up(ez, yhi_ref[1, x]) - _z_up(ey))
-        hy = h_ref[1, x] - TIME_STEP * (_z_up(ex) - (ez_next - ez))
-        hz = h_ref[2, x] - TIME_STEP * ((ey_next - ey) - _y_up(ex, yhi_ref[0, x]))
-        ex_m = ylo_ref[0, x]
-        ey_m = ylo_ref[1, x]
-        ez_m = ylo_ref[2, x]
-        hx_r = ylo_ref[3, x] - TIME_STEP * ((ez[0:1] - ez_m) - _z_up(ey_m))
-        hz_r = ylo_ref[4, x] - TIME_STEP * ((ey_m_next - ey_m) - (ex[0:1] - ex_m))
-        keep = keep_ref[x]
-        drive = drive_ref[x]
-        ex_new = keep * ex + drive * (_y_down(hz, hz_r) - _z_down(hy))
-        ey_new = keep * ey + drive * (_z_down(hx) - (hz - hz_prev))
-        ez_new = keep * ez + drive * ((hy - hy_prev) - _y_down(hx, hx_r))
+        old = _magn_plane(elec, magn, x, planes, xhi_ref, yhi_ref)
+        ex_new, ey_new, ez_new = _elec_plane(
+            x, planes, old, hy_prev, hz_prev, y_ref, c2_ref, keep_ref[x], drive_ref[x]
+        )
+        hx, hy, hz = old[3:]
         e_out[0, x] = ex_new
         e_out[1, x] = ey_new
         e_out[2, x] = ez_new
@@ -120,24 +138,44 @@
         h_out[1, x] = hy
         h_out[2, x] = hz
         last = slice(cells - 1, cells)
-        ylo_out[0, x] = ex_new[last]
-        ylo_out[1, x] = ey_new[last]
-        ylo_out[2, x] = ez_new[last]
-        ylo_out[3, x] = hx[last]
-        ylo_out[4, x] = hz[last]
-        yhi_out[0, x] = ex_new[0:1]
-        yhi_out[1, x] = ez_new[0:1]
-        if x == 0:
-            xhi_out[0] = ey_new
-            xhi_out[1] = ez_new
-        if x == planes - 1:
-            xlo_out[0] = ex_new
-            xlo_out[1] = ey_new
-            xlo_out[2] = ez_new
-            xlo_out[3] = hy
-            xlo_out[4] = hz
+        y_out[0, x] = ex_new[last]
+        y_out[1, x] = ey_new[last]
+        y_out[2, x] = ez_new[last]
+        y_out[3, x] = hx[last]
+        y_out[4, x] = hz[last]
+        y_out[5, x] = ex_new[0:1]
+        y_out[6, x] = ez_new[0:1]
         hy_prev = hy
         hz_prev = hz
+
+
+def _edge_kernel(e_first, e_second, e_penult, e_last, h_first, h_penult, h_last,
+                 keep_first, keep_last, drive_first, drive_last, xlo_ref, xhi_ref, y_ref,
+                 xlo_out, xhi_out, *, planes):
+    c1_ref = y_ref.at[7, 0]
+    c2_ref = y_ref.at[8, 0]
+    yhi_ref = y_ref.at[5:7]
+    e_blocks = {0: e_first, 1: e_second, planes - 2: e_penult, planes - 1: e_last}
+    h_blocks = {0: h_first, planes - 2: h_penult, planes - 1: h_last}
+    elec = lambda comp, x: e_blocks[x][comp, 0]
+    magn = lambda comp, x: h_blocks[x][comp, 0]
+    hy_prev, hz_prev = _magn_before(elec, xlo_ref, c1_ref)
+    old = _magn_plane(elec, magn, 0, planes, xhi_ref, yhi_ref)
+    ex_new, ey_new, ez_new = _elec_plane(
+        0, planes, old, hy_prev, hz_prev, y_ref, c2_ref, keep_first[0], drive_first[0]
+    )
+    xhi_out[0] = ey_new
+    xhi_out[1] = ez_new
+    penult = _magn_plane(elec, magn, planes - 2, planes, xhi_ref, yhi_ref)
+    old = _magn_plane(elec, magn, planes - 1, planes, xhi_ref, yhi_ref)
+    ex_new, ey_new, ez_new = _elec_plane(
+        planes - 1, planes, old, penult[4], penult[5], y_ref, c2_ref, keep_last[0], drive_last[0]
+    )
+    xlo_out[0] = ex_new
+    xlo_out[1] = ey_new
+    xlo_out[2] = ez_new
+    xlo_out[3] = old[4]
+    xlo_out[4] = old[5]
 
 
 def _halo_kernel(e_ref, h_ref, xlo_out, xhi_out, y_out):
@@ -163,21 +201,20 @@
     xlo_out[4] = h_ref[2, planes - 1]
 
 
-def exchange(halo):
-    xlo, xhi, rows = halo
-    xlo = shifted(xlo, "gx", 1)
-    xhi = shifted(xhi, "gx", -1)
+def exchange_x(xlo, xhi):
+    return (shifted(xlo, "gx", 1), shifted(xhi, "gx", -1))
+
+
+def exchange_y(rows, xlo, xhi):
     cells = xhi.shape[1]
     corners = jnp.zeros((2,) + rows.shape[1:], rows.dtype)
     corners = corners.at[0, 0].set(xlo[0, 0:1]).at[1, 0].set(xhi[0, cells - 1:cells])
     message = jnp.concatenate([rows, corners])
     if lax.axis_size("gy") == 2:
-        rows = shifted(message, "gy", 1)
-    else:
-        before = shifted(message, "gy", 1)
-        after = shifted(message, "gy", -1)
-        rows = jnp.concatenate([before[0:5], after[5:8], before[8:9]])
-    return (xlo, xhi, rows)
+        return shifted(message, "gy", 1)
+    before = shifted(message, "gy", 1)
+    after = shifted(message, "gy", -1)
+    return jnp.concatenate([before[0:5], after[5:8], before[8:9]])
 
 
 def trig_basis(angle_orders, cells_x, cells_y):
@@ -238,17 +275,38 @@
     comps, cells_x, cells_y, depth = e_field.shape
     f32 = jnp.float32
     field_shape = jax.ShapeDtypeStruct(e_field.shape, f32)
-    halo_shapes = (
-        jax.ShapeDtypeStruct((5, cells_y, depth), f32),
-        jax.ShapeDtypeStruct((2, cells_y, depth), f32),
-        jax.ShapeDtypeStruct((7, cells_x, 1, depth), f32),
-    )
-    step_call = pl.pallas_call(_step_kernel, out_shape=(field_shape, field_shape) + halo_shapes)
-    halo = pl.pallas_call(_halo_kernel, out_shape=halo_shapes)(e_field, h_field)
-    received = exchange(halo)
+    xlo_shape = jax.ShapeDtypeStruct((5, cells_y, depth), f32)
+    xhi_shape = jax.ShapeDtypeStruct((2, cells_y, depth), f32)
+    rows_shape = jax.ShapeDtypeStruct((7, cells_x, 1, depth), f32)
+    step_call = pl.pallas_call(_step_kernel, out_shape=(field_shape, field_shape, rows_shape))
+    whole = pl.BlockSpec(memory_space=pltpu.VMEM)
+
+    def field_plane(index):
+        return pl.BlockSpec((comps, 1, cells_y, depth), lambda i: (0, index, 0, 0))
+
+    def coef_plane(index):
+        return pl.BlockSpec((1, cells_y, depth), lambda i: (index, 0, 0))
+
+    first = 0
+    last = cells_x - 1
+    edge_call = pl.pallas_call(
+        functools.partial(_edge_kernel, planes=cells_x),
+        out_shape=(xlo_shape, xhi_shape),
+        grid=(1,),
+        in_specs=[field_plane(i) for i in (first, 1, last - 1, last)]
+        + [field_plane(i) for i in (first, last - 1, last)]
+        + [coef_plane(first), coef_plane(last), coef_plane(first), coef_plane(last)]
+        + [whole] * 3,
+        out_specs=(whole, whole),
+    )
+    xlo, xhi, rows = pl.pallas_call(_halo_kernel, out_shape=(xlo_shape, xhi_shape, rows_shape))(
+        e_field, h_field
+    )
+    xlo, xhi = exchange_x(xlo, xhi)
+    rows = exchange_y(rows, xlo, xhi)
     keep, drive = coefficients(material, eps_table, sigma_table)
     basis = trig_basis(angle_orders, cells_x, cells_y)
-    keep, drive, basis, received = lax.optimization_barrier((keep, drive, basis, received))
+    keep, drive, basis, xlo, xhi, rows = lax.optimization_barrier((keep, drive, basis, xlo, xhi, rows))
     angle_count = angle_orders.shape[0]
     elec = e_field
     magn = h_field
@@ -256,12 +314,18 @@
     mon_imag = jnp.zeros((2, cells_x, cells_y), f32)
     early = jnp.zeros((2 * angle_count, 4), f32)
     for number in range(ITERS):
-        if number > 0:
-            received = exchange(halo)
         if number == ITERS - 1 and number > 0:
             early = transform(basis, jnp.concatenate([flat(mon_real), flat(mon_imag)], axis=1))
-            early, received = lax.optimization_barrier((early, received))
-        elec, magn, *halo = step_call(elec, magn, keep, drive, *received)
+            early, xlo, xhi, rows = lax.optimization_barrier((early, xlo, xhi, rows))
+        if number + 1 < ITERS:
+            edges = edge_call(
+                elec, elec, elec, elec, magn, magn, magn, keep, keep, drive, drive, xlo, xhi, rows
+            )
+            next_xlo, next_xhi = exchange_x(*edges)
+        elec, magn, new_rows = step_call(elec, magn, keep, drive, xlo, xhi, rows)
+        if number + 1 < ITERS:
+            xlo, xhi = next_xlo, next_xhi
+            rows = exchange_y(new_rows, xlo, xhi)
         if number < ITERS - 1:
             plane = elec[0:2, :, :, depth - 3]
             mon_real = mon_real + math.cos(PHASE_STEP * (number + 1)) * plane

time: 82.1 us -> 82.4 us (level)
  waiting for transfers between devices: 30.2 us -> 23.3 us
  Pallas kernels: 18 us -> 24.1 us
  starting transfers between devices: 20.6 us -> 21.7 us
    pallas_call x5 -> x8, Pallas kernels: 16 us -> 22.1 us  [the longest x4 13.6 us: local(): elec, magn, new_rows = step_call(elec, magn, keep, drive, xlo, xhi, rows)]
    ppermute x12, waiting for transfers between devices: 17.6 us -> 11.7 us  [shifted(): return lax.ppermute(value, axis, pairs)]
    ppermute x3, waiting for transfers between devices: 11.5 us -> 10.4 us  [scatter_sum(): rows = keep + lax.ppermute(send, axis, pairs)]
    ppermute x3, starting transfers between devices: 0.15 us -> 1.26 us  [scatter_sum(): rows = keep + lax.ppermute(send, axis, pairs)]
    unnamed x34 -> x38, local copies, waits for them, and re-layouts: 3.86 us -> 3.82 us
  transfers between devices with their start and end apart: 16 -> 16, of which waited for: 12 -> 13; matrix products, arithmetic and copies ran while one was open for 4% -> 4% of each run, Pallas kernels for 2% -> 15%
where the time goes in v8:
time: 82.4 us; the launch traced here: 81.8 us
  Pallas kernels  24.1 us (29%)
  waiting for transfers between devices  23.3 us (28%)
  starting transfers between devices  21.7 us (26%)
  local copies, waits for them, and re-layouts  5.77 us (7%)
  other arithmetic  5.53 us (7%)
  between operations  0.84 us (1%)
    ppermute x12, starting transfers between devices, shifted(): return lax.ppermute(value, axis, pairs)  20.5 us
    pallas_call x4, Pallas kernels, local(): elec, magn, new_rows = step_call(elec, magn, keep, drive, xlo, xhi, rows)  13.6 us
    ppermute x12, waiting for transfers between devices, shifted(): return lax.ppermute(value, axis, pairs)  11.7 us
    ppermute x3, waiting for transfers between devices, scatter_sum(): rows = keep + lax.ppermute(send, axis, pairs)  10.4 us
    pallas_call x3, Pallas kernels, local(): edge_call(elec, elec, elec, elec, magn, magn, magn, keep, keep, drive, dr...  6.38 us
    unnamed x38, local copies, waits for them, and re-layouts  3.82 us
    pallas_call x1, Pallas kernels, local(): pl.pallas_call(_halo_kernel, out_shape=(xlo_shape, xhi_shape, rows_shape))  2.08 us
    pallas_call x1, Pallas kernels, coefficients(): pl.pallas_call(_coef_kernel, out_shape=(out, out), in_specs=[scalar, scal...  2.01 us
  transfers between devices with their start and end apart: 16, of which 13 were waited for; matrix products, arithmetic and copies ran while one was open for 4% of the time, Pallas kernels for 15%

profile of v8, /device:TPU:0, one launch (start us, length us, event | category | flops | bytes accessed | tf_op | source)
XLA Modules:
  0.0 81.8 jit_solution(6825722472408362911)
XLA Ops:
  0.6 2.1 %shard_map.86 = (f32[5,64,128]{2,1,0:T(8,128)}, f32[2,64,128]{2,1,0:T(8,128)}, f32[7,8,1,128]{3,2,1,0:T(1,128)}) custom-call(f32[3,8,64,128]{3,2,1,0:T(8,128)} %e_last.1, f32[3,8,64,128]{3,2,1,0:T(8,128)} %h_last.1), custom_call_target="tpu_custom_call" | custom-call | tf_op jit(solution)/shard_map/pallas_call | solution.py:302
  2.7 3.0 %collective-permute-start = (f32[5,64,128]{2,1,0:T(8,128)}, f32[5,64,128]{2,1,0:T(8,128)S(1)}, u32[]{:S(2)}, u32[]{:S(2)}) collective-permute-start(f32[5,64,128]{2,1,0:T(8,128)} %get-tuple-element.133), channel_id=1, source_target_pairs={{0,2},{2,4},{4,6},{6,8},{8,10},{10,12},{12,14},{14,0},{1,3},{3,5},... | collective-permute-start | bytes 491528 | tf_op jit(solution)/shard_map/ppermute | solution.py:21
  5.7 3.0 %collective-permute-start.1 = (f32[2,64,128]{2,1,0:T(8,128)}, f32[2,64,128]{2,1,0:T(8,128)S(1)}, u32[]{:S(2)}, u32[]{:S(2)}) collective-permute-start(f32[2,64,128]{2,1,0:T(8,128)} %get-tuple-element.134), channel_id=1, source_target_pairs={{0,14},{2,0},{4,2},{6,4},{8,6},{10,8},{12,10},{14,12},{1,15},{3,1}... | collective-permute-start | bytes 196616 | tf_op jit(solution)/shard_map/ppermute | solution.py:21
  8.7 0.7 copy-done.16
  9.4 0.1 multiply_multiply_fusion.1
  9.5 0.1 copy.9
  9.6 0.1 multiply_multiply_fusion
  9.6 0.1 broadcast_add_fusion
  9.8 0.1 add.123
  9.9 0.5 fusion.4
  10.4 2.8 %collective-permute-done.xlo_ref = f32[5,64,128]{2,1,0:T(8,128)S(1)} collective-permute-done((f32[5,64,128]{2,1,0:T(8,128)}, f32[5,64,128]{2,1,0:T(8,128)S(1)}, u32[]{:S(2)}, u32[]{:S(2)}) %collective-permute-start) | collective-permute-done | bytes 163872 | tf_op jit(solution)/shard_map/ppermute | solution.py:21
  13.2 0.4 collective-permute-done.1.xhi_ref
  13.7 0.1 collective-permute-start.2
  13.8 0.1 copy-done.2
  13.9 0.4 copy-done.5
  14.3 2.0 %shard_map.85 = (f32[8,64,128]{2,1,0:T(8,128)}, f32[8,64,128]{2,1,0:T(8,128)}) custom-call(f32[6]{0:T(128)} %eps_ref.1, f32[6]{0:T(128)} %sigma_ref.1, s32[8,64,128]{2,1,0:T(8,128)} %mat_ref.1), custom_call_target="tpu_custom_call" | custom-call | tf_op jit(solution)/shard_map/pallas_call | solution.py:43
  16.3 0.6 copy-done.9
  16.9 2.1 %shard_map.88 = (f32[5,64,128]{2,1,0:T(8,128)}, f32[2,64,128]{2,1,0:T(8,128)}) custom-call(f32[3,8,64,128]{3,2,1,0:T(8,128)} %e_last.1, f32[3,8,64,128]{3,2,1,0:T(8,128)} %e_last.1, f32[3,8,64,128]{3,2,1,0:T(8,128)} %e_last.1, f32[3,8,64,128]{3,2,1,0:T(8,128)} %e_last.1, f32[3,8,64,128]{3,2,1,0:T(8,128)} %h_last.1, f32[3,8,64,128]{3,2,1,0:T(8,128)} %h_last.1, ...), custom_call_target="tpu_custom_call" | custom-call | tf_op jit(solution)/shard_map/pallas_call | solution.py:321
  19.1 3.4 %shard_map.87 = (f32[3,8,64,128]{3,2,1,0:T(8,128)}, f32[3,8,64,128]{3,2,1,0:T(8,128)}, f32[7,8,1,128]{3,2,1,0:T(1,128)}) custom-call(f32[3,8,64,128]{3,2,1,0:T(8,128)} %e_last.1, f32[3,8,64,128]{3,2,1,0:T(8,128)} %h_last.1, f32[8,64,128]{2,1,0:T(8,128)} %get-tuple-element.136.keep_ref.keep_first.keep_last, ...), custom_call_target="tpu_custom_call" | custom-call | tf_op jit(solution)/shard_map/pallas_call | solution.py:325
  22.5 4.7 %collective-permute-start.4 = (f32[2,64,128]{2,1,0:T(8,128)S(1)}, f32[2,64,128]{2,1,0:T(8,128)S(1)}, u32[]{:S(2)}, u32[]{:S(2)}) collective-permute-start(f32[2,64,128]{2,1,0:T(8,128)S(1)} %copy-done.18), channel_id=1, source_target_pairs={{0,14},{2,0},{4,2},{6,4},{8,6},{10,8},{12,10},{14,12},{1,15},{3,1}... | collective-permute-start | bytes 196616 | tf_op jit(solution)/shard_map/ppermute | solution.py:21
  27.2 1.1 %collective-permute-done.3.xlo_ref = f32[5,64,128]{2,1,0:T(8,128)S(1)} collective-permute-done((f32[5,64,128]{2,1,0:T(8,128)}, f32[5,64,128]{2,1,0:T(8,128)S(1)}, u32[]{:S(2)}, u32[]{:S(2)}) %collective-permute-start.3) | collective-permute-done | bytes 163872 | tf_op jit(solution)/shard_map/ppermute | solution.py:21
  28.3 1.3 %collective-permute-done.4.xhi_ref = f32[2,64,128]{2,1,0:T(8,128)S(1)} collective-permute-done((f32[2,64,128]{2,1,0:T(8,128)S(1)}, f32[2,64,128]{2,1,0:T(8,128)S(1)}, u32[]{:S(2)}, u32[]{:S(2)}) %collective-permute-start.4) | collective-permute-done | bytes 65568 | tf_op jit(solution)/shard_map/ppermute | solution.py:21
  29.6 0.8 pad_maximum_fusion.2
  30.4 0.1 collective-permute-start.5
  30.5 1.2 %collective-permute-done.5.y_ref = f32[9,8,1,128]{3,2,1,0:T(1,128)S(1)} collective-permute-done((f32[9,8,1,128]{3,2,1,0:T(1,128)S(1)}, f32[9,8,1,128]{3,2,1,0:T(1,128)S(1)}, u32[]{:S(2)}, u32[]{:S(2)}) %collective-permute-start.5) | collective-permute-done | bytes 36896 | tf_op jit(solution)/shard_map/ppermute | solution.py:21
  31.7 0.6 copy-done.10
  32.3 2.1 %shard_map.90 = (f32[5,64,128]{2,1,0:T(8,128)}, f32[2,64,128]{2,1,0:T(8,128)}) custom-call(f32[3,8,64,128]{3,2,1,0:T(8,128)} %get-tuple-element.141.e_ref.e_first.e_second.e_penult.e_last, f32[3,8,64,128]{3,2,1,0:T(8,128)} %get-tuple-element.141.e_ref.e_first.e_second.e_penult.e_last, ...), custom_call_target="tpu_custom_call" | custom-call | tf_op jit(solution)/shard_map/pallas_call | solution.py:321
  34.5 4.7 %collective-permute-start.7 = (f32[2,64,128]{2,1,0:T(8,128)}, f32[2,64,128]{2,1,0:T(8,128)S(1)}, u32[]{:S(2)}, u32[]{:S(2)}) collective-permute-start(f32[2,64,128]{2,1,0:T(8,128)} %get-tuple-element.149), channel_id=1, source_target_pairs={{0,14},{2,0},{4,2},{6,4},{8,6},{10,8},{12,10},{14,12},{1,15},{3,1}... | collective-permute-start | bytes 196616 | tf_op jit(solution)/shard_map/ppermute | solution.py:21
  39.1 3.4 %shard_map.89 = (f32[3,8,64,128]{3,2,1,0:T(8,128)}, f32[3,8,64,128]{3,2,1,0:T(8,128)}, f32[7,8,1,128]{3,2,1,0:T(1,128)}) custom-call(f32[3,8,64,128]{3,2,1,0:T(8,128)} %get-tuple-element.141.e_ref.e_first.e_second.e_penult.e_last, f32[3,8,64,128]{3,2,1,0:T(8,128)} %get-tuple-element.142.h_ref.h_first.h_penult.h_last, ...), custom_call_target="tpu_custom_call" | custom-call | tf_op jit(solution)/shard_map/pallas_call | solution.py:325
  42.5 1.2 %collective-permute-done.6.xlo_ref = f32[5,64,128]{2,1,0:T(8,128)S(1)} collective-permute-done((f32[5,64,128]{2,1,0:T(8,128)}, f32[5,64,128]{2,1,0:T(8,128)S(1)}, u32[]{:S(2)}, u32[]{:S(2)}) %collective-permute-start.6) | collective-permute-done | bytes 163872 | tf_op jit(solution)/shard_map/ppermute | solution.py:21
  43.8 0.8 %pad_maximum_fusion.3 = f32[9,8,1,128]{3,2,1,0:T(1,128)S(1)} fusion(f32[2,8,1,128]{3,2,1,0:T(1,128)S(1)} %constant_dynamic-update-slice_fusion.1, f32[7,8,1,128]{3,2,1,0:T(1,128)} %get-tuple-element.150), kind=kLoop, calls=%fused_computation.13 | loop fusion | flops 9216 | bytes 73728 | tf_op jit(solution)/shard_map/concatenate | solution.py:212
  44.6 0.1 collective-permute-start.8
  44.7 1.2 %collective-permute-done.8.y_ref = f32[9,8,1,128]{3,2,1,0:T(1,128)S(1)} collective-permute-done((f32[9,8,1,128]{3,2,1,0:T(1,128)S(1)}, f32[9,8,1,128]{3,2,1,0:T(1,128)S(1)}, u32[]{:S(2)}, u32[]{:S(2)}) %collective-permute-start.8) | collective-permute-done | bytes 36896 | tf_op jit(solution)/shard_map/ppermute | solution.py:21
  45.9 0.6 copy-done.11
  46.5 2.1 %shard_map.92 = (f32[5,64,128]{2,1,0:T(8,128)}, f32[2,64,128]{2,1,0:T(8,128)}) custom-call(f32[3,8,64,128]{3,2,1,0:T(8,128)} %get-tuple-element.146.e_ref.e_first.e_second.e_penult.e_last, f32[3,8,64,128]{3,2,1,0:T(8,128)} %get-tuple-element.146.e_ref.e_first.e_second.e_penult.e_last, ...), custom_call_target="tpu_custom_call" | custom-call | tf_op jit(solution)/shard_map/pallas_call | solution.py:321
  48.6 0.1 collective-permute-start.9
  48.7 3.5 %shard_map.91 = (f32[3,8,64,128]{3,2,1,0:T(8,128)}, f32[3,8,64,128]{3,2,1,0:T(8,128)}, f32[7,8,1,128]{3,2,1,0:T(1,128)}) custom-call(f32[3,8,64,128]{3,2,1,0:T(8,128)} %get-tuple-element.146.e_ref.e_first.e_second.e_penult.e_last, f32[3,8,64,128]{3,2,1,0:T(8,128)} %get-tuple-element.147.h_ref.h_first.h_penult.h_last, ...), custom_call_target="tpu_custom_call" | custom-call | tf_op jit(solution)/shard_map/pallas_call | solution.py:325
  52.2 1.8 %add_reduce_fusion = (f32[2,8,64]{2,1,0:T(8,128)S(1)}, f32[2,8,64]{2,1,0:T(8,128)S(1)}) fusion(f32[3,8,64,128]{3,2,1,0:T(8,128)} %get-tuple-element.151.e_ref, f32[3,8,64,128]{3,2,1,0:T(8,128)S(1)} %copy-done.1, f32[3,8,64,128]{3,2,1,0:T(8,128)S(1)} %copy-done), kind=kLoop, calls=%fused_computation.2 | loop fusion | flops 11264 | bytes 20480 | tf_op jit(solution)/shard_map/add | solution.py:331
  54.0 0.1 sub.44
  54.1 0.1 add.127
  54.2 4.6 %collective-permute-start.10 = (f32[2,64,128]{2,1,0:T(8,128)S(1)}, f32[2,64,128]{2,1,0:T(8,128)S(1)}, u32[]{:S(2)}, u32[]{:S(2)}) collective-permute-start(f32[2,64,128]{2,1,0:T(8,128)S(1)} %copy-done.17), channel_id=1, source_target_pairs={{0,14},{2,0},{4,2},{6,4},{8,6},{10,8},{12,10},{14,12},{1,15},{3,1}... | collective-permute-start | bytes 196616 | tf_op jit(solution)/shard_map/ppermute | solution.py:21
  58.8 1.9 %collective-permute-done.10.xhi_ref = f32[2,64,128]{2,1,0:T(8,128)S(1)} collective-permute-done((f32[2,64,128]{2,1,0:T(8,128)S(1)}, f32[2,64,128]{2,1,0:T(8,128)S(1)}, u32[]{:S(2)}, u32[]{:S(2)}) %collective-permute-start.10) | collective-permute-done | bytes 65568 | tf_op jit(solution)/shard_map/ppermute | solution.py:21
  60.8 0.1 collective-permute-start.11
  60.8 0.3 fusion.5
  61.1 0.2 copy-done.12
  61.3 0.7 collective-permute-done.11.y_ref
  62.0 0.6 copy-done.13
  62.6 3.4 %shard_map.93 = (f32[3,8,64,128]{3,2,1,0:T(8,128)}, f32[3,8,64,128]{3,2,1,0:T(8,128)}, f32[7,8,1,128]{3,2,1,0:T(1,128)}) custom-call(f32[3,8,64,128]{3,2,1,0:T(8,128)} %get-tuple-element.151.e_ref, f32[3,8,64,128]{3,2,1,0:T(8,128)} %get-tuple-element.152.h_ref, f32[8,64,128]{2,1,0:T(8,128)} %get-tuple-element.136.keep_ref.keep_first.keep_last, ...), custom_call_target="tpu_custom_call" | custom-call | tf_op jit(solution)/shard_map/pallas_call | solution.py:325
  66.0 1.4 %slice_reduce_fusion = f32[2,8,64]{2,1,0:T(8,128)S(1)} fusion(f32[3,8,64,128]{3,2,1,0:T(8,128)} %get-tuple-element.128), kind=kLoop, calls=%fused_computation | loop fusion | bytes 8192 | tf_op jit(solution)/shard_map/slice | solution.py:333
  67.4 0.1 reshape_squeeze.3
  67.5 0.3 fusion.10
  67.8 0.1 subtract_add_fusion.1
  67.9 0.1 slice_select_fusion.2
  68.0 4.5 %collective-permute-done.12 = f32[32,4]{0,1:T(4,128)S(1)} collective-permute-done((f32[32,4]{0,1:T(4,128)S(1)}, f32[32,4]{0,1:T(4,128)S(1)}, u32[]{:S(2)}, u32[]{:S(2)}) %collective-permute-start.12) | collective-permute-done | bytes 544 | tf_op jit(solution)/shard_map/ppermute | solution.py:260
  72.5 0.1 select_add_fusion.2
  72.6 0.1 slice_select_fusion.1
  72.7 3.6 %collective-permute-done.13 = f32[16,4]{0,1:T(4,128)S(1)} collective-permute-done((f32[16,4]{0,1:T(4,128)S(1)}, f32[16,4]{0,1:T(4,128)S(1)}, u32[]{:S(2)}, u32[]{:S(2)}) %collective-permute-start.13) | collective-permute-done | bytes 288 | tf_op jit(solution)/shard_map/ppermute | solution.py:260
  76.2 0.1 select_add_fusion.1
  76.3 0.1 slice_select_fusion
  76.4 1.2 %collective-permute-start.14 = (f32[8,4]{0,1:T(4,128)S(1)}, f32[8,4]{0,1:T(4,128)S(1)}, u32[]{:S(2)}, u32[]{:S(2)}) collective-permute-start(f32[8,4]{0,1:T(4,128)S(1)} %slice_select_fusion), channel_id=1, source_target_pairs={{0,2},{2,0},{4,6},{6,4},{8,10},{10,8},{12,14},{14,12},{1,3},{3,1},... | collective-permute-start | bytes 392 | tf_op jit(solution)/shard_map/ppermute | solution.py:260
  77.6 2.3 %collective-permute-done.14 = f32[8,4]{0,1:T(4,128)S(1)} collective-permute-done((f32[8,4]{0,1:T(4,128)S(1)}, f32[8,4]{0,1:T(4,128)S(1)}, u32[]{:S(2)}, u32[]{:S(2)}) %collective-permute-start.14) | collective-permute-done | bytes 160 | tf_op jit(solution)/shard_map/ppermute | solution.py:260
  80.0 0.1 select_add_fusion
  80.1 1.2 %collective-permute-done.15 = f32[8,4]{0,1:T(4,128)S(1)} collective-permute-done((f32[8,4]{0,1:T(4,128)S(1)}, f32[8,4]{0,1:T(4,128)S(1)}, u32[]{:S(2)}, u32[]{:S(2)}) %collective-permute-start.15) | collective-permute-done | bytes 160 | tf_op jit(solution)/shard_map/ppermute | solution.py:270
  81.2 0.6 add_multiply_fusion
  (57 shorter events, 0.4 us)
Async XLA Ops:
  2.7 10.5 %collective-permute-start = (f32[5,64,128]{2,1,0:T(8,128)}, f32[5,64,128]{2,1,0:T(8,128)S(1)}, u32[]{:S(2)}, u32[]{:S(2)}) collective-permute-start(f32[5,64,128]{2,1,0:T(8,128)} %get-tuple-element.133), channel_id=1, source_target_pairs={{0,2},{2,4},{4,6},{6,8},{8,10},{10,12},{12,14},{14,0},{1,3},{3,5},... | collective-permute-start | bytes 491528 | tf_op jit(solution)/shard_map/ppermute | solution.py:21
  5.7 8.0 %collective-permute-start.1 = (f32[2,64,128]{2,1,0:T(8,128)}, f32[2,64,128]{2,1,0:T(8,128)S(1)}, u32[]{:S(2)}, u32[]{:S(2)}) collective-permute-start(f32[2,64,128]{2,1,0:T(8,128)} %get-tuple-element.134), channel_id=1, source_target_pairs={{0,14},{2,0},{4,2},{6,4},{8,6},{10,8},{12,10},{14,12},{1,15},{3,1}... | collective-permute-start | bytes 196616 | tf_op jit(solution)/shard_map/ppermute | solution.py:21
  8.7 0.7 copy-start.16
  9.9 3.8 %copy-start.14 = (f32[7,8,1,128]{3,2,1,0:T(1,128)S(1)}, f32[7,8,1,128]{3,2,1,0:T(1,128)}, u32[]{:S(2)}) copy-start(f32[7,8,1,128]{3,2,1,0:T(1,128)} %get-tuple-element.135) | copy-start | bytes 86020
  13.2 0.7 copy-start.2
  13.7 0.6 copy-start.5
  13.7 2.6 %collective-permute-start.2 = (f32[9,8,1,128]{3,2,1,0:T(1,128)S(1)}, f32[9,8,1,128]{3,2,1,0:T(1,128)S(1)}, u32[]{:S(2)}, u32[]{:S(2)}) collective-permute-start(f32[9,8,1,128]{3,2,1,0:T(1,128)S(1)} %pad_maximum_fusion.1), channel_id=1, source_target_pairs={{0,1},{1,0},{2,3},{3,2},{4,5},{5,4},{6,7},{7,6},{8,9},{9,8},{10,11... | collective-permute-start | bytes 110600 | tf_op jit(solution)/shard_map/ppermute | solution.py:21
  16.3 0.6 copy-start.9
  19.0 3.4 %copy-start.18 = (f32[2,64,128]{2,1,0:T(8,128)S(1)}, f32[2,64,128]{2,1,0:T(8,128)}, u32[]{:S(2)}) copy-start(f32[2,64,128]{2,1,0:T(8,128)} %get-tuple-element.144) | copy-start | bytes 196612
  19.0 9.2 %collective-permute-start.3 = (f32[5,64,128]{2,1,0:T(8,128)}, f32[5,64,128]{2,1,0:T(8,128)S(1)}, u32[]{:S(2)}, u32[]{:S(2)}) collective-permute-start(f32[5,64,128]{2,1,0:T(8,128)} %get-tuple-element.143), channel_id=1, source_target_pairs={{0,2},{2,4},{4,6},{6,8},{8,10},{10,12},{12,14},{14,0},{1,3},{3,5},... | collective-permute-start | bytes 491528 | tf_op jit(solution)/shard_map/ppermute | solution.py:21
  22.5 7.1 %collective-permute-start.4 = (f32[2,64,128]{2,1,0:T(8,128)S(1)}, f32[2,64,128]{2,1,0:T(8,128)S(1)}, u32[]{:S(2)}, u32[]{:S(2)}) collective-permute-start(f32[2,64,128]{2,1,0:T(8,128)S(1)} %copy-done.18), channel_id=1, source_target_pairs={{0,14},{2,0},{4,2},{6,4},{8,6},{10,8},{12,10},{14,12},{1,15},{3,1}... | collective-permute-start | bytes 196616 | tf_op jit(solution)/shard_map/ppermute | solution.py:21
  28.3 3.4 %copy-start.3 = (f32[5,64,128]{2,1,0:T(8,128)}, f32[5,64,128]{2,1,0:T(8,128)S(1)}, u32[]{:S(2)}) copy-start(f32[5,64,128]{2,1,0:T(8,128)S(1)} %collective-permute-done.3.xlo_ref) | copy-start | bytes 491524
  29.6 2.1 %copy-start.7 = (f32[2,64,128]{2,1,0:T(8,128)}, f32[2,64,128]{2,1,0:T(8,128)S(1)}, u32[]{:S(2)}) copy-start(f32[2,64,128]{2,1,0:T(8,128)S(1)} %collective-permute-done.4.xhi_ref) | copy-start | bytes 196612
  30.4 1.3 %collective-permute-start.5 = (f32[9,8,1,128]{3,2,1,0:T(1,128)S(1)}, f32[9,8,1,128]{3,2,1,0:T(1,128)S(1)}, u32[]{:S(2)}, u32[]{:S(2)}) collective-permute-start(f32[9,8,1,128]{3,2,1,0:T(1,128)S(1)} %pad_maximum_fusion.2), channel_id=1, source_target_pairs={{0,1},{1,0},{2,3},{3,2},{4,5},{5,4},{6,7},{7,6},{8,9},{9,8},{10,11... | collective-permute-start | bytes 110600 | tf_op jit(solution)/shard_map/ppermute | solution.py:21
  31.7 0.6 copy-start.10
  34.4 9.3 %collective-permute-start.6 = (f32[5,64,128]{2,1,0:T(8,128)}, f32[5,64,128]{2,1,0:T(8,128)S(1)}, u32[]{:S(2)}, u32[]{:S(2)}) collective-permute-start(f32[5,64,128]{2,1,0:T(8,128)} %get-tuple-element.148), channel_id=1, source_target_pairs={{0,2},{2,4},{4,6},{6,8},{8,10},{10,12},{12,14},{14,0},{1,3},{3,5},... | collective-permute-start | bytes 491528 | tf_op jit(solution)/shard_map/ppermute | solution.py:21
  34.5 9.3 %collective-permute-start.7 = (f32[2,64,128]{2,1,0:T(8,128)}, f32[2,64,128]{2,1,0:T(8,128)S(1)}, u32[]{:S(2)}, u32[]{:S(2)}) collective-permute-start(f32[2,64,128]{2,1,0:T(8,128)} %get-tuple-element.149), channel_id=1, source_target_pairs={{0,14},{2,0},{4,2},{6,4},{8,6},{10,8},{12,10},{14,12},{1,15},{3,1}... | collective-permute-start | bytes 196616 | tf_op jit(solution)/shard_map/ppermute | solution.py:21
  43.7 2.2 %copy-start.4 = (f32[5,64,128]{2,1,0:T(8,128)}, f32[5,64,128]{2,1,0:T(8,128)S(1)}, u32[]{:S(2)}) copy-start(f32[5,64,128]{2,1,0:T(8,128)S(1)} %collective-permute-done.6.xlo_ref) | copy-start | bytes 491524
  43.7 2.1 %copy-start.6 = (f32[2,64,128]{2,1,0:T(8,128)}, f32[2,64,128]{2,1,0:T(8,128)S(1)}, u32[]{:S(2)}) copy-start(f32[2,64,128]{2,1,0:T(8,128)S(1)} %collective-permute-done.7.xhi_ref) | copy-start | bytes 196612
  44.6 1.3 %collective-permute-start.8 = (f32[9,8,1,128]{3,2,1,0:T(1,128)S(1)}, f32[9,8,1,128]{3,2,1,0:T(1,128)S(1)}, u32[]{:S(2)}, u32[]{:S(2)}) collective-permute-start(f32[9,8,1,128]{3,2,1,0:T(1,128)S(1)} %pad_maximum_fusion.3), channel_id=1, source_target_pairs={{0,1},{1,0},{2,3},{3,2},{4,5},{5,4},{6,7},{7,6},{8,9},{9,8},{10,11... | collective-permute-start | bytes 110600 | tf_op jit(solution)/shard_map/ppermute | solution.py:21
  45.9 0.6 copy-start.11
  48.6 3.5 %copy-start = (f32[3,8,64,128]{3,2,1,0:T(8,128)S(1)}, f32[3,8,64,128]{3,2,1,0:T(8,128)}, u32[]{:S(2)}) copy-start(f32[3,8,64,128]{3,2,1,0:T(8,128)} %get-tuple-element.141.e_ref.e_first.e_second.e_penult.e_last) | copy-start | bytes 2359300
  48.6 3.5 %copy-start.1 = (f32[3,8,64,128]{3,2,1,0:T(8,128)S(1)}, f32[3,8,64,128]{3,2,1,0:T(8,128)}, u32[]{:S(2)}) copy-start(f32[3,8,64,128]{3,2,1,0:T(8,128)} %get-tuple-element.146.e_ref.e_first.e_second.e_penult.e_last) | copy-start | bytes 2359300
  48.6 10.2 %collective-permute-start.9 = (f32[5,64,128]{2,1,0:T(8,128)}, f32[5,64,128]{2,1,0:T(8,128)S(1)}, u32[]{:S(2)}, u32[]{:S(2)}) collective-permute-start(f32[5,64,128]{2,1,0:T(8,128)} %get-tuple-element.154), channel_id=1, source_target_pairs={{0,2},{2,4},{4,6},{6,8},{8,10},{10,12},{12,14},{14,0},{1,3},{3,5},... | collective-permute-start | bytes 491528 | tf_op jit(solution)/shard_map/ppermute | solution.py:21
  52.2 2.0 %copy-start.17 = (f32[2,64,128]{2,1,0:T(8,128)S(1)}, f32[2,64,128]{2,1,0:T(8,128)}, u32[]{:S(2)}) copy-start(f32[2,64,128]{2,1,0:T(8,128)} %get-tuple-element.155) | copy-start | bytes 196612
  54.0 6.7 %copy-start.15 = (f32[7,8,1,128]{3,2,1,0:T(1,128)S(1)}, f32[7,8,1,128]{3,2,1,0:T(1,128)}, u32[]{:S(2)}) copy-start(f32[7,8,1,128]{3,2,1,0:T(1,128)} %get-tuple-element.156) | copy-start | bytes 86020
  54.2 6.5 %collective-permute-start.10 = (f32[2,64,128]{2,1,0:T(8,128)S(1)}, f32[2,64,128]{2,1,0:T(8,128)S(1)}, u32[]{:S(2)}, u32[]{:S(2)}) collective-permute-start(f32[2,64,128]{2,1,0:T(8,128)S(1)} %copy-done.17), channel_id=1, source_target_pairs={{0,14},{2,0},{4,2},{6,4},{8,6},{10,8},{12,10},{14,12},{1,15},{3,1}... | collective-permute-start | bytes 196616 | tf_op jit(solution)/shard_map/ppermute | solution.py:21
  58.8 2.3 %copy-start.8 = (f32[5,64,128]{2,1,0:T(8,128)}, f32[5,64,128]{2,1,0:T(8,128)S(1)}, u32[]{:S(2)}) copy-start(f32[5,64,128]{2,1,0:T(8,128)S(1)} %collective-permute-done.9.xlo_ref) | copy-start | bytes 491524
  60.7 0.6 copy-start.12
  60.8 1.3 %collective-permute-start.11 = (f32[9,8,1,128]{3,2,1,0:T(1,128)S(1)}, f32[9,8,1,128]{3,2,1,0:T(1,128)S(1)}, u32[]{:S(2)}, u32[]{:S(2)}) collective-permute-start(f32[9,8,1,128]{3,2,1,0:T(1,128)S(1)} %pad_maximum_fusion.4), channel_id=1, source_target_pairs={{0,1},{1,0},{2,3},{3,2},{4,5},{5,4},{6,7},{7,6},{8,9},{9,8},{10,11... | collective-permute-start | bytes 110600 | tf_op jit(solution)/shard_map/ppermute | solution.py:21
  62.0 0.6 copy-start.13
  68.0 4.5 %collective-permute-start.12 = (f32[32,4]{0,1:T(4,128)S(1)}, f32[32,4]{0,1:T(4,128)S(1)}, u32[]{:S(2)}, u32[]{:S(2)}) collective-permute-start(f32[32,4]{0,1:T(4,128)S(1)} %slice_select_fusion.2), channel_id=1, source_target_pairs={{0,8},{2,10},{4,12},{6,14},{8,0},{10,2},{12,4},{14,6},{1,9},{3,11}... | collective-permute-start | bytes 1544 | tf_op jit(solution)/shard_map/ppermute | solution.py:260
  72.7 3.6 %collective-permute-start.13 = (f32[16,4]{0,1:T(4,128)S(1)}, f32[16,4]{0,1:T(4,128)S(1)}, u32[]{:S(2)}, u32[]{:S(2)}) collective-permute-start(f32[16,4]{0,1:T(4,128)S(1)} %slice_select_fusion.1), channel_id=1, source_target_pairs={{0,4},{2,6},{4,0},{6,2},{8,12},{10,14},{12,8},{14,10},{1,5},{3,7},... | collective-permute-start | bytes 776 | tf_op jit(solution)/shard_map/ppermute | solution.py:260
  76.4 3.6 %collective-permute-start.14 = (f32[8,4]{0,1:T(4,128)S(1)}, f32[8,4]{0,1:T(4,128)S(1)}, u32[]{:S(2)}, u32[]{:S(2)}) collective-permute-start(f32[8,4]{0,1:T(4,128)S(1)} %slice_select_fusion), channel_id=1, source_target_pairs={{0,2},{2,0},{4,6},{6,4},{8,10},{10,8},{12,14},{14,12},{1,3},{3,1},... | collective-permute-start | bytes 392 | tf_op jit(solution)/shard_map/ppermute | solution.py:260
  80.1 1.2 %collective-permute-start.15 = (f32[8,4]{0,1:T(4,128)S(1)}, f32[8,4]{0,1:T(4,128)S(1)}, u32[]{:S(2)}, u32[]{:S(2)}) collective-permute-start(f32[8,4]{0,1:T(4,128)S(1)} %select_add_fusion), channel_id=1, source_target_pairs={{0,1},{1,0},{2,3},{3,2},{4,5},{5,4},{6,7},{7,6},{8,9},{9,8},{10,11... | collective-permute-start | bytes 392 | tf_op jit(solution)/shard_map/ppermute | solution.py:270

commit v9 on v8

--- a/solution.py
+++ b/solution.py
@@ -116,7 +116,8 @@
     return (ex_new, ey_new, ez_new)
 
 
-def _step_kernel(e_ref, h_ref, keep_ref, drive_ref, xlo_ref, xhi_ref, y_ref, e_out, h_out, y_out):
+def _step_kernel(e_ref, h_ref, keep_ref, drive_ref, xlo_ref, xhi_ref, y_ref, basis_ref,
+                 e_out, h_out, y_out, g_out):
     c1_ref = y_ref.at[7, 0]
     c2_ref = y_ref.at[8, 0]
     yhi_ref = y_ref.at[5:7]
@@ -125,6 +126,7 @@
     elec = lambda comp, x: e_ref[comp, x]
     magn = lambda comp, x: h_ref[comp, x]
     hy_prev, hz_prev = _magn_before(elec, xlo_ref, c1_ref)
+    sums = [None, None]
     for x in range(planes):
         old = _magn_plane(elec, magn, x, planes, xhi_ref, yhi_ref)
         ex_new, ey_new, ez_new = _elec_plane(
@@ -147,6 +149,12 @@
         y_out[6, x] = ez_new[0:1]
         hy_prev = hy
         hz_prev = hz
+        for comp, field in ((0, ex_new), (1, ey_new)):
+            part = jnp.dot(basis_ref[x], field, precision=lax.Precision.HIGHEST,
+                           preferred_element_type=jnp.float32)
+            sums[comp] = part if sums[comp] is None else sums[comp] + part
+    g_out[0] = sums[0]
+    g_out[1] = sums[1]
 
 
 def _edge_kernel(e_first, e_second, e_penult, e_last, h_first, h_penult, h_last,
@@ -278,7 +286,11 @@
     xlo_shape = jax.ShapeDtypeStruct((5, cells_y, depth), f32)
     xhi_shape = jax.ShapeDtypeStruct((2, cells_y, depth), f32)
     rows_shape = jax.ShapeDtypeStruct((7, cells_x, 1, depth), f32)
-    step_call = pl.pallas_call(_step_kernel, out_shape=(field_shape, field_shape, rows_shape))
+    angle_count = angle_orders.shape[0]
+    sums_shape = jax.ShapeDtypeStruct((2, 2 * angle_count, depth), f32)
+    step_call = pl.pallas_call(
+        _step_kernel, out_shape=(field_shape, field_shape, rows_shape, sums_shape)
+    )
     whole = pl.BlockSpec(memory_space=pltpu.VMEM)
 
     def field_plane(index):
@@ -303,45 +315,41 @@
         e_field, h_field
     )
     xlo, xhi = exchange_x(xlo, xhi)
+    keep, drive = coefficients(material, eps_table, sigma_table)
+    keep, drive, xlo, xhi = lax.optimization_barrier((keep, drive, xlo, xhi))
     rows = exchange_y(rows, xlo, xhi)
-    keep, drive = coefficients(material, eps_table, sigma_table)
     basis = trig_basis(angle_orders, cells_x, cells_y)
-    keep, drive, basis, xlo, xhi, rows = lax.optimization_barrier((keep, drive, basis, xlo, xhi, rows))
-    angle_count = angle_orders.shape[0]
+    basis = basis.reshape(2 * angle_count, cells_x, cells_y).transpose(1, 0, 2)
+    basis, rows = lax.optimization_barrier((basis, rows))
     elec = e_field
     magn = h_field
-    mon_real = jnp.zeros((2, cells_x, cells_y), f32)
-    mon_imag = jnp.zeros((2, cells_x, cells_y), f32)
-    early = jnp.zeros((2 * angle_count, 4), f32)
+    columns = [[], []]
     for number in range(ITERS):
-        if number == ITERS - 1 and number > 0:
-            early = transform(basis, jnp.concatenate([flat(mon_real), flat(mon_imag)], axis=1))
-            early, xlo, xhi, rows = lax.optimization_barrier((early, xlo, xhi, rows))
         if number + 1 < ITERS:
             edges = edge_call(
                 elec, elec, elec, elec, magn, magn, magn, keep, keep, drive, drive, xlo, xhi, rows
             )
             next_xlo, next_xhi = exchange_x(*edges)
-        elec, magn, new_rows = step_call(elec, magn, keep, drive, xlo, xhi, rows)
+        elec, magn, new_rows, sums = step_call(elec, magn, keep, drive, xlo, xhi, rows, basis)
         if number + 1 < ITERS:
             xlo, xhi = next_xlo, next_xhi
             rows = exchange_y(new_rows, xlo, xhi)
-        if number < ITERS - 1:
-            plane = elec[0:2, :, :, depth - 3]
-            mon_real = mon_real + math.cos(PHASE_STEP * (number + 1)) * plane
-            mon_imag = mon_imag - math.sin(PHASE_STEP * (number + 1)) * plane
-    late = transform(basis, flat(elec[0:2, :, :, depth - 3]))
-    cos_last = math.cos(PHASE_STEP * ITERS)
-    sin_last = math.sin(PHASE_STEP * ITERS)
-    cos_rows = slice(0, angle_count)
-    sin_rows = slice(angle_count, 2 * angle_count)
-    columns = []
+        weight_cos = math.cos(PHASE_STEP * (number + 1))
+        weight_sin = math.sin(PHASE_STEP * (number + 1))
+        picked = sums[:, :, depth - 3]
+        for comp in range(2):
+            cos_p = picked[comp, :angle_count]
+            sin_p = picked[comp, angle_count:]
+            columns[comp].append((weight_cos * cos_p - weight_sin * sin_p, -weight_sin * cos_p - weight_cos * sin_p))
+    stacked = []
     for comp in range(2):
-        cos_p = late[cos_rows, comp]
-        sin_p = late[sin_rows, comp]
-        real = early[cos_rows, comp] + early[sin_rows, 2 + comp] + (cos_last * cos_p - sin_last * sin_p)
-        imag = early[cos_rows, 2 + comp] - early[sin_rows, comp] - (sin_last * cos_p + cos_last * sin_p)
-        columns += [real, imag]
+        real = columns[comp][0][0]
+        imag = columns[comp][0][1]
+        for more_real, more_imag in columns[comp][1:]:
+            real = real + more_real
+            imag = imag + more_imag
+        stacked += [real, imag]
+    columns = stacked
     terms = jnp.stack(columns, axis=1)
     owned = angle_count // lax.axis_size("gx")
     scale = 1.0 / math.sqrt(cells_x * lax.axis_size("gx") * cells_y * lax.axis_size("gy"))

time: 82.4 us -> 81.6 us (level)
  starting transfers between devices: 21.7 us -> 19.9 us
  waiting for transfers between devices: 23.3 us -> 21.6 us
  Pallas kernels: 24.1 us -> 25.7 us
  local copies, waits for them, and re-layouts: 5.77 us -> 7.05 us
    ppermute x12, waiting for transfers between devices: 11.7 us -> 8.75 us  [shifted(): return lax.ppermute(value, axis, pairs)]
    add x3 -> x2, other arithmetic: 2.1 us -> 0.16 us  [the longest x1 0.08 us: local(): imag = imag + more_imag]
    pallas_call x4, Pallas kernels: 13.6 us -> 15.2 us  [local(): step_call(elec, magn, keep, drive, xlo, xhi, rows, basis)]
    ppermute x3, waiting for transfers between devices: 10.4 us -> 11.7 us  [scatter_sum(): rows = keep + lax.ppermute(send, axis, pairs)]
    ppermute x3, starting transfers between devices: 1.26 us -> 0.02 us  [scatter_sum(): rows = keep + lax.ppermute(send, axis, pairs)]
    slice x1 -> x4, local copies, waits for them, and re-layouts: 1.43 us -> 2.51 us  [local(): picked = sums[:, :, depth - 3]]
    transpose x0 -> x1, other arithmetic: none -> 0.84 us  [local(): basis = basis.reshape(2 * angle_count, cells_x, cells_y).transpose(1, 0, 2)]
    unnamed x38 -> x34, local copies, waits for them, and re-layouts: 3.82 us -> 4.45 us
  transfers between devices with their start and end apart: 16 -> 16, of which waited for: 13 -> 11; matrix products, arithmetic and copies ran while one was open for 4% -> 4% of each run, Pallas kernels for 15% -> 17%
where the time goes in v9:
time: 81.6 us; the launch traced here: 80.9 us
  Pallas kernels  25.7 us (31%)
  waiting for transfers between devices  21.6 us (26%)
  starting transfers between devices  19.9 us (24%)
  local copies, waits for them, and re-layouts  7.05 us (9%)
  other arithmetic  5.78 us (7%)
  between operations  0.89 us (1%)
    ppermute x12, starting transfers between devices, shifted(): return lax.ppermute(value, axis, pairs)  19.8 us
    pallas_call x4, Pallas kernels, local(): step_call(elec, magn, keep, drive, xlo, xhi, rows, basis)  15.2 us
    ppermute x3, waiting for transfers between devices, scatter_sum(): rows = keep + lax.ppermute(send, axis, pairs)  11.7 us
    ppermute x12, waiting for transfers between devices, shifted(): return lax.ppermute(value, axis, pairs)  8.75 us
    pallas_call x3, Pallas kernels, local(): edge_call(elec, elec, elec, elec, magn, magn, magn, keep, keep, drive, dr...  6.41 us
    unnamed x34, local copies, waits for them, and re-layouts  4.45 us
    slice x4, local copies, waits for them, and re-layouts, local(): picked = sums[:, :, depth - 3]  2.51 us
    concatenate x4, other arithmetic, exchange_y(): message = jnp.concatenate([rows, corners])  2.49 us
  transfers between devices with their start and end apart: 16, of which 11 were waited for; matrix products, arithmetic and copies ran while one was open for 4% of the time, Pallas kernels for 17%

profile of v9, /device:TPU:0, one launch (start us, length us, event | category | flops | bytes accessed | tf_op | source)
XLA Modules:
  0.0 80.9 jit_solution(18113341245845014415)
XLA Ops:
  0.6 2.1 %shard_map.86 = (f32[5,64,128]{2,1,0:T(8,128)}, f32[2,64,128]{2,1,0:T(8,128)}, f32[7,8,1,128]{3,2,1,0:T(1,128)}) custom-call(f32[3,8,64,128]{3,2,1,0:T(8,128)} %e_last.1, f32[3,8,64,128]{3,2,1,0:T(8,128)} %h_last.1), custom_call_target="tpu_custom_call" | custom-call | tf_op jit(solution)/shard_map/pallas_call | solution.py:314
  2.7 6.0 %collective-permute-start.1 = (f32[2,64,128]{2,1,0:T(8,128)}, f32[2,64,128]{2,1,0:T(8,128)S(1)}, u32[]{:S(2)}, u32[]{:S(2)}) collective-permute-start(f32[2,64,128]{2,1,0:T(8,128)} %get-tuple-element.134), channel_id=1, source_target_pairs={{0,14},{2,0},{4,2},{6,4},{8,6},{10,8},{12,10},{14,12},{1,15},{3,1}... | collective-permute-start | bytes 196616 | tf_op jit(solution)/shard_map/ppermute | solution.py:21
  8.7 0.0 collective-permute-start
  8.7 0.7 copy-done.15
  9.4 0.1 multiply_multiply_fusion.1
  9.5 0.1 multiply_multiply_fusion
  9.5 1.1 %fusion.4 = (f32[64,8,64]{2,0,1:T(8,128)S(1)}, f32[64,8,64]{2,0,1:T(8,128)S(1)}) fusion(s32[64,64]{1,0:T(8,128)S(1)} %multiply_multiply_fusion, s32[64,8]{0,1:T(8,128)S(1)} %multiply_multiply_fusion.1), kind=kLoop, calls=%fused_computation.14 | loop fusion | flops 458752 | bytes 280576 | tf_op jit(solution)/shard_map/cos | solution.py:243
  10.7 2.0 %shard_map.85 = (f32[8,64,128]{2,1,0:T(8,128)}, f32[8,64,128]{2,1,0:T(8,128)}) custom-call(f32[6]{0:T(128)} %eps_ref.1, f32[6]{0:T(128)} %sigma_ref.1, s32[8,64,128]{2,1,0:T(8,128)} %mat_ref.1), custom_call_target="tpu_custom_call" | custom-call | tf_op jit(solution)/shard_map/pallas_call | solution.py:43
  12.7 0.0 collective-permute-done.1.xhi_ref
  12.7 4.6 %collective-permute-done.xlo_ref = f32[5,64,128]{2,1,0:T(8,128)S(1)} collective-permute-done((f32[5,64,128]{2,1,0:T(8,128)}, f32[5,64,128]{2,1,0:T(8,128)S(1)}, u32[]{:S(2)}, u32[]{:S(2)}) %collective-permute-start) | collective-permute-done | bytes 163872 | tf_op jit(solution)/shard_map/ppermute | solution.py:21
  17.4 0.1 collective-permute-start.2
  17.4 0.8 %maximum_bitcast_fusion.basis_ref = f32[8,128,64]{2,1,0:T(8,128)} fusion(f32[64,8,64]{2,0,1:T(8,128)S(1)} %get-tuple-element.164, f32[64,8,64]{2,0,1:T(8,128)S(1)} %get-tuple-element.163), kind=kLoop, calls=%fused_computation | loop fusion | flops 65536 | bytes 524288 | tf_op jit(solution)/shard_map/transpose | solution.py:322
  18.3 0.4 collective-permute-done.2.y_ref
  18.6 0.6 copy-done.8
  19.2 2.1 %shard_map.88 = (f32[5,64,128]{2,1,0:T(8,128)}, f32[2,64,128]{2,1,0:T(8,128)}) custom-call(f32[3,8,64,128]{3,2,1,0:T(8,128)} %e_last.1, f32[3,8,64,128]{3,2,1,0:T(8,128)} %e_last.1, f32[3,8,64,128]{3,2,1,0:T(8,128)} %e_last.1, f32[3,8,64,128]{3,2,1,0:T(8,128)} %e_last.1, f32[3,8,64,128]{3,2,1,0:T(8,128)} %h_last.1, f32[3,8,64,128]{3,2,1,0:T(8,128)} %h_last.1, ...), custom_call_target="tpu_custom_call" | custom-call | tf_op jit(solution)/shard_map/pallas_call | solution.py:329
  21.4 0.0 collective-permute-start.3
  21.4 4.7 %collective-permute-start.4 = (f32[2,64,128]{2,1,0:T(8,128)}, f32[2,64,128]{2,1,0:T(8,128)S(1)}, u32[]{:S(2)}, u32[]{:S(2)}) collective-permute-start(f32[2,64,128]{2,1,0:T(8,128)} %get-tuple-element.145), channel_id=1, source_target_pairs={{0,14},{2,0},{4,2},{6,4},{8,6},{10,8},{12,10},{14,12},{1,15},{3,1}... | collective-permute-start | bytes 196616 | tf_op jit(solution)/shard_map/ppermute | solution.py:21
  26.1 3.8 %shard_map.87 = (f32[3,8,64,128]{3,2,1,0:T(8,128)}, f32[3,8,64,128]{3,2,1,0:T(8,128)}, f32[7,8,1,128]{3,2,1,0:T(1,128)}, f32[2,128,128]{2,1,0:T(8,128)}) custom-call(f32[3,8,64,128]{3,2,1,0:T(8,128)} %e_last.1, f32[3,8,64,128]{3,2,1,0:T(8,128)} %h_last.1, f32[8,64,128]{2,1,0:T(8,128)} %get-tuple-element.135.keep_ref.keep_first.keep_last, ...), custom_call_target="tpu_custom_call" | custom-call | tf_op jit(solution)/shard_map/pallas_call | solution.py:333
  29.9 0.7 collective-permute-done.3.xlo_ref
  30.6 0.0 collective-permute-done.4.xhi_ref
  30.6 0.8 %pad_maximum_fusion.1 = f32[9,8,1,128]{3,2,1,0:T(1,128)S(1)} fusion(f32[2,8,1,128]{3,2,1,0:T(1,128)S(1)} %constant_dynamic-update-slice_fusion.2, f32[7,8,1,128]{3,2,1,0:T(1,128)} %get-tuple-element.146), kind=kLoop, calls=%fused_computation.16 | loop fusion | flops 9216 | bytes 73728 | tf_op jit(solution)/shard_map/concatenate | solution.py:220
  31.4 0.1 collective-permute-start.5
  31.5 1.2 %collective-permute-done.5.y_ref = f32[9,8,1,128]{3,2,1,0:T(1,128)S(1)} collective-permute-done((f32[9,8,1,128]{3,2,1,0:T(1,128)S(1)}, f32[9,8,1,128]{3,2,1,0:T(1,128)S(1)}, u32[]{:S(2)}, u32[]{:S(2)}) %collective-permute-start.5) | collective-permute-done | bytes 36896 | tf_op jit(solution)/shard_map/ppermute | solution.py:21
  32.7 0.6 copy-done.9
  33.3 2.1 %shard_map.90 = (f32[5,64,128]{2,1,0:T(8,128)}, f32[2,64,128]{2,1,0:T(8,128)}) custom-call(f32[3,8,64,128]{3,2,1,0:T(8,128)} %get-tuple-element.142.e_ref.e_first.e_second.e_penult.e_last, f32[3,8,64,128]{3,2,1,0:T(8,128)} %get-tuple-element.142.e_ref.e_first.e_second.e_penult.e_last, ...), custom_call_target="tpu_custom_call" | custom-call | tf_op jit(solution)/shard_map/pallas_call | solution.py:329
  35.4 0.0 collective-permute-start.6
  35.5 4.7 %collective-permute-start.7 = (f32[2,64,128]{2,1,0:T(8,128)}, f32[2,64,128]{2,1,0:T(8,128)S(1)}, u32[]{:S(2)}, u32[]{:S(2)}) collective-permute-start(f32[2,64,128]{2,1,0:T(8,128)} %get-tuple-element.150), channel_id=1, source_target_pairs={{0,14},{2,0},{4,2},{6,4},{8,6},{10,8},{12,10},{14,12},{1,15},{3,1}... | collective-permute-start | bytes 196616 | tf_op jit(solution)/shard_map/ppermute | solution.py:21
  40.2 3.8 %shard_map.89 = (f32[3,8,64,128]{3,2,1,0:T(8,128)}, f32[3,8,64,128]{3,2,1,0:T(8,128)}, f32[7,8,1,128]{3,2,1,0:T(1,128)}, f32[2,128,128]{2,1,0:T(8,128)}) custom-call(f32[3,8,64,128]{3,2,1,0:T(8,128)} %get-tuple-element.142.e_ref.e_first.e_second.e_penult.e_last, f32[3,8,64,128]{3,2,1,0:T(8,128)} %get-tuple-element.143.h_ref.h_first.h_penult.h_last, ...), custom_call_target="tpu_custom_call" | custom-call | tf_op jit(solution)/shard_map/pallas_call | solution.py:333
  44.0 0.6 collective-permute-done.6.xlo_ref
  44.7 0.8 %pad_maximum_fusion.2 = f32[9,8,1,128]{3,2,1,0:T(1,128)S(1)} fusion(f32[2,8,1,128]{3,2,1,0:T(1,128)S(1)} %constant_dynamic-update-slice_fusion.1, f32[7,8,1,128]{3,2,1,0:T(1,128)} %get-tuple-element.151), kind=kLoop, calls=%fused_computation.17 | loop fusion | flops 9216 | bytes 73728 | tf_op jit(solution)/shard_map/concatenate | solution.py:220
  45.5 0.1 collective-permute-start.8
  45.6 1.2 %collective-permute-done.8.y_ref = f32[9,8,1,128]{3,2,1,0:T(1,128)S(1)} collective-permute-done((f32[9,8,1,128]{3,2,1,0:T(1,128)S(1)}, f32[9,8,1,128]{3,2,1,0:T(1,128)S(1)}, u32[]{:S(2)}, u32[]{:S(2)}) %collective-permute-start.8) | collective-permute-done | bytes 36896 | tf_op jit(solution)/shard_map/ppermute | solution.py:21
  46.8 0.6 copy-done.7
  47.4 2.2 %shard_map.92 = (f32[5,64,128]{2,1,0:T(8,128)}, f32[2,64,128]{2,1,0:T(8,128)}) custom-call(f32[3,8,64,128]{3,2,1,0:T(8,128)} %get-tuple-element.147.e_ref.e_first.e_second.e_penult.e_last, f32[3,8,64,128]{3,2,1,0:T(8,128)} %get-tuple-element.147.e_ref.e_first.e_second.e_penult.e_last, ...), custom_call_target="tpu_custom_call" | custom-call | tf_op jit(solution)/shard_map/pallas_call | solution.py:329
  49.5 0.1 collective-permute-start.9
  49.6 0.2 slice_reduce_fusion.3
  49.8 0.7 copy-done.11
  50.5 0.2 slice_reduce_fusion.2
  50.6 0.7 copy-done.16
  51.3 4.1 %collective-permute-start.10 = (f32[2,64,128]{2,1,0:T(8,128)S(1)}, f32[2,64,128]{2,1,0:T(8,128)S(1)}, u32[]{:S(2)}, u32[]{:S(2)}) collective-permute-start(f32[2,64,128]{2,1,0:T(8,128)S(1)} %copy-done.16), channel_id=1, source_target_pairs={{0,14},{2,0},{4,2},{6,4},{8,6},{10,8},{12,10},{14,12},{1,15},{3,1}... | collective-permute-start | bytes 196616 | tf_op jit(solution)/shard_map/ppermute | solution.py:21
  55.4 3.8 %shard_map.91 = (f32[3,8,64,128]{3,2,1,0:T(8,128)}, f32[3,8,64,128]{3,2,1,0:T(8,128)}, f32[7,8,1,128]{3,2,1,0:T(1,128)}, f32[2,128,128]{2,1,0:T(8,128)}) custom-call(f32[3,8,64,128]{3,2,1,0:T(8,128)} %get-tuple-element.147.e_ref.e_first.e_second.e_penult.e_last, f32[3,8,64,128]{3,2,1,0:T(8,128)} %get-tuple-element.148.h_ref.h_first.h_penult.h_last, ...), custom_call_target="tpu_custom_call" | custom-call | tf_op jit(solution)/shard_map/pallas_call | solution.py:333
  59.2 0.0 collective-permute-done.9.xlo_ref
  59.2 0.0 collective-permute-done.10.xhi_ref
  59.2 0.8 pad_maximum_fusion.3
  60.0 0.1 collective-permute-start.11
  60.1 1.1 %slice_reduce_fusion.1 = f32[2,128]{1,0:T(2,128)S(1)} fusion(f32[2,128,128]{2,1,0:T(8,128)} %get-tuple-element.161), kind=kLoop, calls=%fused_computation.10 | loop fusion | bytes 2048 | tf_op jit(solution)/shard_map/slice | solution.py:339
  61.2 0.1 collective-permute-done.11.y_ref
  61.3 0.6 copy-done.13
  61.9 3.8 %shard_map.93 = (f32[3,8,64,128]{3,2,1,0:T(8,128)}, f32[3,8,64,128]{3,2,1,0:T(8,128)}, f32[7,8,1,128]{3,2,1,0:T(1,128)}, f32[2,128,128]{2,1,0:T(8,128)}) custom-call(f32[3,8,64,128]{3,2,1,0:T(8,128)} %get-tuple-element.152.e_ref, f32[3,8,64,128]{3,2,1,0:T(8,128)} %get-tuple-element.153.h_ref, f32[8,64,128]{2,1,0:T(8,128)} %get-tuple-element.135.keep_ref.keep_first.keep_last, ...), custom_call_target="tpu_custom_call" | custom-call | tf_op jit(solution)/shard_map/pallas_call | solution.py:333
  65.7 1.1 %slice_reduce_fusion = f32[2,128]{1,0:T(2,128)S(1)} fusion(f32[2,128,128]{2,1,0:T(8,128)} %get-tuple-element.162), kind=kLoop, calls=%fused_computation.9 | loop fusion | bytes 2048 | tf_op jit(solution)/shard_map/slice | solution.py:339
  66.8 0.1 add_bitcast_fusion.3
  66.9 0.1 add_bitcast_fusion.2
  67.0 0.1 slice_select_fusion.2
  67.1 0.0 collective-permute-start.12
  67.1 4.5 %collective-permute-done.12 = f32[32,4]{0,1:T(4,128)S(1)} collective-permute-done((f32[32,4]{0,1:T(4,128)S(1)}, f32[32,4]{0,1:T(4,128)S(1)}, u32[]{:S(2)}, u32[]{:S(2)}) %collective-permute-start.12) | collective-permute-done | bytes 544 | tf_op jit(solution)/shard_map/ppermute | solution.py:268
  71.6 0.1 select_add_fusion.2
  71.7 0.1 slice_select_fusion.1
  71.7 3.6 %collective-permute-done.13 = f32[16,4]{0,1:T(4,128)S(1)} collective-permute-done((f32[16,4]{0,1:T(4,128)S(1)}, f32[16,4]{0,1:T(4,128)S(1)}, u32[]{:S(2)}, u32[]{:S(2)}) %collective-permute-start.13) | collective-permute-done | bytes 288 | tf_op jit(solution)/shard_map/ppermute | solution.py:268
  75.3 0.1 select_add_fusion.1
  75.4 0.1 slice_select_fusion
  75.5 3.6 %collective-permute-done.14 = f32[8,4]{0,1:T(4,128)S(1)} collective-permute-done((f32[8,4]{0,1:T(4,128)S(1)}, f32[8,4]{0,1:T(4,128)S(1)}, u32[]{:S(2)}, u32[]{:S(2)}) %collective-permute-start.14) | collective-permute-done | bytes 160 | tf_op jit(solution)/shard_map/ppermute | solution.py:268
  79.1 0.1 select_add_fusion
  79.1 1.2 %collective-permute-done.15 = f32[8,4]{0,1:T(4,128)S(1)} collective-permute-done((f32[8,4]{0,1:T(4,128)S(1)}, f32[8,4]{0,1:T(4,128)S(1)}, u32[]{:S(2)}, u32[]{:S(2)}) %collective-permute-start.15) | collective-permute-done | bytes 160 | tf_op jit(solution)/shard_map/ppermute | solution.py:278
  80.3 0.6 add_multiply_fusion
  (48 shorter events, 0.2 us)
Async XLA Ops:
  2.7 10.0 %collective-permute-start.1 = (f32[2,64,128]{2,1,0:T(8,128)}, f32[2,64,128]{2,1,0:T(8,128)S(1)}, u32[]{:S(2)}, u32[]{:S(2)}) collective-permute-start(f32[2,64,128]{2,1,0:T(8,128)} %get-tuple-element.134), channel_id=1, source_target_pairs={{0,14},{2,0},{4,2},{6,4},{8,6},{10,8},{12,10},{14,12},{1,15},{3,1}... | collective-permute-start | bytes 196616 | tf_op jit(solution)/shard_map/ppermute | solution.py:21
  8.7 8.6 %collective-permute-start = (f32[5,64,128]{2,1,0:T(8,128)}, f32[5,64,128]{2,1,0:T(8,128)S(1)}, u32[]{:S(2)}, u32[]{:S(2)}) collective-permute-start(f32[5,64,128]{2,1,0:T(8,128)} %get-tuple-element.133), channel_id=1, source_target_pairs={{0,2},{2,4},{4,6},{6,8},{8,10},{10,12},{12,14},{14,0},{1,3},{3,5},... | collective-permute-start | bytes 491528 | tf_op jit(solution)/shard_map/ppermute | solution.py:21
  8.7 0.7 copy-start.15
  10.7 6.7 %copy-start.14 = (f32[7,8,1,128]{3,2,1,0:T(1,128)S(1)}, f32[7,8,1,128]{3,2,1,0:T(1,128)}, u32[]{:S(2)}) copy-start(f32[7,8,1,128]{3,2,1,0:T(1,128)} %get-tuple-element.139) | copy-start | bytes 86020
  12.7 5.6 %copy-start.3 = (f32[2,64,128]{2,1,0:T(8,128)}, f32[2,64,128]{2,1,0:T(8,128)S(1)}, u32[]{:S(2)}) copy-start(f32[2,64,128]{2,1,0:T(8,128)S(1)} %collective-permute-done.1.xhi_ref) | copy-start | bytes 196612
  17.3 1.0 %copy-start = (f32[5,64,128]{2,1,0:T(8,128)}, f32[5,64,128]{2,1,0:T(8,128)S(1)}, u32[]{:S(2)}) copy-start(f32[5,64,128]{2,1,0:T(8,128)S(1)} %collective-permute-done.xlo_ref) | copy-start | bytes 491524
  17.4 1.3 %collective-permute-start.2 = (f32[9,8,1,128]{3,2,1,0:T(1,128)S(1)}, f32[9,8,1,128]{3,2,1,0:T(1,128)S(1)}, u32[]{:S(2)}, u32[]{:S(2)}) collective-permute-start(f32[9,8,1,128]{3,2,1,0:T(1,128)S(1)} %pad_maximum_fusion), channel_id=1, source_target_pairs={{0,1},{1,0},{2,3},{3,2},{4,5},{5,4},{6,7},{7,6},{8,9},{9,8},{10,11... | collective-permute-start | bytes 110600 | tf_op jit(solution)/shard_map/ppermute | solution.py:21
  18.6 0.6 copy-start.8
  21.4 9.2 %collective-permute-start.3 = (f32[5,64,128]{2,1,0:T(8,128)}, f32[5,64,128]{2,1,0:T(8,128)S(1)}, u32[]{:S(2)}, u32[]{:S(2)}) collective-permute-start(f32[5,64,128]{2,1,0:T(8,128)} %get-tuple-element.144), channel_id=1, source_target_pairs={{0,2},{2,4},{4,6},{6,8},{8,10},{10,12},{12,14},{14,0},{1,3},{3,5},... | collective-permute-start | bytes 491528 | tf_op jit(solution)/shard_map/ppermute | solution.py:21
  21.4 9.2 %collective-permute-start.4 = (f32[2,64,128]{2,1,0:T(8,128)}, f32[2,64,128]{2,1,0:T(8,128)S(1)}, u32[]{:S(2)}, u32[]{:S(2)}) collective-permute-start(f32[2,64,128]{2,1,0:T(8,128)} %get-tuple-element.145), channel_id=1, source_target_pairs={{0,14},{2,0},{4,2},{6,4},{8,6},{10,8},{12,10},{14,12},{1,15},{3,1}... | collective-permute-start | bytes 196616 | tf_op jit(solution)/shard_map/ppermute | solution.py:21
  30.5 2.2 %copy-start.2 = (f32[5,64,128]{2,1,0:T(8,128)}, f32[5,64,128]{2,1,0:T(8,128)S(1)}, u32[]{:S(2)}) copy-start(f32[5,64,128]{2,1,0:T(8,128)S(1)} %collective-permute-done.3.xlo_ref) | copy-start | bytes 491524
  30.6 2.1 %copy-start.5 = (f32[2,64,128]{2,1,0:T(8,128)}, f32[2,64,128]{2,1,0:T(8,128)S(1)}, u32[]{:S(2)}) copy-start(f32[2,64,128]{2,1,0:T(8,128)S(1)} %collective-permute-done.4.xhi_ref) | copy-start | bytes 196612
  31.4 1.3 %collective-permute-start.5 = (f32[9,8,1,128]{3,2,1,0:T(1,128)S(1)}, f32[9,8,1,128]{3,2,1,0:T(1,128)S(1)}, u32[]{:S(2)}, u32[]{:S(2)}) collective-permute-start(f32[9,8,1,128]{3,2,1,0:T(1,128)S(1)} %pad_maximum_fusion.1), channel_id=1, source_target_pairs={{0,1},{1,0},{2,3},{3,2},{4,5},{5,4},{6,7},{7,6},{8,9},{9,8},{10,11... | collective-permute-start | bytes 110600 | tf_op jit(solution)/shard_map/ppermute | solution.py:21
  32.7 0.6 copy-start.9
  35.4 9.2 %collective-permute-start.6 = (f32[5,64,128]{2,1,0:T(8,128)}, f32[5,64,128]{2,1,0:T(8,128)S(1)}, u32[]{:S(2)}, u32[]{:S(2)}) collective-permute-start(f32[5,64,128]{2,1,0:T(8,128)} %get-tuple-element.149), channel_id=1, source_target_pairs={{0,2},{2,4},{4,6},{6,8},{8,10},{10,12},{12,14},{14,0},{1,3},{3,5},... | collective-permute-start | bytes 491528 | tf_op jit(solution)/shard_map/ppermute | solution.py:21
  35.5 9.2 %collective-permute-start.7 = (f32[2,64,128]{2,1,0:T(8,128)}, f32[2,64,128]{2,1,0:T(8,128)S(1)}, u32[]{:S(2)}, u32[]{:S(2)}) collective-permute-start(f32[2,64,128]{2,1,0:T(8,128)} %get-tuple-element.150), channel_id=1, source_target_pairs={{0,14},{2,0},{4,2},{6,4},{8,6},{10,8},{12,10},{14,12},{1,15},{3,1}... | collective-permute-start | bytes 196616 | tf_op jit(solution)/shard_map/ppermute | solution.py:21
  44.6 2.2 %copy-start.1 = (f32[5,64,128]{2,1,0:T(8,128)}, f32[5,64,128]{2,1,0:T(8,128)S(1)}, u32[]{:S(2)}) copy-start(f32[5,64,128]{2,1,0:T(8,128)S(1)} %collective-permute-done.6.xlo_ref) | copy-start | bytes 491524
  44.6 2.1 %copy-start.4 = (f32[2,64,128]{2,1,0:T(8,128)}, f32[2,64,128]{2,1,0:T(8,128)S(1)}, u32[]{:S(2)}) copy-start(f32[2,64,128]{2,1,0:T(8,128)S(1)} %collective-permute-done.7.xhi_ref) | copy-start | bytes 196612
  45.5 1.3 %collective-permute-start.8 = (f32[9,8,1,128]{3,2,1,0:T(1,128)S(1)}, f32[9,8,1,128]{3,2,1,0:T(1,128)S(1)}, u32[]{:S(2)}, u32[]{:S(2)}) collective-permute-start(f32[9,8,1,128]{3,2,1,0:T(1,128)S(1)} %pad_maximum_fusion.2), channel_id=1, source_target_pairs={{0,1},{1,0},{2,3},{3,2},{4,5},{5,4},{6,7},{7,6},{8,9},{9,8},{10,11... | collective-permute-start | bytes 110600 | tf_op jit(solution)/shard_map/ppermute | solution.py:21
  46.8 0.6 copy-start.7
  47.4 2.2 %copy-start.10 = (f32[2,128,128]{2,1,0:T(8,128)S(1)}, f32[2,128,128]{2,1,0:T(8,128)}, u32[]{:S(2)}) copy-start(f32[2,128,128]{2,1,0:T(8,128)} %get-tuple-element.159) | copy-start | bytes 393220
  49.5 0.9 %copy-start.11 = (f32[2,128,128]{2,1,0:T(8,128)S(1)}, f32[2,128,128]{2,1,0:T(8,128)}, u32[]{:S(2)}) copy-start(f32[2,128,128]{2,1,0:T(8,128)} %get-tuple-element.160) | copy-start | bytes 393220
  49.5 9.6 %collective-permute-start.9 = (f32[5,64,128]{2,1,0:T(8,128)}, f32[5,64,128]{2,1,0:T(8,128)S(1)}, u32[]{:S(2)}, u32[]{:S(2)}) collective-permute-start(f32[5,64,128]{2,1,0:T(8,128)} %get-tuple-element.154), channel_id=1, source_target_pairs={{0,2},{2,4},{4,6},{6,8},{8,10},{10,12},{12,14},{14,0},{1,3},{3,5},... | collective-permute-start | bytes 491528 | tf_op jit(solution)/shard_map/ppermute | solution.py:21
  50.4 0.8 %copy-start.16 = (f32[2,64,128]{2,1,0:T(8,128)S(1)}, f32[2,64,128]{2,1,0:T(8,128)}, u32[]{:S(2)}) copy-start(f32[2,64,128]{2,1,0:T(8,128)} %get-tuple-element.155) | copy-start | bytes 196612
  51.3 7.9 %collective-permute-start.10 = (f32[2,64,128]{2,1,0:T(8,128)S(1)}, f32[2,64,128]{2,1,0:T(8,128)S(1)}, u32[]{:S(2)}, u32[]{:S(2)}) collective-permute-start(f32[2,64,128]{2,1,0:T(8,128)S(1)} %copy-done.16), channel_id=1, source_target_pairs={{0,14},{2,0},{4,2},{6,4},{8,6},{10,8},{12,10},{14,12},{1,15},{3,1}... | collective-permute-start | bytes 196616 | tf_op jit(solution)/shard_map/ppermute | solution.py:21
  59.2 2.2 %copy-start.6 = (f32[5,64,128]{2,1,0:T(8,128)}, f32[5,64,128]{2,1,0:T(8,128)S(1)}, u32[]{:S(2)}) copy-start(f32[5,64,128]{2,1,0:T(8,128)S(1)} %collective-permute-done.9.xlo_ref) | copy-start | bytes 491524
  59.2 2.1 %copy-start.12 = (f32[2,64,128]{2,1,0:T(8,128)}, f32[2,64,128]{2,1,0:T(8,128)S(1)}, u32[]{:S(2)}) copy-start(f32[2,64,128]{2,1,0:T(8,128)S(1)} %collective-permute-done.10.xhi_ref) | copy-start | bytes 196612
  60.0 1.3 %collective-permute-start.11 = (f32[9,8,1,128]{3,2,1,0:T(1,128)S(1)}, f32[9,8,1,128]{3,2,1,0:T(1,128)S(1)}, u32[]{:S(2)}, u32[]{:S(2)}) collective-permute-start(f32[9,8,1,128]{3,2,1,0:T(1,128)S(1)} %pad_maximum_fusion.3), channel_id=1, source_target_pairs={{0,1},{1,0},{2,3},{3,2},{4,5},{5,4},{6,7},{7,6},{8,9},{9,8},{10,11... | collective-permute-start | bytes 110600 | tf_op jit(solution)/shard_map/ppermute | solution.py:21
  61.3 0.6 copy-start.13
  67.1 4.5 %collective-permute-start.12 = (f32[32,4]{0,1:T(4,128)S(1)}, f32[32,4]{0,1:T(4,128)S(1)}, u32[]{:S(2)}, u32[]{:S(2)}) collective-permute-start(f32[32,4]{0,1:T(4,128)S(1)} %slice_select_fusion.2), channel_id=1, source_target_pairs={{0,8},{2,10},{4,12},{6,14},{8,0},{10,2},{12,4},{14,6},{1,9},{3,11}... | collective-permute-start | bytes 1544 | tf_op jit(solution)/shard_map/ppermute | solution.py:268
  71.7 3.6 %collective-permute-start.13 = (f32[16,4]{0,1:T(4,128)S(1)}, f32[16,4]{0,1:T(4,128)S(1)}, u32[]{:S(2)}, u32[]{:S(2)}) collective-permute-start(f32[16,4]{0,1:T(4,128)S(1)} %slice_select_fusion.1), channel_id=1, source_target_pairs={{0,4},{2,6},{4,0},{6,2},{8,12},{10,14},{12,8},{14,10},{1,5},{3,7},... | collective-permute-start | bytes 776 | tf_op jit(solution)/shard_map/ppermute | solution.py:268
  75.5 3.6 %collective-permute-start.14 = (f32[8,4]{0,1:T(4,128)S(1)}, f32[8,4]{0,1:T(4,128)S(1)}, u32[]{:S(2)}, u32[]{:S(2)}) collective-permute-start(f32[8,4]{0,1:T(4,128)S(1)} %slice_select_fusion), channel_id=1, source_target_pairs={{0,2},{2,0},{4,6},{6,4},{8,10},{10,8},{12,14},{14,12},{1,3},{3,1},... | collective-permute-start | bytes 392 | tf_op jit(solution)/shard_map/ppermute | solution.py:268
  79.1 1.2 %collective-permute-start.15 = (f32[8,4]{0,1:T(4,128)S(1)}, f32[8,4]{0,1:T(4,128)S(1)}, u32[]{:S(2)}, u32[]{:S(2)}) collective-permute-start(f32[8,4]{0,1:T(4,128)S(1)} %select_add_fusion), channel_id=1, source_target_pairs={{0,1},{1,0},{2,3},{3,2},{4,5},{5,4},{6,7},{7,6},{8,9},{9,8},{10,11... | collective-permute-start | bytes 392 | tf_op jit(solution)/shard_map/ppermute | solution.py:278

commit v10 on v9

--- a/solution.py
+++ b/solution.py
@@ -153,8 +153,9 @@
             part = jnp.dot(basis_ref[x], field, precision=lax.Precision.HIGHEST,
                            preferred_element_type=jnp.float32)
             sums[comp] = part if sums[comp] is None else sums[comp] + part
-    g_out[0] = sums[0]
-    g_out[1] = sums[1]
+    depth = e_ref.shape[3]
+    for comp in range(2):
+        g_out[comp] = sums[comp].T[depth - 3:depth - 2]
 
 
 def _edge_kernel(e_first, e_second, e_penult, e_last, h_first, h_penult, h_last,
@@ -186,27 +187,25 @@
     xlo_out[4] = old[5]
 
 
-def _halo_kernel(e_ref, h_ref, xlo_out, xhi_out, y_out):
-    planes = e_ref.shape[1]
-    cells = e_ref.shape[2]
-    last = slice(cells - 1, cells)
+def _halo_kernel(e_first, e_last, h_last, e_top, e_bottom, h_bottom, xlo_out, xhi_out, y_out):
+    planes = e_top.shape[1]
+    slab = e_top.shape[2]
+    last = slice(slab - 1, slab)
     for x in range(planes):
-        ex = e_ref[0, x]
-        ez = e_ref[2, x]
-        y_out[0, x] = ex[last]
-        y_out[1, x] = e_ref[1, x][last]
-        y_out[2, x] = ez[last]
-        y_out[3, x] = h_ref[0, x][last]
-        y_out[4, x] = h_ref[2, x][last]
-        y_out[5, x] = ex[0:1]
-        y_out[6, x] = ez[0:1]
-    xhi_out[0] = e_ref[1, 0]
-    xhi_out[1] = e_ref[2, 0]
-    xlo_out[0] = e_ref[0, planes - 1]
-    xlo_out[1] = e_ref[1, planes - 1]
-    xlo_out[2] = e_ref[2, planes - 1]
-    xlo_out[3] = h_ref[1, planes - 1]
-    xlo_out[4] = h_ref[2, planes - 1]
+        y_out[0, x] = e_bottom[0, x][last]
+        y_out[1, x] = e_bottom[1, x][last]
+        y_out[2, x] = e_bottom[2, x][last]
+        y_out[3, x] = h_bottom[0, x][last]
+        y_out[4, x] = h_bottom[2, x][last]
+        y_out[5, x] = e_top[0, x][0:1]
+        y_out[6, x] = e_top[2, x][0:1]
+    xhi_out[0] = e_first[1, 0]
+    xhi_out[1] = e_first[2, 0]
+    xlo_out[0] = e_last[0, 0]
+    xlo_out[1] = e_last[1, 0]
+    xlo_out[2] = e_last[2, 0]
+    xlo_out[3] = h_last[1, 0]
+    xlo_out[4] = h_last[2, 0]
 
 
 def exchange_x(xlo, xhi):
@@ -287,7 +286,7 @@
     xhi_shape = jax.ShapeDtypeStruct((2, cells_y, depth), f32)
     rows_shape = jax.ShapeDtypeStruct((7, cells_x, 1, depth), f32)
     angle_count = angle_orders.shape[0]
-    sums_shape = jax.ShapeDtypeStruct((2, 2 * angle_count, depth), f32)
+    sums_shape = jax.ShapeDtypeStruct((2, 1, 2 * angle_count), f32)
     step_call = pl.pallas_call(
         _step_kernel, out_shape=(field_shape, field_shape, rows_shape, sums_shape)
     )
@@ -311,9 +310,20 @@
         + [whole] * 3,
         out_specs=(whole, whole),
     )
-    xlo, xhi, rows = pl.pallas_call(_halo_kernel, out_shape=(xlo_shape, xhi_shape, rows_shape))(
-        e_field, h_field
-    )
+    slab = 8
+    slabs = cells_y // slab
+
+    def row_slab(index):
+        return pl.BlockSpec((comps, cells_x, slab, depth), lambda i: (0, 0, index, 0))
+
+    xlo, xhi, rows = pl.pallas_call(
+        _halo_kernel,
+        out_shape=(xlo_shape, xhi_shape, rows_shape),
+        grid=(1,),
+        in_specs=[field_plane(first), field_plane(last), field_plane(last),
+                  row_slab(0), row_slab(slabs - 1), row_slab(slabs - 1)],
+        out_specs=(whole, whole, whole),
+    )(e_field, e_field, h_field, e_field, e_field, h_field)
     xlo, xhi = exchange_x(xlo, xhi)
     keep, drive = coefficients(material, eps_table, sigma_table)
     keep, drive, xlo, xhi = lax.optimization_barrier((keep, drive, xlo, xhi))
@@ -336,7 +346,7 @@
             rows = exchange_y(new_rows, xlo, xhi)
         weight_cos = math.cos(PHASE_STEP * (number + 1))
         weight_sin = math.sin(PHASE_STEP * (number + 1))
-        picked = sums[:, :, depth - 3]
+        picked = sums[:, 0]
         for comp in range(2):
             cos_p = picked[comp, :angle_count]
             sin_p = picked[comp, angle_count:]

time: 81.6 us -> 78.7 us (0.964)
  local copies, waits for them, and re-layouts: 7.05 us -> 3.89 us
  starting transfers between devices: 19.9 us -> 20.9 us
    slice x4 -> x0, local copies, waits for them, and re-layouts: 2.51 us -> none  [local(): picked = sums[:, :, depth - 3]]
    ppermute x12, starting transfers between devices: 19.8 us -> 20.8 us  [shifted(): return lax.ppermute(value, axis, pairs)]
    unnamed x34 -> x38, local copies, waits for them, and re-layouts: 4.45 us -> 3.8 us
  transfers between devices with their start and end apart: 16 -> 16, of which waited for: 11 -> 13; matrix products, arithmetic and copies ran while one was open for 4% -> 3% of each run, Pallas kernels for 17% -> 17%
where the time goes in v10:
time: 78.7 us; the launch traced here: 78 us
  Pallas kernels  25.3 us (32%)
  waiting for transfers between devices  21.3 us (27%)
  starting transfers between devices  20.9 us (27%)
  other arithmetic  5.77 us (7%)
  local copies, waits for them, and re-layouts  3.89 us (5%)
  between operations  0.85 us (1%)
    ppermute x12, starting transfers between devices, shifted(): return lax.ppermute(value, axis, pairs)  20.8 us
    pallas_call x4, Pallas kernels, local(): step_call(elec, magn, keep, drive, xlo, xhi, rows, basis)  15.1 us
    ppermute x3, waiting for transfers between devices, scatter_sum(): rows = keep + lax.ppermute(send, axis, pairs)  11.6 us
    ppermute x12, waiting for transfers between devices, shifted(): return lax.ppermute(value, axis, pairs)  8.5 us
    pallas_call x3, Pallas kernels, local(): edge_call(elec, elec, elec, elec, magn, magn, magn, keep, keep, drive, dr...  6.39 us
    unnamed x38, local copies, waits for them, and re-layouts  3.8 us
    concatenate x4, other arithmetic, exchange_y(): message = jnp.concatenate([rows, corners])  2.49 us
    pallas_call x1, Pallas kernels, coefficients(): pl.pallas_call(_coef_kernel, out_shape=(out, out), in_specs=[scalar, scal...  2.02 us
  transfers between devices with their start and end apart: 16, of which 13 were waited for; matrix products, arithmetic and copies ran while one was open for 3% of the time, Pallas kernels for 17%

profile of v10, /device:TPU:0, one launch (start us, length us, event | category | flops | bytes accessed | tf_op | source)
XLA Modules:
  0.0 78.0 jit_solution(17642332517455040222)
XLA Ops:
  0.6 1.9 %shard_map.86 = (f32[5,64,128]{2,1,0:T(8,128)}, f32[2,64,128]{2,1,0:T(8,128)}, f32[7,8,1,128]{3,2,1,0:T(1,128)}) custom-call(f32[3,8,64,128]{3,2,1,0:T(8,128)} %e_last.3, f32[3,8,64,128]{3,2,1,0:T(8,128)} %e_last.3, f32[3,8,64,128]{3,2,1,0:T(8,128)} %h_last.3, f32[3,8,64,128]{3,2,1,0:T(8,128)} %e_last.3, f32[3,8,64,128]{3,2,1,0:T(8,128)} %e_last.3, ...), custom_call_target="tpu_custom_call" | custom-call | tf_op jit(solution)/shard_map/pallas_call | solution.py:319
  2.5 3.0 %collective-permute-start = (f32[5,64,128]{2,1,0:T(8,128)}, f32[5,64,128]{2,1,0:T(8,128)S(1)}, u32[]{:S(2)}, u32[]{:S(2)}) collective-permute-start(f32[5,64,128]{2,1,0:T(8,128)} %get-tuple-element.133), channel_id=1, source_target_pairs={{0,2},{2,4},{4,6},{6,8},{8,10},{10,12},{12,14},{14,0},{1,3},{3,5},... | collective-permute-start | bytes 491528 | tf_op jit(solution)/shard_map/ppermute | solution.py:21
  5.4 3.0 %collective-permute-start.1 = (f32[2,64,128]{2,1,0:T(8,128)}, f32[2,64,128]{2,1,0:T(8,128)S(1)}, u32[]{:S(2)}, u32[]{:S(2)}) collective-permute-start(f32[2,64,128]{2,1,0:T(8,128)} %get-tuple-element.134), channel_id=1, source_target_pairs={{0,14},{2,0},{4,2},{6,4},{8,6},{10,8},{12,10},{14,12},{1,15},{3,1}... | collective-permute-start | bytes 196616 | tf_op jit(solution)/shard_map/ppermute | solution.py:21
  8.5 0.7 copy-done.17
  9.2 0.1 multiply_multiply_fusion
  9.3 0.1 multiply_multiply_fusion.1
  9.3 1.1 %fusion.4 = (f32[64,8,64]{2,0,1:T(8,128)S(1)}, f32[64,8,64]{2,0,1:T(8,128)S(1)}) fusion(s32[64,64]{1,0:T(8,128)S(1)} %multiply_multiply_fusion, s32[64,8]{0,1:T(8,128)S(1)} %multiply_multiply_fusion.1), kind=kLoop, calls=%fused_computation.10 | loop fusion | flops 458752 | bytes 280576 | tf_op jit(solution)/shard_map/cos | solution.py:242
  10.4 2.0 %shard_map.85 = (f32[8,64,128]{2,1,0:T(8,128)}, f32[8,64,128]{2,1,0:T(8,128)}) custom-call(f32[6]{0:T(128)} %eps_ref.1, f32[6]{0:T(128)} %sigma_ref.1, s32[8,64,128]{2,1,0:T(8,128)} %mat_ref.1), custom_call_target="tpu_custom_call" | custom-call | tf_op jit(solution)/shard_map/pallas_call | solution.py:43
  12.5 1.0 %collective-permute-done.1.xhi_ref = f32[2,64,128]{2,1,0:T(8,128)S(1)} collective-permute-done((f32[2,64,128]{2,1,0:T(8,128)}, f32[2,64,128]{2,1,0:T(8,128)S(1)}, u32[]{:S(2)}, u32[]{:S(2)}) %collective-permute-start.1) | collective-permute-done | bytes 65568 | tf_op jit(solution)/shard_map/ppermute | solution.py:21
  13.4 0.0 collective-permute-done.xlo_ref
  13.5 0.1 collective-permute-start.2
  13.6 0.8 %maximum_bitcast_fusion.basis_ref = f32[8,128,64]{2,1,0:T(8,128)} fusion(f32[64,8,64]{2,0,1:T(8,128)S(1)} %get-tuple-element.164, f32[64,8,64]{2,0,1:T(8,128)S(1)} %get-tuple-element.163), kind=kLoop, calls=%fused_computation | loop fusion | flops 65536 | bytes 524288 | tf_op jit(solution)/shard_map/transpose | solution.py:332
  14.5 0.4 collective-permute-done.2.y_ref
  14.8 0.6 copy-done.9
  15.4 2.1 %shard_map.88 = (f32[5,64,128]{2,1,0:T(8,128)}, f32[2,64,128]{2,1,0:T(8,128)}) custom-call(f32[3,8,64,128]{3,2,1,0:T(8,128)} %e_last.3, f32[3,8,64,128]{3,2,1,0:T(8,128)} %e_last.3, f32[3,8,64,128]{3,2,1,0:T(8,128)} %e_last.3, f32[3,8,64,128]{3,2,1,0:T(8,128)} %e_last.3, f32[3,8,64,128]{3,2,1,0:T(8,128)} %h_last.3, f32[3,8,64,128]{3,2,1,0:T(8,128)} %h_last.3, ...), custom_call_target="tpu_custom_call" | custom-call | tf_op jit(solution)/shard_map/pallas_call | solution.py:339
  17.6 0.1 collective-permute-start.3
  17.6 3.8 %shard_map.87 = (f32[3,8,64,128]{3,2,1,0:T(8,128)}, f32[3,8,64,128]{3,2,1,0:T(8,128)}, f32[7,8,1,128]{3,2,1,0:T(1,128)}, f32[2,1,128]{2,1,0:T(1,128)}) custom-call(f32[3,8,64,128]{3,2,1,0:T(8,128)} %e_last.3, f32[3,8,64,128]{3,2,1,0:T(8,128)} %h_last.3, f32[8,64,128]{2,1,0:T(8,128)} %get-tuple-element.135.keep_ref.keep_first.keep_last, ...), custom_call_target="tpu_custom_call" | custom-call | tf_op jit(solution)/shard_map/pallas_call | solution.py:343
  21.4 4.8 %collective-permute-start.4 = (f32[2,64,128]{2,1,0:T(8,128)S(1)}, f32[2,64,128]{2,1,0:T(8,128)S(1)}, u32[]{:S(2)}, u32[]{:S(2)}) collective-permute-start(f32[2,64,128]{2,1,0:T(8,128)S(1)} %copy-done.18), channel_id=1, source_target_pairs={{0,14},{2,0},{4,2},{6,4},{8,6},{10,8},{12,10},{14,12},{1,15},{3,1}... | collective-permute-start | bytes 196616 | tf_op jit(solution)/shard_map/ppermute | solution.py:21
  26.1 0.7 collective-permute-done.3.xlo_ref
  26.9 1.3 %collective-permute-done.4.xhi_ref = f32[2,64,128]{2,1,0:T(8,128)S(1)} collective-permute-done((f32[2,64,128]{2,1,0:T(8,128)S(1)}, f32[2,64,128]{2,1,0:T(8,128)S(1)}, u32[]{:S(2)}, u32[]{:S(2)}) %collective-permute-start.4) | collective-permute-done | bytes 65568 | tf_op jit(solution)/shard_map/ppermute | solution.py:21
  28.2 0.8 %pad_maximum_fusion.1 = f32[9,8,1,128]{3,2,1,0:T(1,128)S(1)} fusion(f32[2,8,1,128]{3,2,1,0:T(1,128)S(1)} %constant_dynamic-update-slice_fusion.2, f32[7,8,1,128]{3,2,1,0:T(1,128)} %get-tuple-element.146), kind=kLoop, calls=%fused_computation.12 | loop fusion | flops 9216 | bytes 73728 | tf_op jit(solution)/shard_map/concatenate | solution.py:219
  29.0 0.1 collective-permute-start.5
  29.1 1.2 %collective-permute-done.5.y_ref = f32[9,8,1,128]{3,2,1,0:T(1,128)S(1)} collective-permute-done((f32[9,8,1,128]{3,2,1,0:T(1,128)S(1)}, f32[9,8,1,128]{3,2,1,0:T(1,128)S(1)}, u32[]{:S(2)}, u32[]{:S(2)}) %collective-permute-start.5) | collective-permute-done | bytes 36896 | tf_op jit(solution)/shard_map/ppermute | solution.py:21
  30.3 0.6 copy-done.7
  30.9 2.1 %shard_map.90 = (f32[5,64,128]{2,1,0:T(8,128)}, f32[2,64,128]{2,1,0:T(8,128)}) custom-call(f32[3,8,64,128]{3,2,1,0:T(8,128)} %get-tuple-element.142.e_ref.e_first.e_second.e_penult.e_last, f32[3,8,64,128]{3,2,1,0:T(8,128)} %get-tuple-element.142.e_ref.e_first.e_second.e_penult.e_last, ...), custom_call_target="tpu_custom_call" | custom-call | tf_op jit(solution)/shard_map/pallas_call | solution.py:339
  33.0 0.4 collective-permute-start.6
  33.4 4.6 %collective-permute-start.7 = (f32[2,64,128]{2,1,0:T(8,128)}, f32[2,64,128]{2,1,0:T(8,128)S(1)}, u32[]{:S(2)}, u32[]{:S(2)}) collective-permute-start(f32[2,64,128]{2,1,0:T(8,128)} %get-tuple-element.150), channel_id=1, source_target_pairs={{0,14},{2,0},{4,2},{6,4},{8,6},{10,8},{12,10},{14,12},{1,15},{3,1}... | collective-permute-start | bytes 196616 | tf_op jit(solution)/shard_map/ppermute | solution.py:21
  38.0 3.8 %shard_map.89 = (f32[3,8,64,128]{3,2,1,0:T(8,128)}, f32[3,8,64,128]{3,2,1,0:T(8,128)}, f32[7,8,1,128]{3,2,1,0:T(1,128)}, f32[2,1,128]{2,1,0:T(1,128)}) custom-call(f32[3,8,64,128]{3,2,1,0:T(8,128)} %get-tuple-element.142.e_ref.e_first.e_second.e_penult.e_last, f32[3,8,64,128]{3,2,1,0:T(8,128)} %get-tuple-element.143.h_ref.h_first.h_penult.h_last, ...), custom_call_target="tpu_custom_call" | custom-call | tf_op jit(solution)/shard_map/pallas_call | solution.py:343
  41.8 0.9 %collective-permute-done.6.xlo_ref = f32[5,64,128]{2,1,0:T(8,128)S(1)} collective-permute-done((f32[5,64,128]{2,1,0:T(8,128)}, f32[5,64,128]{2,1,0:T(8,128)S(1)}, u32[]{:S(2)}, u32[]{:S(2)}) %collective-permute-start.6) | collective-permute-done | bytes 163872 | tf_op jit(solution)/shard_map/ppermute | solution.py:21
  42.7 0.0 collective-permute-done.7.xhi_ref
  42.7 0.8 %pad_maximum_fusion.2 = f32[9,8,1,128]{3,2,1,0:T(1,128)S(1)} fusion(f32[2,8,1,128]{3,2,1,0:T(1,128)S(1)} %constant_dynamic-update-slice_fusion.1, f32[7,8,1,128]{3,2,1,0:T(1,128)} %get-tuple-element.151), kind=kLoop, calls=%fused_computation.13 | loop fusion | flops 9216 | bytes 73728 | tf_op jit(solution)/shard_map/concatenate | solution.py:219
  43.6 0.1 collective-permute-start.8
  43.6 1.2 %collective-permute-done.8.y_ref = f32[9,8,1,128]{3,2,1,0:T(1,128)S(1)} collective-permute-done((f32[9,8,1,128]{3,2,1,0:T(1,128)S(1)}, f32[9,8,1,128]{3,2,1,0:T(1,128)S(1)}, u32[]{:S(2)}, u32[]{:S(2)}) %collective-permute-start.8) | collective-permute-done | bytes 36896 | tf_op jit(solution)/shard_map/ppermute | solution.py:21
  44.8 0.6 copy-done.8
  45.4 2.1 %shard_map.92 = (f32[5,64,128]{2,1,0:T(8,128)}, f32[2,64,128]{2,1,0:T(8,128)}) custom-call(f32[3,8,64,128]{3,2,1,0:T(8,128)} %get-tuple-element.147.e_ref.e_first.e_second.e_penult.e_last, f32[3,8,64,128]{3,2,1,0:T(8,128)} %get-tuple-element.147.e_ref.e_first.e_second.e_penult.e_last, ...), custom_call_target="tpu_custom_call" | custom-call | tf_op jit(solution)/shard_map/pallas_call | solution.py:339
  47.6 0.0 collective-permute-start.9
  47.6 4.7 %collective-permute-start.10 = (f32[2,64,128]{2,1,0:T(8,128)}, f32[2,64,128]{2,1,0:T(8,128)S(1)}, u32[]{:S(2)}, u32[]{:S(2)}) collective-permute-start(f32[2,64,128]{2,1,0:T(8,128)} %get-tuple-element.155), channel_id=1, source_target_pairs={{0,14},{2,0},{4,2},{6,4},{8,6},{10,8},{12,10},{14,12},{1,15},{3,1}... | collective-permute-start | bytes 196616 | tf_op jit(solution)/shard_map/ppermute | solution.py:21
  52.3 3.8 %shard_map.91 = (f32[3,8,64,128]{3,2,1,0:T(8,128)}, f32[3,8,64,128]{3,2,1,0:T(8,128)}, f32[7,8,1,128]{3,2,1,0:T(1,128)}, f32[2,1,128]{2,1,0:T(1,128)}) custom-call(f32[3,8,64,128]{3,2,1,0:T(8,128)} %get-tuple-element.147.e_ref.e_first.e_second.e_penult.e_last, f32[3,8,64,128]{3,2,1,0:T(8,128)} %get-tuple-element.148.h_ref.h_first.h_penult.h_last, ...), custom_call_target="tpu_custom_call" | custom-call | tf_op jit(solution)/shard_map/pallas_call | solution.py:343
  56.1 0.7 collective-permute-done.9.xlo_ref
  56.7 0.0 collective-permute-done.10.xhi_ref
  56.8 0.8 %pad_maximum_fusion.3 = f32[9,8,1,128]{3,2,1,0:T(1,128)S(1)} fusion(f32[2,8,1,128]{3,2,1,0:T(1,128)S(1)} %constant_dynamic-update-slice_fusion, f32[7,8,1,128]{3,2,1,0:T(1,128)} %get-tuple-element.156), kind=kLoop, calls=%fused_computation.14 | loop fusion | flops 9216 | bytes 73728 | tf_op jit(solution)/shard_map/concatenate | solution.py:219
  57.6 0.1 collective-permute-start.11
  57.7 1.2 %collective-permute-done.11.y_ref = f32[9,8,1,128]{3,2,1,0:T(1,128)S(1)} collective-permute-done((f32[9,8,1,128]{3,2,1,0:T(1,128)S(1)}, f32[9,8,1,128]{3,2,1,0:T(1,128)S(1)}, u32[]{:S(2)}, u32[]{:S(2)}) %collective-permute-start.11) | collective-permute-done | bytes 36896 | tf_op jit(solution)/shard_map/ppermute | solution.py:21
  58.9 0.6 copy-done.11
  59.5 3.8 %shard_map.93 = (f32[3,8,64,128]{3,2,1,0:T(8,128)}, f32[3,8,64,128]{3,2,1,0:T(8,128)}, f32[7,8,1,128]{3,2,1,0:T(1,128)}, f32[2,1,128]{2,1,0:T(1,128)}) custom-call(f32[3,8,64,128]{3,2,1,0:T(8,128)} %get-tuple-element.152.e_ref, f32[3,8,64,128]{3,2,1,0:T(8,128)} %get-tuple-element.153.h_ref, f32[8,64,128]{2,1,0:T(8,128)} %get-tuple-element.135.keep_ref.keep_first.keep_last, ...), custom_call_target="tpu_custom_call" | custom-call | tf_op jit(solution)/shard_map/pallas_call | solution.py:343
  63.3 0.0 copy-start.13
  63.3 0.6 copy-done.16
  63.9 0.0 copy-done.14
  63.9 0.0 copy-done.13
  63.9 0.1 add_bitcast_fusion.2
  64.0 0.1 add_bitcast_fusion.3
  64.1 0.1 slice_select_fusion.2
  64.2 0.0 collective-permute-start.12
  64.2 4.5 %collective-permute-done.12 = f32[32,4]{0,1:T(4,128)S(1)} collective-permute-done((f32[32,4]{0,1:T(4,128)S(1)}, f32[32,4]{0,1:T(4,128)S(1)}, u32[]{:S(2)}, u32[]{:S(2)}) %collective-permute-start.12) | collective-permute-done | bytes 544 | tf_op jit(solution)/shard_map/ppermute | solution.py:267
  68.7 0.1 select_add_fusion.2
  68.8 0.1 slice_select_fusion.1
  68.8 3.6 %collective-permute-done.13 = f32[16,4]{0,1:T(4,128)S(1)} collective-permute-done((f32[16,4]{0,1:T(4,128)S(1)}, f32[16,4]{0,1:T(4,128)S(1)}, u32[]{:S(2)}, u32[]{:S(2)}) %collective-permute-start.13) | collective-permute-done | bytes 288 | tf_op jit(solution)/shard_map/ppermute | solution.py:267
  72.4 0.1 select_add_fusion.1
  72.5 0.1 slice_select_fusion
  72.6 3.6 %collective-permute-done.14 = f32[8,4]{0,1:T(4,128)S(1)} collective-permute-done((f32[8,4]{0,1:T(4,128)S(1)}, f32[8,4]{0,1:T(4,128)S(1)}, u32[]{:S(2)}, u32[]{:S(2)}) %collective-permute-start.14) | collective-permute-done | bytes 160 | tf_op jit(solution)/shard_map/ppermute | solution.py:267
  76.2 0.1 select_add_fusion
  76.2 0.0 collective-permute-start.15
  76.2 1.2 %collective-permute-done.15 = f32[8,4]{0,1:T(4,128)S(1)} collective-permute-done((f32[8,4]{0,1:T(4,128)S(1)}, f32[8,4]{0,1:T(4,128)S(1)}, u32[]{:S(2)}, u32[]{:S(2)}) %collective-permute-start.15) | collective-permute-done | bytes 160 | tf_op jit(solution)/shard_map/ppermute | solution.py:277
  77.4 0.6 add_multiply_fusion
  (48 shorter events, 0.2 us)
Async XLA Ops:
  2.5 11.0 %collective-permute-start = (f32[5,64,128]{2,1,0:T(8,128)}, f32[5,64,128]{2,1,0:T(8,128)S(1)}, u32[]{:S(2)}, u32[]{:S(2)}) collective-permute-start(f32[5,64,128]{2,1,0:T(8,128)} %get-tuple-element.133), channel_id=1, source_target_pairs={{0,2},{2,4},{4,6},{6,8},{8,10},{10,12},{12,14},{14,0},{1,3},{3,5},... | collective-permute-start | bytes 491528 | tf_op jit(solution)/shard_map/ppermute | solution.py:21
  5.4 8.0 %collective-permute-start.1 = (f32[2,64,128]{2,1,0:T(8,128)}, f32[2,64,128]{2,1,0:T(8,128)S(1)}, u32[]{:S(2)}, u32[]{:S(2)}) collective-permute-start(f32[2,64,128]{2,1,0:T(8,128)} %get-tuple-element.134), channel_id=1, source_target_pairs={{0,14},{2,0},{4,2},{6,4},{8,6},{10,8},{12,10},{14,12},{1,15},{3,1}... | collective-permute-start | bytes 196616 | tf_op jit(solution)/shard_map/ppermute | solution.py:21
  8.5 0.7 copy-start.17
  10.4 3.1 %copy-start.12 = (f32[7,8,1,128]{3,2,1,0:T(1,128)S(1)}, f32[7,8,1,128]{3,2,1,0:T(1,128)}, u32[]{:S(2)}) copy-start(f32[7,8,1,128]{3,2,1,0:T(1,128)} %get-tuple-element.139) | copy-start | bytes 86020
  13.4 1.0 %copy-start.3 = (f32[2,64,128]{2,1,0:T(8,128)}, f32[2,64,128]{2,1,0:T(8,128)S(1)}, u32[]{:S(2)}) copy-start(f32[2,64,128]{2,1,0:T(8,128)S(1)} %collective-permute-done.1.xhi_ref) | copy-start | bytes 196612
  13.4 1.0 %copy-start = (f32[5,64,128]{2,1,0:T(8,128)}, f32[5,64,128]{2,1,0:T(8,128)S(1)}, u32[]{:S(2)}) copy-start(f32[5,64,128]{2,1,0:T(8,128)S(1)} %collective-permute-done.xlo_ref) | copy-start | bytes 491524
  13.5 1.3 %collective-permute-start.2 = (f32[9,8,1,128]{3,2,1,0:T(1,128)S(1)}, f32[9,8,1,128]{3,2,1,0:T(1,128)S(1)}, u32[]{:S(2)}, u32[]{:S(2)}) collective-permute-start(f32[9,8,1,128]{3,2,1,0:T(1,128)S(1)} %pad_maximum_fusion), channel_id=1, source_target_pairs={{0,1},{1,0},{2,3},{3,2},{4,5},{5,4},{6,7},{7,6},{8,9},{9,8},{10,11... | collective-permute-start | bytes 110600 | tf_op jit(solution)/shard_map/ppermute | solution.py:21
  14.8 0.6 copy-start.9
  17.6 3.8 %copy-start.18 = (f32[2,64,128]{2,1,0:T(8,128)S(1)}, f32[2,64,128]{2,1,0:T(8,128)}, u32[]{:S(2)}) copy-start(f32[2,64,128]{2,1,0:T(8,128)} %get-tuple-element.145) | copy-start | bytes 196612
  17.6 9.3 %collective-permute-start.3 = (f32[5,64,128]{2,1,0:T(8,128)}, f32[5,64,128]{2,1,0:T(8,128)S(1)}, u32[]{:S(2)}, u32[]{:S(2)}) collective-permute-start(f32[5,64,128]{2,1,0:T(8,128)} %get-tuple-element.144), channel_id=1, source_target_pairs={{0,2},{2,4},{4,6},{6,8},{8,10},{10,12},{12,14},{14,0},{1,3},{3,5},... | collective-permute-start | bytes 491528 | tf_op jit(solution)/shard_map/ppermute | solution.py:21
  21.4 6.8 %collective-permute-start.4 = (f32[2,64,128]{2,1,0:T(8,128)S(1)}, f32[2,64,128]{2,1,0:T(8,128)S(1)}, u32[]{:S(2)}, u32[]{:S(2)}) collective-permute-start(f32[2,64,128]{2,1,0:T(8,128)S(1)} %copy-done.18), channel_id=1, source_target_pairs={{0,14},{2,0},{4,2},{6,4},{8,6},{10,8},{12,10},{14,12},{1,15},{3,1}... | collective-permute-start | bytes 196616 | tf_op jit(solution)/shard_map/ppermute | solution.py:21
  26.9 3.4 %copy-start.2 = (f32[5,64,128]{2,1,0:T(8,128)}, f32[5,64,128]{2,1,0:T(8,128)S(1)}, u32[]{:S(2)}) copy-start(f32[5,64,128]{2,1,0:T(8,128)S(1)} %collective-permute-done.3.xlo_ref) | copy-start | bytes 491524
  28.2 2.1 %copy-start.5 = (f32[2,64,128]{2,1,0:T(8,128)}, f32[2,64,128]{2,1,0:T(8,128)S(1)}, u32[]{:S(2)}) copy-start(f32[2,64,128]{2,1,0:T(8,128)S(1)} %collective-permute-done.4.xhi_ref) | copy-start | bytes 196612
  29.0 1.3 %collective-permute-start.5 = (f32[9,8,1,128]{3,2,1,0:T(1,128)S(1)}, f32[9,8,1,128]{3,2,1,0:T(1,128)S(1)}, u32[]{:S(2)}, u32[]{:S(2)}) collective-permute-start(f32[9,8,1,128]{3,2,1,0:T(1,128)S(1)} %pad_maximum_fusion.1), channel_id=1, source_target_pairs={{0,1},{1,0},{2,3},{3,2},{4,5},{5,4},{6,7},{7,6},{8,9},{9,8},{10,11... | collective-permute-start | bytes 110600 | tf_op jit(solution)/shard_map/ppermute | solution.py:21
  30.3 0.6 copy-start.7
  33.0 9.7 %collective-permute-start.6 = (f32[5,64,128]{2,1,0:T(8,128)}, f32[5,64,128]{2,1,0:T(8,128)S(1)}, u32[]{:S(2)}, u32[]{:S(2)}) collective-permute-start(f32[5,64,128]{2,1,0:T(8,128)} %get-tuple-element.149), channel_id=1, source_target_pairs={{0,2},{2,4},{4,6},{6,8},{8,10},{10,12},{12,14},{14,0},{1,3},{3,5},... | collective-permute-start | bytes 491528 | tf_op jit(solution)/shard_map/ppermute | solution.py:21
  33.4 9.3 %collective-permute-start.7 = (f32[2,64,128]{2,1,0:T(8,128)}, f32[2,64,128]{2,1,0:T(8,128)S(1)}, u32[]{:S(2)}, u32[]{:S(2)}) collective-permute-start(f32[2,64,128]{2,1,0:T(8,128)} %get-tuple-element.150), channel_id=1, source_target_pairs={{0,14},{2,0},{4,2},{6,4},{8,6},{10,8},{12,10},{14,12},{1,15},{3,1}... | collective-permute-start | bytes 196616 | tf_op jit(solution)/shard_map/ppermute | solution.py:21
  42.7 2.2 %copy-start.1 = (f32[5,64,128]{2,1,0:T(8,128)}, f32[5,64,128]{2,1,0:T(8,128)S(1)}, u32[]{:S(2)}) copy-start(f32[5,64,128]{2,1,0:T(8,128)S(1)} %collective-permute-done.6.xlo_ref) | copy-start | bytes 491524
  42.7 2.1 %copy-start.4 = (f32[2,64,128]{2,1,0:T(8,128)}, f32[2,64,128]{2,1,0:T(8,128)S(1)}, u32[]{:S(2)}) copy-start(f32[2,64,128]{2,1,0:T(8,128)S(1)} %collective-permute-done.7.xhi_ref) | copy-start | bytes 196612
  43.6 1.3 %collective-permute-start.8 = (f32[9,8,1,128]{3,2,1,0:T(1,128)S(1)}, f32[9,8,1,128]{3,2,1,0:T(1,128)S(1)}, u32[]{:S(2)}, u32[]{:S(2)}) collective-permute-start(f32[9,8,1,128]{3,2,1,0:T(1,128)S(1)} %pad_maximum_fusion.2), channel_id=1, source_target_pairs={{0,1},{1,0},{2,3},{3,2},{4,5},{5,4},{6,7},{7,6},{8,9},{9,8},{10,11... | collective-permute-start | bytes 110600 | tf_op jit(solution)/shard_map/ppermute | solution.py:21
  44.8 0.6 copy-start.8
  47.6 9.2 %collective-permute-start.9 = (f32[5,64,128]{2,1,0:T(8,128)}, f32[5,64,128]{2,1,0:T(8,128)S(1)}, u32[]{:S(2)}, u32[]{:S(2)}) collective-permute-start(f32[5,64,128]{2,1,0:T(8,128)} %get-tuple-element.154), channel_id=1, source_target_pairs={{0,2},{2,4},{4,6},{6,8},{8,10},{10,12},{12,14},{14,0},{1,3},{3,5},... | collective-permute-start | bytes 491528 | tf_op jit(solution)/shard_map/ppermute | solution.py:21
  47.6 9.2 %collective-permute-start.10 = (f32[2,64,128]{2,1,0:T(8,128)}, f32[2,64,128]{2,1,0:T(8,128)S(1)}, u32[]{:S(2)}, u32[]{:S(2)}) collective-permute-start(f32[2,64,128]{2,1,0:T(8,128)} %get-tuple-element.155), channel_id=1, source_target_pairs={{0,14},{2,0},{4,2},{6,4},{8,6},{10,8},{12,10},{14,12},{1,15},{3,1}... | collective-permute-start | bytes 196616 | tf_op jit(solution)/shard_map/ppermute | solution.py:21
  56.7 2.2 %copy-start.6 = (f32[5,64,128]{2,1,0:T(8,128)}, f32[5,64,128]{2,1,0:T(8,128)S(1)}, u32[]{:S(2)}) copy-start(f32[5,64,128]{2,1,0:T(8,128)S(1)} %collective-permute-done.9.xlo_ref) | copy-start | bytes 491524
  56.8 2.1 %copy-start.10 = (f32[2,64,128]{2,1,0:T(8,128)}, f32[2,64,128]{2,1,0:T(8,128)S(1)}, u32[]{:S(2)}) copy-start(f32[2,64,128]{2,1,0:T(8,128)S(1)} %collective-permute-done.10.xhi_ref) | copy-start | bytes 196612
  57.6 1.3 %collective-permute-start.11 = (f32[9,8,1,128]{3,2,1,0:T(1,128)S(1)}, f32[9,8,1,128]{3,2,1,0:T(1,128)S(1)}, u32[]{:S(2)}, u32[]{:S(2)}) collective-permute-start(f32[9,8,1,128]{3,2,1,0:T(1,128)S(1)} %pad_maximum_fusion.3), channel_id=1, source_target_pairs={{0,1},{1,0},{2,3},{3,2},{4,5},{5,4},{6,7},{7,6},{8,9},{9,8},{10,11... | collective-permute-start | bytes 110600 | tf_op jit(solution)/shard_map/ppermute | solution.py:21
  58.9 0.6 copy-start.11
  63.2 0.6 copy-start.16
  63.2 0.7 copy-start.14
  63.3 0.7 copy-start.15
  63.3 0.7 copy-start.13
  64.2 4.5 %collective-permute-start.12 = (f32[32,4]{0,1:T(4,128)S(1)}, f32[32,4]{0,1:T(4,128)S(1)}, u32[]{:S(2)}, u32[]{:S(2)}) collective-permute-start(f32[32,4]{0,1:T(4,128)S(1)} %slice_select_fusion.2), channel_id=1, source_target_pairs={{0,8},{2,10},{4,12},{6,14},{8,0},{10,2},{12,4},{14,6},{1,9},{3,11}... | collective-permute-start | bytes 1544 | tf_op jit(solution)/shard_map/ppermute | solution.py:267
  68.8 3.6 %collective-permute-start.13 = (f32[16,4]{0,1:T(4,128)S(1)}, f32[16,4]{0,1:T(4,128)S(1)}, u32[]{:S(2)}, u32[]{:S(2)}) collective-permute-start(f32[16,4]{0,1:T(4,128)S(1)} %slice_select_fusion.1), channel_id=1, source_target_pairs={{0,4},{2,6},{4,0},{6,2},{8,12},{10,14},{12,8},{14,10},{1,5},{3,7},... | collective-permute-start | bytes 776 | tf_op jit(solution)/shard_map/ppermute | solution.py:267
  72.6 3.6 %collective-permute-start.14 = (f32[8,4]{0,1:T(4,128)S(1)}, f32[8,4]{0,1:T(4,128)S(1)}, u32[]{:S(2)}, u32[]{:S(2)}) collective-permute-start(f32[8,4]{0,1:T(4,128)S(1)} %slice_select_fusion), channel_id=1, source_target_pairs={{0,2},{2,0},{4,6},{6,4},{8,10},{10,8},{12,14},{14,12},{1,3},{3,1},... | collective-permute-start | bytes 392 | tf_op jit(solution)/shard_map/ppermute | solution.py:267
  76.2 1.2 %collective-permute-start.15 = (f32[8,4]{0,1:T(4,128)S(1)}, f32[8,4]{0,1:T(4,128)S(1)}, u32[]{:S(2)}, u32[]{:S(2)}) collective-permute-start(f32[8,4]{0,1:T(4,128)S(1)} %select_add_fusion), channel_id=1, source_target_pairs={{0,1},{1,0},{2,3},{3,2},{4,5},{5,4},{6,7},{7,6},{8,9},{9,8},{10,11... | collective-permute-start | bytes 392 | tf_op jit(solution)/shard_map/ppermute | solution.py:277

commit v11 on v10

--- a/solution.py
+++ b/solution.py
@@ -214,9 +214,8 @@
 
 def exchange_y(rows, xlo, xhi):
     cells = xhi.shape[1]
-    corners = jnp.zeros((2,) + rows.shape[1:], rows.dtype)
-    corners = corners.at[0, 0].set(xlo[0, 0:1]).at[1, 0].set(xhi[0, cells - 1:cells])
-    message = jnp.concatenate([rows, corners])
+    corners = jnp.stack([xlo[0, 0:1], xhi[0, cells - 1:cells]])[:, None]
+    message = lax.dynamic_update_slice(rows, corners, (7, 0, 0, 0))
     if lax.axis_size("gy") == 2:
         return shifted(message, "gy", 1)
     before = shifted(message, "gy", 1)
@@ -284,7 +283,7 @@
     field_shape = jax.ShapeDtypeStruct(e_field.shape, f32)
     xlo_shape = jax.ShapeDtypeStruct((5, cells_y, depth), f32)
     xhi_shape = jax.ShapeDtypeStruct((2, cells_y, depth), f32)
-    rows_shape = jax.ShapeDtypeStruct((7, cells_x, 1, depth), f32)
+    rows_shape = jax.ShapeDtypeStruct((9, cells_x, 1, depth), f32)
     angle_count = angle_orders.shape[0]
     sums_shape = jax.ShapeDtypeStruct((2, 1, 2 * angle_count), f32)
     step_call = pl.pallas_call(

time: 78.7 us -> 90.1 us (1.14)
  local copies, waits for them, and re-layouts: 3.89 us -> 15.3 us
  waiting for transfers between devices: 21.3 us -> 23.9 us
  other arithmetic: 5.77 us -> 3.31 us
    pallas_call x0 -> x8, local copies, waits for them, and re-layouts: none -> 4.42 us  [the longest x6 3.31 us: local(): edge_call(elec, elec, elec, elec, magn, magn, magn, keep, keep, drive, dr...]
    ppermute x0 -> x6, local copies, waits for them, and re-layouts: none -> 3.95 us  [shifted(): return lax.ppermute(value, axis, pairs)]
    ppermute x12, waiting for transfers between devices: 8.5 us -> 11.4 us  [shifted(): return lax.ppermute(value, axis, pairs)]
    concatenate x4 -> x0, other arithmetic: 2.49 us -> none  [exchange_y(): message = jnp.concatenate([rows, corners])]
    dynamic_update_slice x0 -> x4, local copies, waits for them, and re-layouts: none -> 1.76 us  [exchange_y(): message = lax.dynamic_update_slice(rows, corners, (7, 0, 0, 0))]
    optimization_barrier x0 -> x2, local copies, waits for them, and re-layouts: none -> 1.32 us  [local(): keep, drive, xlo, xhi = lax.optimization_barrier((keep, drive, xlo, xhi))]
    unnamed x38 -> x28, local copies, waits for them, and re-layouts: 3.8 us -> 3.82 us
  transfers between devices with their start and end apart: 16 -> 16, of which waited for: 13 -> 11; matrix products, arithmetic and copies ran while one was open for 3% -> 8% of each run, Pallas kernels for 17% -> 15%
where the time goes in v11:
time: 90.1 us; the launch traced here: 89.6 us
  Pallas kernels  25.4 us (28%)
  waiting for transfers between devices  23.9 us (27%)
  starting transfers between devices  20.9 us (23%)
  local copies, waits for them, and re-layouts  15.3 us (17%)
  other arithmetic  3.31 us (4%)
    ppermute x12, starting transfers between devices, shifted(): return lax.ppermute(value, axis, pairs)  20.6 us
    pallas_call x4, Pallas kernels, local(): step_call(elec, magn, keep, drive, xlo, xhi, rows, basis)  15.1 us
    ppermute x3, waiting for transfers between devices, scatter_sum(): rows = keep + lax.ppermute(send, axis, pairs)  11.4 us
    ppermute x12, waiting for transfers between devices, shifted(): return lax.ppermute(value, axis, pairs)  11.4 us
    pallas_call x3, Pallas kernels, local(): edge_call(elec, elec, elec, elec, magn, magn, magn, keep, keep, drive, dr...  6.39 us
    ppermute x6, local copies, waits for them, and re-layouts, shifted(): return lax.ppermute(value, axis, pairs)  3.95 us
    unnamed x28, local copies, waits for them, and re-layouts  3.82 us
    pallas_call x6, local copies, waits for them, and re-layouts, local(): edge_call(elec, elec, elec, elec, magn, magn, magn, keep, keep, drive, dr...  3.31 us
  transfers between devices with their start and end apart: 16, of which 11 were waited for; matrix products, arithmetic and copies ran while one was open for 8% of the time, Pallas kernels for 15%

profile of v11, /device:TPU:0, one launch (start us, length us, event | category | flops | bytes accessed | tf_op | source)
XLA Modules:
  0.0 89.6 jit_solution(11121618605664720680)
XLA Ops:
  0.6 1.9 %shard_map.86 = (f32[5,64,128]{2,1,0:T(8,128)}, f32[2,64,128]{2,1,0:T(8,128)}, f32[9,8,1,128]{3,2,1,0:T(1,128)}) custom-call(f32[3,8,64,128]{3,2,1,0:T(8,128)} %e_last.3, f32[3,8,64,128]{3,2,1,0:T(8,128)} %e_last.3, f32[3,8,64,128]{3,2,1,0:T(8,128)} %h_last.3, f32[3,8,64,128]{3,2,1,0:T(8,128)} %e_last.3, f32[3,8,64,128]{3,2,1,0:T(8,128)} %e_last.3, ...), custom_call_target="tpu_custom_call" | custom-call | tf_op jit(solution)/shard_map/pallas_call | solution.py:318
  2.5 1.1 %copy.9 = f32[5,64,128]{2,0,1:T(8,128)S(1)} copy(f32[5,64,128]{2,1,0:T(8,128)} %get-tuple-element.37) | data formatting | bytes 327680 | tf_op jit(solution)/shard_map/pallas_call | solution.py:318
  3.5 3.0 %collective-permute-start = (f32[5,64,128]{2,0,1:T(8,128)S(1)}, f32[5,64,128]{2,0,1:T(8,128)S(1)}, u32[]{:S(2)}, u32[]{:S(2)}) collective-permute-start(f32[5,64,128]{2,0,1:T(8,128)S(1)} %copy.9), channel_id=1, source_target_pairs={{0,2},{2,4},{4,6},{6,8},{8,10},{10,12},{12,14},{14,0},{1,3},{3,5},... | collective-permute-start | bytes 491528 | tf_op jit(solution)/shard_map/ppermute | solution.py:21
  6.6 3.1 %collective-permute-start.1 = (f32[2,64,128]{2,0,1:T(2,128)S(1)}, f32[2,64,128]{2,0,1:T(2,128)S(1)}, u32[]{:S(2)}, u32[]{:S(2)}) collective-permute-start(f32[2,64,128]{2,0,1:T(2,128)S(1)} %copy.10), channel_id=1, source_target_pairs={{0,14},{2,0},{4,2},{6,4},{8,6},{10,8},{12,10},{14,12},{1,15},{3,1}... | collective-permute-start | bytes 196616 | tf_op jit(solution)/shard_map/ppermute | solution.py:21
  9.7 0.7 copy-done.12
  10.4 0.1 multiply_multiply_fusion
  10.5 0.1 multiply_multiply_fusion.1
  10.6 1.1 %fusion.4 = (f32[64,8,64]{2,0,1:T(8,128)S(1)}, f32[64,8,64]{2,0,1:T(8,128)S(1)}) fusion(s32[64,64]{1,0:T(8,128)S(1)} %multiply_multiply_fusion, s32[64,8]{0,1:T(8,128)S(1)} %multiply_multiply_fusion.1), kind=kLoop, calls=%fused_computation.10 | loop fusion | flops 458752 | bytes 280576 | tf_op jit(solution)/shard_map/cos | solution.py:241
  11.7 2.0 %shard_map.85 = (f32[8,64,128]{2,1,0:T(8,128)}, f32[8,64,128]{2,1,0:T(8,128)}) custom-call(f32[6]{0:T(128)} %eps_ref.1, f32[6]{0:T(128)} %sigma_ref.1, s32[8,64,128]{2,1,0:T(8,128)} %mat_ref.1), custom_call_target="tpu_custom_call" | custom-call | tf_op jit(solution)/shard_map/pallas_call | solution.py:43
  13.7 2.8 %collective-permute-done.1 = f32[2,64,128]{2,0,1:T(2,128)S(1)} collective-permute-done((f32[2,64,128]{2,0,1:T(2,128)S(1)}, f32[2,64,128]{2,0,1:T(2,128)S(1)}, u32[]{:S(2)}, u32[]{:S(2)}) %collective-permute-start.1) | collective-permute-done | bytes 65568 | tf_op jit(solution)/shard_map/ppermute | solution.py:21
  16.6 0.1 collective-permute-start.2
  16.7 0.8 maximum_bitcast_fusion.basis_ref
  17.5 0.7 copy.11.xlo_ref
  18.2 0.6 copy.12.xhi_ref
  18.8 0.6 copy-done
  19.4 2.1 %shard_map.88 = (f32[5,64,128]{2,1,0:T(8,128)}, f32[2,64,128]{2,1,0:T(8,128)}) custom-call(f32[3,8,64,128]{3,2,1,0:T(8,128)} %e_last.3, f32[3,8,64,128]{3,2,1,0:T(8,128)} %e_last.3, f32[3,8,64,128]{3,2,1,0:T(8,128)} %e_last.3, f32[3,8,64,128]{3,2,1,0:T(8,128)} %e_last.3, f32[3,8,64,128]{3,2,1,0:T(8,128)} %h_last.3, f32[3,8,64,128]{3,2,1,0:T(8,128)} %h_last.3, ...), custom_call_target="tpu_custom_call" | custom-call | tf_op jit(solution)/shard_map/pallas_call | solution.py:338
  21.6 1.1 %copy.15 = f32[5,64,128]{2,0,1:T(8,128)S(1)} copy(f32[5,64,128]{2,1,0:T(8,128)} %get-tuple-element.48) | data formatting | bytes 327680 | tf_op jit(solution)/shard_map/pallas_call | solution.py:338
  22.6 0.1 collective-permute-start.3
  22.7 4.7 %collective-permute-start.4 = (f32[2,64,128]{2,0,1:T(2,128)S(1)}, f32[2,64,128]{2,0,1:T(2,128)S(1)}, u32[]{:S(2)}, u32[]{:S(2)}) collective-permute-start(f32[2,64,128]{2,0,1:T(2,128)S(1)} %copy.16), channel_id=1, source_target_pairs={{0,14},{2,0},{4,2},{6,4},{8,6},{10,8},{12,10},{14,12},{1,15},{3,1}... | collective-permute-start | bytes 196616 | tf_op jit(solution)/shard_map/ppermute | solution.py:21
  27.5 3.8 %shard_map.87 = (f32[3,8,64,128]{3,2,1,0:T(8,128)}, f32[3,8,64,128]{3,2,1,0:T(8,128)}, f32[9,8,1,128]{3,2,1,0:T(1,128)}, f32[2,1,128]{2,1,0:T(1,128)}) custom-call(f32[3,8,64,128]{3,2,1,0:T(8,128)} %e_last.3, f32[3,8,64,128]{3,2,1,0:T(8,128)} %h_last.3, f32[8,64,128]{2,1,0:T(8,128)} %get-tuple-element.39.keep_ref.keep_first.keep_last, ...), custom_call_target="tpu_custom_call" | custom-call | tf_op jit(solution)/shard_map/pallas_call | solution.py:342
  31.3 2.8 %collective-permute-done.3 = f32[5,64,128]{2,0,1:T(8,128)S(1)} collective-permute-done((f32[5,64,128]{2,0,1:T(8,128)S(1)}, f32[5,64,128]{2,0,1:T(8,128)S(1)}, u32[]{:S(2)}, u32[]{:S(2)}) %collective-permute-start.3) | collective-permute-done | bytes 163872 | tf_op jit(solution)/shard_map/ppermute | solution.py:21
  34.1 0.6 constant_dynamic-update-slice_fusion.2
  34.7 0.6 copy.18.xhi_ref
  35.3 0.7 copy.17.xlo_ref
  36.0 0.1 collective-permute-done.5.y_ref
  36.1 0.6 copy-done.1
  36.7 2.1 %shard_map.90 = (f32[5,64,128]{2,1,0:T(8,128)}, f32[2,64,128]{2,1,0:T(8,128)}) custom-call(f32[3,8,64,128]{3,2,1,0:T(8,128)} %get-tuple-element.46.e_ref.e_first.e_second.e_penult.e_last, f32[3,8,64,128]{3,2,1,0:T(8,128)} %get-tuple-element.46.e_ref.e_first.e_second.e_penult.e_last, ...), custom_call_target="tpu_custom_call" | custom-call | tf_op jit(solution)/shard_map/pallas_call | solution.py:338
  38.9 1.1 %copy.21 = f32[5,64,128]{2,0,1:T(8,128)S(1)} copy(f32[5,64,128]{2,1,0:T(8,128)} %get-tuple-element.53) | data formatting | bytes 327680 | tf_op jit(solution)/shard_map/pallas_call | solution.py:338
  39.9 0.1 collective-permute-start.6
  40.0 4.7 %collective-permute-start.7 = (f32[2,64,128]{2,0,1:T(2,128)S(1)}, f32[2,64,128]{2,0,1:T(2,128)S(1)}, u32[]{:S(2)}, u32[]{:S(2)}) collective-permute-start(f32[2,64,128]{2,0,1:T(2,128)S(1)} %copy.22), channel_id=1, source_target_pairs={{0,14},{2,0},{4,2},{6,4},{8,6},{10,8},{12,10},{14,12},{1,15},{3,1}... | collective-permute-start | bytes 196616 | tf_op jit(solution)/shard_map/ppermute | solution.py:21
  44.8 3.8 %shard_map.89 = (f32[3,8,64,128]{3,2,1,0:T(8,128)}, f32[3,8,64,128]{3,2,1,0:T(8,128)}, f32[9,8,1,128]{3,2,1,0:T(1,128)}, f32[2,1,128]{2,1,0:T(1,128)}) custom-call(f32[3,8,64,128]{3,2,1,0:T(8,128)} %get-tuple-element.46.e_ref.e_first.e_second.e_penult.e_last, f32[3,8,64,128]{3,2,1,0:T(8,128)} %get-tuple-element.47.h_ref.h_first.h_penult.h_last, ...), custom_call_target="tpu_custom_call" | custom-call | tf_op jit(solution)/shard_map/pallas_call | solution.py:342
  48.6 2.7 %collective-permute-done.6 = f32[5,64,128]{2,0,1:T(8,128)S(1)} collective-permute-done((f32[5,64,128]{2,0,1:T(8,128)S(1)}, f32[5,64,128]{2,0,1:T(8,128)S(1)}, u32[]{:S(2)}, u32[]{:S(2)}) %collective-permute-start.6) | collective-permute-done | bytes 163872 | tf_op jit(solution)/shard_map/ppermute | solution.py:21
  51.3 0.6 constant_dynamic-update-slice_fusion.1
  51.9 0.6 copy.24.xhi_ref
  52.5 0.7 copy.23.xlo_ref
  53.2 0.1 collective-permute-done.8.y_ref
  53.3 0.6 copy-done.2
  53.9 2.1 %shard_map.92 = (f32[5,64,128]{2,1,0:T(8,128)}, f32[2,64,128]{2,1,0:T(8,128)}) custom-call(f32[3,8,64,128]{3,2,1,0:T(8,128)} %get-tuple-element.51.e_ref.e_first.e_second.e_penult.e_last, f32[3,8,64,128]{3,2,1,0:T(8,128)} %get-tuple-element.51.e_ref.e_first.e_second.e_penult.e_last, ...), custom_call_target="tpu_custom_call" | custom-call | tf_op jit(solution)/shard_map/pallas_call | solution.py:338
  56.1 1.1 %copy.27 = f32[5,64,128]{2,0,1:T(8,128)S(1)} copy(f32[5,64,128]{2,1,0:T(8,128)} %get-tuple-element.58) | data formatting | bytes 327680 | tf_op jit(solution)/shard_map/pallas_call | solution.py:338
  57.1 0.1 collective-permute-start.9
  57.3 4.7 %collective-permute-start.10 = (f32[2,64,128]{2,0,1:T(2,128)S(1)}, f32[2,64,128]{2,0,1:T(2,128)S(1)}, u32[]{:S(2)}, u32[]{:S(2)}) collective-permute-start(f32[2,64,128]{2,0,1:T(2,128)S(1)} %copy.28), channel_id=1, source_target_pairs={{0,14},{2,0},{4,2},{6,4},{8,6},{10,8},{12,10},{14,12},{1,15},{3,1}... | collective-permute-start | bytes 196616 | tf_op jit(solution)/shard_map/ppermute | solution.py:21
  62.0 3.8 %shard_map.91 = (f32[3,8,64,128]{3,2,1,0:T(8,128)}, f32[3,8,64,128]{3,2,1,0:T(8,128)}, f32[9,8,1,128]{3,2,1,0:T(1,128)}, f32[2,1,128]{2,1,0:T(1,128)}) custom-call(f32[3,8,64,128]{3,2,1,0:T(8,128)} %get-tuple-element.51.e_ref.e_first.e_second.e_penult.e_last, f32[3,8,64,128]{3,2,1,0:T(8,128)} %get-tuple-element.52.h_ref.h_first.h_penult.h_last, ...), custom_call_target="tpu_custom_call" | custom-call | tf_op jit(solution)/shard_map/pallas_call | solution.py:342
  65.8 2.7 %collective-permute-done.9 = f32[5,64,128]{2,0,1:T(8,128)S(1)} collective-permute-done((f32[5,64,128]{2,0,1:T(8,128)S(1)}, f32[5,64,128]{2,0,1:T(8,128)S(1)}, u32[]{:S(2)}, u32[]{:S(2)}) %collective-permute-start.9) | collective-permute-done | bytes 163872 | tf_op jit(solution)/shard_map/ppermute | solution.py:21
  68.5 0.6 constant_dynamic-update-slice_fusion
  69.1 0.6 copy.30.xhi_ref
  69.7 0.7 copy.29.xlo_ref
  70.4 0.1 collective-permute-done.11.y_ref
  70.5 0.6 copy-done.7
  71.1 3.8 %shard_map.93 = (f32[3,8,64,128]{3,2,1,0:T(8,128)}, f32[3,8,64,128]{3,2,1,0:T(8,128)}, f32[9,8,1,128]{3,2,1,0:T(1,128)}, f32[2,1,128]{2,1,0:T(1,128)}) custom-call(f32[3,8,64,128]{3,2,1,0:T(8,128)} %get-tuple-element.56.e_ref, f32[3,8,64,128]{3,2,1,0:T(8,128)} %get-tuple-element.57.h_ref, f32[8,64,128]{2,1,0:T(8,128)} %get-tuple-element.39.keep_ref.keep_first.keep_last, ...), custom_call_target="tpu_custom_call" | custom-call | tf_op jit(solution)/shard_map/pallas_call | solution.py:342
  74.9 0.6 copy-done.11
  75.6 0.1 add_bitcast_fusion.2
  75.7 0.1 add_bitcast_fusion.3
  75.8 0.1 slice_select_fusion.2
  75.8 0.3 collective-permute-start.12
  76.1 4.2 %collective-permute-done.12 = f32[32,4]{0,1:T(4,128)S(1)} collective-permute-done((f32[32,4]{0,1:T(4,128)S(1)}, f32[32,4]{0,1:T(4,128)S(1)}, u32[]{:S(2)}, u32[]{:S(2)}) %collective-permute-start.12) | collective-permute-done | bytes 544 | tf_op jit(solution)/shard_map/ppermute | solution.py:266
  80.3 0.1 select_add_fusion.2
  80.4 0.1 slice_select_fusion.1
  80.5 3.6 %collective-permute-done.13 = f32[16,4]{0,1:T(4,128)S(1)} collective-permute-done((f32[16,4]{0,1:T(4,128)S(1)}, f32[16,4]{0,1:T(4,128)S(1)}, u32[]{:S(2)}, u32[]{:S(2)}) %collective-permute-start.13) | collective-permute-done | bytes 288 | tf_op jit(solution)/shard_map/ppermute | solution.py:266
  84.1 0.1 select_add_fusion.1
  84.1 0.1 slice_select_fusion
  84.2 3.6 %collective-permute-done.14 = f32[8,4]{0,1:T(4,128)S(1)} collective-permute-done((f32[8,4]{0,1:T(4,128)S(1)}, f32[8,4]{0,1:T(4,128)S(1)}, u32[]{:S(2)}, u32[]{:S(2)}) %collective-permute-start.14) | collective-permute-done | bytes 160 | tf_op jit(solution)/shard_map/ppermute | solution.py:266
  87.8 0.1 select_add_fusion
  87.9 1.2 %collective-permute-done.15 = f32[8,4]{0,1:T(4,128)S(1)} collective-permute-done((f32[8,4]{0,1:T(4,128)S(1)}, f32[8,4]{0,1:T(4,128)S(1)}, u32[]{:S(2)}, u32[]{:S(2)}) %collective-permute-start.15) | collective-permute-done | bytes 160 | tf_op jit(solution)/shard_map/ppermute | solution.py:276
  89.0 0.6 add_multiply_fusion
  (54 shorter events, 0.4 us)
Async XLA Ops:
  2.5 4.1 %copy-start.3 = (f32[2,64,128]{2,1,0:T(8,128)S(1)}, f32[2,64,128]{2,1,0:T(8,128)}, u32[]{:S(2)}) copy-start(f32[2,64,128]{2,1,0:T(8,128)} %get-tuple-element.38) | copy-start | bytes 196612
  3.5 13.0 %collective-permute-start = (f32[5,64,128]{2,0,1:T(8,128)S(1)}, f32[5,64,128]{2,0,1:T(8,128)S(1)}, u32[]{:S(2)}, u32[]{:S(2)}) collective-permute-start(f32[5,64,128]{2,0,1:T(8,128)S(1)} %copy.9), channel_id=1, source_target_pairs={{0,2},{2,4},{4,6},{6,8},{8,10},{10,12},{12,14},{14,0},{1,3},{3,5},... | collective-permute-start | bytes 491528 | tf_op jit(solution)/shard_map/ppermute | solution.py:21
  6.6 9.9 %collective-permute-start.1 = (f32[2,64,128]{2,0,1:T(2,128)S(1)}, f32[2,64,128]{2,0,1:T(2,128)S(1)}, u32[]{:S(2)}, u32[]{:S(2)}) collective-permute-start(f32[2,64,128]{2,0,1:T(2,128)S(1)} %copy.10), channel_id=1, source_target_pairs={{0,14},{2,0},{4,2},{6,4},{8,6},{10,8},{12,10},{14,12},{1,15},{3,1}... | collective-permute-start | bytes 196616 | tf_op jit(solution)/shard_map/ppermute | solution.py:21
  9.7 0.7 copy-start.12
  11.7 4.9 %copy-start.13 = (f32[9,8,1,128]{3,2,1,0:T(1,128)S(1)}, f32[9,8,1,128]{3,2,1,0:T(1,128)}, u32[]{:S(2)}) copy-start(f32[9,8,1,128]{3,2,1,0:T(1,128)} %get-tuple-element.43) | copy-start | bytes 110596
  16.6 2.2 %collective-permute-start.2 = (f32[9,8,1,128]{3,2,1,0:T(1,128)S(1)}, f32[9,8,1,128]{3,2,1,0:T(1,128)S(1)}, u32[]{:S(2)}, u32[]{:S(2)}) collective-permute-start(f32[9,8,1,128]{3,2,1,0:T(1,128)S(1)} %constant_dynamic-update-slice_fusion.3), channel_id=1, source_target_pairs={{0,1},{1,0},{2,3},{3,2},{4,5},{5,4},{6,7},{7,6},{8,9},{9,8},{10,11... | collective-permute-start | bytes 110600 | tf_op jit(solution)/shard_map/ppermute | solution.py:21
  18.8 0.6 copy-start
  21.6 1.1 %copy-start.4 = (f32[2,64,128]{2,1,0:T(8,128)S(1)}, f32[2,64,128]{2,1,0:T(8,128)}, u32[]{:S(2)}) copy-start(f32[2,64,128]{2,1,0:T(8,128)} %get-tuple-element.49) | copy-start | bytes 196612
  22.6 11.5 %collective-permute-start.3 = (f32[5,64,128]{2,0,1:T(8,128)S(1)}, f32[5,64,128]{2,0,1:T(8,128)S(1)}, u32[]{:S(2)}, u32[]{:S(2)}) collective-permute-start(f32[5,64,128]{2,0,1:T(8,128)S(1)} %copy.15), channel_id=1, source_target_pairs={{0,2},{2,4},{4,6},{6,8},{8,10},{10,12},{12,14},{14,0},{1,3},{3,5},... | collective-permute-start | bytes 491528 | tf_op jit(solution)/shard_map/ppermute | solution.py:21
  22.7 8.5 %collective-permute-start.4 = (f32[2,64,128]{2,0,1:T(2,128)S(1)}, f32[2,64,128]{2,0,1:T(2,128)S(1)}, u32[]{:S(2)}, u32[]{:S(2)}) collective-permute-start(f32[2,64,128]{2,0,1:T(2,128)S(1)} %copy.16), channel_id=1, source_target_pairs={{0,14},{2,0},{4,2},{6,4},{8,6},{10,8},{12,10},{14,12},{1,15},{3,1}... | collective-permute-start | bytes 196616 | tf_op jit(solution)/shard_map/ppermute | solution.py:21
  34.7 1.4 %collective-permute-start.5 = (f32[9,8,1,128]{3,2,1,0:T(1,128)}, f32[9,8,1,128]{3,2,1,0:T(1,128)S(1)}, u32[]{:S(2)}, u32[]{:S(2)}) collective-permute-start(f32[9,8,1,128]{3,2,1,0:T(1,128)} %constant_dynamic-update-slice_fusion.2), channel_id=1, source_target_pairs={{0,1},{1,0},{2,3},{3,2},{4,5},{5,4},{6,7},{7,6},{8,9},{9,8},{10,11... | collective-permute-start | bytes 110600 | tf_op jit(solution)/shard_map/ppermute | solution.py:21
  36.1 0.6 copy-start.1
  38.8 1.1 %copy-start.5 = (f32[2,64,128]{2,1,0:T(8,128)S(1)}, f32[2,64,128]{2,1,0:T(8,128)}, u32[]{:S(2)}) copy-start(f32[2,64,128]{2,1,0:T(8,128)} %get-tuple-element.54) | copy-start | bytes 196612
  39.9 11.4 %collective-permute-start.6 = (f32[5,64,128]{2,0,1:T(8,128)S(1)}, f32[5,64,128]{2,0,1:T(8,128)S(1)}, u32[]{:S(2)}, u32[]{:S(2)}) collective-permute-start(f32[5,64,128]{2,0,1:T(8,128)S(1)} %copy.21), channel_id=1, source_target_pairs={{0,2},{2,4},{4,6},{6,8},{8,10},{10,12},{12,14},{14,0},{1,3},{3,5},... | collective-permute-start | bytes 491528 | tf_op jit(solution)/shard_map/ppermute | solution.py:21
  40.0 8.6 %collective-permute-start.7 = (f32[2,64,128]{2,0,1:T(2,128)S(1)}, f32[2,64,128]{2,0,1:T(2,128)S(1)}, u32[]{:S(2)}, u32[]{:S(2)}) collective-permute-start(f32[2,64,128]{2,0,1:T(2,128)S(1)} %copy.22), channel_id=1, source_target_pairs={{0,14},{2,0},{4,2},{6,4},{8,6},{10,8},{12,10},{14,12},{1,15},{3,1}... | collective-permute-start | bytes 196616 | tf_op jit(solution)/shard_map/ppermute | solution.py:21
  51.9 1.4 %collective-permute-start.8 = (f32[9,8,1,128]{3,2,1,0:T(1,128)}, f32[9,8,1,128]{3,2,1,0:T(1,128)S(1)}, u32[]{:S(2)}, u32[]{:S(2)}) collective-permute-start(f32[9,8,1,128]{3,2,1,0:T(1,128)} %constant_dynamic-update-slice_fusion.1), channel_id=1, source_target_pairs={{0,1},{1,0},{2,3},{3,2},{4,5},{5,4},{6,7},{7,6},{8,9},{9,8},{10,11... | collective-permute-start | bytes 110600 | tf_op jit(solution)/shard_map/ppermute | solution.py:21
  53.3 0.6 copy-start.2
  56.1 1.1 %copy-start.6 = (f32[2,64,128]{2,1,0:T(8,128)S(1)}, f32[2,64,128]{2,1,0:T(8,128)}, u32[]{:S(2)}) copy-start(f32[2,64,128]{2,1,0:T(8,128)} %get-tuple-element.59) | copy-start | bytes 196612
  57.1 11.4 %collective-permute-start.9 = (f32[5,64,128]{2,0,1:T(8,128)S(1)}, f32[5,64,128]{2,0,1:T(8,128)S(1)}, u32[]{:S(2)}, u32[]{:S(2)}) collective-permute-start(f32[5,64,128]{2,0,1:T(8,128)S(1)} %copy.27), channel_id=1, source_target_pairs={{0,2},{2,4},{4,6},{6,8},{8,10},{10,12},{12,14},{14,0},{1,3},{3,5},... | collective-permute-start | bytes 491528 | tf_op jit(solution)/shard_map/ppermute | solution.py:21
  57.3 8.5 %collective-permute-start.10 = (f32[2,64,128]{2,0,1:T(2,128)S(1)}, f32[2,64,128]{2,0,1:T(2,128)S(1)}, u32[]{:S(2)}, u32[]{:S(2)}) collective-permute-start(f32[2,64,128]{2,0,1:T(2,128)S(1)} %copy.28), channel_id=1, source_target_pairs={{0,14},{2,0},{4,2},{6,4},{8,6},{10,8},{12,10},{14,12},{1,15},{3,1}... | collective-permute-start | bytes 196616 | tf_op jit(solution)/shard_map/ppermute | solution.py:21
  69.1 1.4 %collective-permute-start.11 = (f32[9,8,1,128]{3,2,1,0:T(1,128)}, f32[9,8,1,128]{3,2,1,0:T(1,128)S(1)}, u32[]{:S(2)}, u32[]{:S(2)}) collective-permute-start(f32[9,8,1,128]{3,2,1,0:T(1,128)} %constant_dynamic-update-slice_fusion), channel_id=1, source_target_pairs={{0,1},{1,0},{2,3},{3,2},{4,5},{5,4},{6,7},{7,6},{8,9},{9,8},{10,11... | collective-permute-start | bytes 110600 | tf_op jit(solution)/shard_map/ppermute | solution.py:21
  70.5 0.6 copy-start.7
  74.9 0.7 copy-start.11
  74.9 0.7 copy-start.9
  74.9 0.7 copy-start.10
  74.9 0.7 copy-start.8
  75.8 4.5 %collective-permute-start.12 = (f32[32,4]{0,1:T(4,128)S(1)}, f32[32,4]{0,1:T(4,128)S(1)}, u32[]{:S(2)}, u32[]{:S(2)}) collective-permute-start(f32[32,4]{0,1:T(4,128)S(1)} %slice_select_fusion.2), channel_id=1, source_target_pairs={{0,8},{2,10},{4,12},{6,14},{8,0},{10,2},{12,4},{14,6},{1,9},{3,11}... | collective-permute-start | bytes 1544 | tf_op jit(solution)/shard_map/ppermute | solution.py:266
  80.5 3.6 %collective-permute-start.13 = (f32[16,4]{0,1:T(4,128)S(1)}, f32[16,4]{0,1:T(4,128)S(1)}, u32[]{:S(2)}, u32[]{:S(2)}) collective-permute-start(f32[16,4]{0,1:T(4,128)S(1)} %slice_select_fusion.1), channel_id=1, source_target_pairs={{0,4},{2,6},{4,0},{6,2},{8,12},{10,14},{12,8},{14,10},{1,5},{3,7},... | collective-permute-start | bytes 776 | tf_op jit(solution)/shard_map/ppermute | solution.py:266
  84.2 3.6 %collective-permute-start.14 = (f32[8,4]{0,1:T(4,128)S(1)}, f32[8,4]{0,1:T(4,128)S(1)}, u32[]{:S(2)}, u32[]{:S(2)}) collective-permute-start(f32[8,4]{0,1:T(4,128)S(1)} %slice_select_fusion), channel_id=1, source_target_pairs={{0,2},{2,0},{4,6},{6,4},{8,10},{10,8},{12,14},{14,12},{1,3},{3,1},... | collective-permute-start | bytes 392 | tf_op jit(solution)/shard_map/ppermute | solution.py:266
  87.9 1.2 %collective-permute-start.15 = (f32[8,4]{0,1:T(4,128)S(1)}, f32[8,4]{0,1:T(4,128)S(1)}, u32[]{:S(2)}, u32[]{:S(2)}) collective-permute-start(f32[8,4]{0,1:T(4,128)S(1)} %select_add_fusion), channel_id=1, source_target_pairs={{0,1},{1,0},{2,3},{3,2},{4,5},{5,4},{6,7},{7,6},{8,9},{9,8},{10,11... | collective-permute-start | bytes 392 | tf_op jit(solution)/shard_map/ppermute | solution.py:276

commit v12 on v10

--- a/solution.py
+++ b/solution.py
@@ -187,10 +187,14 @@
     xlo_out[4] = old[5]
 
 
-def _halo_kernel(e_first, e_last, h_last, e_top, e_bottom, h_bottom, xlo_out, xhi_out, y_out):
+def _halo_kernel(e_first, e_last, h_last, e_top, e_bottom, h_bottom, xlo_out, xhi_out, y_out,
+                 c1_out, c2_out):
     planes = e_top.shape[1]
     slab = e_top.shape[2]
     last = slice(slab - 1, slab)
+    cells = e_first.shape[2]
+    c1_out[...] = e_last[0, 0][0:1]
+    c2_out[...] = e_first[1, 0][cells - 1:cells]
     for x in range(planes):
         y_out[0, x] = e_bottom[0, x][last]
         y_out[1, x] = e_bottom[1, x][last]
@@ -206,6 +210,17 @@
     xlo_out[2] = e_last[2, 0]
     xlo_out[3] = h_last[1, 0]
     xlo_out[4] = h_last[2, 0]
+
+
+def diagonal(value, step_x, step_y):
+    count_x = lax.axis_size("gx")
+    count_y = lax.axis_size("gy")
+    pairs = []
+    for a in range(count_x):
+        for b in range(count_y):
+            target = ((a + step_x) % count_x) * count_y + (b + step_y) % count_y
+            pairs.append((a * count_y + b, target))
+    return lax.ppermute(value, ("gx", "gy"), pairs)
 
 
 def exchange_x(xlo, xhi):
@@ -316,18 +331,27 @@
     def row_slab(index):
         return pl.BlockSpec((comps, cells_x, slab, depth), lambda i: (0, 0, index, 0))
 
-    xlo, xhi, rows = pl.pallas_call(
+    corner_shape = jax.ShapeDtypeStruct((1, depth), f32)
+    xlo, xhi, rows, corner_1, corner_2 = pl.pallas_call(
         _halo_kernel,
-        out_shape=(xlo_shape, xhi_shape, rows_shape),
+        out_shape=(xlo_shape, xhi_shape, rows_shape, corner_shape, corner_shape),
         grid=(1,),
         in_specs=[field_plane(first), field_plane(last), field_plane(last),
                   row_slab(0), row_slab(slabs - 1), row_slab(slabs - 1)],
-        out_specs=(whole, whole, whole),
+        out_specs=(whole,) * 5,
     )(e_field, e_field, h_field, e_field, e_field, h_field)
     xlo, xhi = exchange_x(xlo, xhi)
+    if lax.axis_size("gy") == 2:
+        rows = shifted(rows, "gy", 1)
+    else:
+        rows = jnp.concatenate([shifted(rows[0:5], "gy", 1), shifted(rows[5:7], "gy", -1)])
+    corner_1 = diagonal(corner_1, 1, -1)
+    corner_2 = diagonal(corner_2, -1, 1)
     keep, drive = coefficients(material, eps_table, sigma_table)
     keep, drive, xlo, xhi = lax.optimization_barrier((keep, drive, xlo, xhi))
-    rows = exchange_y(rows, xlo, xhi)
+    corners = jnp.zeros((2,) + rows.shape[1:], f32)
+    corners = corners.at[0, 0].set(corner_1).at[1, 0].set(corner_2)
+    rows = jnp.concatenate([rows, corners])
     basis = trig_basis(angle_orders, cells_x, cells_y)
     basis = basis.reshape(2 * angle_count, cells_x, cells_y).transpose(1, 0, 2)
     basis, rows = lax.optimization_barrier((basis, rows))

time: 78.7 us -> 82.5 us (1.048)
  starting transfers between devices: 20.9 us -> 24.5 us
  waiting for transfers between devices: 21.3 us -> 20.2 us
    ppermute x0 -> x2, starting transfers between devices: none -> 3.83 us  [diagonal(): return lax.ppermute(value, ('gx', 'gy'), pairs)]
    ppermute x12, waiting for transfers between devices: 8.5 us -> 7.4 us  [shifted(): return lax.ppermute(value, axis, pairs)]
    concatenate x4 -> x3, other arithmetic: 2.49 us -> 2.45 us  [exchange_y(): message = jnp.concatenate([rows, corners])]
  transfers between devices with their start and end apart: 16 -> 18, of which waited for: 13 -> 11; matrix products, arithmetic and copies ran while one was open for 3% -> 3% of each run, Pallas kernels for 17% -> 16%
where the time goes in v12:
time: 82.5 us; the launch traced here: 81.8 us
  Pallas kernels  25.4 us (31%)
  starting transfers between devices  24.5 us (30%)
  waiting for transfers between devices  20.2 us (24%)
  other arithmetic  6.39 us (8%)
  local copies, waits for them, and re-layouts  4.55 us (6%)
  between operations  0.84 us (1%)
    ppermute x12, starting transfers between devices, shifted(): return lax.ppermute(value, axis, pairs)  20.6 us
    pallas_call x4, Pallas kernels, local(): step_call(elec, magn, keep, drive, xlo, xhi, rows, basis)  15.1 us
    ppermute x3, waiting for transfers between devices, scatter_sum(): rows = keep + lax.ppermute(send, axis, pairs)  11.6 us
    ppermute x12, waiting for transfers between devices, shifted(): return lax.ppermute(value, axis, pairs)  7.4 us
    pallas_call x3, Pallas kernels, local(): edge_call(elec, elec, elec, elec, magn, magn, magn, keep, keep, drive, dr...  6.42 us
    unnamed x38, local copies, waits for them, and re-layouts  4.47 us
    ppermute x2, starting transfers between devices, diagonal(): return lax.ppermute(value, ('gx', 'gy'), pairs)  3.83 us
    concatenate x3, other arithmetic, exchange_y(): message = jnp.concatenate([rows, corners])  2.45 us
  transfers between devices with their start and end apart: 18, of which 11 were waited for; matrix products, arithmetic and copies ran while one was open for 3% of the time, Pallas kernels for 16%

profile of v12, /device:TPU:0, one launch (start us, length us, event | category | flops | bytes accessed | tf_op | source)
XLA Modules:
  0.0 81.8 jit_solution(9430337075784656181)
XLA Ops:
  0.6 1.9 %shard_map.86 = (f32[5,64,128]{2,1,0:T(8,128)}, f32[2,64,128]{2,1,0:T(8,128)}, f32[7,8,1,128]{3,2,1,0:T(1,128)}, f32[1,128]{1,0:T(1,128)}, f32[1,128]{1,0:T(1,128)}) custom-call(f32[3,8,64,128]{3,2,1,0:T(8,128)} %e_last.3, f32[3,8,64,128]{3,2,1,0:T(8,128)} %e_last.3, f32[3,8,64,128]{3,2,1,0:T(8,128)} %h_last.3, f32[3,8,64,128]{3,2,1,0:T(8,128)} %e_last.3, ...), custom_call_target="tpu_custom_call" | custom-call | tf_op jit(solution)/shard_map/pallas_call | solution.py:335
  2.5 3.0 %collective-permute-start = (f32[5,64,128]{2,1,0:T(8,128)}, f32[5,64,128]{2,1,0:T(8,128)S(1)}, u32[]{:S(2)}, u32[]{:S(2)}) collective-permute-start(f32[5,64,128]{2,1,0:T(8,128)} %get-tuple-element.135), channel_id=1, source_target_pairs={{0,2},{2,4},{4,6},{6,8},{8,10},{10,12},{12,14},{14,0},{1,3},{3,5},... | collective-permute-start | bytes 491528 | tf_op jit(solution)/shard_map/ppermute | solution.py:21
  5.5 3.1 %collective-permute-start.1 = (f32[2,64,128]{2,1,0:T(8,128)}, f32[2,64,128]{2,1,0:T(8,128)S(1)}, u32[]{:S(2)}, u32[]{:S(2)}) collective-permute-start(f32[2,64,128]{2,1,0:T(8,128)} %get-tuple-element.136), channel_id=1, source_target_pairs={{0,14},{2,0},{4,2},{6,4},{8,6},{10,8},{12,10},{14,12},{1,15},{3,1}... | collective-permute-start | bytes 196616 | tf_op jit(solution)/shard_map/ppermute | solution.py:21
  8.6 0.6 copy-done.17
  9.2 3.8 %collective-permute-start.4 = (f32[1,128]{1,0:T(1,128)S(1)}, f32[1,128]{1,0:T(1,128)S(1)}, u32[]{:S(2)}, u32[]{:S(2)}) collective-permute-start(f32[1,128]{1,0:T(1,128)S(1)} %copy-done.17), channel_id=1, source_target_pairs={{0,15},{1,14},{2,1},{3,0},{4,3},{5,2},{6,5},{7,4},{8,7},{9,6},{10,... | collective-permute-start | bytes 1544 | tf_op jit(solution)/shard_map/ppermute | solution.py:223
  13.0 0.7 copy-done.15
  13.7 0.1 multiply_multiply_fusion
  13.8 0.1 multiply_multiply_fusion.1
  13.9 1.1 %fusion.4 = (f32[64,8,64]{2,0,1:T(8,128)S(1)}, f32[64,8,64]{2,0,1:T(8,128)S(1)}) fusion(s32[64,64]{1,0:T(8,128)S(1)} %multiply_multiply_fusion, s32[64,8]{0,1:T(8,128)S(1)} %multiply_multiply_fusion.1), kind=kLoop, calls=%fused_computation.10 | loop fusion | flops 458752 | bytes 280576 | tf_op jit(solution)/shard_map/cos | solution.py:257
  15.0 0.8 %maximum_bitcast_fusion.basis_ref = f32[8,128,64]{2,1,0:T(8,128)} fusion(f32[64,8,64]{2,0,1:T(8,128)S(1)} %get-tuple-element.168, f32[64,8,64]{2,0,1:T(8,128)S(1)} %get-tuple-element.167), kind=kLoop, calls=%fused_computation | loop fusion | flops 65536 | bytes 524288 | tf_op jit(solution)/shard_map/transpose | solution.py:356
  15.8 2.0 %shard_map.85 = (f32[8,64,128]{2,1,0:T(8,128)}, f32[8,64,128]{2,1,0:T(8,128)}) custom-call(f32[6]{0:T(128)} %eps_ref.1, f32[6]{0:T(128)} %sigma_ref.1, s32[8,64,128]{2,1,0:T(8,128)} %mat_ref.1), custom_call_target="tpu_custom_call" | custom-call | tf_op jit(solution)/shard_map/pallas_call | solution.py:43
  17.8 0.0 collective-permute-done.3
  17.9 0.0 collective-permute-done.2
  17.9 0.6 pad_maximum_fusion.y_ref
  18.5 0.0 collective-permute-done.xlo_ref
  18.5 0.6 copy-done.3
  19.1 0.1 copy-done
  19.2 2.1 %shard_map.88 = (f32[5,64,128]{2,1,0:T(8,128)}, f32[2,64,128]{2,1,0:T(8,128)}) custom-call(f32[3,8,64,128]{3,2,1,0:T(8,128)} %e_last.3, f32[3,8,64,128]{3,2,1,0:T(8,128)} %e_last.3, f32[3,8,64,128]{3,2,1,0:T(8,128)} %e_last.3, f32[3,8,64,128]{3,2,1,0:T(8,128)} %e_last.3, f32[3,8,64,128]{3,2,1,0:T(8,128)} %h_last.3, f32[3,8,64,128]{3,2,1,0:T(8,128)} %h_last.3, ...), custom_call_target="tpu_custom_call" | custom-call | tf_op jit(solution)/shard_map/pallas_call | solution.py:363
  21.4 0.1 collective-permute-start.5
  21.4 3.8 %shard_map.87 = (f32[3,8,64,128]{3,2,1,0:T(8,128)}, f32[3,8,64,128]{3,2,1,0:T(8,128)}, f32[7,8,1,128]{3,2,1,0:T(1,128)}, f32[2,1,128]{2,1,0:T(1,128)}) custom-call(f32[3,8,64,128]{3,2,1,0:T(8,128)} %e_last.3, f32[3,8,64,128]{3,2,1,0:T(8,128)} %h_last.3, f32[8,64,128]{2,1,0:T(8,128)} %get-tuple-element.137.keep_ref.keep_first.keep_last, ...), custom_call_target="tpu_custom_call" | custom-call | tf_op jit(solution)/shard_map/pallas_call | solution.py:367
  25.2 4.8 %collective-permute-start.6 = (f32[2,64,128]{2,1,0:T(8,128)S(1)}, f32[2,64,128]{2,1,0:T(8,128)S(1)}, u32[]{:S(2)}, u32[]{:S(2)}) collective-permute-start(f32[2,64,128]{2,1,0:T(8,128)S(1)} %copy-done.16), channel_id=1, source_target_pairs={{0,14},{2,0},{4,2},{6,4},{8,6},{10,8},{12,10},{14,12},{1,15},{3,1}... | collective-permute-start | bytes 196616 | tf_op jit(solution)/shard_map/ppermute | solution.py:21
  29.9 1.1 %collective-permute-done.5.xlo_ref = f32[5,64,128]{2,1,0:T(8,128)S(1)} collective-permute-done((f32[5,64,128]{2,1,0:T(8,128)}, f32[5,64,128]{2,1,0:T(8,128)S(1)}, u32[]{:S(2)}, u32[]{:S(2)}) %collective-permute-start.5) | collective-permute-done | bytes 163872 | tf_op jit(solution)/shard_map/ppermute | solution.py:21
  31.0 1.3 %collective-permute-done.6.xhi_ref = f32[2,64,128]{2,1,0:T(8,128)S(1)} collective-permute-done((f32[2,64,128]{2,1,0:T(8,128)S(1)}, f32[2,64,128]{2,1,0:T(8,128)S(1)}, u32[]{:S(2)}, u32[]{:S(2)}) %collective-permute-start.6) | collective-permute-done | bytes 65568 | tf_op jit(solution)/shard_map/ppermute | solution.py:21
  32.3 0.8 pad_maximum_fusion.1
  33.1 0.1 collective-permute-start.7
  33.3 1.1 %collective-permute-done.7.y_ref = f32[9,8,1,128]{3,2,1,0:T(1,128)S(1)} collective-permute-done((f32[9,8,1,128]{3,2,1,0:T(1,128)S(1)}, f32[9,8,1,128]{3,2,1,0:T(1,128)S(1)}, u32[]{:S(2)}, u32[]{:S(2)}) %collective-permute-start.7) | collective-permute-done | bytes 36896 | tf_op jit(solution)/shard_map/ppermute | solution.py:21
  34.4 0.6 copy-done.7
  35.0 2.1 %shard_map.90 = (f32[5,64,128]{2,1,0:T(8,128)}, f32[2,64,128]{2,1,0:T(8,128)}) custom-call(f32[3,8,64,128]{3,2,1,0:T(8,128)} %get-tuple-element.146.e_ref.e_first.e_second.e_penult.e_last, f32[3,8,64,128]{3,2,1,0:T(8,128)} %get-tuple-element.146.e_ref.e_first.e_second.e_penult.e_last, ...), custom_call_target="tpu_custom_call" | custom-call | tf_op jit(solution)/shard_map/pallas_call | solution.py:363
  37.2 0.0 collective-permute-start.8
  37.2 4.7 %collective-permute-start.9 = (f32[2,64,128]{2,1,0:T(8,128)}, f32[2,64,128]{2,1,0:T(8,128)S(1)}, u32[]{:S(2)}, u32[]{:S(2)}) collective-permute-start(f32[2,64,128]{2,1,0:T(8,128)} %get-tuple-element.154), channel_id=1, source_target_pairs={{0,14},{2,0},{4,2},{6,4},{8,6},{10,8},{12,10},{14,12},{1,15},{3,1}... | collective-permute-start | bytes 196616 | tf_op jit(solution)/shard_map/ppermute | solution.py:21
  41.9 3.8 %shard_map.89 = (f32[3,8,64,128]{3,2,1,0:T(8,128)}, f32[3,8,64,128]{3,2,1,0:T(8,128)}, f32[7,8,1,128]{3,2,1,0:T(1,128)}, f32[2,1,128]{2,1,0:T(1,128)}) custom-call(f32[3,8,64,128]{3,2,1,0:T(8,128)} %get-tuple-element.146.e_ref.e_first.e_second.e_penult.e_last, f32[3,8,64,128]{3,2,1,0:T(8,128)} %get-tuple-element.147.h_ref.h_first.h_penult.h_last, ...), custom_call_target="tpu_custom_call" | custom-call | tf_op jit(solution)/shard_map/pallas_call | solution.py:367
  45.7 0.8 collective-permute-done.8.xlo_ref
  46.5 0.8 %pad_maximum_fusion.2 = f32[9,8,1,128]{3,2,1,0:T(1,128)S(1)} fusion(f32[2,8,1,128]{3,2,1,0:T(1,128)S(1)} %constant_dynamic-update-slice_fusion.1, f32[7,8,1,128]{3,2,1,0:T(1,128)} %get-tuple-element.155), kind=kLoop, calls=%fused_computation.13 | loop fusion | flops 9216 | bytes 73728 | tf_op jit(solution)/shard_map/concatenate | solution.py:234
  47.4 0.1 collective-permute-start.10
  47.5 1.2 %collective-permute-done.10.y_ref = f32[9,8,1,128]{3,2,1,0:T(1,128)S(1)} collective-permute-done((f32[9,8,1,128]{3,2,1,0:T(1,128)S(1)}, f32[9,8,1,128]{3,2,1,0:T(1,128)S(1)}, u32[]{:S(2)}, u32[]{:S(2)}) %collective-permute-start.10) | collective-permute-done | bytes 36896 | tf_op jit(solution)/shard_map/ppermute | solution.py:21
  48.7 0.6 copy-done.8
  49.3 2.1 %shard_map.92 = (f32[5,64,128]{2,1,0:T(8,128)}, f32[2,64,128]{2,1,0:T(8,128)}) custom-call(f32[3,8,64,128]{3,2,1,0:T(8,128)} %get-tuple-element.151.e_ref.e_first.e_second.e_penult.e_last, f32[3,8,64,128]{3,2,1,0:T(8,128)} %get-tuple-element.151.e_ref.e_first.e_second.e_penult.e_last, ...), custom_call_target="tpu_custom_call" | custom-call | tf_op jit(solution)/shard_map/pallas_call | solution.py:363
  51.4 4.7 %collective-permute-start.12 = (f32[2,64,128]{2,1,0:T(8,128)}, f32[2,64,128]{2,1,0:T(8,128)S(1)}, u32[]{:S(2)}, u32[]{:S(2)}) collective-permute-start(f32[2,64,128]{2,1,0:T(8,128)} %get-tuple-element.159), channel_id=1, source_target_pairs={{0,14},{2,0},{4,2},{6,4},{8,6},{10,8},{12,10},{14,12},{1,15},{3,1}... | collective-permute-start | bytes 196616 | tf_op jit(solution)/shard_map/ppermute | solution.py:21
  56.1 3.8 %shard_map.91 = (f32[3,8,64,128]{3,2,1,0:T(8,128)}, f32[3,8,64,128]{3,2,1,0:T(8,128)}, f32[7,8,1,128]{3,2,1,0:T(1,128)}, f32[2,1,128]{2,1,0:T(1,128)}) custom-call(f32[3,8,64,128]{3,2,1,0:T(8,128)} %get-tuple-element.151.e_ref.e_first.e_second.e_penult.e_last, f32[3,8,64,128]{3,2,1,0:T(8,128)} %get-tuple-element.152.h_ref.h_first.h_penult.h_last, ...), custom_call_target="tpu_custom_call" | custom-call | tf_op jit(solution)/shard_map/pallas_call | solution.py:367
  59.9 0.7 collective-permute-done.11.xlo_ref
  60.6 0.8 %pad_maximum_fusion.3 = f32[9,8,1,128]{3,2,1,0:T(1,128)S(1)} fusion(f32[2,8,1,128]{3,2,1,0:T(1,128)S(1)} %constant_dynamic-update-slice_fusion, f32[7,8,1,128]{3,2,1,0:T(1,128)} %get-tuple-element.160), kind=kLoop, calls=%fused_computation.14 | loop fusion | flops 9216 | bytes 73728 | tf_op jit(solution)/shard_map/concatenate | solution.py:234
  61.4 0.1 collective-permute-start.13
  61.5 1.2 %collective-permute-done.13.y_ref = f32[9,8,1,128]{3,2,1,0:T(1,128)S(1)} collective-permute-done((f32[9,8,1,128]{3,2,1,0:T(1,128)S(1)}, f32[9,8,1,128]{3,2,1,0:T(1,128)S(1)}, u32[]{:S(2)}, u32[]{:S(2)}) %collective-permute-start.13) | collective-permute-done | bytes 36896 | tf_op jit(solution)/shard_map/ppermute | solution.py:21
  62.7 0.6 copy-done.10
  63.3 3.8 %shard_map.93 = (f32[3,8,64,128]{3,2,1,0:T(8,128)}, f32[3,8,64,128]{3,2,1,0:T(8,128)}, f32[7,8,1,128]{3,2,1,0:T(1,128)}, f32[2,1,128]{2,1,0:T(1,128)}) custom-call(f32[3,8,64,128]{3,2,1,0:T(8,128)} %get-tuple-element.156.e_ref, f32[3,8,64,128]{3,2,1,0:T(8,128)} %get-tuple-element.157.h_ref, f32[8,64,128]{2,1,0:T(8,128)} %get-tuple-element.137.keep_ref.keep_first.keep_last, ...), custom_call_target="tpu_custom_call" | custom-call | tf_op jit(solution)/shard_map/pallas_call | solution.py:367
  67.1 0.0 copy-start.11
  67.1 0.6 copy-done.14
  67.7 0.1 copy-done.12
  67.7 0.0 copy-done.13
  67.7 0.0 copy-done.11
  67.8 0.1 add_bitcast_fusion.2
  67.8 0.1 add_bitcast_fusion.3
  67.9 0.1 slice_select_fusion.2
  68.0 0.0 collective-permute-start.14
  68.0 4.5 %collective-permute-done.14 = f32[32,4]{0,1:T(4,128)S(1)} collective-permute-done((f32[32,4]{0,1:T(4,128)S(1)}, f32[32,4]{0,1:T(4,128)S(1)}, u32[]{:S(2)}, u32[]{:S(2)}) %collective-permute-start.14) | collective-permute-done | bytes 544 | tf_op jit(solution)/shard_map/ppermute | solution.py:282
  72.5 0.1 select_add_fusion.2
  72.6 0.1 slice_select_fusion.1
  72.7 3.6 %collective-permute-done.15 = f32[16,4]{0,1:T(4,128)S(1)} collective-permute-done((f32[16,4]{0,1:T(4,128)S(1)}, f32[16,4]{0,1:T(4,128)S(1)}, u32[]{:S(2)}, u32[]{:S(2)}) %collective-permute-start.15) | collective-permute-done | bytes 288 | tf_op jit(solution)/shard_map/ppermute | solution.py:282
  76.2 0.1 select_add_fusion.1
  76.3 0.1 slice_select_fusion
  76.4 3.6 %collective-permute-done.16 = f32[8,4]{0,1:T(4,128)S(1)} collective-permute-done((f32[8,4]{0,1:T(4,128)S(1)}, f32[8,4]{0,1:T(4,128)S(1)}, u32[]{:S(2)}, u32[]{:S(2)}) %collective-permute-start.16) | collective-permute-done | bytes 160 | tf_op jit(solution)/shard_map/ppermute | solution.py:282
  80.0 0.1 select_add_fusion
  80.1 1.2 %collective-permute-done.17 = f32[8,4]{0,1:T(4,128)S(1)} collective-permute-done((f32[8,4]{0,1:T(4,128)S(1)}, f32[8,4]{0,1:T(4,128)S(1)}, u32[]{:S(2)}, u32[]{:S(2)}) %collective-permute-start.17) | collective-permute-done | bytes 160 | tf_op jit(solution)/shard_map/ppermute | solution.py:292
  81.2 0.6 add_multiply_fusion
  (51 shorter events, 0.2 us)
Async XLA Ops:
  2.5 16.0 %collective-permute-start = (f32[5,64,128]{2,1,0:T(8,128)}, f32[5,64,128]{2,1,0:T(8,128)S(1)}, u32[]{:S(2)}, u32[]{:S(2)}) collective-permute-start(f32[5,64,128]{2,1,0:T(8,128)} %get-tuple-element.135), channel_id=1, source_target_pairs={{0,2},{2,4},{4,6},{6,8},{8,10},{10,12},{12,14},{14,0},{1,3},{3,5},... | collective-permute-start | bytes 491528 | tf_op jit(solution)/shard_map/ppermute | solution.py:21
  5.5 3.1 %copy-start.18 = (f32[1,128]{1,0:T(1,128)S(1)}, f32[1,128]{1,0:T(1,128)}, u32[]{:S(2)}) copy-start(f32[1,128]{1,0:T(1,128)} %get-tuple-element.142) | copy-start | bytes 1540
  5.5 13.1 %collective-permute-start.1 = (f32[2,64,128]{2,1,0:T(8,128)}, f32[2,64,128]{2,1,0:T(8,128)S(1)}, u32[]{:S(2)}, u32[]{:S(2)}) collective-permute-start(f32[2,64,128]{2,1,0:T(8,128)} %get-tuple-element.136), channel_id=1, source_target_pairs={{0,14},{2,0},{4,2},{6,4},{8,6},{10,8},{12,10},{14,12},{1,15},{3,1}... | collective-permute-start | bytes 196616 | tf_op jit(solution)/shard_map/ppermute | solution.py:21
  8.6 0.6 copy-start.17
  8.6 9.3 %collective-permute-start.3 = (f32[1,128]{1,0:T(1,128)S(1)}, f32[1,128]{1,0:T(1,128)S(1)}, u32[]{:S(2)}, u32[]{:S(2)}) collective-permute-start(f32[1,128]{1,0:T(1,128)S(1)} %copy-done.18), channel_id=1, source_target_pairs={{0,3},{1,2},{2,5},{3,4},{4,7},{5,6},{6,9},{7,8},{8,11},{9,10},{10,... | collective-permute-start | bytes 1544 | tf_op jit(solution)/shard_map/ppermute | solution.py:223
  9.2 8.7 %collective-permute-start.4 = (f32[1,128]{1,0:T(1,128)S(1)}, f32[1,128]{1,0:T(1,128)S(1)}, u32[]{:S(2)}, u32[]{:S(2)}) collective-permute-start(f32[1,128]{1,0:T(1,128)S(1)} %copy-done.17), channel_id=1, source_target_pairs={{0,15},{1,14},{2,1},{3,0},{4,3},{5,2},{6,5},{7,4},{8,7},{9,6},{10,... | collective-permute-start | bytes 1544 | tf_op jit(solution)/shard_map/ppermute | solution.py:223
  13.0 4.8 %collective-permute-start.2 = (f32[7,8,1,128]{3,2,1,0:T(1,128)}, f32[7,8,1,128]{3,2,1,0:T(1,128)S(1)}, u32[]{:S(2)}, u32[]{:S(2)}) collective-permute-start(f32[7,8,1,128]{3,2,1,0:T(1,128)} %get-tuple-element.141), channel_id=1, source_target_pairs={{0,1},{1,0},{2,3},{3,2},{4,5},{5,4},{6,7},{7,6},{8,9},{9,8},{10,11... | collective-permute-start | bytes 86024 | tf_op jit(solution)/shard_map/ppermute | solution.py:21
  13.0 0.7 copy-start.15
  18.5 0.6 copy-start.3
  18.5 0.7 copy-start
  21.4 3.8 %copy-start.16 = (f32[2,64,128]{2,1,0:T(8,128)S(1)}, f32[2,64,128]{2,1,0:T(8,128)}, u32[]{:S(2)}) copy-start(f32[2,64,128]{2,1,0:T(8,128)} %get-tuple-element.149) | copy-start | bytes 196612
  21.4 9.7 %collective-permute-start.5 = (f32[5,64,128]{2,1,0:T(8,128)}, f32[5,64,128]{2,1,0:T(8,128)S(1)}, u32[]{:S(2)}, u32[]{:S(2)}) collective-permute-start(f32[5,64,128]{2,1,0:T(8,128)} %get-tuple-element.148), channel_id=1, source_target_pairs={{0,2},{2,4},{4,6},{6,8},{8,10},{10,12},{12,14},{14,0},{1,3},{3,5},... | collective-permute-start | bytes 491528 | tf_op jit(solution)/shard_map/ppermute | solution.py:21
  25.2 7.1 %collective-permute-start.6 = (f32[2,64,128]{2,1,0:T(8,128)S(1)}, f32[2,64,128]{2,1,0:T(8,128)S(1)}, u32[]{:S(2)}, u32[]{:S(2)}) collective-permute-start(f32[2,64,128]{2,1,0:T(8,128)S(1)} %copy-done.16), channel_id=1, source_target_pairs={{0,14},{2,0},{4,2},{6,4},{8,6},{10,8},{12,10},{14,12},{1,15},{3,1}... | collective-permute-start | bytes 196616 | tf_op jit(solution)/shard_map/ppermute | solution.py:21
  31.0 3.4 %copy-start.2 = (f32[5,64,128]{2,1,0:T(8,128)}, f32[5,64,128]{2,1,0:T(8,128)S(1)}, u32[]{:S(2)}) copy-start(f32[5,64,128]{2,1,0:T(8,128)S(1)} %collective-permute-done.5.xlo_ref) | copy-start | bytes 491524
  32.3 2.1 %copy-start.5 = (f32[2,64,128]{2,1,0:T(8,128)}, f32[2,64,128]{2,1,0:T(8,128)S(1)}, u32[]{:S(2)}) copy-start(f32[2,64,128]{2,1,0:T(8,128)S(1)} %collective-permute-done.6.xhi_ref) | copy-start | bytes 196612
  33.1 1.3 %collective-permute-start.7 = (f32[9,8,1,128]{3,2,1,0:T(1,128)S(1)}, f32[9,8,1,128]{3,2,1,0:T(1,128)S(1)}, u32[]{:S(2)}, u32[]{:S(2)}) collective-permute-start(f32[9,8,1,128]{3,2,1,0:T(1,128)S(1)} %pad_maximum_fusion.1), channel_id=1, source_target_pairs={{0,1},{1,0},{2,3},{3,2},{4,5},{5,4},{6,7},{7,6},{8,9},{9,8},{10,11... | collective-permute-start | bytes 110600 | tf_op jit(solution)/shard_map/ppermute | solution.py:21
  34.4 0.6 copy-start.7
  37.2 9.3 %collective-permute-start.8 = (f32[5,64,128]{2,1,0:T(8,128)}, f32[5,64,128]{2,1,0:T(8,128)S(1)}, u32[]{:S(2)}, u32[]{:S(2)}) collective-permute-start(f32[5,64,128]{2,1,0:T(8,128)} %get-tuple-element.153), channel_id=1, source_target_pairs={{0,2},{2,4},{4,6},{6,8},{8,10},{10,12},{12,14},{14,0},{1,3},{3,5},... | collective-permute-start | bytes 491528 | tf_op jit(solution)/shard_map/ppermute | solution.py:21
  37.2 9.3 %collective-permute-start.9 = (f32[2,64,128]{2,1,0:T(8,128)}, f32[2,64,128]{2,1,0:T(8,128)S(1)}, u32[]{:S(2)}, u32[]{:S(2)}) collective-permute-start(f32[2,64,128]{2,1,0:T(8,128)} %get-tuple-element.154), channel_id=1, source_target_pairs={{0,14},{2,0},{4,2},{6,4},{8,6},{10,8},{12,10},{14,12},{1,15},{3,1}... | collective-permute-start | bytes 196616 | tf_op jit(solution)/shard_map/ppermute | solution.py:21
  46.5 2.2 %copy-start.1 = (f32[5,64,128]{2,1,0:T(8,128)}, f32[5,64,128]{2,1,0:T(8,128)S(1)}, u32[]{:S(2)}) copy-start(f32[5,64,128]{2,1,0:T(8,128)S(1)} %collective-permute-done.8.xlo_ref) | copy-start | bytes 491524
  46.5 2.1 %copy-start.4 = (f32[2,64,128]{2,1,0:T(8,128)}, f32[2,64,128]{2,1,0:T(8,128)S(1)}, u32[]{:S(2)}) copy-start(f32[2,64,128]{2,1,0:T(8,128)S(1)} %collective-permute-done.9.xhi_ref) | copy-start | bytes 196612
  47.4 1.3 %collective-permute-start.10 = (f32[9,8,1,128]{3,2,1,0:T(1,128)S(1)}, f32[9,8,1,128]{3,2,1,0:T(1,128)S(1)}, u32[]{:S(2)}, u32[]{:S(2)}) collective-permute-start(f32[9,8,1,128]{3,2,1,0:T(1,128)S(1)} %pad_maximum_fusion.2), channel_id=1, source_target_pairs={{0,1},{1,0},{2,3},{3,2},{4,5},{5,4},{6,7},{7,6},{8,9},{9,8},{10,11... | collective-permute-start | bytes 110600 | tf_op jit(solution)/shard_map/ppermute | solution.py:21
  48.7 0.6 copy-start.8
  51.4 9.2 %collective-permute-start.11 = (f32[5,64,128]{2,1,0:T(8,128)}, f32[5,64,128]{2,1,0:T(8,128)S(1)}, u32[]{:S(2)}, u32[]{:S(2)}) collective-permute-start(f32[5,64,128]{2,1,0:T(8,128)} %get-tuple-element.158), channel_id=1, source_target_pairs={{0,2},{2,4},{4,6},{6,8},{8,10},{10,12},{12,14},{14,0},{1,3},{3,5},... | collective-permute-start | bytes 491528 | tf_op jit(solution)/shard_map/ppermute | solution.py:21
  51.4 9.2 %collective-permute-start.12 = (f32[2,64,128]{2,1,0:T(8,128)}, f32[2,64,128]{2,1,0:T(8,128)S(1)}, u32[]{:S(2)}, u32[]{:S(2)}) collective-permute-start(f32[2,64,128]{2,1,0:T(8,128)} %get-tuple-element.159), channel_id=1, source_target_pairs={{0,14},{2,0},{4,2},{6,4},{8,6},{10,8},{12,10},{14,12},{1,15},{3,1}... | collective-permute-start | bytes 196616 | tf_op jit(solution)/shard_map/ppermute | solution.py:21
  60.6 2.2 %copy-start.6 = (f32[5,64,128]{2,1,0:T(8,128)}, f32[5,64,128]{2,1,0:T(8,128)S(1)}, u32[]{:S(2)}) copy-start(f32[5,64,128]{2,1,0:T(8,128)S(1)} %collective-permute-done.11.xlo_ref) | copy-start | bytes 491524
  60.6 2.1 %copy-start.9 = (f32[2,64,128]{2,1,0:T(8,128)}, f32[2,64,128]{2,1,0:T(8,128)S(1)}, u32[]{:S(2)}) copy-start(f32[2,64,128]{2,1,0:T(8,128)S(1)} %collective-permute-done.12.xhi_ref) | copy-start | bytes 196612
  61.4 1.3 %collective-permute-start.13 = (f32[9,8,1,128]{3,2,1,0:T(1,128)S(1)}, f32[9,8,1,128]{3,2,1,0:T(1,128)S(1)}, u32[]{:S(2)}, u32[]{:S(2)}) collective-permute-start(f32[9,8,1,128]{3,2,1,0:T(1,128)S(1)} %pad_maximum_fusion.3), channel_id=1, source_target_pairs={{0,1},{1,0},{2,3},{3,2},{4,5},{5,4},{6,7},{7,6},{8,9},{9,8},{10,11... | collective-permute-start | bytes 110600 | tf_op jit(solution)/shard_map/ppermute | solution.py:21
  62.7 0.6 copy-start.10
  67.1 0.6 copy-start.14
  67.1 0.7 copy-start.12
  67.1 0.7 copy-start.13
  67.1 0.7 copy-start.11
  68.0 4.5 %collective-permute-start.14 = (f32[32,4]{0,1:T(4,128)S(1)}, f32[32,4]{0,1:T(4,128)S(1)}, u32[]{:S(2)}, u32[]{:S(2)}) collective-permute-start(f32[32,4]{0,1:T(4,128)S(1)} %slice_select_fusion.2), channel_id=1, source_target_pairs={{0,8},{2,10},{4,12},{6,14},{8,0},{10,2},{12,4},{14,6},{1,9},{3,11}... | collective-permute-start | bytes 1544 | tf_op jit(solution)/shard_map/ppermute | solution.py:282
  72.7 3.6 %collective-permute-start.15 = (f32[16,4]{0,1:T(4,128)S(1)}, f32[16,4]{0,1:T(4,128)S(1)}, u32[]{:S(2)}, u32[]{:S(2)}) collective-permute-start(f32[16,4]{0,1:T(4,128)S(1)} %slice_select_fusion.1), channel_id=1, source_target_pairs={{0,4},{2,6},{4,0},{6,2},{8,12},{10,14},{12,8},{14,10},{1,5},{3,7},... | collective-permute-start | bytes 776 | tf_op jit(solution)/shard_map/ppermute | solution.py:282
  76.4 3.6 %collective-permute-start.16 = (f32[8,4]{0,1:T(4,128)S(1)}, f32[8,4]{0,1:T(4,128)S(1)}, u32[]{:S(2)}, u32[]{:S(2)}) collective-permute-start(f32[8,4]{0,1:T(4,128)S(1)} %slice_select_fusion), channel_id=1, source_target_pairs={{0,2},{2,0},{4,6},{6,4},{8,10},{10,8},{12,14},{14,12},{1,3},{3,1},... | collective-permute-start | bytes 392 | tf_op jit(solution)/shard_map/ppermute | solution.py:282
  80.1 1.2 %collective-permute-start.17 = (f32[8,4]{0,1:T(4,128)S(1)}, f32[8,4]{0,1:T(4,128)S(1)}, u32[]{:S(2)}, u32[]{:S(2)}) collective-permute-start(f32[8,4]{0,1:T(4,128)S(1)} %select_add_fusion), channel_id=1, source_target_pairs={{0,1},{1,0},{2,3},{3,2},{4,5},{5,4},{6,7},{7,6},{8,9},{9,8},{10,11... | collective-permute-start | bytes 392 | tf_op jit(solution)/shard_map/ppermute | solution.py:292

commit v13 on v10

--- a/solution.py
+++ b/solution.py
@@ -84,9 +84,9 @@
     else:
         ey_next = xhi_ref[0]
         ez_next = xhi_ref[1]
-    hx = magn(0, x) - TIME_STEP * (_y_up(ez, yhi_ref[1, x]) - _z_up(ey))
+    hx = magn(0, x) - TIME_STEP * (_y_up(ez, yhi_ref[1, x:x + 1]) - _z_up(ey))
     hy = magn(1, x) - TIME_STEP * (_z_up(ex) - (ez_next - ez))
-    hz = magn(2, x) - TIME_STEP * ((ey_next - ey) - _y_up(ex, yhi_ref[0, x]))
+    hz = magn(2, x) - TIME_STEP * ((ey_next - ey) - _y_up(ex, yhi_ref[0, x:x + 1]))
     return (ex, ey, ez, hx, hy, hz)
 
 
@@ -102,14 +102,14 @@
 def _elec_plane(x, planes, old, hy_prev, hz_prev, ylo_ref, c2_ref, keep, drive):
     ex, ey, ez, hx, hy, hz = old
     if x + 1 < planes:
-        ey_m_next = ylo_ref[1, x + 1]
+        ey_m_next = ylo_ref[1, x + 1:x + 2]
     else:
         ey_m_next = c2_ref[...]
-    ex_m = ylo_ref[0, x]
-    ey_m = ylo_ref[1, x]
-    ez_m = ylo_ref[2, x]
-    hx_r = ylo_ref[3, x] - TIME_STEP * ((ez[0:1] - ez_m) - _z_up(ey_m))
-    hz_r = ylo_ref[4, x] - TIME_STEP * ((ey_m_next - ey_m) - (ex[0:1] - ex_m))
+    ex_m = ylo_ref[0, x:x + 1]
+    ey_m = ylo_ref[1, x:x + 1]
+    ez_m = ylo_ref[2, x:x + 1]
+    hx_r = ylo_ref[3, x:x + 1] - TIME_STEP * ((ez[0:1] - ez_m) - _z_up(ey_m))
+    hz_r = ylo_ref[4, x:x + 1] - TIME_STEP * ((ey_m_next - ey_m) - (ex[0:1] - ex_m))
     ex_new = keep * ex + drive * (_y_down(hz, hz_r) - _z_down(hy))
     ey_new = keep * ey + drive * (_z_down(hx) - (hz - hz_prev))
     ez_new = keep * ez + drive * ((hy - hy_prev) - _y_down(hx, hx_r))
@@ -118,8 +118,8 @@
 
 def _step_kernel(e_ref, h_ref, keep_ref, drive_ref, xlo_ref, xhi_ref, y_ref, basis_ref,
                  e_out, h_out, y_out, g_out):
-    c1_ref = y_ref.at[7, 0]
-    c2_ref = y_ref.at[8, 0]
+    c1_ref = y_ref.at[7, 0:1]
+    c2_ref = y_ref.at[8, 0:1]
     yhi_ref = y_ref.at[5:7]
     planes = e_ref.shape[1]
     cells = e_ref.shape[2]
@@ -140,13 +140,13 @@
         h_out[1, x] = hy
         h_out[2, x] = hz
         last = slice(cells - 1, cells)
-        y_out[0, x] = ex_new[last]
-        y_out[1, x] = ey_new[last]
-        y_out[2, x] = ez_new[last]
-        y_out[3, x] = hx[last]
-        y_out[4, x] = hz[last]
-        y_out[5, x] = ex_new[0:1]
-        y_out[6, x] = ez_new[0:1]
+        y_out[0, x:x + 1] = ex_new[last]
+        y_out[1, x:x + 1] = ey_new[last]
+        y_out[2, x:x + 1] = ez_new[last]
+        y_out[3, x:x + 1] = hx[last]
+        y_out[4, x:x + 1] = hz[last]
+        y_out[5, x:x + 1] = ex_new[0:1]
+        y_out[6, x:x + 1] = ez_new[0:1]
         hy_prev = hy
         hz_prev = hz
         for comp, field in ((0, ex_new), (1, ey_new)):
@@ -161,8 +161,8 @@
 def _edge_kernel(e_first, e_second, e_penult, e_last, h_first, h_penult, h_last,
                  keep_first, keep_last, drive_first, drive_last, xlo_ref, xhi_ref, y_ref,
                  xlo_out, xhi_out, *, planes):
-    c1_ref = y_ref.at[7, 0]
-    c2_ref = y_ref.at[8, 0]
+    c1_ref = y_ref.at[7, 0:1]
+    c2_ref = y_ref.at[8, 0:1]
     yhi_ref = y_ref.at[5:7]
     e_blocks = {0: e_first, 1: e_second, planes - 2: e_penult, planes - 1: e_last}
     h_blocks = {0: h_first, planes - 2: h_penult, planes - 1: h_last}
@@ -192,13 +192,13 @@
     slab = e_top.shape[2]
     last = slice(slab - 1, slab)
     for x in range(planes):
-        y_out[0, x] = e_bottom[0, x][last]
-        y_out[1, x] = e_bottom[1, x][last]
-        y_out[2, x] = e_bottom[2, x][last]
-        y_out[3, x] = h_bottom[0, x][last]
-        y_out[4, x] = h_bottom[2, x][last]
-        y_out[5, x] = e_top[0, x][0:1]
-        y_out[6, x] = e_top[2, x][0:1]
+        y_out[0, x:x + 1] = e_bottom[0, x][last]
+        y_out[1, x:x + 1] = e_bottom[1, x][last]
+        y_out[2, x:x + 1] = e_bottom[2, x][last]
+        y_out[3, x:x + 1] = h_bottom[0, x][last]
+        y_out[4, x:x + 1] = h_bottom[2, x][last]
+        y_out[5, x:x + 1] = e_top[0, x][0:1]
+        y_out[6, x:x + 1] = e_top[2, x][0:1]
     xhi_out[0] = e_first[1, 0]
     xhi_out[1] = e_first[2, 0]
     xlo_out[0] = e_last[0, 0]
@@ -215,7 +215,7 @@
 def exchange_y(rows, xlo, xhi):
     cells = xhi.shape[1]
     corners = jnp.zeros((2,) + rows.shape[1:], rows.dtype)
-    corners = corners.at[0, 0].set(xlo[0, 0:1]).at[1, 0].set(xhi[0, cells - 1:cells])
+    corners = corners.at[0, 0:1].set(xlo[0, 0:1]).at[1, 0:1].set(xhi[0, cells - 1:cells])
     message = jnp.concatenate([rows, corners])
     if lax.axis_size("gy") == 2:
         return shifted(message, "gy", 1)
@@ -284,7 +284,7 @@
     field_shape = jax.ShapeDtypeStruct(e_field.shape, f32)
     xlo_shape = jax.ShapeDtypeStruct((5, cells_y, depth), f32)
     xhi_shape = jax.ShapeDtypeStruct((2, cells_y, depth), f32)
-    rows_shape = jax.ShapeDtypeStruct((7, cells_x, 1, depth), f32)
+    rows_shape = jax.ShapeDtypeStruct((7, cells_x, depth), f32)
     angle_count = angle_orders.shape[0]
     sums_shape = jax.ShapeDtypeStruct((2, 1, 2 * angle_count), f32)
     step_call = pl.pallas_call(

time: 78.7 us -> 76.5 us (0.972)
  waiting for transfers between devices: 21.3 us -> 19.4 us
    ppermute x12, waiting for transfers between devices: 8.5 us -> 6.95 us  [shifted(): return lax.ppermute(value, axis, pairs)]
    unnamed x38 -> x36, local copies, waits for them, and re-layouts: 3.8 us -> 3.82 us
  transfers between devices with their start and end apart: 16 -> 16, of which waited for: 13 -> 12; matrix products, arithmetic and copies ran while one was open for 3% -> 3% of each run, Pallas kernels for 17% -> 18%
where the time goes in v13:
time: 76.5 us; the launch traced here: 75.8 us
  Pallas kernels  25.3 us (33%)
  starting transfers between devices  20.6 us (27%)
  waiting for transfers between devices  19.4 us (25%)
  other arithmetic  5.63 us (7%)
  local copies, waits for them, and re-layouts  4.01 us (5%)
  between operations  0.82 us (1%)
    ppermute x12, starting transfers between devices, shifted(): return lax.ppermute(value, axis, pairs)  20.2 us
    pallas_call x4, Pallas kernels, local(): step_call(elec, magn, keep, drive, xlo, xhi, rows, basis)  15 us
    ppermute x3, waiting for transfers between devices, scatter_sum(): rows = keep + lax.ppermute(send, axis, pairs)  11.3 us
    ppermute x12, waiting for transfers between devices, shifted(): return lax.ppermute(value, axis, pairs)  6.95 us
    pallas_call x3, Pallas kernels, local(): edge_call(elec, elec, elec, elec, magn, magn, magn, keep, keep, drive, dr...  6.39 us
    unnamed x36, local copies, waits for them, and re-layouts  3.82 us
    concatenate x4, other arithmetic, exchange_y(): message = jnp.concatenate([rows, corners])  2.35 us
    pallas_call x1, Pallas kernels, coefficients(): pl.pallas_call(_coef_kernel, out_shape=(out, out), in_specs=[scalar, scal...  2.03 us
  transfers between devices with their start and end apart: 16, of which 12 were waited for; matrix products, arithmetic and copies ran while one was open for 3% of the time, Pallas kernels for 18%

profile of v13, /device:TPU:0, one launch (start us, length us, event | category | flops | bytes accessed | tf_op | source)
XLA Modules:
  0.0 75.8 jit_solution(2047082467438074445)
XLA Ops:
  0.6 1.9 %shard_map.86 = (f32[5,64,128]{2,1,0:T(8,128)}, f32[2,64,128]{2,1,0:T(8,128)}, f32[7,8,128]{2,1,0:T(8,128)}) custom-call(f32[3,8,64,128]{3,2,1,0:T(8,128)} %e_last.3, f32[3,8,64,128]{3,2,1,0:T(8,128)} %e_last.3, f32[3,8,64,128]{3,2,1,0:T(8,128)} %h_last.3, f32[3,8,64,128]{3,2,1,0:T(8,128)} %e_last.3, f32[3,8,64,128]{3,2,1,0:T(8,128)} %e_last.3, ...), custom_call_target="tpu_custom_call" | custom-call | tf_op jit(solution)/shard_map/pallas_call | solution.py:319
  2.5 3.0 %collective-permute-start = (f32[5,64,128]{2,1,0:T(8,128)}, f32[5,64,128]{2,1,0:T(8,128)S(1)}, u32[]{:S(2)}, u32[]{:S(2)}) collective-permute-start(f32[5,64,128]{2,1,0:T(8,128)} %get-tuple-element.133), channel_id=1, source_target_pairs={{0,2},{2,4},{4,6},{6,8},{8,10},{10,12},{12,14},{14,0},{1,3},{3,5},... | collective-permute-start | bytes 491528 | tf_op jit(solution)/shard_map/ppermute | solution.py:21
  5.4 3.0 %collective-permute-start.1 = (f32[2,64,128]{2,1,0:T(8,128)}, f32[2,64,128]{2,1,0:T(8,128)S(1)}, u32[]{:S(2)}, u32[]{:S(2)}) collective-permute-start(f32[2,64,128]{2,1,0:T(8,128)} %get-tuple-element.134), channel_id=1, source_target_pairs={{0,14},{2,0},{4,2},{6,4},{8,6},{10,8},{12,10},{14,12},{1,15},{3,1}... | collective-permute-start | bytes 196616 | tf_op jit(solution)/shard_map/ppermute | solution.py:21
  8.5 0.7 copy-done.17
  9.2 0.1 multiply_multiply_fusion
  9.3 0.1 multiply_multiply_fusion.1
  9.3 1.1 %fusion.4 = (f32[64,8,64]{2,0,1:T(8,128)S(1)}, f32[64,8,64]{2,0,1:T(8,128)S(1)}) fusion(s32[64,64]{1,0:T(8,128)S(1)} %multiply_multiply_fusion, s32[64,8]{0,1:T(8,128)S(1)} %multiply_multiply_fusion.1), kind=kLoop, calls=%fused_computation.10 | loop fusion | flops 458752 | bytes 280576 | tf_op jit(solution)/shard_map/cos | solution.py:242
  10.4 2.0 %shard_map.85 = (f32[8,64,128]{2,1,0:T(8,128)}, f32[8,64,128]{2,1,0:T(8,128)}) custom-call(f32[6]{0:T(128)} %eps_ref.1, f32[6]{0:T(128)} %sigma_ref.1, s32[8,64,128]{2,1,0:T(8,128)} %mat_ref.1), custom_call_target="tpu_custom_call" | custom-call | tf_op jit(solution)/shard_map/pallas_call | solution.py:43
  12.5 1.0 %collective-permute-done.1.xhi_ref = f32[2,64,128]{2,1,0:T(8,128)S(1)} collective-permute-done((f32[2,64,128]{2,1,0:T(8,128)}, f32[2,64,128]{2,1,0:T(8,128)S(1)}, u32[]{:S(2)}, u32[]{:S(2)}) %collective-permute-start.1) | collective-permute-done | bytes 65568 | tf_op jit(solution)/shard_map/ppermute | solution.py:21
  13.4 0.0 collective-permute-done.xlo_ref
  13.5 0.1 collective-permute-start.2
  13.6 0.8 %maximum_bitcast_fusion.basis_ref = f32[8,128,64]{2,1,0:T(8,128)} fusion(f32[64,8,64]{2,0,1:T(8,128)S(1)} %get-tuple-element.164, f32[64,8,64]{2,0,1:T(8,128)S(1)} %get-tuple-element.163), kind=kLoop, calls=%fused_computation | loop fusion | flops 65536 | bytes 524288 | tf_op jit(solution)/shard_map/transpose | solution.py:332
  14.4 0.4 collective-permute-done.2.y_ref
  14.8 0.6 copy-done.7
  15.4 2.1 %shard_map.88 = (f32[5,64,128]{2,1,0:T(8,128)}, f32[2,64,128]{2,1,0:T(8,128)}) custom-call(f32[3,8,64,128]{3,2,1,0:T(8,128)} %e_last.3, f32[3,8,64,128]{3,2,1,0:T(8,128)} %e_last.3, f32[3,8,64,128]{3,2,1,0:T(8,128)} %e_last.3, f32[3,8,64,128]{3,2,1,0:T(8,128)} %e_last.3, f32[3,8,64,128]{3,2,1,0:T(8,128)} %h_last.3, f32[3,8,64,128]{3,2,1,0:T(8,128)} %h_last.3, ...), custom_call_target="tpu_custom_call" | custom-call | tf_op jit(solution)/shard_map/pallas_call | solution.py:339
  17.6 0.0 collective-permute-start.3
  17.6 4.7 %collective-permute-start.4 = (f32[2,64,128]{2,1,0:T(8,128)}, f32[2,64,128]{2,1,0:T(8,128)S(1)}, u32[]{:S(2)}, u32[]{:S(2)}) collective-permute-start(f32[2,64,128]{2,1,0:T(8,128)} %get-tuple-element.145), channel_id=1, source_target_pairs={{0,14},{2,0},{4,2},{6,4},{8,6},{10,8},{12,10},{14,12},{1,15},{3,1}... | collective-permute-start | bytes 196616 | tf_op jit(solution)/shard_map/ppermute | solution.py:21
  22.3 3.8 %shard_map.87 = (f32[3,8,64,128]{3,2,1,0:T(8,128)}, f32[3,8,64,128]{3,2,1,0:T(8,128)}, f32[7,8,128]{2,1,0:T(8,128)}, f32[2,1,128]{2,1,0:T(1,128)}) custom-call(f32[3,8,64,128]{3,2,1,0:T(8,128)} %e_last.3, f32[3,8,64,128]{3,2,1,0:T(8,128)} %h_last.3, f32[8,64,128]{2,1,0:T(8,128)} %get-tuple-element.135.keep_ref.keep_first.keep_last, ...), custom_call_target="tpu_custom_call" | custom-call | tf_op jit(solution)/shard_map/pallas_call | solution.py:343
  26.0 0.0 collective-permute-done.4.xhi_ref
  26.1 0.7 collective-permute-done.3.xlo_ref
  26.8 0.8 %pad_maximum_fusion.1 = f32[9,8,128]{2,1,0:T(8,128)S(1)} fusion(f32[2,8,128]{2,1,0:T(8,128)S(1)} %scatter.31, f32[7,8,128]{2,1,0:T(8,128)} %get-tuple-element.146), kind=kLoop, calls=%fused_computation.12 | loop fusion | flops 9216 | bytes 73728 | tf_op jit(solution)/shard_map/concatenate | solution.py:219
  27.6 0.0 collective-permute-start.5
  27.6 1.2 %collective-permute-done.5.y_ref = f32[9,8,128]{2,1,0:T(8,128)S(1)} collective-permute-done((f32[9,8,128]{2,1,0:T(8,128)S(1)}, f32[9,8,128]{2,1,0:T(8,128)S(1)}, u32[]{:S(2)}, u32[]{:S(2)}) %collective-permute-start.5) | collective-permute-done | bytes 36896 | tf_op jit(solution)/shard_map/ppermute | solution.py:21
  28.8 0.6 copy-done.8
  29.4 2.1 %shard_map.90 = (f32[5,64,128]{2,1,0:T(8,128)}, f32[2,64,128]{2,1,0:T(8,128)}) custom-call(f32[3,8,64,128]{3,2,1,0:T(8,128)} %get-tuple-element.142.e_ref.e_first.e_second.e_penult.e_last, f32[3,8,64,128]{3,2,1,0:T(8,128)} %get-tuple-element.142.e_ref.e_first.e_second.e_penult.e_last, ...), custom_call_target="tpu_custom_call" | custom-call | tf_op jit(solution)/shard_map/pallas_call | solution.py:339
  31.5 0.0 collective-permute-start.6
  31.5 4.7 %collective-permute-start.7 = (f32[2,64,128]{2,1,0:T(8,128)}, f32[2,64,128]{2,1,0:T(8,128)S(1)}, u32[]{:S(2)}, u32[]{:S(2)}) collective-permute-start(f32[2,64,128]{2,1,0:T(8,128)} %get-tuple-element.150), channel_id=1, source_target_pairs={{0,14},{2,0},{4,2},{6,4},{8,6},{10,8},{12,10},{14,12},{1,15},{3,1}... | collective-permute-start | bytes 196616 | tf_op jit(solution)/shard_map/ppermute | solution.py:21
  36.3 3.8 %shard_map.89 = (f32[3,8,64,128]{3,2,1,0:T(8,128)}, f32[3,8,64,128]{3,2,1,0:T(8,128)}, f32[7,8,128]{2,1,0:T(8,128)}, f32[2,1,128]{2,1,0:T(1,128)}) custom-call(f32[3,8,64,128]{3,2,1,0:T(8,128)} %get-tuple-element.142.e_ref.e_first.e_second.e_penult.e_last, f32[3,8,64,128]{3,2,1,0:T(8,128)} %get-tuple-element.143.h_ref.h_first.h_penult.h_last, ...), custom_call_target="tpu_custom_call" | custom-call | tf_op jit(solution)/shard_map/pallas_call | solution.py:343
  40.0 0.0 collective-permute-done.7.xhi_ref
  40.0 0.7 collective-permute-done.6.xlo_ref
  40.7 0.8 %pad_maximum_fusion.2 = f32[9,8,128]{2,1,0:T(8,128)S(1)} fusion(f32[2,8,128]{2,1,0:T(8,128)S(1)} %scatter.35, f32[7,8,128]{2,1,0:T(8,128)} %get-tuple-element.151), kind=kLoop, calls=%fused_computation.13 | loop fusion | flops 9216 | bytes 73728 | tf_op jit(solution)/shard_map/concatenate | solution.py:219
  41.5 0.0 collective-permute-start.8
  41.5 1.2 %collective-permute-done.8.y_ref = f32[9,8,128]{2,1,0:T(8,128)S(1)} collective-permute-done((f32[9,8,128]{2,1,0:T(8,128)S(1)}, f32[9,8,128]{2,1,0:T(8,128)S(1)}, u32[]{:S(2)}, u32[]{:S(2)}) %collective-permute-start.8) | collective-permute-done | bytes 36896 | tf_op jit(solution)/shard_map/ppermute | solution.py:21
  42.8 0.6 copy-done.9
  43.4 2.1 %shard_map.92 = (f32[5,64,128]{2,1,0:T(8,128)}, f32[2,64,128]{2,1,0:T(8,128)}) custom-call(f32[3,8,64,128]{3,2,1,0:T(8,128)} %get-tuple-element.147.e_ref.e_first.e_second.e_penult.e_last, f32[3,8,64,128]{3,2,1,0:T(8,128)} %get-tuple-element.147.e_ref.e_first.e_second.e_penult.e_last, ...), custom_call_target="tpu_custom_call" | custom-call | tf_op jit(solution)/shard_map/pallas_call | solution.py:339
  45.5 0.0 collective-permute-start.9
  45.5 4.7 %collective-permute-start.10 = (f32[2,64,128]{2,1,0:T(8,128)}, f32[2,64,128]{2,1,0:T(8,128)S(1)}, u32[]{:S(2)}, u32[]{:S(2)}) collective-permute-start(f32[2,64,128]{2,1,0:T(8,128)} %get-tuple-element.155), channel_id=1, source_target_pairs={{0,14},{2,0},{4,2},{6,4},{8,6},{10,8},{12,10},{14,12},{1,15},{3,1}... | collective-permute-start | bytes 196616 | tf_op jit(solution)/shard_map/ppermute | solution.py:21
  50.2 3.8 %shard_map.91 = (f32[3,8,64,128]{3,2,1,0:T(8,128)}, f32[3,8,64,128]{3,2,1,0:T(8,128)}, f32[7,8,128]{2,1,0:T(8,128)}, f32[2,1,128]{2,1,0:T(1,128)}) custom-call(f32[3,8,64,128]{3,2,1,0:T(8,128)} %get-tuple-element.147.e_ref.e_first.e_second.e_penult.e_last, f32[3,8,64,128]{3,2,1,0:T(8,128)} %get-tuple-element.148.h_ref.h_first.h_penult.h_last, ...), custom_call_target="tpu_custom_call" | custom-call | tf_op jit(solution)/shard_map/pallas_call | solution.py:343
  54.0 0.0 collective-permute-done.10.xhi_ref
  54.0 0.7 collective-permute-done.9.xlo_ref
  54.7 0.8 %pad_maximum_fusion.3 = f32[9,8,128]{2,1,0:T(8,128)S(1)} fusion(f32[2,8,128]{2,1,0:T(8,128)S(1)} %scatter.39, f32[7,8,128]{2,1,0:T(8,128)} %get-tuple-element.156), kind=kLoop, calls=%fused_computation.14 | loop fusion | flops 9216 | bytes 73728 | tf_op jit(solution)/shard_map/concatenate | solution.py:219
  55.5 0.0 collective-permute-start.11
  55.5 1.2 %collective-permute-done.11.y_ref = f32[9,8,128]{2,1,0:T(8,128)S(1)} collective-permute-done((f32[9,8,128]{2,1,0:T(8,128)S(1)}, f32[9,8,128]{2,1,0:T(8,128)S(1)}, u32[]{:S(2)}, u32[]{:S(2)}) %collective-permute-start.11) | collective-permute-done | bytes 36896 | tf_op jit(solution)/shard_map/ppermute | solution.py:21
  56.7 0.6 copy-done.11
  57.3 3.8 %shard_map.93 = (f32[3,8,64,128]{3,2,1,0:T(8,128)}, f32[3,8,64,128]{3,2,1,0:T(8,128)}, f32[7,8,128]{2,1,0:T(8,128)}, f32[2,1,128]{2,1,0:T(1,128)}) custom-call(f32[3,8,64,128]{3,2,1,0:T(8,128)} %get-tuple-element.152.e_ref, f32[3,8,64,128]{3,2,1,0:T(8,128)} %get-tuple-element.153.h_ref, f32[8,64,128]{2,1,0:T(8,128)} %get-tuple-element.135.keep_ref.keep_first.keep_last, ...), custom_call_target="tpu_custom_call" | custom-call | tf_op jit(solution)/shard_map/pallas_call | solution.py:343
  61.1 0.0 copy-start.13
  61.1 0.6 copy-done.16
  61.7 0.0 copy-done.15
  61.7 0.0 copy-done.13
  61.8 0.1 add_bitcast_fusion.2
  61.8 0.1 add_bitcast_fusion.3
  61.9 0.1 slice_select_fusion.2
  62.0 0.4 collective-permute-start.12
  62.4 4.1 %collective-permute-done.12 = f32[32,4]{0,1:T(4,128)S(1)} collective-permute-done((f32[32,4]{0,1:T(4,128)S(1)}, f32[32,4]{0,1:T(4,128)S(1)}, u32[]{:S(2)}, u32[]{:S(2)}) %collective-permute-start.12) | collective-permute-done | bytes 544 | tf_op jit(solution)/shard_map/ppermute | solution.py:267
  66.5 0.1 select_add_fusion.2
  66.6 0.1 slice_select_fusion.1
  66.7 3.6 %collective-permute-done.13 = f32[16,4]{0,1:T(4,128)S(1)} collective-permute-done((f32[16,4]{0,1:T(4,128)S(1)}, f32[16,4]{0,1:T(4,128)S(1)}, u32[]{:S(2)}, u32[]{:S(2)}) %collective-permute-start.13) | collective-permute-done | bytes 288 | tf_op jit(solution)/shard_map/ppermute | solution.py:267
  70.2 0.1 select_add_fusion.1
  70.3 0.1 slice_select_fusion
  70.4 0.0 collective-permute-start.14
  70.4 3.6 %collective-permute-done.14 = f32[8,4]{0,1:T(4,128)S(1)} collective-permute-done((f32[8,4]{0,1:T(4,128)S(1)}, f32[8,4]{0,1:T(4,128)S(1)}, u32[]{:S(2)}, u32[]{:S(2)}) %collective-permute-start.14) | collective-permute-done | bytes 160 | tf_op jit(solution)/shard_map/ppermute | solution.py:267
  74.0 0.1 select_add_fusion
  74.0 1.2 %collective-permute-done.15 = f32[8,4]{0,1:T(4,128)S(1)} collective-permute-done((f32[8,4]{0,1:T(4,128)S(1)}, f32[8,4]{0,1:T(4,128)S(1)}, u32[]{:S(2)}, u32[]{:S(2)}) %collective-permute-start.15) | collective-permute-done | bytes 160 | tf_op jit(solution)/shard_map/ppermute | solution.py:277
  75.2 0.6 add_multiply_fusion
  (50 shorter events, 0.3 us)
Async XLA Ops:
  2.5 11.0 %collective-permute-start = (f32[5,64,128]{2,1,0:T(8,128)}, f32[5,64,128]{2,1,0:T(8,128)S(1)}, u32[]{:S(2)}, u32[]{:S(2)}) collective-permute-start(f32[5,64,128]{2,1,0:T(8,128)} %get-tuple-element.133), channel_id=1, source_target_pairs={{0,2},{2,4},{4,6},{6,8},{8,10},{10,12},{12,14},{14,0},{1,3},{3,5},... | collective-permute-start | bytes 491528 | tf_op jit(solution)/shard_map/ppermute | solution.py:21
  5.4 8.0 %collective-permute-start.1 = (f32[2,64,128]{2,1,0:T(8,128)}, f32[2,64,128]{2,1,0:T(8,128)S(1)}, u32[]{:S(2)}, u32[]{:S(2)}) collective-permute-start(f32[2,64,128]{2,1,0:T(8,128)} %get-tuple-element.134), channel_id=1, source_target_pairs={{0,14},{2,0},{4,2},{6,4},{8,6},{10,8},{12,10},{14,12},{1,15},{3,1}... | collective-permute-start | bytes 196616 | tf_op jit(solution)/shard_map/ppermute | solution.py:21
  8.5 0.7 copy-start.17
  10.4 3.1 %copy-start.12 = (f32[7,8,128]{2,1,0:T(8,128)S(1)}, f32[7,8,128]{2,1,0:T(8,128)}, u32[]{:S(2)}) copy-start(f32[7,8,128]{2,1,0:T(8,128)} %get-tuple-element.139) | copy-start | bytes 86020
  13.4 1.0 %copy-start.3 = (f32[2,64,128]{2,1,0:T(8,128)}, f32[2,64,128]{2,1,0:T(8,128)S(1)}, u32[]{:S(2)}) copy-start(f32[2,64,128]{2,1,0:T(8,128)S(1)} %collective-permute-done.1.xhi_ref) | copy-start | bytes 196612
  13.4 1.0 %copy-start = (f32[5,64,128]{2,1,0:T(8,128)}, f32[5,64,128]{2,1,0:T(8,128)S(1)}, u32[]{:S(2)}) copy-start(f32[5,64,128]{2,1,0:T(8,128)S(1)} %collective-permute-done.xlo_ref) | copy-start | bytes 491524
  13.5 1.3 %collective-permute-start.2 = (f32[9,8,128]{2,1,0:T(8,128)S(1)}, f32[9,8,128]{2,1,0:T(8,128)S(1)}, u32[]{:S(2)}, u32[]{:S(2)}) collective-permute-start(f32[9,8,128]{2,1,0:T(8,128)S(1)} %pad_maximum_fusion), channel_id=1, source_target_pairs={{0,1},{1,0},{2,3},{3,2},{4,5},{5,4},{6,7},{7,6},{8,9},{9,8},{10,11... | collective-permute-start | bytes 110600 | tf_op jit(solution)/shard_map/ppermute | solution.py:21
  14.8 0.6 copy-start.7
  17.6 9.2 %collective-permute-start.3 = (f32[5,64,128]{2,1,0:T(8,128)}, f32[5,64,128]{2,1,0:T(8,128)S(1)}, u32[]{:S(2)}, u32[]{:S(2)}) collective-permute-start(f32[5,64,128]{2,1,0:T(8,128)} %get-tuple-element.144), channel_id=1, source_target_pairs={{0,2},{2,4},{4,6},{6,8},{8,10},{10,12},{12,14},{14,0},{1,3},{3,5},... | collective-permute-start | bytes 491528 | tf_op jit(solution)/shard_map/ppermute | solution.py:21
  17.6 8.5 %collective-permute-start.4 = (f32[2,64,128]{2,1,0:T(8,128)}, f32[2,64,128]{2,1,0:T(8,128)S(1)}, u32[]{:S(2)}, u32[]{:S(2)}) collective-permute-start(f32[2,64,128]{2,1,0:T(8,128)} %get-tuple-element.145), channel_id=1, source_target_pairs={{0,14},{2,0},{4,2},{6,4},{8,6},{10,8},{12,10},{14,12},{1,15},{3,1}... | collective-permute-start | bytes 196616 | tf_op jit(solution)/shard_map/ppermute | solution.py:21
  26.0 2.7 %copy-start.5 = (f32[2,64,128]{2,1,0:T(8,128)}, f32[2,64,128]{2,1,0:T(8,128)S(1)}, u32[]{:S(2)}) copy-start(f32[2,64,128]{2,1,0:T(8,128)S(1)} %collective-permute-done.4.xhi_ref) | copy-start | bytes 196612
  26.7 2.1 %copy-start.2 = (f32[5,64,128]{2,1,0:T(8,128)}, f32[5,64,128]{2,1,0:T(8,128)S(1)}, u32[]{:S(2)}) copy-start(f32[5,64,128]{2,1,0:T(8,128)S(1)} %collective-permute-done.3.xlo_ref) | copy-start | bytes 491524
  27.6 1.2 %collective-permute-start.5 = (f32[9,8,128]{2,1,0:T(8,128)S(1)}, f32[9,8,128]{2,1,0:T(8,128)S(1)}, u32[]{:S(2)}, u32[]{:S(2)}) collective-permute-start(f32[9,8,128]{2,1,0:T(8,128)S(1)} %pad_maximum_fusion.1), channel_id=1, source_target_pairs={{0,1},{1,0},{2,3},{3,2},{4,5},{5,4},{6,7},{7,6},{8,9},{9,8},{10,11... | collective-permute-start | bytes 110600 | tf_op jit(solution)/shard_map/ppermute | solution.py:21
  28.8 0.6 copy-start.8
  31.5 9.2 %collective-permute-start.6 = (f32[5,64,128]{2,1,0:T(8,128)}, f32[5,64,128]{2,1,0:T(8,128)S(1)}, u32[]{:S(2)}, u32[]{:S(2)}) collective-permute-start(f32[5,64,128]{2,1,0:T(8,128)} %get-tuple-element.149), channel_id=1, source_target_pairs={{0,2},{2,4},{4,6},{6,8},{8,10},{10,12},{12,14},{14,0},{1,3},{3,5},... | collective-permute-start | bytes 491528 | tf_op jit(solution)/shard_map/ppermute | solution.py:21
  31.5 8.5 %collective-permute-start.7 = (f32[2,64,128]{2,1,0:T(8,128)}, f32[2,64,128]{2,1,0:T(8,128)S(1)}, u32[]{:S(2)}, u32[]{:S(2)}) collective-permute-start(f32[2,64,128]{2,1,0:T(8,128)} %get-tuple-element.150), channel_id=1, source_target_pairs={{0,14},{2,0},{4,2},{6,4},{8,6},{10,8},{12,10},{14,12},{1,15},{3,1}... | collective-permute-start | bytes 196616 | tf_op jit(solution)/shard_map/ppermute | solution.py:21
  40.0 2.7 %copy-start.4 = (f32[2,64,128]{2,1,0:T(8,128)}, f32[2,64,128]{2,1,0:T(8,128)S(1)}, u32[]{:S(2)}) copy-start(f32[2,64,128]{2,1,0:T(8,128)S(1)} %collective-permute-done.7.xhi_ref) | copy-start | bytes 196612
  40.7 2.1 %copy-start.1 = (f32[5,64,128]{2,1,0:T(8,128)}, f32[5,64,128]{2,1,0:T(8,128)S(1)}, u32[]{:S(2)}) copy-start(f32[5,64,128]{2,1,0:T(8,128)S(1)} %collective-permute-done.6.xlo_ref) | copy-start | bytes 491524
  41.5 1.2 %collective-permute-start.8 = (f32[9,8,128]{2,1,0:T(8,128)S(1)}, f32[9,8,128]{2,1,0:T(8,128)S(1)}, u32[]{:S(2)}, u32[]{:S(2)}) collective-permute-start(f32[9,8,128]{2,1,0:T(8,128)S(1)} %pad_maximum_fusion.2), channel_id=1, source_target_pairs={{0,1},{1,0},{2,3},{3,2},{4,5},{5,4},{6,7},{7,6},{8,9},{9,8},{10,11... | collective-permute-start | bytes 110600 | tf_op jit(solution)/shard_map/ppermute | solution.py:21
  42.7 0.6 copy-start.9
  45.5 9.2 %collective-permute-start.9 = (f32[5,64,128]{2,1,0:T(8,128)}, f32[5,64,128]{2,1,0:T(8,128)S(1)}, u32[]{:S(2)}, u32[]{:S(2)}) collective-permute-start(f32[5,64,128]{2,1,0:T(8,128)} %get-tuple-element.154), channel_id=1, source_target_pairs={{0,2},{2,4},{4,6},{6,8},{8,10},{10,12},{12,14},{14,0},{1,3},{3,5},... | collective-permute-start | bytes 491528 | tf_op jit(solution)/shard_map/ppermute | solution.py:21
  45.5 8.5 %collective-permute-start.10 = (f32[2,64,128]{2,1,0:T(8,128)}, f32[2,64,128]{2,1,0:T(8,128)S(1)}, u32[]{:S(2)}, u32[]{:S(2)}) collective-permute-start(f32[2,64,128]{2,1,0:T(8,128)} %get-tuple-element.155), channel_id=1, source_target_pairs={{0,14},{2,0},{4,2},{6,4},{8,6},{10,8},{12,10},{14,12},{1,15},{3,1}... | collective-permute-start | bytes 196616 | tf_op jit(solution)/shard_map/ppermute | solution.py:21
  54.0 2.7 %copy-start.10 = (f32[2,64,128]{2,1,0:T(8,128)}, f32[2,64,128]{2,1,0:T(8,128)S(1)}, u32[]{:S(2)}) copy-start(f32[2,64,128]{2,1,0:T(8,128)S(1)} %collective-permute-done.10.xhi_ref) | copy-start | bytes 196612
  54.7 2.1 %copy-start.6 = (f32[5,64,128]{2,1,0:T(8,128)}, f32[5,64,128]{2,1,0:T(8,128)S(1)}, u32[]{:S(2)}) copy-start(f32[5,64,128]{2,1,0:T(8,128)S(1)} %collective-permute-done.9.xlo_ref) | copy-start | bytes 491524
  55.5 1.2 %collective-permute-start.11 = (f32[9,8,128]{2,1,0:T(8,128)S(1)}, f32[9,8,128]{2,1,0:T(8,128)S(1)}, u32[]{:S(2)}, u32[]{:S(2)}) collective-permute-start(f32[9,8,128]{2,1,0:T(8,128)S(1)} %pad_maximum_fusion.3), channel_id=1, source_target_pairs={{0,1},{1,0},{2,3},{3,2},{4,5},{5,4},{6,7},{7,6},{8,9},{9,8},{10,11... | collective-permute-start | bytes 110600 | tf_op jit(solution)/shard_map/ppermute | solution.py:21
  56.7 0.6 copy-start.11
  61.1 0.7 copy-start.16
  61.1 0.7 copy-start.14
  61.1 0.7 copy-start.15
  61.1 0.7 copy-start.13
  62.0 4.5 %collective-permute-start.12 = (f32[32,4]{0,1:T(4,128)S(1)}, f32[32,4]{0,1:T(4,128)S(1)}, u32[]{:S(2)}, u32[]{:S(2)}) collective-permute-start(f32[32,4]{0,1:T(4,128)S(1)} %slice_select_fusion.2), channel_id=1, source_target_pairs={{0,8},{2,10},{4,12},{6,14},{8,0},{10,2},{12,4},{14,6},{1,9},{3,11}... | collective-permute-start | bytes 1544 | tf_op jit(solution)/shard_map/ppermute | solution.py:267
  66.7 3.6 %collective-permute-start.13 = (f32[16,4]{0,1:T(4,128)S(1)}, f32[16,4]{0,1:T(4,128)S(1)}, u32[]{:S(2)}, u32[]{:S(2)}) collective-permute-start(f32[16,4]{0,1:T(4,128)S(1)} %slice_select_fusion.1), channel_id=1, source_target_pairs={{0,4},{2,6},{4,0},{6,2},{8,12},{10,14},{12,8},{14,10},{1,5},{3,7},... | collective-permute-start | bytes 776 | tf_op jit(solution)/shard_map/ppermute | solution.py:267
  70.4 3.6 %collective-permute-start.14 = (f32[8,4]{0,1:T(4,128)S(1)}, f32[8,4]{0,1:T(4,128)S(1)}, u32[]{:S(2)}, u32[]{:S(2)}) collective-permute-start(f32[8,4]{0,1:T(4,128)S(1)} %slice_select_fusion), channel_id=1, source_target_pairs={{0,2},{2,0},{4,6},{6,4},{8,10},{10,8},{12,14},{14,12},{1,3},{3,1},... | collective-permute-start | bytes 392 | tf_op jit(solution)/shard_map/ppermute | solution.py:267
  74.0 1.2 %collective-permute-start.15 = (f32[8,4]{0,1:T(4,128)S(1)}, f32[8,4]{0,1:T(4,128)S(1)}, u32[]{:S(2)}, u32[]{:S(2)}) collective-permute-start(f32[8,4]{0,1:T(4,128)S(1)} %select_add_fusion), channel_id=1, source_target_pairs={{0,1},{1,0},{2,3},{3,2},{4,5},{5,4},{6,7},{7,6},{8,9},{9,8},{10,11... | collective-permute-start | bytes 392 | tf_op jit(solution)/shard_map/ppermute | solution.py:277

commit v14 on v13

--- a/solution.py
+++ b/solution.py
@@ -127,6 +127,7 @@
     magn = lambda comp, x: h_ref[comp, x]
     hy_prev, hz_prev = _magn_before(elec, xlo_ref, c1_ref)
     sums = [None, None]
+    pending = []
     for x in range(planes):
         old = _magn_plane(elec, magn, x, planes, xhi_ref, yhi_ref)
         ex_new, ey_new, ez_new = _elec_plane(
@@ -149,10 +150,16 @@
         y_out[6, x:x + 1] = ez_new[0:1]
         hy_prev = hy
         hz_prev = hz
-        for comp, field in ((0, ex_new), (1, ey_new)):
-            part = jnp.dot(basis_ref[x], field, precision=lax.Precision.HIGHEST,
-                           preferred_element_type=jnp.float32)
-            sums[comp] = part if sums[comp] is None else sums[comp] + part
+        group = basis_ref.shape[2] // cells
+        pending.append((ex_new, ey_new))
+        if len(pending) == group:
+            for comp in range(2):
+                fields = [planes_done[comp] for planes_done in pending]
+                stacked = fields[0] if group == 1 else jnp.concatenate(fields, axis=0)
+                part = jnp.dot(basis_ref[x // group], stacked, precision=lax.Precision.HIGHEST,
+                               preferred_element_type=jnp.float32)
+                sums[comp] = part if sums[comp] is None else sums[comp] + part
+            pending = []
     depth = e_ref.shape[3]
     for comp in range(2):
         g_out[comp] = sums[comp].T[depth - 3:depth - 2]
@@ -329,7 +336,8 @@
     keep, drive, xlo, xhi = lax.optimization_barrier((keep, drive, xlo, xhi))
     rows = exchange_y(rows, xlo, xhi)
     basis = trig_basis(angle_orders, cells_x, cells_y)
-    basis = basis.reshape(2 * angle_count, cells_x, cells_y).transpose(1, 0, 2)
+    group = 2 if cells_x % 2 == 0 else 1
+    basis = basis.reshape(2 * angle_count, cells_x // group, group * cells_y).transpose(1, 0, 2)
     basis, rows = lax.optimization_barrier((basis, rows))
     elec = e_field
     magn = h_field

time: 76.5 us -> 76.2 us (level)
  waiting for transfers between devices: 19.4 us -> 20.6 us
  Pallas kernels: 25.3 us -> 24.2 us
    ppermute x12, waiting for transfers between devices: 6.95 us -> 8.13 us  [shifted(): return lax.ppermute(value, axis, pairs)]
    pallas_call x4, Pallas kernels: 15 us -> 13.9 us  [local(): step_call(elec, magn, keep, drive, xlo, xhi, rows, basis)]
  transfers between devices with their start and end apart: 16 -> 16, of which waited for: 12 -> 12; matrix products, arithmetic and copies ran while one was open for 3% -> 2% of each run, Pallas kernels for 18% -> 17%
where the time goes in v14:
time: 76.2 us; the launch traced here: 75.5 us
  Pallas kernels  24.2 us (32%)
  starting transfers between devices  20.6 us (27%)
  waiting for transfers between devices  20.6 us (27%)
  other arithmetic  5.08 us (7%)
  local copies, waits for them, and re-layouts  4.22 us (6%)
  between operations  0.82 us (1%)
    ppermute x12, starting transfers between devices, shifted(): return lax.ppermute(value, axis, pairs)  20.2 us
    pallas_call x4, Pallas kernels, local(): step_call(elec, magn, keep, drive, xlo, xhi, rows, basis)  13.9 us
    ppermute x3, waiting for transfers between devices, scatter_sum(): rows = keep + lax.ppermute(send, axis, pairs)  11.3 us
    ppermute x12, waiting for transfers between devices, shifted(): return lax.ppermute(value, axis, pairs)  8.13 us
    pallas_call x3, Pallas kernels, local(): edge_call(elec, elec, elec, elec, magn, magn, magn, keep, keep, drive, dr...  6.39 us
    unnamed x36, local copies, waits for them, and re-layouts  3.83 us
    concatenate x4, other arithmetic, exchange_y(): message = jnp.concatenate([rows, corners])  2.35 us
    pallas_call x1, Pallas kernels, coefficients(): pl.pallas_call(_coef_kernel, out_shape=(out, out), in_specs=[scalar, scal...  2.01 us
  transfers between devices with their start and end apart: 16, of which 12 were waited for; matrix products, arithmetic and copies ran while one was open for 2% of the time, Pallas kernels for 17%

profile of v14, /device:TPU:0, one launch (start us, length us, event | category | flops | bytes accessed | tf_op | source)
XLA Modules:
  0.0 75.5 jit_solution(1459592499558312844)
XLA Ops:
  0.6 1.9 %shard_map.86 = (f32[5,64,128]{2,1,0:T(8,128)}, f32[2,64,128]{2,1,0:T(8,128)}, f32[7,8,128]{2,1,0:T(8,128)}) custom-call(f32[3,8,64,128]{3,2,1,0:T(8,128)} %e_last.3, f32[3,8,64,128]{3,2,1,0:T(8,128)} %e_last.3, f32[3,8,64,128]{3,2,1,0:T(8,128)} %h_last.3, f32[3,8,64,128]{3,2,1,0:T(8,128)} %e_last.3, f32[3,8,64,128]{3,2,1,0:T(8,128)} %e_last.3, ...), custom_call_target="tpu_custom_call" | custom-call | tf_op jit(solution)/shard_map/pallas_call | solution.py:326
  2.5 3.0 %collective-permute-start = (f32[5,64,128]{2,1,0:T(8,128)}, f32[5,64,128]{2,1,0:T(8,128)S(1)}, u32[]{:S(2)}, u32[]{:S(2)}) collective-permute-start(f32[5,64,128]{2,1,0:T(8,128)} %get-tuple-element.133), channel_id=1, source_target_pairs={{0,2},{2,4},{4,6},{6,8},{8,10},{10,12},{12,14},{14,0},{1,3},{3,5},... | collective-permute-start | bytes 491528 | tf_op jit(solution)/shard_map/ppermute | solution.py:21
  5.4 3.0 %collective-permute-start.1 = (f32[2,64,128]{2,1,0:T(8,128)}, f32[2,64,128]{2,1,0:T(8,128)S(1)}, u32[]{:S(2)}, u32[]{:S(2)}) collective-permute-start(f32[2,64,128]{2,1,0:T(8,128)} %get-tuple-element.134), channel_id=1, source_target_pairs={{0,14},{2,0},{4,2},{6,4},{8,6},{10,8},{12,10},{14,12},{1,15},{3,1}... | collective-permute-start | bytes 196616 | tf_op jit(solution)/shard_map/ppermute | solution.py:21
  8.5 0.7 copy-done.17
  9.2 0.1 multiply_multiply_fusion.1
  9.3 0.1 copy.12
  9.3 0.1 multiply_multiply_fusion
  9.4 0.1 broadcast_add_fusion
  9.6 0.1 add.227
  9.7 0.5 fusion.4
  10.2 2.0 %shard_map.85 = (f32[8,64,128]{2,1,0:T(8,128)}, f32[8,64,128]{2,1,0:T(8,128)}) custom-call(f32[6]{0:T(128)} %eps_ref.1, f32[6]{0:T(128)} %sigma_ref.1, s32[8,64,128]{2,1,0:T(8,128)} %mat_ref.1), custom_call_target="tpu_custom_call" | custom-call | tf_op jit(solution)/shard_map/pallas_call | solution.py:43
  12.2 1.2 %collective-permute-done.1.xhi_ref = f32[2,64,128]{2,1,0:T(8,128)S(1)} collective-permute-done((f32[2,64,128]{2,1,0:T(8,128)}, f32[2,64,128]{2,1,0:T(8,128)S(1)}, u32[]{:S(2)}, u32[]{:S(2)}) %collective-permute-start.1) | collective-permute-done | bytes 65568 | tf_op jit(solution)/shard_map/ppermute | solution.py:21
  13.4 0.0 collective-permute-done.xlo_ref
  13.5 0.1 collective-permute-start.2
  13.6 0.7 maximum_bitcast_fusion.basis_ref
  14.3 0.5 collective-permute-done.2.y_ref
  14.8 0.6 copy-done.7
  15.4 2.1 %shard_map.88 = (f32[5,64,128]{2,1,0:T(8,128)}, f32[2,64,128]{2,1,0:T(8,128)}) custom-call(f32[3,8,64,128]{3,2,1,0:T(8,128)} %e_last.3, f32[3,8,64,128]{3,2,1,0:T(8,128)} %e_last.3, f32[3,8,64,128]{3,2,1,0:T(8,128)} %e_last.3, f32[3,8,64,128]{3,2,1,0:T(8,128)} %e_last.3, f32[3,8,64,128]{3,2,1,0:T(8,128)} %h_last.3, f32[3,8,64,128]{3,2,1,0:T(8,128)} %h_last.3, ...), custom_call_target="tpu_custom_call" | custom-call | tf_op jit(solution)/shard_map/pallas_call | solution.py:347
  17.6 0.0 collective-permute-start.3
  17.6 4.7 %collective-permute-start.4 = (f32[2,64,128]{2,1,0:T(8,128)}, f32[2,64,128]{2,1,0:T(8,128)S(1)}, u32[]{:S(2)}, u32[]{:S(2)}) collective-permute-start(f32[2,64,128]{2,1,0:T(8,128)} %get-tuple-element.145), channel_id=1, source_target_pairs={{0,14},{2,0},{4,2},{6,4},{8,6},{10,8},{12,10},{14,12},{1,15},{3,1}... | collective-permute-start | bytes 196616 | tf_op jit(solution)/shard_map/ppermute | solution.py:21
  22.3 3.5 %shard_map.87 = (f32[3,8,64,128]{3,2,1,0:T(8,128)}, f32[3,8,64,128]{3,2,1,0:T(8,128)}, f32[7,8,128]{2,1,0:T(8,128)}, f32[2,1,128]{2,1,0:T(1,128)}) custom-call(f32[3,8,64,128]{3,2,1,0:T(8,128)} %e_last.3, f32[3,8,64,128]{3,2,1,0:T(8,128)} %h_last.3, f32[8,64,128]{2,1,0:T(8,128)} %get-tuple-element.135.keep_ref.keep_first.keep_last, ...), custom_call_target="tpu_custom_call" | custom-call | tf_op jit(solution)/shard_map/pallas_call | solution.py:351
  25.8 0.0 collective-permute-done.4.xhi_ref
  25.8 1.0 %collective-permute-done.3.xlo_ref = f32[5,64,128]{2,1,0:T(8,128)S(1)} collective-permute-done((f32[5,64,128]{2,1,0:T(8,128)}, f32[5,64,128]{2,1,0:T(8,128)S(1)}, u32[]{:S(2)}, u32[]{:S(2)}) %collective-permute-start.3) | collective-permute-done | bytes 163872 | tf_op jit(solution)/shard_map/ppermute | solution.py:21
  26.8 0.8 %pad_maximum_fusion.1 = f32[9,8,128]{2,1,0:T(8,128)S(1)} fusion(f32[2,8,128]{2,1,0:T(8,128)S(1)} %scatter.31, f32[7,8,128]{2,1,0:T(8,128)} %get-tuple-element.146), kind=kLoop, calls=%fused_computation.9 | loop fusion | flops 9216 | bytes 73728 | tf_op jit(solution)/shard_map/concatenate | solution.py:226
  27.6 0.0 collective-permute-start.5
  27.6 1.2 %collective-permute-done.5.y_ref = f32[9,8,128]{2,1,0:T(8,128)S(1)} collective-permute-done((f32[9,8,128]{2,1,0:T(8,128)S(1)}, f32[9,8,128]{2,1,0:T(8,128)S(1)}, u32[]{:S(2)}, u32[]{:S(2)}) %collective-permute-start.5) | collective-permute-done | bytes 36896 | tf_op jit(solution)/shard_map/ppermute | solution.py:21
  28.8 0.6 copy-done.8
  29.4 2.1 %shard_map.90 = (f32[5,64,128]{2,1,0:T(8,128)}, f32[2,64,128]{2,1,0:T(8,128)}) custom-call(f32[3,8,64,128]{3,2,1,0:T(8,128)} %get-tuple-element.142.e_ref.e_first.e_second.e_penult.e_last, f32[3,8,64,128]{3,2,1,0:T(8,128)} %get-tuple-element.142.e_ref.e_first.e_second.e_penult.e_last, ...), custom_call_target="tpu_custom_call" | custom-call | tf_op jit(solution)/shard_map/pallas_call | solution.py:347
  31.5 0.0 collective-permute-start.6
  31.5 4.7 %collective-permute-start.7 = (f32[2,64,128]{2,1,0:T(8,128)}, f32[2,64,128]{2,1,0:T(8,128)S(1)}, u32[]{:S(2)}, u32[]{:S(2)}) collective-permute-start(f32[2,64,128]{2,1,0:T(8,128)} %get-tuple-element.150), channel_id=1, source_target_pairs={{0,14},{2,0},{4,2},{6,4},{8,6},{10,8},{12,10},{14,12},{1,15},{3,1}... | collective-permute-start | bytes 196616 | tf_op jit(solution)/shard_map/ppermute | solution.py:21
  36.3 3.5 %shard_map.89 = (f32[3,8,64,128]{3,2,1,0:T(8,128)}, f32[3,8,64,128]{3,2,1,0:T(8,128)}, f32[7,8,128]{2,1,0:T(8,128)}, f32[2,1,128]{2,1,0:T(1,128)}) custom-call(f32[3,8,64,128]{3,2,1,0:T(8,128)} %get-tuple-element.142.e_ref.e_first.e_second.e_penult.e_last, f32[3,8,64,128]{3,2,1,0:T(8,128)} %get-tuple-element.143.h_ref.h_first.h_penult.h_last, ...), custom_call_target="tpu_custom_call" | custom-call | tf_op jit(solution)/shard_map/pallas_call | solution.py:351
  39.7 0.0 collective-permute-done.7.xhi_ref
  39.8 0.9 %collective-permute-done.6.xlo_ref = f32[5,64,128]{2,1,0:T(8,128)S(1)} collective-permute-done((f32[5,64,128]{2,1,0:T(8,128)}, f32[5,64,128]{2,1,0:T(8,128)S(1)}, u32[]{:S(2)}, u32[]{:S(2)}) %collective-permute-start.6) | collective-permute-done | bytes 163872 | tf_op jit(solution)/shard_map/ppermute | solution.py:21
  40.7 0.8 %pad_maximum_fusion.2 = f32[9,8,128]{2,1,0:T(8,128)S(1)} fusion(f32[2,8,128]{2,1,0:T(8,128)S(1)} %scatter.35, f32[7,8,128]{2,1,0:T(8,128)} %get-tuple-element.151), kind=kLoop, calls=%fused_computation.10 | loop fusion | flops 9216 | bytes 73728 | tf_op jit(solution)/shard_map/concatenate | solution.py:226
  41.5 1.2 %collective-permute-done.8.y_ref = f32[9,8,128]{2,1,0:T(8,128)S(1)} collective-permute-done((f32[9,8,128]{2,1,0:T(8,128)S(1)}, f32[9,8,128]{2,1,0:T(8,128)S(1)}, u32[]{:S(2)}, u32[]{:S(2)}) %collective-permute-start.8) | collective-permute-done | bytes 36896 | tf_op jit(solution)/shard_map/ppermute | solution.py:21
  42.8 0.6 copy-done.9
  43.4 2.1 %shard_map.92 = (f32[5,64,128]{2,1,0:T(8,128)}, f32[2,64,128]{2,1,0:T(8,128)}) custom-call(f32[3,8,64,128]{3,2,1,0:T(8,128)} %get-tuple-element.147.e_ref.e_first.e_second.e_penult.e_last, f32[3,8,64,128]{3,2,1,0:T(8,128)} %get-tuple-element.147.e_ref.e_first.e_second.e_penult.e_last, ...), custom_call_target="tpu_custom_call" | custom-call | tf_op jit(solution)/shard_map/pallas_call | solution.py:347
  45.5 0.0 collective-permute-start.9
  45.5 4.7 %collective-permute-start.10 = (f32[2,64,128]{2,1,0:T(8,128)}, f32[2,64,128]{2,1,0:T(8,128)S(1)}, u32[]{:S(2)}, u32[]{:S(2)}) collective-permute-start(f32[2,64,128]{2,1,0:T(8,128)} %get-tuple-element.155), channel_id=1, source_target_pairs={{0,14},{2,0},{4,2},{6,4},{8,6},{10,8},{12,10},{14,12},{1,15},{3,1}... | collective-permute-start | bytes 196616 | tf_op jit(solution)/shard_map/ppermute | solution.py:21
  50.2 3.5 %shard_map.91 = (f32[3,8,64,128]{3,2,1,0:T(8,128)}, f32[3,8,64,128]{3,2,1,0:T(8,128)}, f32[7,8,128]{2,1,0:T(8,128)}, f32[2,1,128]{2,1,0:T(1,128)}) custom-call(f32[3,8,64,128]{3,2,1,0:T(8,128)} %get-tuple-element.147.e_ref.e_first.e_second.e_penult.e_last, f32[3,8,64,128]{3,2,1,0:T(8,128)} %get-tuple-element.148.h_ref.h_first.h_penult.h_last, ...), custom_call_target="tpu_custom_call" | custom-call | tf_op jit(solution)/shard_map/pallas_call | solution.py:351
  53.7 0.0 collective-permute-done.10.xhi_ref
  53.7 0.9 %collective-permute-done.9.xlo_ref = f32[5,64,128]{2,1,0:T(8,128)S(1)} collective-permute-done((f32[5,64,128]{2,1,0:T(8,128)}, f32[5,64,128]{2,1,0:T(8,128)S(1)}, u32[]{:S(2)}, u32[]{:S(2)}) %collective-permute-start.9) | collective-permute-done | bytes 163872 | tf_op jit(solution)/shard_map/ppermute | solution.py:21
  54.7 0.8 %pad_maximum_fusion.3 = f32[9,8,128]{2,1,0:T(8,128)S(1)} fusion(f32[2,8,128]{2,1,0:T(8,128)S(1)} %scatter.39, f32[7,8,128]{2,1,0:T(8,128)} %get-tuple-element.156), kind=kLoop, calls=%fused_computation.11 | loop fusion | flops 9216 | bytes 73728 | tf_op jit(solution)/shard_map/concatenate | solution.py:226
  55.5 1.2 %collective-permute-done.11.y_ref = f32[9,8,128]{2,1,0:T(8,128)S(1)} collective-permute-done((f32[9,8,128]{2,1,0:T(8,128)S(1)}, f32[9,8,128]{2,1,0:T(8,128)S(1)}, u32[]{:S(2)}, u32[]{:S(2)}) %collective-permute-start.11) | collective-permute-done | bytes 36896 | tf_op jit(solution)/shard_map/ppermute | solution.py:21
  56.7 0.6 copy-done.11
  57.3 3.5 %shard_map.93 = (f32[3,8,64,128]{3,2,1,0:T(8,128)}, f32[3,8,64,128]{3,2,1,0:T(8,128)}, f32[7,8,128]{2,1,0:T(8,128)}, f32[2,1,128]{2,1,0:T(1,128)}) custom-call(f32[3,8,64,128]{3,2,1,0:T(8,128)} %get-tuple-element.152.e_ref, f32[3,8,64,128]{3,2,1,0:T(8,128)} %get-tuple-element.153.h_ref, f32[8,64,128]{2,1,0:T(8,128)} %get-tuple-element.135.keep_ref.keep_first.keep_last, ...), custom_call_target="tpu_custom_call" | custom-call | tf_op jit(solution)/shard_map/pallas_call | solution.py:351
  60.8 0.0 copy-start.13
  60.8 0.7 copy-done.16
  61.5 0.0 copy-done.15
  61.5 0.0 copy-done.13
  61.5 0.1 add_bitcast_fusion.2
  61.6 0.1 add_bitcast_fusion.3
  61.7 0.1 slice_select_fusion.2
  61.7 0.4 collective-permute-start.12
  62.1 4.1 %collective-permute-done.12 = f32[32,4]{0,1:T(4,128)S(1)} collective-permute-done((f32[32,4]{0,1:T(4,128)S(1)}, f32[32,4]{0,1:T(4,128)S(1)}, u32[]{:S(2)}, u32[]{:S(2)}) %collective-permute-start.12) | collective-permute-done | bytes 544 | tf_op jit(solution)/shard_map/ppermute | solution.py:274
  66.2 0.1 select_add_fusion.2
  66.3 0.1 slice_select_fusion.1
  66.4 3.6 %collective-permute-done.13 = f32[16,4]{0,1:T(4,128)S(1)} collective-permute-done((f32[16,4]{0,1:T(4,128)S(1)}, f32[16,4]{0,1:T(4,128)S(1)}, u32[]{:S(2)}, u32[]{:S(2)}) %collective-permute-start.13) | collective-permute-done | bytes 288 | tf_op jit(solution)/shard_map/ppermute | solution.py:274
  70.0 0.1 select_add_fusion.1
  70.0 0.1 slice_select_fusion
  70.1 3.6 %collective-permute-done.14 = f32[8,4]{0,1:T(4,128)S(1)} collective-permute-done((f32[8,4]{0,1:T(4,128)S(1)}, f32[8,4]{0,1:T(4,128)S(1)}, u32[]{:S(2)}, u32[]{:S(2)}) %collective-permute-start.14) | collective-permute-done | bytes 160 | tf_op jit(solution)/shard_map/ppermute | solution.py:274
  73.7 0.1 select_add_fusion
  73.8 1.2 %collective-permute-done.15 = f32[8,4]{0,1:T(4,128)S(1)} collective-permute-done((f32[8,4]{0,1:T(4,128)S(1)}, f32[8,4]{0,1:T(4,128)S(1)}, u32[]{:S(2)}, u32[]{:S(2)}) %collective-permute-start.15) | collective-permute-done | bytes 160 | tf_op jit(solution)/shard_map/ppermute | solution.py:284
  74.9 0.6 add_multiply_fusion
  (53 shorter events, 0.3 us)
Async XLA Ops:
  2.5 11.0 %collective-permute-start = (f32[5,64,128]{2,1,0:T(8,128)}, f32[5,64,128]{2,1,0:T(8,128)S(1)}, u32[]{:S(2)}, u32[]{:S(2)}) collective-permute-start(f32[5,64,128]{2,1,0:T(8,128)} %get-tuple-element.133), channel_id=1, source_target_pairs={{0,2},{2,4},{4,6},{6,8},{8,10},{10,12},{12,14},{14,0},{1,3},{3,5},... | collective-permute-start | bytes 491528 | tf_op jit(solution)/shard_map/ppermute | solution.py:21
  5.4 8.0 %collective-permute-start.1 = (f32[2,64,128]{2,1,0:T(8,128)}, f32[2,64,128]{2,1,0:T(8,128)S(1)}, u32[]{:S(2)}, u32[]{:S(2)}) collective-permute-start(f32[2,64,128]{2,1,0:T(8,128)} %get-tuple-element.134), channel_id=1, source_target_pairs={{0,14},{2,0},{4,2},{6,4},{8,6},{10,8},{12,10},{14,12},{1,15},{3,1}... | collective-permute-start | bytes 196616 | tf_op jit(solution)/shard_map/ppermute | solution.py:21
  8.5 0.7 copy-start.17
  10.2 3.3 %copy-start.12 = (f32[7,8,128]{2,1,0:T(8,128)S(1)}, f32[7,8,128]{2,1,0:T(8,128)}, u32[]{:S(2)}) copy-start(f32[7,8,128]{2,1,0:T(8,128)} %get-tuple-element.139) | copy-start | bytes 86020
  13.4 0.9 %copy-start.3 = (f32[2,64,128]{2,1,0:T(8,128)}, f32[2,64,128]{2,1,0:T(8,128)S(1)}, u32[]{:S(2)}) copy-start(f32[2,64,128]{2,1,0:T(8,128)S(1)} %collective-permute-done.1.xhi_ref) | copy-start | bytes 196612
  13.4 0.9 %copy-start = (f32[5,64,128]{2,1,0:T(8,128)}, f32[5,64,128]{2,1,0:T(8,128)S(1)}, u32[]{:S(2)}) copy-start(f32[5,64,128]{2,1,0:T(8,128)S(1)} %collective-permute-done.xlo_ref) | copy-start | bytes 491524
  13.5 1.3 %collective-permute-start.2 = (f32[9,8,128]{2,1,0:T(8,128)S(1)}, f32[9,8,128]{2,1,0:T(8,128)S(1)}, u32[]{:S(2)}, u32[]{:S(2)}) collective-permute-start(f32[9,8,128]{2,1,0:T(8,128)S(1)} %pad_maximum_fusion), channel_id=1, source_target_pairs={{0,1},{1,0},{2,3},{3,2},{4,5},{5,4},{6,7},{7,6},{8,9},{9,8},{10,11... | collective-permute-start | bytes 110600 | tf_op jit(solution)/shard_map/ppermute | solution.py:21
  14.8 0.6 copy-start.7
  17.6 9.2 %collective-permute-start.3 = (f32[5,64,128]{2,1,0:T(8,128)}, f32[5,64,128]{2,1,0:T(8,128)S(1)}, u32[]{:S(2)}, u32[]{:S(2)}) collective-permute-start(f32[5,64,128]{2,1,0:T(8,128)} %get-tuple-element.144), channel_id=1, source_target_pairs={{0,2},{2,4},{4,6},{6,8},{8,10},{10,12},{12,14},{14,0},{1,3},{3,5},... | collective-permute-start | bytes 491528 | tf_op jit(solution)/shard_map/ppermute | solution.py:21
  17.6 8.2 %collective-permute-start.4 = (f32[2,64,128]{2,1,0:T(8,128)}, f32[2,64,128]{2,1,0:T(8,128)S(1)}, u32[]{:S(2)}, u32[]{:S(2)}) collective-permute-start(f32[2,64,128]{2,1,0:T(8,128)} %get-tuple-element.145), channel_id=1, source_target_pairs={{0,14},{2,0},{4,2},{6,4},{8,6},{10,8},{12,10},{14,12},{1,15},{3,1}... | collective-permute-start | bytes 196616 | tf_op jit(solution)/shard_map/ppermute | solution.py:21
  25.8 3.0 %copy-start.5 = (f32[2,64,128]{2,1,0:T(8,128)}, f32[2,64,128]{2,1,0:T(8,128)S(1)}, u32[]{:S(2)}) copy-start(f32[2,64,128]{2,1,0:T(8,128)S(1)} %collective-permute-done.4.xhi_ref) | copy-start | bytes 196612
  26.7 2.1 %copy-start.2 = (f32[5,64,128]{2,1,0:T(8,128)}, f32[5,64,128]{2,1,0:T(8,128)S(1)}, u32[]{:S(2)}) copy-start(f32[5,64,128]{2,1,0:T(8,128)S(1)} %collective-permute-done.3.xlo_ref) | copy-start | bytes 491524
  27.6 1.2 %collective-permute-start.5 = (f32[9,8,128]{2,1,0:T(8,128)S(1)}, f32[9,8,128]{2,1,0:T(8,128)S(1)}, u32[]{:S(2)}, u32[]{:S(2)}) collective-permute-start(f32[9,8,128]{2,1,0:T(8,128)S(1)} %pad_maximum_fusion.1), channel_id=1, source_target_pairs={{0,1},{1,0},{2,3},{3,2},{4,5},{5,4},{6,7},{7,6},{8,9},{9,8},{10,11... | collective-permute-start | bytes 110600 | tf_op jit(solution)/shard_map/ppermute | solution.py:21
  28.8 0.6 copy-start.8
  31.5 9.2 %collective-permute-start.6 = (f32[5,64,128]{2,1,0:T(8,128)}, f32[5,64,128]{2,1,0:T(8,128)S(1)}, u32[]{:S(2)}, u32[]{:S(2)}) collective-permute-start(f32[5,64,128]{2,1,0:T(8,128)} %get-tuple-element.149), channel_id=1, source_target_pairs={{0,2},{2,4},{4,6},{6,8},{8,10},{10,12},{12,14},{14,0},{1,3},{3,5},... | collective-permute-start | bytes 491528 | tf_op jit(solution)/shard_map/ppermute | solution.py:21
  31.5 8.2 %collective-permute-start.7 = (f32[2,64,128]{2,1,0:T(8,128)}, f32[2,64,128]{2,1,0:T(8,128)S(1)}, u32[]{:S(2)}, u32[]{:S(2)}) collective-permute-start(f32[2,64,128]{2,1,0:T(8,128)} %get-tuple-element.150), channel_id=1, source_target_pairs={{0,14},{2,0},{4,2},{6,4},{8,6},{10,8},{12,10},{14,12},{1,15},{3,1}... | collective-permute-start | bytes 196616 | tf_op jit(solution)/shard_map/ppermute | solution.py:21
  39.7 3.0 %copy-start.4 = (f32[2,64,128]{2,1,0:T(8,128)}, f32[2,64,128]{2,1,0:T(8,128)S(1)}, u32[]{:S(2)}) copy-start(f32[2,64,128]{2,1,0:T(8,128)S(1)} %collective-permute-done.7.xhi_ref) | copy-start | bytes 196612
  40.7 2.1 %copy-start.1 = (f32[5,64,128]{2,1,0:T(8,128)}, f32[5,64,128]{2,1,0:T(8,128)S(1)}, u32[]{:S(2)}) copy-start(f32[5,64,128]{2,1,0:T(8,128)S(1)} %collective-permute-done.6.xlo_ref) | copy-start | bytes 491524
  41.5 1.2 %collective-permute-start.8 = (f32[9,8,128]{2,1,0:T(8,128)S(1)}, f32[9,8,128]{2,1,0:T(8,128)S(1)}, u32[]{:S(2)}, u32[]{:S(2)}) collective-permute-start(f32[9,8,128]{2,1,0:T(8,128)S(1)} %pad_maximum_fusion.2), channel_id=1, source_target_pairs={{0,1},{1,0},{2,3},{3,2},{4,5},{5,4},{6,7},{7,6},{8,9},{9,8},{10,11... | collective-permute-start | bytes 110600 | tf_op jit(solution)/shard_map/ppermute | solution.py:21
  42.7 0.6 copy-start.9
  45.5 9.2 %collective-permute-start.9 = (f32[5,64,128]{2,1,0:T(8,128)}, f32[5,64,128]{2,1,0:T(8,128)S(1)}, u32[]{:S(2)}, u32[]{:S(2)}) collective-permute-start(f32[5,64,128]{2,1,0:T(8,128)} %get-tuple-element.154), channel_id=1, source_target_pairs={{0,2},{2,4},{4,6},{6,8},{8,10},{10,12},{12,14},{14,0},{1,3},{3,5},... | collective-permute-start | bytes 491528 | tf_op jit(solution)/shard_map/ppermute | solution.py:21
  45.5 8.2 %collective-permute-start.10 = (f32[2,64,128]{2,1,0:T(8,128)}, f32[2,64,128]{2,1,0:T(8,128)S(1)}, u32[]{:S(2)}, u32[]{:S(2)}) collective-permute-start(f32[2,64,128]{2,1,0:T(8,128)} %get-tuple-element.155), channel_id=1, source_target_pairs={{0,14},{2,0},{4,2},{6,4},{8,6},{10,8},{12,10},{14,12},{1,15},{3,1}... | collective-permute-start | bytes 196616 | tf_op jit(solution)/shard_map/ppermute | solution.py:21
  53.7 3.0 %copy-start.10 = (f32[2,64,128]{2,1,0:T(8,128)}, f32[2,64,128]{2,1,0:T(8,128)S(1)}, u32[]{:S(2)}) copy-start(f32[2,64,128]{2,1,0:T(8,128)S(1)} %collective-permute-done.10.xhi_ref) | copy-start | bytes 196612
  54.7 2.1 %copy-start.6 = (f32[5,64,128]{2,1,0:T(8,128)}, f32[5,64,128]{2,1,0:T(8,128)S(1)}, u32[]{:S(2)}) copy-start(f32[5,64,128]{2,1,0:T(8,128)S(1)} %collective-permute-done.9.xlo_ref) | copy-start | bytes 491524
  55.5 1.2 %collective-permute-start.11 = (f32[9,8,128]{2,1,0:T(8,128)S(1)}, f32[9,8,128]{2,1,0:T(8,128)S(1)}, u32[]{:S(2)}, u32[]{:S(2)}) collective-permute-start(f32[9,8,128]{2,1,0:T(8,128)S(1)} %pad_maximum_fusion.3), channel_id=1, source_target_pairs={{0,1},{1,0},{2,3},{3,2},{4,5},{5,4},{6,7},{7,6},{8,9},{9,8},{10,11... | collective-permute-start | bytes 110600 | tf_op jit(solution)/shard_map/ppermute | solution.py:21
  56.7 0.6 copy-start.11
  60.8 0.7 copy-start.16
  60.8 0.7 copy-start.14
  60.8 0.7 copy-start.15
  60.8 0.7 copy-start.13
  61.7 4.5 %collective-permute-start.12 = (f32[32,4]{0,1:T(4,128)S(1)}, f32[32,4]{0,1:T(4,128)S(1)}, u32[]{:S(2)}, u32[]{:S(2)}) collective-permute-start(f32[32,4]{0,1:T(4,128)S(1)} %slice_select_fusion.2), channel_id=1, source_target_pairs={{0,8},{2,10},{4,12},{6,14},{8,0},{10,2},{12,4},{14,6},{1,9},{3,11}... | collective-permute-start | bytes 1544 | tf_op jit(solution)/shard_map/ppermute | solution.py:274
  66.4 3.6 %collective-permute-start.13 = (f32[16,4]{0,1:T(4,128)S(1)}, f32[16,4]{0,1:T(4,128)S(1)}, u32[]{:S(2)}, u32[]{:S(2)}) collective-permute-start(f32[16,4]{0,1:T(4,128)S(1)} %slice_select_fusion.1), channel_id=1, source_target_pairs={{0,4},{2,6},{4,0},{6,2},{8,12},{10,14},{12,8},{14,10},{1,5},{3,7},... | collective-permute-start | bytes 776 | tf_op jit(solution)/shard_map/ppermute | solution.py:274
  70.1 3.6 %collective-permute-start.14 = (f32[8,4]{0,1:T(4,128)S(1)}, f32[8,4]{0,1:T(4,128)S(1)}, u32[]{:S(2)}, u32[]{:S(2)}) collective-permute-start(f32[8,4]{0,1:T(4,128)S(1)} %slice_select_fusion), channel_id=1, source_target_pairs={{0,2},{2,0},{4,6},{6,4},{8,10},{10,8},{12,14},{14,12},{1,3},{3,1},... | collective-permute-start | bytes 392 | tf_op jit(solution)/shard_map/ppermute | solution.py:274
  73.8 1.2 %collective-permute-start.15 = (f32[8,4]{0,1:T(4,128)S(1)}, f32[8,4]{0,1:T(4,128)S(1)}, u32[]{:S(2)}, u32[]{:S(2)}) collective-permute-start(f32[8,4]{0,1:T(4,128)S(1)} %select_add_fusion), channel_id=1, source_target_pairs={{0,1},{1,0},{2,3},{3,2},{4,5},{5,4},{6,7},{7,6},{8,9},{9,8},{10,11... | collective-permute-start | bytes 392 | tf_op jit(solution)/shard_map/ppermute | solution.py:284

commit v15 on v14

--- a/solution.py
+++ b/solution.py
@@ -165,16 +165,16 @@
         g_out[comp] = sums[comp].T[depth - 3:depth - 2]
 
 
-def _edge_kernel(e_first, e_second, e_penult, e_last, h_first, h_penult, h_last,
+def _edge_kernel(e_low, e_high, h_first, h_high,
                  keep_first, keep_last, drive_first, drive_last, xlo_ref, xhi_ref, y_ref,
                  xlo_out, xhi_out, *, planes):
     c1_ref = y_ref.at[7, 0:1]
     c2_ref = y_ref.at[8, 0:1]
     yhi_ref = y_ref.at[5:7]
-    e_blocks = {0: e_first, 1: e_second, planes - 2: e_penult, planes - 1: e_last}
-    h_blocks = {0: h_first, planes - 2: h_penult, planes - 1: h_last}
-    elec = lambda comp, x: e_blocks[x][comp, 0]
-    magn = lambda comp, x: h_blocks[x][comp, 0]
+    e_blocks = {0: (e_low, 0), 1: (e_low, 1), planes - 2: (e_high, 0), planes - 1: (e_high, 1)}
+    h_blocks = {0: (h_first, 0), planes - 2: (h_high, 0), planes - 1: (h_high, 1)}
+    elec = lambda comp, x: e_blocks[x][0][comp, e_blocks[x][1]]
+    magn = lambda comp, x: h_blocks[x][0][comp, h_blocks[x][1]]
     hy_prev, hz_prev = _magn_before(elec, xlo_ref, c1_ref)
     old = _magn_plane(elec, magn, 0, planes, xhi_ref, yhi_ref)
     ex_new, ey_new, ez_new = _elec_plane(
@@ -302,6 +302,9 @@
     def field_plane(index):
         return pl.BlockSpec((comps, 1, cells_y, depth), lambda i: (0, index, 0, 0))
 
+    def field_pair(index):
+        return pl.BlockSpec((comps, 2, cells_y, depth), lambda i: (0, index, 0, 0))
+
     def coef_plane(index):
         return pl.BlockSpec((1, cells_y, depth), lambda i: (index, 0, 0))
 
@@ -311,8 +314,8 @@
         functools.partial(_edge_kernel, planes=cells_x),
         out_shape=(xlo_shape, xhi_shape),
         grid=(1,),
-        in_specs=[field_plane(i) for i in (first, 1, last - 1, last)]
-        + [field_plane(i) for i in (first, last - 1, last)]
+        in_specs=[field_pair(0), field_pair(cells_x // 2 - 1), field_plane(first),
+                  field_pair(cells_x // 2 - 1)]
         + [coef_plane(first), coef_plane(last), coef_plane(first), coef_plane(last)]
         + [whole] * 3,
         out_specs=(whole, whole),
@@ -345,7 +348,7 @@
     for number in range(ITERS):
         if number + 1 < ITERS:
             edges = edge_call(
-                elec, elec, elec, elec, magn, magn, magn, keep, keep, drive, drive, xlo, xhi, rows
+                elec, elec, magn, magn, keep, keep, drive, drive, xlo, xhi, rows
             )
             next_xlo, next_xhi = exchange_x(*edges)
         elec, magn, new_rows, sums = step_call(elec, magn, keep, drive, xlo, xhi, rows, basis)

time: 76.2 us -> 76.4 us (level)
  transfers between devices with their start and end apart: 16 -> 16, of which waited for: 12 -> 12; matrix products, arithmetic and copies ran while one was open for 2% -> 2% of each run, Pallas kernels for 17% -> 16%
where the time goes in v15:
time: 76.4 us; the launch traced here: 75.7 us
  Pallas kernels  24.4 us (32%)
  starting transfers between devices  20.6 us (27%)
  waiting for transfers between devices  20.6 us (27%)
  other arithmetic  5.08 us (7%)
  local copies, waits for them, and re-layouts  4.22 us (6%)
  between operations  0.81 us (1%)
    ppermute x12, starting transfers between devices, shifted(): return lax.ppermute(value, axis, pairs)  20.3 us
    pallas_call x4, Pallas kernels, local(): step_call(elec, magn, keep, drive, xlo, xhi, rows, basis)  13.9 us
    ppermute x3, waiting for transfers between devices, scatter_sum(): rows = keep + lax.ppermute(send, axis, pairs)  11.3 us
    ppermute x12, waiting for transfers between devices, shifted(): return lax.ppermute(value, axis, pairs)  8.13 us
    pallas_call x3, Pallas kernels, local(): edge_call(elec, elec, magn, magn, keep, keep, drive, drive, xlo, xhi, rows)  6.59 us
    unnamed x36, local copies, waits for them, and re-layouts  3.83 us
    concatenate x4, other arithmetic, exchange_y(): message = jnp.concatenate([rows, corners])  2.35 us
    pallas_call x1, Pallas kernels, coefficients(): pl.pallas_call(_coef_kernel, out_shape=(out, out), in_specs=[scalar, scal...  2.01 us
  transfers between devices with their start and end apart: 16, of which 12 were waited for; matrix products, arithmetic and copies ran while one was open for 2% of the time, Pallas kernels for 16%

profile of v15, /device:TPU:0, one launch (start us, length us, event | category | flops | bytes accessed | tf_op | source)
XLA Modules:
  0.0 75.7 jit_solution(2347982928763172424)
XLA Ops:
  0.6 1.9 %shard_map.86 = (f32[5,64,128]{2,1,0:T(8,128)}, f32[2,64,128]{2,1,0:T(8,128)}, f32[7,8,128]{2,1,0:T(8,128)}) custom-call(f32[3,8,64,128]{3,2,1,0:T(8,128)} %e_high.1, f32[3,8,64,128]{3,2,1,0:T(8,128)} %e_high.1, f32[3,8,64,128]{3,2,1,0:T(8,128)} %h_high.1, f32[3,8,64,128]{3,2,1,0:T(8,128)} %e_high.1, f32[3,8,64,128]{3,2,1,0:T(8,128)} %e_high.1, ...), custom_call_target="tpu_custom_call" | custom-call | tf_op jit(solution)/shard_map/pallas_call | solution.py:329
  2.5 3.0 %collective-permute-start = (f32[5,64,128]{2,1,0:T(8,128)}, f32[5,64,128]{2,1,0:T(8,128)S(1)}, u32[]{:S(2)}, u32[]{:S(2)}) collective-permute-start(f32[5,64,128]{2,1,0:T(8,128)} %get-tuple-element.133), channel_id=1, source_target_pairs={{0,2},{2,4},{4,6},{6,8},{8,10},{10,12},{12,14},{14,0},{1,3},{3,5},... | collective-permute-start | bytes 491528 | tf_op jit(solution)/shard_map/ppermute | solution.py:21
  5.4 3.0 %collective-permute-start.1 = (f32[2,64,128]{2,1,0:T(8,128)}, f32[2,64,128]{2,1,0:T(8,128)S(1)}, u32[]{:S(2)}, u32[]{:S(2)}) collective-permute-start(f32[2,64,128]{2,1,0:T(8,128)} %get-tuple-element.134), channel_id=1, source_target_pairs={{0,14},{2,0},{4,2},{6,4},{8,6},{10,8},{12,10},{14,12},{1,15},{3,1}... | collective-permute-start | bytes 196616 | tf_op jit(solution)/shard_map/ppermute | solution.py:21
  8.5 0.7 copy-done.17
  9.2 0.1 multiply_multiply_fusion.1
  9.3 0.1 copy.12
  9.3 0.1 multiply_multiply_fusion
  9.4 0.1 broadcast_add_fusion
  9.6 0.1 add.227
  9.7 0.5 fusion.4
  10.2 2.0 %shard_map.85 = (f32[8,64,128]{2,1,0:T(8,128)}, f32[8,64,128]{2,1,0:T(8,128)}) custom-call(f32[6]{0:T(128)} %eps_ref.1, f32[6]{0:T(128)} %sigma_ref.1, s32[8,64,128]{2,1,0:T(8,128)} %mat_ref.1), custom_call_target="tpu_custom_call" | custom-call | tf_op jit(solution)/shard_map/pallas_call | solution.py:43
  12.2 1.2 %collective-permute-done.1.xhi_ref = f32[2,64,128]{2,1,0:T(8,128)S(1)} collective-permute-done((f32[2,64,128]{2,1,0:T(8,128)}, f32[2,64,128]{2,1,0:T(8,128)S(1)}, u32[]{:S(2)}, u32[]{:S(2)}) %collective-permute-start.1) | collective-permute-done | bytes 65568 | tf_op jit(solution)/shard_map/ppermute | solution.py:21
  13.4 0.0 collective-permute-done.xlo_ref
  13.5 0.1 collective-permute-start.2
  13.6 0.7 maximum_bitcast_fusion.basis_ref
  14.3 0.5 collective-permute-done.2.y_ref
  14.8 0.6 copy-done.7
  15.4 2.2 %shard_map.88 = (f32[5,64,128]{2,1,0:T(8,128)}, f32[2,64,128]{2,1,0:T(8,128)}) custom-call(f32[3,8,64,128]{3,2,1,0:T(8,128)} %e_high.1, f32[3,8,64,128]{3,2,1,0:T(8,128)} %e_high.1, f32[3,8,64,128]{3,2,1,0:T(8,128)} %h_high.1, f32[3,8,64,128]{3,2,1,0:T(8,128)} %h_high.1, f32[8,64,128]{2,1,0:T(8,128)} %get-tuple-element.135.keep_ref.keep_first.keep_last, ...), custom_call_target="tpu_custom_call" | custom-call | tf_op jit(solution)/shard_map/pallas_call | solution.py:350
  17.6 0.0 collective-permute-start.3
  17.6 4.7 %collective-permute-start.4 = (f32[2,64,128]{2,1,0:T(8,128)}, f32[2,64,128]{2,1,0:T(8,128)S(1)}, u32[]{:S(2)}, u32[]{:S(2)}) collective-permute-start(f32[2,64,128]{2,1,0:T(8,128)} %get-tuple-element.145), channel_id=1, source_target_pairs={{0,14},{2,0},{4,2},{6,4},{8,6},{10,8},{12,10},{14,12},{1,15},{3,1}... | collective-permute-start | bytes 196616 | tf_op jit(solution)/shard_map/ppermute | solution.py:21
  22.4 3.5 %shard_map.87 = (f32[3,8,64,128]{3,2,1,0:T(8,128)}, f32[3,8,64,128]{3,2,1,0:T(8,128)}, f32[7,8,128]{2,1,0:T(8,128)}, f32[2,1,128]{2,1,0:T(1,128)}) custom-call(f32[3,8,64,128]{3,2,1,0:T(8,128)} %e_high.1, f32[3,8,64,128]{3,2,1,0:T(8,128)} %h_high.1, f32[8,64,128]{2,1,0:T(8,128)} %get-tuple-element.135.keep_ref.keep_first.keep_last, ...), custom_call_target="tpu_custom_call" | custom-call | tf_op jit(solution)/shard_map/pallas_call | solution.py:354
  25.8 0.0 collective-permute-done.4.xhi_ref
  25.8 1.0 %collective-permute-done.3.xlo_ref = f32[5,64,128]{2,1,0:T(8,128)S(1)} collective-permute-done((f32[5,64,128]{2,1,0:T(8,128)}, f32[5,64,128]{2,1,0:T(8,128)S(1)}, u32[]{:S(2)}, u32[]{:S(2)}) %collective-permute-start.3) | collective-permute-done | bytes 163872 | tf_op jit(solution)/shard_map/ppermute | solution.py:21
  26.8 0.8 %pad_maximum_fusion.1 = f32[9,8,128]{2,1,0:T(8,128)S(1)} fusion(f32[2,8,128]{2,1,0:T(8,128)S(1)} %scatter.31, f32[7,8,128]{2,1,0:T(8,128)} %get-tuple-element.146), kind=kLoop, calls=%fused_computation.9 | loop fusion | flops 9216 | bytes 73728 | tf_op jit(solution)/shard_map/concatenate | solution.py:226
  27.6 1.2 %collective-permute-done.5.y_ref = f32[9,8,128]{2,1,0:T(8,128)S(1)} collective-permute-done((f32[9,8,128]{2,1,0:T(8,128)S(1)}, f32[9,8,128]{2,1,0:T(8,128)S(1)}, u32[]{:S(2)}, u32[]{:S(2)}) %collective-permute-start.5) | collective-permute-done | bytes 36896 | tf_op jit(solution)/shard_map/ppermute | solution.py:21
  28.9 0.6 copy-done.8
  29.5 2.2 %shard_map.90 = (f32[5,64,128]{2,1,0:T(8,128)}, f32[2,64,128]{2,1,0:T(8,128)}) custom-call(f32[3,8,64,128]{3,2,1,0:T(8,128)} %get-tuple-element.142.e_ref.e_low.e_high, f32[3,8,64,128]{3,2,1,0:T(8,128)} %get-tuple-element.142.e_ref.e_low.e_high, f32[3,8,64,128]{3,2,1,0:T(8,128)} %get-tuple-element.143.h_ref.h_first.h_high, ...), custom_call_target="tpu_custom_call" | custom-call | tf_op jit(solution)/shard_map/pallas_call | solution.py:350
  31.7 4.7 %collective-permute-start.7 = (f32[2,64,128]{2,1,0:T(8,128)}, f32[2,64,128]{2,1,0:T(8,128)S(1)}, u32[]{:S(2)}, u32[]{:S(2)}) collective-permute-start(f32[2,64,128]{2,1,0:T(8,128)} %get-tuple-element.150), channel_id=1, source_target_pairs={{0,14},{2,0},{4,2},{6,4},{8,6},{10,8},{12,10},{14,12},{1,15},{3,1}... | collective-permute-start | bytes 196616 | tf_op jit(solution)/shard_map/ppermute | solution.py:21
  36.4 3.5 %shard_map.89 = (f32[3,8,64,128]{3,2,1,0:T(8,128)}, f32[3,8,64,128]{3,2,1,0:T(8,128)}, f32[7,8,128]{2,1,0:T(8,128)}, f32[2,1,128]{2,1,0:T(1,128)}) custom-call(f32[3,8,64,128]{3,2,1,0:T(8,128)} %get-tuple-element.142.e_ref.e_low.e_high, f32[3,8,64,128]{3,2,1,0:T(8,128)} %get-tuple-element.143.h_ref.h_first.h_high, ...), custom_call_target="tpu_custom_call" | custom-call | tf_op jit(solution)/shard_map/pallas_call | solution.py:354
  39.9 0.9 %collective-permute-done.6.xlo_ref = f32[5,64,128]{2,1,0:T(8,128)S(1)} collective-permute-done((f32[5,64,128]{2,1,0:T(8,128)}, f32[5,64,128]{2,1,0:T(8,128)S(1)}, u32[]{:S(2)}, u32[]{:S(2)}) %collective-permute-start.6) | collective-permute-done | bytes 163872 | tf_op jit(solution)/shard_map/ppermute | solution.py:21
  40.9 0.8 %pad_maximum_fusion.2 = f32[9,8,128]{2,1,0:T(8,128)S(1)} fusion(f32[2,8,128]{2,1,0:T(8,128)S(1)} %scatter.35, f32[7,8,128]{2,1,0:T(8,128)} %get-tuple-element.151), kind=kLoop, calls=%fused_computation.10 | loop fusion | flops 9216 | bytes 73728 | tf_op jit(solution)/shard_map/concatenate | solution.py:226
  41.7 0.0 collective-permute-start.8
  41.7 1.2 %collective-permute-done.8.y_ref = f32[9,8,128]{2,1,0:T(8,128)S(1)} collective-permute-done((f32[9,8,128]{2,1,0:T(8,128)S(1)}, f32[9,8,128]{2,1,0:T(8,128)S(1)}, u32[]{:S(2)}, u32[]{:S(2)}) %collective-permute-start.8) | collective-permute-done | bytes 36896 | tf_op jit(solution)/shard_map/ppermute | solution.py:21
  42.9 0.6 copy-done.9
  43.5 2.2 %shard_map.92 = (f32[5,64,128]{2,1,0:T(8,128)}, f32[2,64,128]{2,1,0:T(8,128)}) custom-call(f32[3,8,64,128]{3,2,1,0:T(8,128)} %get-tuple-element.147.e_ref.e_low.e_high, f32[3,8,64,128]{3,2,1,0:T(8,128)} %get-tuple-element.147.e_ref.e_low.e_high, f32[3,8,64,128]{3,2,1,0:T(8,128)} %get-tuple-element.148.h_ref.h_first.h_high, ...), custom_call_target="tpu_custom_call" | custom-call | tf_op jit(solution)/shard_map/pallas_call | solution.py:350
  45.7 0.0 collective-permute-start.9
  45.7 4.7 %collective-permute-start.10 = (f32[2,64,128]{2,1,0:T(8,128)}, f32[2,64,128]{2,1,0:T(8,128)S(1)}, u32[]{:S(2)}, u32[]{:S(2)}) collective-permute-start(f32[2,64,128]{2,1,0:T(8,128)} %get-tuple-element.155), channel_id=1, source_target_pairs={{0,14},{2,0},{4,2},{6,4},{8,6},{10,8},{12,10},{14,12},{1,15},{3,1}... | collective-permute-start | bytes 196616 | tf_op jit(solution)/shard_map/ppermute | solution.py:21
  50.4 3.5 %shard_map.91 = (f32[3,8,64,128]{3,2,1,0:T(8,128)}, f32[3,8,64,128]{3,2,1,0:T(8,128)}, f32[7,8,128]{2,1,0:T(8,128)}, f32[2,1,128]{2,1,0:T(1,128)}) custom-call(f32[3,8,64,128]{3,2,1,0:T(8,128)} %get-tuple-element.147.e_ref.e_low.e_high, f32[3,8,64,128]{3,2,1,0:T(8,128)} %get-tuple-element.148.h_ref.h_first.h_high, ...), custom_call_target="tpu_custom_call" | custom-call | tf_op jit(solution)/shard_map/pallas_call | solution.py:354
  53.9 0.0 collective-permute-done.10.xhi_ref
  53.9 0.9 %collective-permute-done.9.xlo_ref = f32[5,64,128]{2,1,0:T(8,128)S(1)} collective-permute-done((f32[5,64,128]{2,1,0:T(8,128)}, f32[5,64,128]{2,1,0:T(8,128)S(1)}, u32[]{:S(2)}, u32[]{:S(2)}) %collective-permute-start.9) | collective-permute-done | bytes 163872 | tf_op jit(solution)/shard_map/ppermute | solution.py:21
  54.9 0.8 %pad_maximum_fusion.3 = f32[9,8,128]{2,1,0:T(8,128)S(1)} fusion(f32[2,8,128]{2,1,0:T(8,128)S(1)} %scatter.39, f32[7,8,128]{2,1,0:T(8,128)} %get-tuple-element.156), kind=kLoop, calls=%fused_computation.11 | loop fusion | flops 9216 | bytes 73728 | tf_op jit(solution)/shard_map/concatenate | solution.py:226
  55.7 0.0 collective-permute-start.11
  55.7 1.2 %collective-permute-done.11.y_ref = f32[9,8,128]{2,1,0:T(8,128)S(1)} collective-permute-done((f32[9,8,128]{2,1,0:T(8,128)S(1)}, f32[9,8,128]{2,1,0:T(8,128)S(1)}, u32[]{:S(2)}, u32[]{:S(2)}) %collective-permute-start.11) | collective-permute-done | bytes 36896 | tf_op jit(solution)/shard_map/ppermute | solution.py:21
  56.9 0.6 copy-done.11
  57.5 3.5 %shard_map.93 = (f32[3,8,64,128]{3,2,1,0:T(8,128)}, f32[3,8,64,128]{3,2,1,0:T(8,128)}, f32[7,8,128]{2,1,0:T(8,128)}, f32[2,1,128]{2,1,0:T(1,128)}) custom-call(f32[3,8,64,128]{3,2,1,0:T(8,128)} %get-tuple-element.152.e_ref, f32[3,8,64,128]{3,2,1,0:T(8,128)} %get-tuple-element.153.h_ref, f32[8,64,128]{2,1,0:T(8,128)} %get-tuple-element.135.keep_ref.keep_first.keep_last, ...), custom_call_target="tpu_custom_call" | custom-call | tf_op jit(solution)/shard_map/pallas_call | solution.py:354
  61.0 0.0 copy-start.13
  61.0 0.7 copy-done.16
  61.7 0.0 copy-done.15
  61.7 0.0 copy-done.13
  61.7 0.1 add_bitcast_fusion.2
  61.8 0.1 add_bitcast_fusion.3
  61.9 0.1 slice_select_fusion.2
  61.9 0.4 collective-permute-start.12
  62.3 4.1 %collective-permute-done.12 = f32[32,4]{0,1:T(4,128)S(1)} collective-permute-done((f32[32,4]{0,1:T(4,128)S(1)}, f32[32,4]{0,1:T(4,128)S(1)}, u32[]{:S(2)}, u32[]{:S(2)}) %collective-permute-start.12) | collective-permute-done | bytes 544 | tf_op jit(solution)/shard_map/ppermute | solution.py:274
  66.4 0.1 select_add_fusion.2
  66.5 0.1 slice_select_fusion.1
  66.6 3.6 %collective-permute-done.13 = f32[16,4]{0,1:T(4,128)S(1)} collective-permute-done((f32[16,4]{0,1:T(4,128)S(1)}, f32[16,4]{0,1:T(4,128)S(1)}, u32[]{:S(2)}, u32[]{:S(2)}) %collective-permute-start.13) | collective-permute-done | bytes 288 | tf_op jit(solution)/shard_map/ppermute | solution.py:274
  70.2 0.1 select_add_fusion.1
  70.2 0.1 slice_select_fusion
  70.3 0.0 collective-permute-start.14
  70.3 3.6 %collective-permute-done.14 = f32[8,4]{0,1:T(4,128)S(1)} collective-permute-done((f32[8,4]{0,1:T(4,128)S(1)}, f32[8,4]{0,1:T(4,128)S(1)}, u32[]{:S(2)}, u32[]{:S(2)}) %collective-permute-start.14) | collective-permute-done | bytes 160 | tf_op jit(solution)/shard_map/ppermute | solution.py:274
  73.9 0.1 select_add_fusion
  74.0 1.2 %collective-permute-done.15 = f32[8,4]{0,1:T(4,128)S(1)} collective-permute-done((f32[8,4]{0,1:T(4,128)S(1)}, f32[8,4]{0,1:T(4,128)S(1)}, u32[]{:S(2)}, u32[]{:S(2)}) %collective-permute-start.15) | collective-permute-done | bytes 160 | tf_op jit(solution)/shard_map/ppermute | solution.py:284
  75.1 0.6 add_multiply_fusion
  (53 shorter events, 0.3 us)
Async XLA Ops:
  2.5 11.0 %collective-permute-start = (f32[5,64,128]{2,1,0:T(8,128)}, f32[5,64,128]{2,1,0:T(8,128)S(1)}, u32[]{:S(2)}, u32[]{:S(2)}) collective-permute-start(f32[5,64,128]{2,1,0:T(8,128)} %get-tuple-element.133), channel_id=1, source_target_pairs={{0,2},{2,4},{4,6},{6,8},{8,10},{10,12},{12,14},{14,0},{1,3},{3,5},... | collective-permute-start | bytes 491528 | tf_op jit(solution)/shard_map/ppermute | solution.py:21
  5.4 8.0 %collective-permute-start.1 = (f32[2,64,128]{2,1,0:T(8,128)}, f32[2,64,128]{2,1,0:T(8,128)S(1)}, u32[]{:S(2)}, u32[]{:S(2)}) collective-permute-start(f32[2,64,128]{2,1,0:T(8,128)} %get-tuple-element.134), channel_id=1, source_target_pairs={{0,14},{2,0},{4,2},{6,4},{8,6},{10,8},{12,10},{14,12},{1,15},{3,1}... | collective-permute-start | bytes 196616 | tf_op jit(solution)/shard_map/ppermute | solution.py:21
  8.5 0.7 copy-start.17
  10.2 3.3 %copy-start.12 = (f32[7,8,128]{2,1,0:T(8,128)S(1)}, f32[7,8,128]{2,1,0:T(8,128)}, u32[]{:S(2)}) copy-start(f32[7,8,128]{2,1,0:T(8,128)} %get-tuple-element.139) | copy-start | bytes 86020
  13.4 0.9 %copy-start.3 = (f32[2,64,128]{2,1,0:T(8,128)}, f32[2,64,128]{2,1,0:T(8,128)S(1)}, u32[]{:S(2)}) copy-start(f32[2,64,128]{2,1,0:T(8,128)S(1)} %collective-permute-done.1.xhi_ref) | copy-start | bytes 196612
  13.4 0.9 %copy-start = (f32[5,64,128]{2,1,0:T(8,128)}, f32[5,64,128]{2,1,0:T(8,128)S(1)}, u32[]{:S(2)}) copy-start(f32[5,64,128]{2,1,0:T(8,128)S(1)} %collective-permute-done.xlo_ref) | copy-start | bytes 491524
  13.5 1.3 %collective-permute-start.2 = (f32[9,8,128]{2,1,0:T(8,128)S(1)}, f32[9,8,128]{2,1,0:T(8,128)S(1)}, u32[]{:S(2)}, u32[]{:S(2)}) collective-permute-start(f32[9,8,128]{2,1,0:T(8,128)S(1)} %pad_maximum_fusion), channel_id=1, source_target_pairs={{0,1},{1,0},{2,3},{3,2},{4,5},{5,4},{6,7},{7,6},{8,9},{9,8},{10,11... | collective-permute-start | bytes 110600 | tf_op jit(solution)/shard_map/ppermute | solution.py:21
  14.8 0.6 copy-start.7
  17.6 9.2 %collective-permute-start.3 = (f32[5,64,128]{2,1,0:T(8,128)}, f32[5,64,128]{2,1,0:T(8,128)S(1)}, u32[]{:S(2)}, u32[]{:S(2)}) collective-permute-start(f32[5,64,128]{2,1,0:T(8,128)} %get-tuple-element.144), channel_id=1, source_target_pairs={{0,2},{2,4},{4,6},{6,8},{8,10},{10,12},{12,14},{14,0},{1,3},{3,5},... | collective-permute-start | bytes 491528 | tf_op jit(solution)/shard_map/ppermute | solution.py:21
  17.6 8.2 %collective-permute-start.4 = (f32[2,64,128]{2,1,0:T(8,128)}, f32[2,64,128]{2,1,0:T(8,128)S(1)}, u32[]{:S(2)}, u32[]{:S(2)}) collective-permute-start(f32[2,64,128]{2,1,0:T(8,128)} %get-tuple-element.145), channel_id=1, source_target_pairs={{0,14},{2,0},{4,2},{6,4},{8,6},{10,8},{12,10},{14,12},{1,15},{3,1}... | collective-permute-start | bytes 196616 | tf_op jit(solution)/shard_map/ppermute | solution.py:21
  25.8 3.0 %copy-start.5 = (f32[2,64,128]{2,1,0:T(8,128)}, f32[2,64,128]{2,1,0:T(8,128)S(1)}, u32[]{:S(2)}) copy-start(f32[2,64,128]{2,1,0:T(8,128)S(1)} %collective-permute-done.4.xhi_ref) | copy-start | bytes 196612
  26.8 2.1 %copy-start.2 = (f32[5,64,128]{2,1,0:T(8,128)}, f32[5,64,128]{2,1,0:T(8,128)S(1)}, u32[]{:S(2)}) copy-start(f32[5,64,128]{2,1,0:T(8,128)S(1)} %collective-permute-done.3.xlo_ref) | copy-start | bytes 491524
  27.6 1.2 %collective-permute-start.5 = (f32[9,8,128]{2,1,0:T(8,128)S(1)}, f32[9,8,128]{2,1,0:T(8,128)S(1)}, u32[]{:S(2)}, u32[]{:S(2)}) collective-permute-start(f32[9,8,128]{2,1,0:T(8,128)S(1)} %pad_maximum_fusion.1), channel_id=1, source_target_pairs={{0,1},{1,0},{2,3},{3,2},{4,5},{5,4},{6,7},{7,6},{8,9},{9,8},{10,11... | collective-permute-start | bytes 110600 | tf_op jit(solution)/shard_map/ppermute | solution.py:21
  28.8 0.6 copy-start.8
  31.7 9.2 %collective-permute-start.6 = (f32[5,64,128]{2,1,0:T(8,128)}, f32[5,64,128]{2,1,0:T(8,128)S(1)}, u32[]{:S(2)}, u32[]{:S(2)}) collective-permute-start(f32[5,64,128]{2,1,0:T(8,128)} %get-tuple-element.149), channel_id=1, source_target_pairs={{0,2},{2,4},{4,6},{6,8},{8,10},{10,12},{12,14},{14,0},{1,3},{3,5},... | collective-permute-start | bytes 491528 | tf_op jit(solution)/shard_map/ppermute | solution.py:21
  31.7 8.2 %collective-permute-start.7 = (f32[2,64,128]{2,1,0:T(8,128)}, f32[2,64,128]{2,1,0:T(8,128)S(1)}, u32[]{:S(2)}, u32[]{:S(2)}) collective-permute-start(f32[2,64,128]{2,1,0:T(8,128)} %get-tuple-element.150), channel_id=1, source_target_pairs={{0,14},{2,0},{4,2},{6,4},{8,6},{10,8},{12,10},{14,12},{1,15},{3,1}... | collective-permute-start | bytes 196616 | tf_op jit(solution)/shard_map/ppermute | solution.py:21
  39.9 3.0 %copy-start.4 = (f32[2,64,128]{2,1,0:T(8,128)}, f32[2,64,128]{2,1,0:T(8,128)S(1)}, u32[]{:S(2)}) copy-start(f32[2,64,128]{2,1,0:T(8,128)S(1)} %collective-permute-done.7.xhi_ref) | copy-start | bytes 196612
  40.8 2.1 %copy-start.1 = (f32[5,64,128]{2,1,0:T(8,128)}, f32[5,64,128]{2,1,0:T(8,128)S(1)}, u32[]{:S(2)}) copy-start(f32[5,64,128]{2,1,0:T(8,128)S(1)} %collective-permute-done.6.xlo_ref) | copy-start | bytes 491524
  41.7 1.2 %collective-permute-start.8 = (f32[9,8,128]{2,1,0:T(8,128)S(1)}, f32[9,8,128]{2,1,0:T(8,128)S(1)}, u32[]{:S(2)}, u32[]{:S(2)}) collective-permute-start(f32[9,8,128]{2,1,0:T(8,128)S(1)} %pad_maximum_fusion.2), channel_id=1, source_target_pairs={{0,1},{1,0},{2,3},{3,2},{4,5},{5,4},{6,7},{7,6},{8,9},{9,8},{10,11... | collective-permute-start | bytes 110600 | tf_op jit(solution)/shard_map/ppermute | solution.py:21
  42.9 0.6 copy-start.9
  45.7 9.2 %collective-permute-start.9 = (f32[5,64,128]{2,1,0:T(8,128)}, f32[5,64,128]{2,1,0:T(8,128)S(1)}, u32[]{:S(2)}, u32[]{:S(2)}) collective-permute-start(f32[5,64,128]{2,1,0:T(8,128)} %get-tuple-element.154), channel_id=1, source_target_pairs={{0,2},{2,4},{4,6},{6,8},{8,10},{10,12},{12,14},{14,0},{1,3},{3,5},... | collective-permute-start | bytes 491528 | tf_op jit(solution)/shard_map/ppermute | solution.py:21
  45.7 8.2 %collective-permute-start.10 = (f32[2,64,128]{2,1,0:T(8,128)}, f32[2,64,128]{2,1,0:T(8,128)S(1)}, u32[]{:S(2)}, u32[]{:S(2)}) collective-permute-start(f32[2,64,128]{2,1,0:T(8,128)} %get-tuple-element.155), channel_id=1, source_target_pairs={{0,14},{2,0},{4,2},{6,4},{8,6},{10,8},{12,10},{14,12},{1,15},{3,1}... | collective-permute-start | bytes 196616 | tf_op jit(solution)/shard_map/ppermute | solution.py:21
  53.9 3.0 %copy-start.10 = (f32[2,64,128]{2,1,0:T(8,128)}, f32[2,64,128]{2,1,0:T(8,128)S(1)}, u32[]{:S(2)}) copy-start(f32[2,64,128]{2,1,0:T(8,128)S(1)} %collective-permute-done.10.xhi_ref) | copy-start | bytes 196612
  54.9 2.1 %copy-start.6 = (f32[5,64,128]{2,1,0:T(8,128)}, f32[5,64,128]{2,1,0:T(8,128)S(1)}, u32[]{:S(2)}) copy-start(f32[5,64,128]{2,1,0:T(8,128)S(1)} %collective-permute-done.9.xlo_ref) | copy-start | bytes 491524
  55.7 1.2 %collective-permute-start.11 = (f32[9,8,128]{2,1,0:T(8,128)S(1)}, f32[9,8,128]{2,1,0:T(8,128)S(1)}, u32[]{:S(2)}, u32[]{:S(2)}) collective-permute-start(f32[9,8,128]{2,1,0:T(8,128)S(1)} %pad_maximum_fusion.3), channel_id=1, source_target_pairs={{0,1},{1,0},{2,3},{3,2},{4,5},{5,4},{6,7},{7,6},{8,9},{9,8},{10,11... | collective-permute-start | bytes 110600 | tf_op jit(solution)/shard_map/ppermute | solution.py:21
  56.9 0.6 copy-start.11
  61.0 0.7 copy-start.16
  61.0 0.7 copy-start.14
  61.0 0.7 copy-start.15
  61.0 0.7 copy-start.13
  61.9 4.5 %collective-permute-start.12 = (f32[32,4]{0,1:T(4,128)S(1)}, f32[32,4]{0,1:T(4,128)S(1)}, u32[]{:S(2)}, u32[]{:S(2)}) collective-permute-start(f32[32,4]{0,1:T(4,128)S(1)} %slice_select_fusion.2), channel_id=1, source_target_pairs={{0,8},{2,10},{4,12},{6,14},{8,0},{10,2},{12,4},{14,6},{1,9},{3,11}... | collective-permute-start | bytes 1544 | tf_op jit(solution)/shard_map/ppermute | solution.py:274
  66.6 3.6 %collective-permute-start.13 = (f32[16,4]{0,1:T(4,128)S(1)}, f32[16,4]{0,1:T(4,128)S(1)}, u32[]{:S(2)}, u32[]{:S(2)}) collective-permute-start(f32[16,4]{0,1:T(4,128)S(1)} %slice_select_fusion.1), channel_id=1, source_target_pairs={{0,4},{2,6},{4,0},{6,2},{8,12},{10,14},{12,8},{14,10},{1,5},{3,7},... | collective-permute-start | bytes 776 | tf_op jit(solution)/shard_map/ppermute | solution.py:274
  70.3 3.6 %collective-permute-start.14 = (f32[8,4]{0,1:T(4,128)S(1)}, f32[8,4]{0,1:T(4,128)S(1)}, u32[]{:S(2)}, u32[]{:S(2)}) collective-permute-start(f32[8,4]{0,1:T(4,128)S(1)} %slice_select_fusion), channel_id=1, source_target_pairs={{0,2},{2,0},{4,6},{6,4},{8,10},{10,8},{12,14},{14,12},{1,3},{3,1},... | collective-permute-start | bytes 392 | tf_op jit(solution)/shard_map/ppermute | solution.py:274
  74.0 1.2 %collective-permute-start.15 = (f32[8,4]{0,1:T(4,128)S(1)}, f32[8,4]{0,1:T(4,128)S(1)}, u32[]{:S(2)}, u32[]{:S(2)}) collective-permute-start(f32[8,4]{0,1:T(4,128)S(1)} %select_add_fusion), channel_id=1, source_target_pairs={{0,1},{1,0},{2,3},{3,2},{4,5},{5,4},{6,7},{7,6},{8,9},{9,8},{10,11... | collective-permute-start | bytes 392 | tf_op jit(solution)/shard_map/ppermute | solution.py:284

commit v16 on v14

--- a/solution.py
+++ b/solution.py
@@ -116,10 +116,10 @@
     return (ex_new, ey_new, ez_new)
 
 
-def _step_kernel(e_ref, h_ref, keep_ref, drive_ref, xlo_ref, xhi_ref, y_ref, basis_ref,
+def _step_kernel(e_ref, h_ref, keep_ref, drive_ref, xlo_ref, xhi_ref, y_ref, corner_ref, basis_ref,
                  e_out, h_out, y_out, g_out):
-    c1_ref = y_ref.at[7, 0:1]
-    c2_ref = y_ref.at[8, 0:1]
+    c1_ref = corner_ref.at[0, 0:1]
+    c2_ref = corner_ref.at[1, 0:1]
     yhi_ref = y_ref.at[5:7]
     planes = e_ref.shape[1]
     cells = e_ref.shape[2]
@@ -166,10 +166,10 @@
 
 
 def _edge_kernel(e_first, e_second, e_penult, e_last, h_first, h_penult, h_last,
-                 keep_first, keep_last, drive_first, drive_last, xlo_ref, xhi_ref, y_ref,
+                 keep_first, keep_last, drive_first, drive_last, xlo_ref, xhi_ref, y_ref, corner_ref,
                  xlo_out, xhi_out, *, planes):
-    c1_ref = y_ref.at[7, 0:1]
-    c2_ref = y_ref.at[8, 0:1]
+    c1_ref = corner_ref.at[0, 0:1]
+    c2_ref = corner_ref.at[1, 0:1]
     yhi_ref = y_ref.at[5:7]
     e_blocks = {0: e_first, 1: e_second, planes - 2: e_penult, planes - 1: e_last}
     h_blocks = {0: h_first, planes - 2: h_penult, planes - 1: h_last}
@@ -219,16 +219,23 @@
     return (shifted(xlo, "gx", 1), shifted(xhi, "gx", -1))
 
 
-def exchange_y(rows, xlo, xhi):
+def exchange_y(rows):
+    if lax.axis_size("gy") == 2:
+        return shifted(rows, "gy", 1)
+    before = shifted(rows, "gy", 1)
+    after = shifted(rows, "gy", -1)
+    return jnp.concatenate([before[0:5], after[5:7]])
+
+
+def exchange_corners(xlo, xhi, like):
     cells = xhi.shape[1]
-    corners = jnp.zeros((2,) + rows.shape[1:], rows.dtype)
+    corners = jnp.zeros((2,) + like.shape[1:], like.dtype)
     corners = corners.at[0, 0:1].set(xlo[0, 0:1]).at[1, 0:1].set(xhi[0, cells - 1:cells])
-    message = jnp.concatenate([rows, corners])
     if lax.axis_size("gy") == 2:
-        return shifted(message, "gy", 1)
-    before = shifted(message, "gy", 1)
-    after = shifted(message, "gy", -1)
-    return jnp.concatenate([before[0:5], after[5:8], before[8:9]])
+        return shifted(corners, "gy", 1)
+    before = shifted(corners, "gy", 1)
+    after = shifted(corners, "gy", -1)
+    return jnp.concatenate([after[0:1], before[1:2]])
 
 
 def trig_basis(angle_orders, cells_x, cells_y):
@@ -314,7 +321,7 @@
         in_specs=[field_plane(i) for i in (first, 1, last - 1, last)]
         + [field_plane(i) for i in (first, last - 1, last)]
         + [coef_plane(first), coef_plane(last), coef_plane(first), coef_plane(last)]
-        + [whole] * 3,
+        + [whole] * 4,
         out_specs=(whole, whole),
     )
     slab = 8
@@ -334,24 +341,26 @@
     xlo, xhi = exchange_x(xlo, xhi)
     keep, drive = coefficients(material, eps_table, sigma_table)
     keep, drive, xlo, xhi = lax.optimization_barrier((keep, drive, xlo, xhi))
-    rows = exchange_y(rows, xlo, xhi)
+    rows = exchange_y(rows)
+    corners = exchange_corners(xlo, xhi, rows)
     basis = trig_basis(angle_orders, cells_x, cells_y)
     group = 2 if cells_x % 2 == 0 else 1
     basis = basis.reshape(2 * angle_count, cells_x // group, group * cells_y).transpose(1, 0, 2)
-    basis, rows = lax.optimization_barrier((basis, rows))
+    basis, rows, corners = lax.optimization_barrier((basis, rows, corners))
     elec = e_field
     magn = h_field
     columns = [[], []]
     for number in range(ITERS):
         if number + 1 < ITERS:
             edges = edge_call(
-                elec, elec, elec, elec, magn, magn, magn, keep, keep, drive, drive, xlo, xhi, rows
+                elec, elec, elec, elec, magn, magn, magn, keep, keep, drive, drive, xlo, xhi, rows, corners
             )
             next_xlo, next_xhi = exchange_x(*edges)
-        elec, magn, new_rows, sums = step_call(elec, magn, keep, drive, xlo, xhi, rows, basis)
+        elec, magn, new_rows, sums = step_call(elec, magn, keep, drive, xlo, xhi, rows, corners, basis)
         if number + 1 < ITERS:
+            rows = exchange_y(new_rows)
             xlo, xhi = next_xlo, next_xhi
-            rows = exchange_y(new_rows, xlo, xhi)
+            corners = exchange_corners(xlo, xhi, rows)
         weight_cos = math.cos(PHASE_STEP * (number + 1))
         weight_sin = math.sin(PHASE_STEP * (number + 1))
         picked = sums[:, 0]

time: 76.2 us -> 74.1 us (0.972)
  other arithmetic: 5.08 us -> 2.74 us
    concatenate x4 -> x0, other arithmetic: 2.35 us -> none  [exchange_y(): message = jnp.concatenate([rows, corners])]
    ppermute x12 -> x16, starting transfers between devices: 20.2 us -> 20.5 us  [shifted(): return lax.ppermute(value, axis, pairs)]
    unnamed x36 -> x42, local copies, waits for them, and re-layouts: 3.83 us -> 3.95 us
    ppermute x12 -> x16, waiting for transfers between devices: 8.13 us -> 8.17 us  [shifted(): return lax.ppermute(value, axis, pairs)]
  transfers between devices with their start and end apart: 16 -> 20, of which waited for: 12 -> 14; matrix products, arithmetic and copies ran while one was open for 2% -> 3% of each run, Pallas kernels for 17% -> 17%
where the time goes in v16:
time: 74.1 us; the launch traced here: 73.7 us
  Pallas kernels  24.2 us (33%)
  starting transfers between devices  20.9 us (28%)
  waiting for transfers between devices  20.6 us (28%)
  local copies, waits for them, and re-layouts  4.34 us (6%)
  other arithmetic  2.74 us (4%)
  between operations  0.89 us (1%)
    ppermute x16, starting transfers between devices, shifted(): return lax.ppermute(value, axis, pairs)  20.5 us
    pallas_call x4, Pallas kernels, local(): step_call(elec, magn, keep, drive, xlo, xhi, rows, corners, basis)  14 us
    ppermute x3, waiting for transfers between devices, scatter_sum(): rows = keep + lax.ppermute(send, axis, pairs)  11.3 us
    ppermute x16, waiting for transfers between devices, shifted(): return lax.ppermute(value, axis, pairs)  8.17 us
    pallas_call x3, Pallas kernels, local(): edge_call(elec, elec, elec, elec, magn, magn, magn, keep, keep, drive, dr...  6.4 us
    unnamed x42, local copies, waits for them, and re-layouts  3.95 us
    pallas_call x1, Pallas kernels, coefficients(): pl.pallas_call(_coef_kernel, out_shape=(out, out), in_specs=[scalar, scal...  2.01 us
    pallas_call x1, Pallas kernels, local(): pl.pallas_call(_halo_kernel, out_shape=(xlo_shape, xhi_shape, rows_shape)...  1.85 us
  transfers between devices with their start and end apart: 20, of which 14 were waited for; matrix products, arithmetic and copies ran while one was open for 3% of the time, Pallas kernels for 17%

profile of v16, /device:TPU:0, one launch (start us, length us, event | category | flops | bytes accessed | tf_op | source)
XLA Modules:
  0.0 73.7 jit_solution(11702472809273538390)
XLA Ops:
  0.6 1.9 %shard_map.86 = (f32[5,64,128]{2,1,0:T(8,128)}, f32[2,64,128]{2,1,0:T(8,128)}, f32[7,8,128]{2,1,0:T(8,128)}) custom-call(f32[3,8,64,128]{3,2,1,0:T(8,128)} %e_last.3, f32[3,8,64,128]{3,2,1,0:T(8,128)} %e_last.3, f32[3,8,64,128]{3,2,1,0:T(8,128)} %h_last.3, f32[3,8,64,128]{3,2,1,0:T(8,128)} %e_last.3, f32[3,8,64,128]{3,2,1,0:T(8,128)} %e_last.3, ...), custom_call_target="tpu_custom_call" | custom-call | tf_op jit(solution)/shard_map/pallas_call | solution.py:333
  2.5 3.0 %collective-permute-start = (f32[5,64,128]{2,1,0:T(8,128)}, f32[5,64,128]{2,1,0:T(8,128)S(1)}, u32[]{:S(2)}, u32[]{:S(2)}) collective-permute-start(f32[5,64,128]{2,1,0:T(8,128)} %get-tuple-element.134), channel_id=1, source_target_pairs={{0,2},{2,4},{4,6},{6,8},{8,10},{10,12},{12,14},{14,0},{1,3},{3,5},... | collective-permute-start | bytes 491528 | tf_op jit(solution)/shard_map/ppermute | solution.py:21
  5.4 3.0 %collective-permute-start.1 = (f32[2,64,128]{2,1,0:T(8,128)}, f32[2,64,128]{2,1,0:T(8,128)S(1)}, u32[]{:S(2)}, u32[]{:S(2)}) collective-permute-start(f32[2,64,128]{2,1,0:T(8,128)} %get-tuple-element.135), channel_id=1, source_target_pairs={{0,14},{2,0},{4,2},{6,4},{8,6},{10,8},{12,10},{14,12},{1,15},{3,1}... | collective-permute-start | bytes 196616 | tf_op jit(solution)/shard_map/ppermute | solution.py:21
  8.5 0.0 collective-permute-start.2
  8.5 0.7 copy-done.20
  9.2 0.1 multiply_multiply_fusion.1
  9.3 0.1 copy.12
  9.3 0.1 multiply_multiply_fusion
  9.4 0.1 broadcast_add_fusion
  9.6 0.1 add.227
  9.7 0.5 fusion.4
  10.2 2.0 %shard_map.85 = (f32[8,64,128]{2,1,0:T(8,128)}, f32[8,64,128]{2,1,0:T(8,128)}) custom-call(f32[6]{0:T(128)} %eps_ref.1, f32[6]{0:T(128)} %sigma_ref.1, s32[8,64,128]{2,1,0:T(8,128)} %mat_ref.1), custom_call_target="tpu_custom_call" | custom-call | tf_op jit(solution)/shard_map/pallas_call | solution.py:43
  12.2 1.2 %collective-permute-done.1.xhi_ref = f32[2,64,128]{2,1,0:T(8,128)S(1)} collective-permute-done((f32[2,64,128]{2,1,0:T(8,128)}, f32[2,64,128]{2,1,0:T(8,128)S(1)}, u32[]{:S(2)}, u32[]{:S(2)}) %collective-permute-start.1) | collective-permute-done | bytes 65568 | tf_op jit(solution)/shard_map/ppermute | solution.py:21
  13.4 0.0 collective-permute-done.xlo_ref
  13.5 0.1 collective-permute-start.3
  13.6 0.7 %maximum_bitcast_fusion.basis_ref = f32[4,128,128]{2,1,0:T(8,128)} fusion(f32[64,4,128]{2,0,1:T(8,128)S(1)} %get-tuple-element.166, f32[64,4,128]{2,0,1:T(8,128)S(1)} %get-tuple-element.165), kind=kLoop, calls=%fused_computation | loop fusion | flops 65536 | bytes 524288 | tf_op jit(solution)/shard_map/transpose | solution.py:348
  14.4 0.4 collective-permute-done.3.corner_ref
  14.7 0.2 copy-done.7
  14.9 0.6 copy-done.11
  15.5 2.1 %shard_map.88 = (f32[5,64,128]{2,1,0:T(8,128)}, f32[2,64,128]{2,1,0:T(8,128)}) custom-call(f32[3,8,64,128]{3,2,1,0:T(8,128)} %e_last.3, f32[3,8,64,128]{3,2,1,0:T(8,128)} %e_last.3, f32[3,8,64,128]{3,2,1,0:T(8,128)} %e_last.3, f32[3,8,64,128]{3,2,1,0:T(8,128)} %e_last.3, f32[3,8,64,128]{3,2,1,0:T(8,128)} %h_last.3, f32[3,8,64,128]{3,2,1,0:T(8,128)} %h_last.3, ...), custom_call_target="tpu_custom_call" | custom-call | tf_op jit(solution)/shard_map/pallas_call | solution.py:355
  17.7 4.7 %collective-permute-start.5 = (f32[2,64,128]{2,1,0:T(8,128)}, f32[2,64,128]{2,1,0:T(8,128)S(1)}, u32[]{:S(2)}, u32[]{:S(2)}) collective-permute-start(f32[2,64,128]{2,1,0:T(8,128)} %get-tuple-element.147), channel_id=1, source_target_pairs={{0,14},{2,0},{4,2},{6,4},{8,6},{10,8},{12,10},{14,12},{1,15},{3,1}... | collective-permute-start | bytes 196616 | tf_op jit(solution)/shard_map/ppermute | solution.py:21
  22.4 3.5 %shard_map.87 = (f32[3,8,64,128]{3,2,1,0:T(8,128)}, f32[3,8,64,128]{3,2,1,0:T(8,128)}, f32[7,8,128]{2,1,0:T(8,128)}, f32[2,1,128]{2,1,0:T(1,128)}) custom-call(f32[3,8,64,128]{3,2,1,0:T(8,128)} %e_last.3, f32[3,8,64,128]{3,2,1,0:T(8,128)} %h_last.3, f32[8,64,128]{2,1,0:T(8,128)} %get-tuple-element.136.keep_ref.keep_first.keep_last, ...), custom_call_target="tpu_custom_call" | custom-call | tf_op jit(solution)/shard_map/pallas_call | solution.py:359
  25.9 0.0 collective-permute-done.5.xhi_ref
  25.9 1.3 %collective-permute-done.4.xlo_ref = f32[5,64,128]{2,1,0:T(8,128)S(1)} collective-permute-done((f32[5,64,128]{2,1,0:T(8,128)}, f32[5,64,128]{2,1,0:T(8,128)S(1)}, u32[]{:S(2)}, u32[]{:S(2)}) %collective-permute-start.4) | collective-permute-done | bytes 163872 | tf_op jit(solution)/shard_map/ppermute | solution.py:21
  27.2 0.1 collective-permute-start.7
  27.3 0.0 collective-permute-done.6.y_ref
  27.3 1.1 %collective-permute-done.7.corner_ref = f32[2,8,128]{2,1,0:T(8,128)S(1)} collective-permute-done((f32[2,8,128]{2,1,0:T(8,128)S(1)}, f32[2,8,128]{2,1,0:T(8,128)S(1)}, u32[]{:S(2)}, u32[]{:S(2)}) %collective-permute-start.7) | collective-permute-done | bytes 8224 | tf_op jit(solution)/shard_map/ppermute | solution.py:21
  28.5 0.6 copy-done.12
  29.1 2.1 %shard_map.90 = (f32[5,64,128]{2,1,0:T(8,128)}, f32[2,64,128]{2,1,0:T(8,128)}) custom-call(f32[3,8,64,128]{3,2,1,0:T(8,128)} %get-tuple-element.144.e_ref.e_first.e_second.e_penult.e_last, f32[3,8,64,128]{3,2,1,0:T(8,128)} %get-tuple-element.144.e_ref.e_first.e_second.e_penult.e_last, ...), custom_call_target="tpu_custom_call" | custom-call | tf_op jit(solution)/shard_map/pallas_call | solution.py:355
  31.2 4.7 %collective-permute-start.9 = (f32[2,64,128]{2,1,0:T(8,128)}, f32[2,64,128]{2,1,0:T(8,128)S(1)}, u32[]{:S(2)}, u32[]{:S(2)}) collective-permute-start(f32[2,64,128]{2,1,0:T(8,128)} %get-tuple-element.152), channel_id=1, source_target_pairs={{0,14},{2,0},{4,2},{6,4},{8,6},{10,8},{12,10},{14,12},{1,15},{3,1}... | collective-permute-start | bytes 196616 | tf_op jit(solution)/shard_map/ppermute | solution.py:21
  35.9 3.5 %shard_map.89 = (f32[3,8,64,128]{3,2,1,0:T(8,128)}, f32[3,8,64,128]{3,2,1,0:T(8,128)}, f32[7,8,128]{2,1,0:T(8,128)}, f32[2,1,128]{2,1,0:T(1,128)}) custom-call(f32[3,8,64,128]{3,2,1,0:T(8,128)} %get-tuple-element.144.e_ref.e_first.e_second.e_penult.e_last, f32[3,8,64,128]{3,2,1,0:T(8,128)} %get-tuple-element.145.h_ref.h_first.h_penult.h_last, ...), custom_call_target="tpu_custom_call" | custom-call | tf_op jit(solution)/shard_map/pallas_call | solution.py:359
  39.4 0.9 %collective-permute-done.8.xlo_ref = f32[5,64,128]{2,1,0:T(8,128)S(1)} collective-permute-done((f32[5,64,128]{2,1,0:T(8,128)}, f32[5,64,128]{2,1,0:T(8,128)S(1)}, u32[]{:S(2)}, u32[]{:S(2)}) %collective-permute-start.8) | collective-permute-done | bytes 163872 | tf_op jit(solution)/shard_map/ppermute | solution.py:21
  40.4 0.1 collective-permute-start.11
  40.5 0.3 collective-permute-done.10.y_ref
  40.8 0.8 %collective-permute-done.11.corner_ref = f32[2,8,128]{2,1,0:T(8,128)S(1)} collective-permute-done((f32[2,8,128]{2,1,0:T(8,128)S(1)}, f32[2,8,128]{2,1,0:T(8,128)S(1)}, u32[]{:S(2)}, u32[]{:S(2)}) %collective-permute-start.11) | collective-permute-done | bytes 8224 | tf_op jit(solution)/shard_map/ppermute | solution.py:21
  41.7 0.6 copy-done.13
  42.3 2.1 %shard_map.92 = (f32[5,64,128]{2,1,0:T(8,128)}, f32[2,64,128]{2,1,0:T(8,128)}) custom-call(f32[3,8,64,128]{3,2,1,0:T(8,128)} %get-tuple-element.149.e_ref.e_first.e_second.e_penult.e_last, f32[3,8,64,128]{3,2,1,0:T(8,128)} %get-tuple-element.149.e_ref.e_first.e_second.e_penult.e_last, ...), custom_call_target="tpu_custom_call" | custom-call | tf_op jit(solution)/shard_map/pallas_call | solution.py:355
  44.4 4.7 %collective-permute-start.13 = (f32[2,64,128]{2,1,0:T(8,128)}, f32[2,64,128]{2,1,0:T(8,128)S(1)}, u32[]{:S(2)}, u32[]{:S(2)}) collective-permute-start(f32[2,64,128]{2,1,0:T(8,128)} %get-tuple-element.157), channel_id=1, source_target_pairs={{0,14},{2,0},{4,2},{6,4},{8,6},{10,8},{12,10},{14,12},{1,15},{3,1}... | collective-permute-start | bytes 196616 | tf_op jit(solution)/shard_map/ppermute | solution.py:21
  49.1 3.5 %shard_map.91 = (f32[3,8,64,128]{3,2,1,0:T(8,128)}, f32[3,8,64,128]{3,2,1,0:T(8,128)}, f32[7,8,128]{2,1,0:T(8,128)}, f32[2,1,128]{2,1,0:T(1,128)}) custom-call(f32[3,8,64,128]{3,2,1,0:T(8,128)} %get-tuple-element.149.e_ref.e_first.e_second.e_penult.e_last, f32[3,8,64,128]{3,2,1,0:T(8,128)} %get-tuple-element.150.h_ref.h_first.h_penult.h_last, ...), custom_call_target="tpu_custom_call" | custom-call | tf_op jit(solution)/shard_map/pallas_call | solution.py:359
  52.7 0.9 %collective-permute-done.12.xlo_ref = f32[5,64,128]{2,1,0:T(8,128)S(1)} collective-permute-done((f32[5,64,128]{2,1,0:T(8,128)}, f32[5,64,128]{2,1,0:T(8,128)S(1)}, u32[]{:S(2)}, u32[]{:S(2)}) %collective-permute-start.12) | collective-permute-done | bytes 163872 | tf_op jit(solution)/shard_map/ppermute | solution.py:21
  53.6 0.1 collective-permute-start.15
  53.7 0.3 collective-permute-done.14.y_ref
  54.0 0.8 %collective-permute-done.15.corner_ref = f32[2,8,128]{2,1,0:T(8,128)S(1)} collective-permute-done((f32[2,8,128]{2,1,0:T(8,128)S(1)}, f32[2,8,128]{2,1,0:T(8,128)S(1)}, u32[]{:S(2)}, u32[]{:S(2)}) %collective-permute-start.15) | collective-permute-done | bytes 8224 | tf_op jit(solution)/shard_map/ppermute | solution.py:21
  54.9 0.6 copy-done.19
  55.5 3.5 %shard_map.93 = (f32[3,8,64,128]{3,2,1,0:T(8,128)}, f32[3,8,64,128]{3,2,1,0:T(8,128)}, f32[7,8,128]{2,1,0:T(8,128)}, f32[2,1,128]{2,1,0:T(1,128)}) custom-call(f32[3,8,64,128]{3,2,1,0:T(8,128)} %get-tuple-element.154.e_ref, f32[3,8,64,128]{3,2,1,0:T(8,128)} %get-tuple-element.155.h_ref, f32[8,64,128]{2,1,0:T(8,128)} %get-tuple-element.136.keep_ref.keep_first.keep_last, ...), custom_call_target="tpu_custom_call" | custom-call | tf_op jit(solution)/shard_map/pallas_call | solution.py:359
  59.0 0.0 copy-start.15
  59.0 0.6 copy-done.18
  59.6 0.0 copy-done.16
  59.6 0.0 copy-done.17
  59.6 0.0 copy-done.15
  59.6 0.1 add_bitcast_fusion.2
  59.7 0.1 add_bitcast_fusion.3
  59.8 0.1 slice_select_fusion.2
  59.9 0.4 collective-permute-start.16
  60.3 4.1 %collective-permute-done.16 = f32[32,4]{0,1:T(4,128)S(1)} collective-permute-done((f32[32,4]{0,1:T(4,128)S(1)}, f32[32,4]{0,1:T(4,128)S(1)}, u32[]{:S(2)}, u32[]{:S(2)}) %collective-permute-start.16) | collective-permute-done | bytes 544 | tf_op jit(solution)/shard_map/ppermute | solution.py:281
  64.4 0.1 select_add_fusion.2
  64.5 0.1 slice_select_fusion.1
  64.5 3.6 %collective-permute-done.17 = f32[16,4]{0,1:T(4,128)S(1)} collective-permute-done((f32[16,4]{0,1:T(4,128)S(1)}, f32[16,4]{0,1:T(4,128)S(1)}, u32[]{:S(2)}, u32[]{:S(2)}) %collective-permute-start.17) | collective-permute-done | bytes 288 | tf_op jit(solution)/shard_map/ppermute | solution.py:281
  68.1 0.1 select_add_fusion.1
  68.2 0.1 slice_select_fusion
  68.3 3.6 %collective-permute-done.18 = f32[8,4]{0,1:T(4,128)S(1)} collective-permute-done((f32[8,4]{0,1:T(4,128)S(1)}, f32[8,4]{0,1:T(4,128)S(1)}, u32[]{:S(2)}, u32[]{:S(2)}) %collective-permute-start.18) | collective-permute-done | bytes 160 | tf_op jit(solution)/shard_map/ppermute | solution.py:281
  71.8 0.1 select_add_fusion
  71.9 1.2 %collective-permute-done.19 = f32[8,4]{0,1:T(4,128)S(1)} collective-permute-done((f32[8,4]{0,1:T(4,128)S(1)}, f32[8,4]{0,1:T(4,128)S(1)}, u32[]{:S(2)}, u32[]{:S(2)}) %collective-permute-start.19) | collective-permute-done | bytes 160 | tf_op jit(solution)/shard_map/ppermute | solution.py:291
  73.1 0.6 add_multiply_fusion
  (63 shorter events, 0.3 us)
Async XLA Ops:
  2.5 11.0 %collective-permute-start = (f32[5,64,128]{2,1,0:T(8,128)}, f32[5,64,128]{2,1,0:T(8,128)S(1)}, u32[]{:S(2)}, u32[]{:S(2)}) collective-permute-start(f32[5,64,128]{2,1,0:T(8,128)} %get-tuple-element.134), channel_id=1, source_target_pairs={{0,2},{2,4},{4,6},{6,8},{8,10},{10,12},{12,14},{14,0},{1,3},{3,5},... | collective-permute-start | bytes 491528 | tf_op jit(solution)/shard_map/ppermute | solution.py:21
  5.4 8.0 %collective-permute-start.1 = (f32[2,64,128]{2,1,0:T(8,128)}, f32[2,64,128]{2,1,0:T(8,128)S(1)}, u32[]{:S(2)}, u32[]{:S(2)}) collective-permute-start(f32[2,64,128]{2,1,0:T(8,128)} %get-tuple-element.135), channel_id=1, source_target_pairs={{0,14},{2,0},{4,2},{6,4},{8,6},{10,8},{12,10},{14,12},{1,15},{3,1}... | collective-permute-start | bytes 196616 | tf_op jit(solution)/shard_map/ppermute | solution.py:21
  8.5 5.8 %collective-permute-start.2 = (f32[7,8,128]{2,1,0:T(8,128)}, f32[7,8,128]{2,1,0:T(8,128)S(1)}, u32[]{:S(2)}, u32[]{:S(2)}) collective-permute-start(f32[7,8,128]{2,1,0:T(8,128)} %get-tuple-element.140), channel_id=1, source_target_pairs={{0,1},{1,0},{2,3},{3,2},{4,5},{5,4},{6,7},{7,6},{8,9},{9,8},{10,11... | collective-permute-start | bytes 86024 | tf_op jit(solution)/shard_map/ppermute | solution.py:21
  8.5 0.7 copy-start.20
  13.4 0.9 %copy-start.3 = (f32[2,64,128]{2,1,0:T(8,128)}, f32[2,64,128]{2,1,0:T(8,128)S(1)}, u32[]{:S(2)}) copy-start(f32[2,64,128]{2,1,0:T(8,128)S(1)} %collective-permute-done.1.xhi_ref) | copy-start | bytes 196612
  13.4 0.9 %copy-start = (f32[5,64,128]{2,1,0:T(8,128)}, f32[5,64,128]{2,1,0:T(8,128)S(1)}, u32[]{:S(2)}) copy-start(f32[5,64,128]{2,1,0:T(8,128)S(1)} %collective-permute-done.xlo_ref) | copy-start | bytes 491524
  13.5 1.2 %collective-permute-start.3 = (f32[2,8,128]{2,1,0:T(8,128)S(1)}, f32[2,8,128]{2,1,0:T(8,128)S(1)}, u32[]{:S(2)}, u32[]{:S(2)}) collective-permute-start(f32[2,8,128]{2,1,0:T(8,128)S(1)} %scatter.29), channel_id=1, source_target_pairs={{0,1},{1,0},{2,3},{3,2},{4,5},{5,4},{6,7},{7,6},{8,9},{9,8},{10,11... | collective-permute-start | bytes 24584 | tf_op jit(solution)/shard_map/ppermute | solution.py:21
  14.3 0.6 copy-start.7
  14.9 0.6 copy-start.11
  17.7 9.5 %collective-permute-start.4 = (f32[5,64,128]{2,1,0:T(8,128)}, f32[5,64,128]{2,1,0:T(8,128)S(1)}, u32[]{:S(2)}, u32[]{:S(2)}) collective-permute-start(f32[5,64,128]{2,1,0:T(8,128)} %get-tuple-element.146), channel_id=1, source_target_pairs={{0,2},{2,4},{4,6},{6,8},{8,10},{10,12},{12,14},{14,0},{1,3},{3,5},... | collective-permute-start | bytes 491528 | tf_op jit(solution)/shard_map/ppermute | solution.py:21
  17.7 8.2 %collective-permute-start.5 = (f32[2,64,128]{2,1,0:T(8,128)}, f32[2,64,128]{2,1,0:T(8,128)S(1)}, u32[]{:S(2)}, u32[]{:S(2)}) collective-permute-start(f32[2,64,128]{2,1,0:T(8,128)} %get-tuple-element.147), channel_id=1, source_target_pairs={{0,14},{2,0},{4,2},{6,4},{8,6},{10,8},{12,10},{14,12},{1,15},{3,1}... | collective-permute-start | bytes 196616 | tf_op jit(solution)/shard_map/ppermute | solution.py:21
  25.9 1.4 %collective-permute-start.6 = (f32[7,8,128]{2,1,0:T(8,128)}, f32[7,8,128]{2,1,0:T(8,128)S(1)}, u32[]{:S(2)}, u32[]{:S(2)}) collective-permute-start(f32[7,8,128]{2,1,0:T(8,128)} %get-tuple-element.148), channel_id=1, source_target_pairs={{0,1},{1,0},{2,3},{3,2},{4,5},{5,4},{6,7},{7,6},{8,9},{9,8},{10,11... | collective-permute-start | bytes 86024 | tf_op jit(solution)/shard_map/ppermute | solution.py:21
  25.9 2.6 %copy-start.5 = (f32[2,64,128]{2,1,0:T(8,128)}, f32[2,64,128]{2,1,0:T(8,128)S(1)}, u32[]{:S(2)}) copy-start(f32[2,64,128]{2,1,0:T(8,128)S(1)} %collective-permute-done.5.xhi_ref) | copy-start | bytes 196612
  27.2 1.3 %copy-start.2 = (f32[5,64,128]{2,1,0:T(8,128)}, f32[5,64,128]{2,1,0:T(8,128)S(1)}, u32[]{:S(2)}) copy-start(f32[5,64,128]{2,1,0:T(8,128)S(1)} %collective-permute-done.4.xlo_ref) | copy-start | bytes 491524
  27.2 1.2 %collective-permute-start.7 = (f32[2,8,128]{2,1,0:T(8,128)S(1)}, f32[2,8,128]{2,1,0:T(8,128)S(1)}, u32[]{:S(2)}, u32[]{:S(2)}) collective-permute-start(f32[2,8,128]{2,1,0:T(8,128)S(1)} %scatter.31), channel_id=1, source_target_pairs={{0,1},{1,0},{2,3},{3,2},{4,5},{5,4},{6,7},{7,6},{8,9},{9,8},{10,11... | collective-permute-start | bytes 24584 | tf_op jit(solution)/shard_map/ppermute | solution.py:21
  27.3 1.2 %copy-start.8 = (f32[7,8,128]{2,1,0:T(8,128)}, f32[7,8,128]{2,1,0:T(8,128)S(1)}, u32[]{:S(2)}) copy-start(f32[7,8,128]{2,1,0:T(8,128)S(1)} %collective-permute-done.6.y_ref) | copy-start | bytes 86020
  28.5 0.6 copy-start.12
  31.2 9.2 %collective-permute-start.8 = (f32[5,64,128]{2,1,0:T(8,128)}, f32[5,64,128]{2,1,0:T(8,128)S(1)}, u32[]{:S(2)}, u32[]{:S(2)}) collective-permute-start(f32[5,64,128]{2,1,0:T(8,128)} %get-tuple-element.151), channel_id=1, source_target_pairs={{0,2},{2,4},{4,6},{6,8},{8,10},{10,12},{12,14},{14,0},{1,3},{3,5},... | collective-permute-start | bytes 491528 | tf_op jit(solution)/shard_map/ppermute | solution.py:21
  31.2 8.2 %collective-permute-start.9 = (f32[2,64,128]{2,1,0:T(8,128)}, f32[2,64,128]{2,1,0:T(8,128)S(1)}, u32[]{:S(2)}, u32[]{:S(2)}) collective-permute-start(f32[2,64,128]{2,1,0:T(8,128)} %get-tuple-element.152), channel_id=1, source_target_pairs={{0,14},{2,0},{4,2},{6,4},{8,6},{10,8},{12,10},{14,12},{1,15},{3,1}... | collective-permute-start | bytes 196616 | tf_op jit(solution)/shard_map/ppermute | solution.py:21
  39.4 1.4 %collective-permute-start.10 = (f32[7,8,128]{2,1,0:T(8,128)}, f32[7,8,128]{2,1,0:T(8,128)S(1)}, u32[]{:S(2)}, u32[]{:S(2)}) collective-permute-start(f32[7,8,128]{2,1,0:T(8,128)} %get-tuple-element.153), channel_id=1, source_target_pairs={{0,1},{1,0},{2,3},{3,2},{4,5},{5,4},{6,7},{7,6},{8,9},{9,8},{10,11... | collective-permute-start | bytes 86024 | tf_op jit(solution)/shard_map/ppermute | solution.py:21
  39.4 2.2 %copy-start.4 = (f32[2,64,128]{2,1,0:T(8,128)}, f32[2,64,128]{2,1,0:T(8,128)S(1)}, u32[]{:S(2)}) copy-start(f32[2,64,128]{2,1,0:T(8,128)S(1)} %collective-permute-done.9.xhi_ref) | copy-start | bytes 196612
  40.4 1.3 %copy-start.1 = (f32[5,64,128]{2,1,0:T(8,128)}, f32[5,64,128]{2,1,0:T(8,128)S(1)}, u32[]{:S(2)}) copy-start(f32[5,64,128]{2,1,0:T(8,128)S(1)} %collective-permute-done.8.xlo_ref) | copy-start | bytes 491524
  40.4 1.2 %collective-permute-start.11 = (f32[2,8,128]{2,1,0:T(8,128)S(1)}, f32[2,8,128]{2,1,0:T(8,128)S(1)}, u32[]{:S(2)}, u32[]{:S(2)}) collective-permute-start(f32[2,8,128]{2,1,0:T(8,128)S(1)} %scatter.35), channel_id=1, source_target_pairs={{0,1},{1,0},{2,3},{3,2},{4,5},{5,4},{6,7},{7,6},{8,9},{9,8},{10,11... | collective-permute-start | bytes 24584 | tf_op jit(solution)/shard_map/ppermute | solution.py:21
  40.8 0.8 %copy-start.9 = (f32[7,8,128]{2,1,0:T(8,128)}, f32[7,8,128]{2,1,0:T(8,128)S(1)}, u32[]{:S(2)}) copy-start(f32[7,8,128]{2,1,0:T(8,128)S(1)} %collective-permute-done.10.y_ref) | copy-start | bytes 86020
  41.7 0.6 copy-start.13
  44.4 9.2 %collective-permute-start.12 = (f32[5,64,128]{2,1,0:T(8,128)}, f32[5,64,128]{2,1,0:T(8,128)S(1)}, u32[]{:S(2)}, u32[]{:S(2)}) collective-permute-start(f32[5,64,128]{2,1,0:T(8,128)} %get-tuple-element.156), channel_id=1, source_target_pairs={{0,2},{2,4},{4,6},{6,8},{8,10},{10,12},{12,14},{14,0},{1,3},{3,5},... | collective-permute-start | bytes 491528 | tf_op jit(solution)/shard_map/ppermute | solution.py:21
  44.4 8.2 %collective-permute-start.13 = (f32[2,64,128]{2,1,0:T(8,128)}, f32[2,64,128]{2,1,0:T(8,128)S(1)}, u32[]{:S(2)}, u32[]{:S(2)}) collective-permute-start(f32[2,64,128]{2,1,0:T(8,128)} %get-tuple-element.157), channel_id=1, source_target_pairs={{0,14},{2,0},{4,2},{6,4},{8,6},{10,8},{12,10},{14,12},{1,15},{3,1}... | collective-permute-start | bytes 196616 | tf_op jit(solution)/shard_map/ppermute | solution.py:21
  52.6 1.4 %collective-permute-start.14 = (f32[7,8,128]{2,1,0:T(8,128)}, f32[7,8,128]{2,1,0:T(8,128)S(1)}, u32[]{:S(2)}, u32[]{:S(2)}) collective-permute-start(f32[7,8,128]{2,1,0:T(8,128)} %get-tuple-element.158), channel_id=1, source_target_pairs={{0,1},{1,0},{2,3},{3,2},{4,5},{5,4},{6,7},{7,6},{8,9},{9,8},{10,11... | collective-permute-start | bytes 86024 | tf_op jit(solution)/shard_map/ppermute | solution.py:21
  52.6 2.2 %copy-start.10 = (f32[2,64,128]{2,1,0:T(8,128)}, f32[2,64,128]{2,1,0:T(8,128)S(1)}, u32[]{:S(2)}) copy-start(f32[2,64,128]{2,1,0:T(8,128)S(1)} %collective-permute-done.13.xhi_ref) | copy-start | bytes 196612
  53.6 1.3 %copy-start.6 = (f32[5,64,128]{2,1,0:T(8,128)}, f32[5,64,128]{2,1,0:T(8,128)S(1)}, u32[]{:S(2)}) copy-start(f32[5,64,128]{2,1,0:T(8,128)S(1)} %collective-permute-done.12.xlo_ref) | copy-start | bytes 491524
  53.6 1.2 %collective-permute-start.15 = (f32[2,8,128]{2,1,0:T(8,128)S(1)}, f32[2,8,128]{2,1,0:T(8,128)S(1)}, u32[]{:S(2)}, u32[]{:S(2)}) collective-permute-start(f32[2,8,128]{2,1,0:T(8,128)S(1)} %scatter.39), channel_id=1, source_target_pairs={{0,1},{1,0},{2,3},{3,2},{4,5},{5,4},{6,7},{7,6},{8,9},{9,8},{10,11... | collective-permute-start | bytes 24584 | tf_op jit(solution)/shard_map/ppermute | solution.py:21
  54.0 0.8 %copy-start.14 = (f32[7,8,128]{2,1,0:T(8,128)}, f32[7,8,128]{2,1,0:T(8,128)S(1)}, u32[]{:S(2)}) copy-start(f32[7,8,128]{2,1,0:T(8,128)S(1)} %collective-permute-done.14.y_ref) | copy-start | bytes 86020
  54.9 0.6 copy-start.19
  58.9 0.7 copy-start.18
  58.9 0.7 copy-start.16
  58.9 0.7 copy-start.17
  59.0 0.7 copy-start.15
  59.9 4.5 %collective-permute-start.16 = (f32[32,4]{0,1:T(4,128)S(1)}, f32[32,4]{0,1:T(4,128)S(1)}, u32[]{:S(2)}, u32[]{:S(2)}) collective-permute-start(f32[32,4]{0,1:T(4,128)S(1)} %slice_select_fusion.2), channel_id=1, source_target_pairs={{0,8},{2,10},{4,12},{6,14},{8,0},{10,2},{12,4},{14,6},{1,9},{3,11}... | collective-permute-start | bytes 1544 | tf_op jit(solution)/shard_map/ppermute | solution.py:281
  64.5 3.6 %collective-permute-start.17 = (f32[16,4]{0,1:T(4,128)S(1)}, f32[16,4]{0,1:T(4,128)S(1)}, u32[]{:S(2)}, u32[]{:S(2)}) collective-permute-start(f32[16,4]{0,1:T(4,128)S(1)} %slice_select_fusion.1), channel_id=1, source_target_pairs={{0,4},{2,6},{4,0},{6,2},{8,12},{10,14},{12,8},{14,10},{1,5},{3,7},... | collective-permute-start | bytes 776 | tf_op jit(solution)/shard_map/ppermute | solution.py:281
  68.3 3.6 %collective-permute-start.18 = (f32[8,4]{0,1:T(4,128)S(1)}, f32[8,4]{0,1:T(4,128)S(1)}, u32[]{:S(2)}, u32[]{:S(2)}) collective-permute-start(f32[8,4]{0,1:T(4,128)S(1)} %slice_select_fusion), channel_id=1, source_target_pairs={{0,2},{2,0},{4,6},{6,4},{8,10},{10,8},{12,14},{14,12},{1,3},{3,1},... | collective-permute-start | bytes 392 | tf_op jit(solution)/shard_map/ppermute | solution.py:281
  71.9 1.2 %collective-permute-start.19 = (f32[8,4]{0,1:T(4,128)S(1)}, f32[8,4]{0,1:T(4,128)S(1)}, u32[]{:S(2)}, u32[]{:S(2)}) collective-permute-start(f32[8,4]{0,1:T(4,128)S(1)} %select_add_fusion), channel_id=1, source_target_pairs={{0,1},{1,0},{2,3},{3,2},{4,5},{5,4},{6,7},{7,6},{8,9},{9,8},{10,11... | collective-permute-start | bytes 392 | tf_op jit(solution)/shard_map/ppermute | solution.py:291

commit v17 on v16

--- a/solution.py
+++ b/solution.py
@@ -194,6 +194,43 @@
     xlo_out[4] = old[5]
 
 
+def _edge_first_kernel(e_first, e_second, h_first, keep_first, drive_first, xlo_ref, y_ref,
+                       corner_ref, xhi_out, *, planes):
+    c1_ref = corner_ref.at[0, 0:1]
+    c2_ref = corner_ref.at[1, 0:1]
+    yhi_ref = y_ref.at[5:7]
+    e_blocks = {0: e_first, 1: e_second}
+    elec = lambda comp, x: e_blocks[x][comp, 0]
+    magn = lambda comp, x: h_first[comp, 0]
+    hy_prev, hz_prev = _magn_before(elec, xlo_ref, c1_ref)
+    old = _magn_plane(elec, magn, 0, planes, None, yhi_ref)
+    ex_new, ey_new, ez_new = _elec_plane(
+        0, planes, old, hy_prev, hz_prev, y_ref, c2_ref, keep_first[0], drive_first[0]
+    )
+    xhi_out[0] = ey_new
+    xhi_out[1] = ez_new
+
+
+def _edge_last_kernel(e_penult, e_last, h_penult, h_last, keep_last, drive_last, xhi_ref, y_ref,
+                      corner_ref, xlo_out, *, planes):
+    c2_ref = corner_ref.at[1, 0:1]
+    yhi_ref = y_ref.at[5:7]
+    e_blocks = {planes - 2: e_penult, planes - 1: e_last}
+    h_blocks = {planes - 2: h_penult, planes - 1: h_last}
+    elec = lambda comp, x: e_blocks[x][comp, 0]
+    magn = lambda comp, x: h_blocks[x][comp, 0]
+    penult = _magn_plane(elec, magn, planes - 2, planes, xhi_ref, yhi_ref)
+    old = _magn_plane(elec, magn, planes - 1, planes, xhi_ref, yhi_ref)
+    ex_new, ey_new, ez_new = _elec_plane(
+        planes - 1, planes, old, penult[4], penult[5], y_ref, c2_ref, keep_last[0], drive_last[0]
+    )
+    xlo_out[0] = ex_new
+    xlo_out[1] = ey_new
+    xlo_out[2] = ez_new
+    xlo_out[3] = old[4]
+    xlo_out[4] = old[5]
+
+
 def _halo_kernel(e_first, e_last, h_last, e_top, e_bottom, h_bottom, xlo_out, xhi_out, y_out):
     planes = e_top.shape[1]
     slab = e_top.shape[2]
@@ -314,15 +351,21 @@
 
     first = 0
     last = cells_x - 1
-    edge_call = pl.pallas_call(
-        functools.partial(_edge_kernel, planes=cells_x),
-        out_shape=(xlo_shape, xhi_shape),
+    edge_first_call = pl.pallas_call(
+        functools.partial(_edge_first_kernel, planes=cells_x),
+        out_shape=xhi_shape,
         grid=(1,),
-        in_specs=[field_plane(i) for i in (first, 1, last - 1, last)]
-        + [field_plane(i) for i in (first, last - 1, last)]
-        + [coef_plane(first), coef_plane(last), coef_plane(first), coef_plane(last)]
-        + [whole] * 4,
-        out_specs=(whole, whole),
+        in_specs=[field_plane(first), field_plane(1), field_plane(first), coef_plane(first),
+                  coef_plane(first)] + [whole] * 3,
+        out_specs=whole,
+    )
+    edge_last_call = pl.pallas_call(
+        functools.partial(_edge_last_kernel, planes=cells_x),
+        out_shape=xlo_shape,
+        grid=(1,),
+        in_specs=[field_plane(last - 1), field_plane(last), field_plane(last - 1), field_plane(last),
+                  coef_plane(last), coef_plane(last)] + [whole] * 3,
+        out_specs=whole,
     )
     slab = 8
     slabs = cells_y // slab
@@ -352,10 +395,10 @@
     columns = [[], []]
     for number in range(ITERS):
         if number + 1 < ITERS:
-            edges = edge_call(
-                elec, elec, elec, elec, magn, magn, magn, keep, keep, drive, drive, xlo, xhi, rows, corners
+            next_xhi = shifted(edge_first_call(elec, elec, magn, keep, drive, xlo, rows, corners), "gx", -1)
+            next_xlo = shifted(
+                edge_last_call(elec, elec, magn, magn, keep, drive, xhi, rows, corners), "gx", 1
             )
-            next_xlo, next_xhi = exchange_x(*edges)
         elec, magn, new_rows, sums = step_call(elec, magn, keep, drive, xlo, xhi, rows, corners, basis)
         if number + 1 < ITERS:
             rows = exchange_y(new_rows)

time: 74.1 us -> 80.9 us (1.092)
  Pallas kernels: 24.2 us -> 29.2 us
  starting transfers between devices: 20.9 us -> 21.9 us
    pallas_call x3 -> x6, Pallas kernels: 6.4 us -> 11.4 us  [the longest x3 5.74 us: local(): edge_last_call(elec, elec, magn, magn, keep, drive, xhi, rows, corners)]
    ppermute x16, starting transfers between devices: 20.5 us -> 21.9 us  [shifted(): return lax.ppermute(value, axis, pairs)]
  transfers between devices with their start and end apart: 20 -> 20, of which waited for: 14 -> 12; matrix products, arithmetic and copies ran while one was open for 3% -> 2% of each run, Pallas kernels for 17% -> 23%
where the time goes in v17:
time: 80.9 us; the launch traced here: 80.3 us
  Pallas kernels  29.2 us (36%)
  starting transfers between devices  21.9 us (27%)
  waiting for transfers between devices  21.2 us (26%)
  local copies, waits for them, and re-layouts  4.33 us (5%)
  other arithmetic  2.72 us (3%)
  between operations  0.93 us (1%)
    ppermute x16, starting transfers between devices, shifted(): return lax.ppermute(value, axis, pairs)  21.9 us
    pallas_call x4, Pallas kernels, local(): step_call(elec, magn, keep, drive, xlo, xhi, rows, corners, basis)  14 us
    ppermute x3, waiting for transfers between devices, scatter_sum(): rows = keep + lax.ppermute(send, axis, pairs)  11.6 us
    ppermute x16, waiting for transfers between devices, shifted(): return lax.ppermute(value, axis, pairs)  8.41 us
    pallas_call x3, Pallas kernels, local(): edge_last_call(elec, elec, magn, magn, keep, drive, xhi, rows, corners)  5.74 us
    pallas_call x3, Pallas kernels, local(): edge_first_call(elec, elec, magn, keep, drive, xlo, rows, corners)  5.62 us
    unnamed x42, local copies, waits for them, and re-layouts  3.94 us
    pallas_call x1, Pallas kernels, coefficients(): pl.pallas_call(_coef_kernel, out_shape=(out, out), in_specs=[scalar, scal...  2.02 us
  transfers between devices with their start and end apart: 20, of which 12 were waited for; matrix products, arithmetic and copies ran while one was open for 2% of the time, Pallas kernels for 23%

profile of v17, /device:TPU:0, one launch (start us, length us, event | category | flops | bytes accessed | tf_op | source)
XLA Modules:
  0.0 80.3 jit_solution(5680664109920327940)
XLA Ops:
  0.6 1.9 %shard_map.86 = (f32[5,64,128]{2,1,0:T(8,128)}, f32[2,64,128]{2,1,0:T(8,128)}, f32[7,8,128]{2,1,0:T(8,128)}) custom-call(f32[3,8,64,128]{3,2,1,0:T(8,128)} %e_second.1, f32[3,8,64,128]{3,2,1,0:T(8,128)} %e_second.1, f32[3,8,64,128]{3,2,1,0:T(8,128)} %h_first.1, f32[3,8,64,128]{3,2,1,0:T(8,128)} %e_second.1, f32[3,8,64,128]{3,2,1,0:T(8,128)} %e_second.1, ...), custom_call_target="tpu_custom_call" | custom-call | tf_op jit(solution)/shard_map/pallas_call | solution.py:376
  2.5 0.5 collective-permute-start.2
  2.9 5.6 %collective-permute-start.1 = (f32[2,64,128]{2,1,0:T(8,128)}, f32[2,64,128]{2,1,0:T(8,128)S(1)}, u32[]{:S(2)}, u32[]{:S(2)}) collective-permute-start(f32[2,64,128]{2,1,0:T(8,128)} %get-tuple-element.129), channel_id=1, source_target_pairs={{0,14},{2,0},{4,2},{6,4},{8,6},{10,8},{12,10},{14,12},{1,15},{3,1}... | collective-permute-start | bytes 196616 | tf_op jit(solution)/shard_map/ppermute | solution.py:21
  8.5 0.7 copy-done.20
  9.2 0.1 multiply_multiply_fusion.1
  9.3 0.1 copy.12
  9.3 0.1 multiply_multiply_fusion
  9.4 0.1 broadcast_add_fusion
  9.6 0.1 add.227
  9.7 0.5 fusion.4
  10.2 2.0 %shard_map.85 = (f32[8,64,128]{2,1,0:T(8,128)}, f32[8,64,128]{2,1,0:T(8,128)}) custom-call(f32[6]{0:T(128)} %eps_ref.1, f32[6]{0:T(128)} %sigma_ref.1, s32[8,64,128]{2,1,0:T(8,128)} %mat_ref.1), custom_call_target="tpu_custom_call" | custom-call | tf_op jit(solution)/shard_map/pallas_call | solution.py:43
  12.2 5.5 %collective-permute-done.xlo_ref = f32[5,64,128]{2,1,0:T(8,128)S(1)} collective-permute-done((f32[5,64,128]{2,1,0:T(8,128)}, f32[5,64,128]{2,1,0:T(8,128)S(1)}, u32[]{:S(2)}, u32[]{:S(2)}) %collective-permute-start) | collective-permute-done | bytes 163872 | tf_op jit(solution)/shard_map/ppermute | solution.py:21
  17.8 0.1 collective-permute-start.3
  17.9 0.7 maximum_bitcast_fusion.basis_ref
  18.6 0.4 collective-permute-done.3.corner_ref
  19.0 0.2 copy-done.6
  19.2 0.6 copy-done.10
  19.8 1.9 %shard_map.88 = f32[5,64,128]{2,1,0:T(8,128)} custom-call(f32[3,8,64,128]{3,2,1,0:T(8,128)} %e_second.1, f32[3,8,64,128]{3,2,1,0:T(8,128)} %e_second.1, f32[3,8,64,128]{3,2,1,0:T(8,128)} %h_first.1, f32[3,8,64,128]{3,2,1,0:T(8,128)} %h_first.1, f32[8,64,128]{2,1,0:T(8,128)} %get-tuple-element.130.keep_ref.keep_last.keep_first, ...), custom_call_target="tpu_custom_call" | custom-call | tf_op jit(solution)/shard_map/pallas_call | solution.py:400
  21.7 1.9 %shard_map.89 = f32[2,64,128]{2,1,0:T(8,128)} custom-call(f32[3,8,64,128]{3,2,1,0:T(8,128)} %e_second.1, f32[3,8,64,128]{3,2,1,0:T(8,128)} %e_second.1, f32[3,8,64,128]{3,2,1,0:T(8,128)} %h_first.1, f32[8,64,128]{2,1,0:T(8,128)} %get-tuple-element.130.keep_ref.keep_last.keep_first, f32[8,64,128]{2,1,0:T(8,128)} %get-tuple-element.131.drive_ref.drive_last.drive_first, ...), custom_call_target="tpu_custom_call" | custom-call | tf_op jit(solution)/shard_map/pallas_call | solution.py:398
  23.6 4.7 %collective-permute-start.5 = (f32[2,64,128]{2,1,0:T(8,128)}, f32[2,64,128]{2,1,0:T(8,128)S(1)}, u32[]{:S(2)}, u32[]{:S(2)}) collective-permute-start(f32[2,64,128]{2,1,0:T(8,128)} %shard_map.89), channel_id=1, source_target_pairs={{0,14},{2,0},{4,2},{6,4},{8,6},{10,8},{12,10},{14,12},{1,15},{3,1}... | collective-permute-start | bytes 196616 | tf_op jit(solution)/shard_map/ppermute | solution.py:21
  28.3 3.5 %shard_map.87 = (f32[3,8,64,128]{3,2,1,0:T(8,128)}, f32[3,8,64,128]{3,2,1,0:T(8,128)}, f32[7,8,128]{2,1,0:T(8,128)}, f32[2,1,128]{2,1,0:T(1,128)}) custom-call(f32[3,8,64,128]{3,2,1,0:T(8,128)} %e_second.1, f32[3,8,64,128]{3,2,1,0:T(8,128)} %h_first.1, f32[8,64,128]{2,1,0:T(8,128)} %get-tuple-element.130.keep_ref.keep_last.keep_first, ...), custom_call_target="tpu_custom_call" | custom-call | tf_op jit(solution)/shard_map/pallas_call | solution.py:402
  31.8 0.0 collective-permute-done.5.xhi_ref
  31.9 0.5 collective-permute-start.7
  32.5 0.7 collective-permute-done.6.y_ref
  33.2 0.1 collective-permute-done.7.corner_ref
  33.3 0.5 copy-done.7
  33.8 0.1 copy-done.11
  33.9 1.9 %shard_map.91 = f32[5,64,128]{2,1,0:T(8,128)} custom-call(f32[3,8,64,128]{3,2,1,0:T(8,128)} %get-tuple-element.138.e_ref.e_penult.e_last.e_first.e_second, f32[3,8,64,128]{3,2,1,0:T(8,128)} %get-tuple-element.138.e_ref.e_penult.e_last.e_first.e_second, f32[3,8,64,128]{3,2,1,0:T(8,128)} %get-tuple-element.139.h_ref.h_penult.h_last.h_first, ...), custom_call_target="tpu_custom_call" | custom-call | tf_op jit(solution)/shard_map/pallas_call | solution.py:400
  35.8 1.9 %shard_map.92 = f32[2,64,128]{2,1,0:T(8,128)} custom-call(f32[3,8,64,128]{3,2,1,0:T(8,128)} %get-tuple-element.138.e_ref.e_penult.e_last.e_first.e_second, f32[3,8,64,128]{3,2,1,0:T(8,128)} %get-tuple-element.138.e_ref.e_penult.e_last.e_first.e_second, f32[3,8,64,128]{3,2,1,0:T(8,128)} %get-tuple-element.139.h_ref.h_penult.h_last.h_first, ...), custom_call_target="tpu_custom_call" | custom-call | tf_op jit(solution)/shard_map/pallas_call | solution.py:398
  37.7 4.7 %collective-permute-start.9 = (f32[2,64,128]{2,1,0:T(8,128)}, f32[2,64,128]{2,1,0:T(8,128)S(1)}, u32[]{:S(2)}, u32[]{:S(2)}) collective-permute-start(f32[2,64,128]{2,1,0:T(8,128)} %shard_map.92), channel_id=1, source_target_pairs={{0,14},{2,0},{4,2},{6,4},{8,6},{10,8},{12,10},{14,12},{1,15},{3,1}... | collective-permute-start | bytes 196616 | tf_op jit(solution)/shard_map/ppermute | solution.py:21
  42.4 3.5 %shard_map.90 = (f32[3,8,64,128]{3,2,1,0:T(8,128)}, f32[3,8,64,128]{3,2,1,0:T(8,128)}, f32[7,8,128]{2,1,0:T(8,128)}, f32[2,1,128]{2,1,0:T(1,128)}) custom-call(f32[3,8,64,128]{3,2,1,0:T(8,128)} %get-tuple-element.138.e_ref.e_penult.e_last.e_first.e_second, f32[3,8,64,128]{3,2,1,0:T(8,128)} %get-tuple-element.139.h_ref.h_penult.h_last.h_first, ...), custom_call_target="tpu_custom_call" | custom-call | tf_op jit(solution)/shard_map/pallas_call | solution.py:402
  46.0 0.6 collective-permute-start.11
  46.6 0.7 collective-permute-done.10.y_ref
  47.3 0.1 collective-permute-done.11.corner_ref
  47.4 0.5 copy-done.8
  47.9 0.1 copy-done.12
  48.0 1.9 %shard_map.94 = f32[5,64,128]{2,1,0:T(8,128)} custom-call(f32[3,8,64,128]{3,2,1,0:T(8,128)} %get-tuple-element.141.e_ref.e_penult.e_last.e_first.e_second, f32[3,8,64,128]{3,2,1,0:T(8,128)} %get-tuple-element.141.e_ref.e_penult.e_last.e_first.e_second, f32[3,8,64,128]{3,2,1,0:T(8,128)} %get-tuple-element.142.h_ref.h_penult.h_last.h_first, ...), custom_call_target="tpu_custom_call" | custom-call | tf_op jit(solution)/shard_map/pallas_call | solution.py:400
  49.9 1.9 %shard_map.95 = f32[2,64,128]{2,1,0:T(8,128)} custom-call(f32[3,8,64,128]{3,2,1,0:T(8,128)} %get-tuple-element.141.e_ref.e_penult.e_last.e_first.e_second, f32[3,8,64,128]{3,2,1,0:T(8,128)} %get-tuple-element.141.e_ref.e_penult.e_last.e_first.e_second, f32[3,8,64,128]{3,2,1,0:T(8,128)} %get-tuple-element.142.h_ref.h_penult.h_last.h_first, ...), custom_call_target="tpu_custom_call" | custom-call | tf_op jit(solution)/shard_map/pallas_call | solution.py:398
  51.8 4.7 %collective-permute-start.13 = (f32[2,64,128]{2,1,0:T(8,128)}, f32[2,64,128]{2,1,0:T(8,128)S(1)}, u32[]{:S(2)}, u32[]{:S(2)}) collective-permute-start(f32[2,64,128]{2,1,0:T(8,128)} %shard_map.95), channel_id=1, source_target_pairs={{0,14},{2,0},{4,2},{6,4},{8,6},{10,8},{12,10},{14,12},{1,15},{3,1}... | collective-permute-start | bytes 196616 | tf_op jit(solution)/shard_map/ppermute | solution.py:21
  56.5 3.5 %shard_map.93 = (f32[3,8,64,128]{3,2,1,0:T(8,128)}, f32[3,8,64,128]{3,2,1,0:T(8,128)}, f32[7,8,128]{2,1,0:T(8,128)}, f32[2,1,128]{2,1,0:T(1,128)}) custom-call(f32[3,8,64,128]{3,2,1,0:T(8,128)} %get-tuple-element.141.e_ref.e_penult.e_last.e_first.e_second, f32[3,8,64,128]{3,2,1,0:T(8,128)} %get-tuple-element.142.h_ref.h_penult.h_last.h_first, ...), custom_call_target="tpu_custom_call" | custom-call | tf_op jit(solution)/shard_map/pallas_call | solution.py:402
  60.1 0.6 collective-permute-start.15
  60.7 0.7 collective-permute-done.14.y_ref
  61.5 0.1 collective-permute-done.15.corner_ref
  61.5 0.5 copy-done.14
  62.1 0.1 copy-done.19
  62.1 3.5 %shard_map.96 = (f32[3,8,64,128]{3,2,1,0:T(8,128)}, f32[3,8,64,128]{3,2,1,0:T(8,128)}, f32[7,8,128]{2,1,0:T(8,128)}, f32[2,1,128]{2,1,0:T(1,128)}) custom-call(f32[3,8,64,128]{3,2,1,0:T(8,128)} %get-tuple-element.144.e_ref, f32[3,8,64,128]{3,2,1,0:T(8,128)} %get-tuple-element.145.h_ref, f32[8,64,128]{2,1,0:T(8,128)} %get-tuple-element.130.keep_ref.keep_last.keep_first, ...), custom_call_target="tpu_custom_call" | custom-call | tf_op jit(solution)/shard_map/pallas_call | solution.py:402
  65.6 0.6 copy-done.18
  66.2 0.0 copy-done.16
  66.3 0.0 copy-done.17
  66.3 0.0 copy-done.15
  66.3 0.1 add_bitcast_fusion.3
  66.4 0.1 add_bitcast_fusion.2
  66.5 0.1 slice_select_fusion.2
  66.6 0.0 collective-permute-start.16
  66.6 4.5 %collective-permute-done.16 = f32[32,4]{0,1:T(4,128)S(1)} collective-permute-done((f32[32,4]{0,1:T(4,128)S(1)}, f32[32,4]{0,1:T(4,128)S(1)}, u32[]{:S(2)}, u32[]{:S(2)}) %collective-permute-start.16) | collective-permute-done | bytes 544 | tf_op jit(solution)/shard_map/ppermute | solution.py:318
  71.1 0.1 select_add_fusion.2
  71.1 0.1 slice_select_fusion.1
  71.2 3.6 %collective-permute-done.17 = f32[16,4]{0,1:T(4,128)S(1)} collective-permute-done((f32[16,4]{0,1:T(4,128)S(1)}, f32[16,4]{0,1:T(4,128)S(1)}, u32[]{:S(2)}, u32[]{:S(2)}) %collective-permute-start.17) | collective-permute-done | bytes 288 | tf_op jit(solution)/shard_map/ppermute | solution.py:318
  74.8 0.1 select_add_fusion.1
  74.9 0.1 slice_select_fusion
  74.9 3.6 %collective-permute-done.18 = f32[8,4]{0,1:T(4,128)S(1)} collective-permute-done((f32[8,4]{0,1:T(4,128)S(1)}, f32[8,4]{0,1:T(4,128)S(1)}, u32[]{:S(2)}, u32[]{:S(2)}) %collective-permute-start.18) | collective-permute-done | bytes 160 | tf_op jit(solution)/shard_map/ppermute | solution.py:318
  78.5 0.1 select_add_fusion
  78.6 1.2 %collective-permute-done.19 = f32[8,4]{0,1:T(4,128)S(1)} collective-permute-done((f32[8,4]{0,1:T(4,128)S(1)}, f32[8,4]{0,1:T(4,128)S(1)}, u32[]{:S(2)}, u32[]{:S(2)}) %collective-permute-start.19) | collective-permute-done | bytes 160 | tf_op jit(solution)/shard_map/ppermute | solution.py:328
  79.8 0.6 add_multiply_fusion
  (66 shorter events, 0.3 us)
Async XLA Ops:
  2.5 16.1 %collective-permute-start.2 = (f32[7,8,128]{2,1,0:T(8,128)}, f32[7,8,128]{2,1,0:T(8,128)S(1)}, u32[]{:S(2)}, u32[]{:S(2)}) collective-permute-start(f32[7,8,128]{2,1,0:T(8,128)} %get-tuple-element.134), channel_id=1, source_target_pairs={{0,1},{1,0},{2,3},{3,2},{4,5},{5,4},{6,7},{7,6},{8,9},{9,8},{10,11... | collective-permute-start | bytes 86024 | tf_op jit(solution)/shard_map/ppermute | solution.py:21
  2.9 9.3 %collective-permute-start.1 = (f32[2,64,128]{2,1,0:T(8,128)}, f32[2,64,128]{2,1,0:T(8,128)S(1)}, u32[]{:S(2)}, u32[]{:S(2)}) collective-permute-start(f32[2,64,128]{2,1,0:T(8,128)} %get-tuple-element.129), channel_id=1, source_target_pairs={{0,14},{2,0},{4,2},{6,4},{8,6},{10,8},{12,10},{14,12},{1,15},{3,1}... | collective-permute-start | bytes 196616 | tf_op jit(solution)/shard_map/ppermute | solution.py:21
  8.5 9.2 %collective-permute-start = (f32[5,64,128]{2,1,0:T(8,128)}, f32[5,64,128]{2,1,0:T(8,128)S(1)}, u32[]{:S(2)}, u32[]{:S(2)}) collective-permute-start(f32[5,64,128]{2,1,0:T(8,128)} %get-tuple-element.128), channel_id=1, source_target_pairs={{0,2},{2,4},{4,6},{6,8},{8,10},{10,12},{12,14},{14,0},{1,3},{3,5},... | collective-permute-start | bytes 491528 | tf_op jit(solution)/shard_map/ppermute | solution.py:21
  8.5 0.7 copy-start.20
  12.2 6.4 %copy-start.3 = (f32[2,64,128]{2,1,0:T(8,128)}, f32[2,64,128]{2,1,0:T(8,128)S(1)}, u32[]{:S(2)}) copy-start(f32[2,64,128]{2,1,0:T(8,128)S(1)} %collective-permute-done.1.xhi_ref) | copy-start | bytes 196612
  17.7 0.9 %copy-start = (f32[5,64,128]{2,1,0:T(8,128)}, f32[5,64,128]{2,1,0:T(8,128)S(1)}, u32[]{:S(2)}) copy-start(f32[5,64,128]{2,1,0:T(8,128)S(1)} %collective-permute-done.xlo_ref) | copy-start | bytes 491524
  17.8 1.2 %collective-permute-start.3 = (f32[2,8,128]{2,1,0:T(8,128)S(1)}, f32[2,8,128]{2,1,0:T(8,128)S(1)}, u32[]{:S(2)}, u32[]{:S(2)}) collective-permute-start(f32[2,8,128]{2,1,0:T(8,128)S(1)} %scatter.29), channel_id=1, source_target_pairs={{0,1},{1,0},{2,3},{3,2},{4,5},{5,4},{6,7},{7,6},{8,9},{9,8},{10,11... | collective-permute-start | bytes 24584 | tf_op jit(solution)/shard_map/ppermute | solution.py:21
  18.6 0.6 copy-start.6
  19.2 0.6 copy-start.10
  21.7 10.1 %collective-permute-start.4 = (f32[5,64,128]{2,1,0:T(8,128)}, f32[5,64,128]{2,1,0:T(8,128)S(1)}, u32[]{:S(2)}, u32[]{:S(2)}) collective-permute-start(f32[5,64,128]{2,1,0:T(8,128)} %shard_map.88), channel_id=1, source_target_pairs={{0,2},{2,4},{4,6},{6,8},{8,10},{10,12},{12,14},{14,0},{1,3},{3,5},... | collective-permute-start | bytes 491528 | tf_op jit(solution)/shard_map/ppermute | solution.py:21
  23.6 8.2 %collective-permute-start.5 = (f32[2,64,128]{2,1,0:T(8,128)}, f32[2,64,128]{2,1,0:T(8,128)S(1)}, u32[]{:S(2)}, u32[]{:S(2)}) collective-permute-start(f32[2,64,128]{2,1,0:T(8,128)} %shard_map.89), channel_id=1, source_target_pairs={{0,14},{2,0},{4,2},{6,4},{8,6},{10,8},{12,10},{14,12},{1,15},{3,1}... | collective-permute-start | bytes 196616 | tf_op jit(solution)/shard_map/ppermute | solution.py:21
  31.8 1.4 %collective-permute-start.6 = (f32[7,8,128]{2,1,0:T(8,128)}, f32[7,8,128]{2,1,0:T(8,128)S(1)}, u32[]{:S(2)}, u32[]{:S(2)}) collective-permute-start(f32[7,8,128]{2,1,0:T(8,128)} %get-tuple-element.140), channel_id=1, source_target_pairs={{0,1},{1,0},{2,3},{3,2},{4,5},{5,4},{6,7},{7,6},{8,9},{9,8},{10,11... | collective-permute-start | bytes 86024 | tf_op jit(solution)/shard_map/ppermute | solution.py:21
  31.8 1.5 %copy-start.5 = (f32[2,64,128]{2,1,0:T(8,128)}, f32[2,64,128]{2,1,0:T(8,128)S(1)}, u32[]{:S(2)}) copy-start(f32[2,64,128]{2,1,0:T(8,128)S(1)} %collective-permute-done.5.xhi_ref) | copy-start | bytes 196612
  31.8 4.0 %copy-start.2 = (f32[5,64,128]{2,1,0:T(8,128)}, f32[5,64,128]{2,1,0:T(8,128)S(1)}, u32[]{:S(2)}) copy-start(f32[5,64,128]{2,1,0:T(8,128)S(1)} %collective-permute-done.4.xlo_ref) | copy-start | bytes 491524
  31.9 1.4 %collective-permute-start.7 = (f32[2,8,128]{2,1,0:T(8,128)S(1)}, f32[2,8,128]{2,1,0:T(8,128)S(1)}, u32[]{:S(2)}, u32[]{:S(2)}) collective-permute-start(f32[2,8,128]{2,1,0:T(8,128)S(1)} %scatter.31), channel_id=1, source_target_pairs={{0,1},{1,0},{2,3},{3,2},{4,5},{5,4},{6,7},{7,6},{8,9},{9,8},{10,11... | collective-permute-start | bytes 24584 | tf_op jit(solution)/shard_map/ppermute | solution.py:21
  33.2 0.6 copy-start.7
  33.3 0.6 copy-start.11
  35.8 10.1 %collective-permute-start.8 = (f32[5,64,128]{2,1,0:T(8,128)}, f32[5,64,128]{2,1,0:T(8,128)S(1)}, u32[]{:S(2)}, u32[]{:S(2)}) collective-permute-start(f32[5,64,128]{2,1,0:T(8,128)} %shard_map.91), channel_id=1, source_target_pairs={{0,2},{2,4},{4,6},{6,8},{8,10},{10,12},{12,14},{14,0},{1,3},{3,5},... | collective-permute-start | bytes 491528 | tf_op jit(solution)/shard_map/ppermute | solution.py:21
  37.7 8.2 %collective-permute-start.9 = (f32[2,64,128]{2,1,0:T(8,128)}, f32[2,64,128]{2,1,0:T(8,128)S(1)}, u32[]{:S(2)}, u32[]{:S(2)}) collective-permute-start(f32[2,64,128]{2,1,0:T(8,128)} %shard_map.92), channel_id=1, source_target_pairs={{0,14},{2,0},{4,2},{6,4},{8,6},{10,8},{12,10},{14,12},{1,15},{3,1}... | collective-permute-start | bytes 196616 | tf_op jit(solution)/shard_map/ppermute | solution.py:21
  45.9 1.4 %collective-permute-start.10 = (f32[7,8,128]{2,1,0:T(8,128)}, f32[7,8,128]{2,1,0:T(8,128)S(1)}, u32[]{:S(2)}, u32[]{:S(2)}) collective-permute-start(f32[7,8,128]{2,1,0:T(8,128)} %get-tuple-element.143), channel_id=1, source_target_pairs={{0,1},{1,0},{2,3},{3,2},{4,5},{5,4},{6,7},{7,6},{8,9},{9,8},{10,11... | collective-permute-start | bytes 86024 | tf_op jit(solution)/shard_map/ppermute | solution.py:21
  45.9 1.5 %copy-start.4 = (f32[2,64,128]{2,1,0:T(8,128)}, f32[2,64,128]{2,1,0:T(8,128)S(1)}, u32[]{:S(2)}) copy-start(f32[2,64,128]{2,1,0:T(8,128)S(1)} %collective-permute-done.9.xhi_ref) | copy-start | bytes 196612
  45.9 4.0 %copy-start.1 = (f32[5,64,128]{2,1,0:T(8,128)}, f32[5,64,128]{2,1,0:T(8,128)S(1)}, u32[]{:S(2)}) copy-start(f32[5,64,128]{2,1,0:T(8,128)S(1)} %collective-permute-done.8.xlo_ref) | copy-start | bytes 491524
  46.0 1.4 %collective-permute-start.11 = (f32[2,8,128]{2,1,0:T(8,128)S(1)}, f32[2,8,128]{2,1,0:T(8,128)S(1)}, u32[]{:S(2)}, u32[]{:S(2)}) collective-permute-start(f32[2,8,128]{2,1,0:T(8,128)S(1)} %scatter.35), channel_id=1, source_target_pairs={{0,1},{1,0},{2,3},{3,2},{4,5},{5,4},{6,7},{7,6},{8,9},{9,8},{10,11... | collective-permute-start | bytes 24584 | tf_op jit(solution)/shard_map/ppermute | solution.py:21
  47.3 0.6 copy-start.8
  47.4 0.6 copy-start.12
  49.9 10.2 %collective-permute-start.12 = (f32[5,64,128]{2,1,0:T(8,128)}, f32[5,64,128]{2,1,0:T(8,128)S(1)}, u32[]{:S(2)}, u32[]{:S(2)}) collective-permute-start(f32[5,64,128]{2,1,0:T(8,128)} %shard_map.94), channel_id=1, source_target_pairs={{0,2},{2,4},{4,6},{6,8},{8,10},{10,12},{12,14},{14,0},{1,3},{3,5},... | collective-permute-start | bytes 491528 | tf_op jit(solution)/shard_map/ppermute | solution.py:21
  51.8 8.2 %collective-permute-start.13 = (f32[2,64,128]{2,1,0:T(8,128)}, f32[2,64,128]{2,1,0:T(8,128)S(1)}, u32[]{:S(2)}, u32[]{:S(2)}) collective-permute-start(f32[2,64,128]{2,1,0:T(8,128)} %shard_map.95), channel_id=1, source_target_pairs={{0,14},{2,0},{4,2},{6,4},{8,6},{10,8},{12,10},{14,12},{1,15},{3,1}... | collective-permute-start | bytes 196616 | tf_op jit(solution)/shard_map/ppermute | solution.py:21
  60.0 1.4 %collective-permute-start.14 = (f32[7,8,128]{2,1,0:T(8,128)}, f32[7,8,128]{2,1,0:T(8,128)S(1)}, u32[]{:S(2)}, u32[]{:S(2)}) collective-permute-start(f32[7,8,128]{2,1,0:T(8,128)} %get-tuple-element.146), channel_id=1, source_target_pairs={{0,1},{1,0},{2,3},{3,2},{4,5},{5,4},{6,7},{7,6},{8,9},{9,8},{10,11... | collective-permute-start | bytes 86024 | tf_op jit(solution)/shard_map/ppermute | solution.py:21
  60.0 1.5 %copy-start.13 = (f32[2,64,128]{2,1,0:T(8,128)}, f32[2,64,128]{2,1,0:T(8,128)S(1)}, u32[]{:S(2)}) copy-start(f32[2,64,128]{2,1,0:T(8,128)S(1)} %collective-permute-done.13.xhi_ref) | copy-start | bytes 196612
  60.1 1.5 %copy-start.9 = (f32[5,64,128]{2,1,0:T(8,128)}, f32[5,64,128]{2,1,0:T(8,128)S(1)}, u32[]{:S(2)}) copy-start(f32[5,64,128]{2,1,0:T(8,128)S(1)} %collective-permute-done.12.xlo_ref) | copy-start | bytes 491524
  60.1 1.4 %collective-permute-start.15 = (f32[2,8,128]{2,1,0:T(8,128)S(1)}, f32[2,8,128]{2,1,0:T(8,128)S(1)}, u32[]{:S(2)}, u32[]{:S(2)}) collective-permute-start(f32[2,8,128]{2,1,0:T(8,128)S(1)} %scatter.39), channel_id=1, source_target_pairs={{0,1},{1,0},{2,3},{3,2},{4,5},{5,4},{6,7},{7,6},{8,9},{9,8},{10,11... | collective-permute-start | bytes 24584 | tf_op jit(solution)/shard_map/ppermute | solution.py:21
  61.5 0.6 copy-start.14
  61.5 0.6 copy-start.19
  65.6 0.6 copy-start.18
  65.6 0.6 copy-start.16
  65.6 0.7 copy-start.17
  65.6 0.7 copy-start.15
  66.6 4.5 %collective-permute-start.16 = (f32[32,4]{0,1:T(4,128)S(1)}, f32[32,4]{0,1:T(4,128)S(1)}, u32[]{:S(2)}, u32[]{:S(2)}) collective-permute-start(f32[32,4]{0,1:T(4,128)S(1)} %slice_select_fusion.2), channel_id=1, source_target_pairs={{0,8},{2,10},{4,12},{6,14},{8,0},{10,2},{12,4},{14,6},{1,9},{3,11}... | collective-permute-start | bytes 1544 | tf_op jit(solution)/shard_map/ppermute | solution.py:318
  71.2 3.6 %collective-permute-start.17 = (f32[16,4]{0,1:T(4,128)S(1)}, f32[16,4]{0,1:T(4,128)S(1)}, u32[]{:S(2)}, u32[]{:S(2)}) collective-permute-start(f32[16,4]{0,1:T(4,128)S(1)} %slice_select_fusion.1), channel_id=1, source_target_pairs={{0,4},{2,6},{4,0},{6,2},{8,12},{10,14},{12,8},{14,10},{1,5},{3,7},... | collective-permute-start | bytes 776 | tf_op jit(solution)/shard_map/ppermute | solution.py:318
  74.9 3.6 %collective-permute-start.18 = (f32[8,4]{0,1:T(4,128)S(1)}, f32[8,4]{0,1:T(4,128)S(1)}, u32[]{:S(2)}, u32[]{:S(2)}) collective-permute-start(f32[8,4]{0,1:T(4,128)S(1)} %slice_select_fusion), channel_id=1, source_target_pairs={{0,2},{2,0},{4,6},{6,4},{8,10},{10,8},{12,14},{14,12},{1,3},{3,1},... | collective-permute-start | bytes 392 | tf_op jit(solution)/shard_map/ppermute | solution.py:318
  78.6 1.2 %collective-permute-start.19 = (f32[8,4]{0,1:T(4,128)S(1)}, f32[8,4]{0,1:T(4,128)S(1)}, u32[]{:S(2)}, u32[]{:S(2)}) collective-permute-start(f32[8,4]{0,1:T(4,128)S(1)} %select_add_fusion), channel_id=1, source_target_pairs={{0,1},{1,0},{2,3},{3,2},{4,5},{5,4},{6,7},{7,6},{8,9},{9,8},{10,11... | collective-permute-start | bytes 392 | tf_op jit(solution)/shard_map/ppermute | solution.py:328
